TPU v7x, 32 devices: a whole 2x2x4 slice. The times are simulated.
32 devices in a mesh: seq: 8 (over y, x, core), ch: 4 (over z).
Axes of the slice: x: 2, y: 2, z: 4, core: 2. Of those that a mesh axis runs over, the one named last changes fastest.
Arguments:
- inputs: bfloat16 [4096, 2048], P('seq', 'ch'), may hold values from -6 to 6
- gate_in: float32 [2048], P('ch'), may hold values from 0.25 to 2
- gate_out: float32 [2048], P('ch'), may hold values from 0.25 to 2
- first_blocks: bfloat16 [8, 512, 512], P('seq'), may hold values from -0.25 to 0.25
- second_blocks: bfloat16 [512, 8, 8], P('seq'), may hold values from -2 to 2
- channel_blocks: bfloat16 [4, 512, 512], P('ch'), may hold values from -0.25 to 0.25
- group_mix: bfloat16 [512, 4, 4], replicated, may hold values from -3 to 3
- cotangent: bfloat16 [4096, 2048], P('seq', 'ch'), may hold values from -6 to 6
Outputs:
- outputs: bfloat16 [4096, 2048], P('seq', 'ch')
- input_grad: bfloat16 [4096, 2048], P('seq', 'ch')
- channel_grad: float32 [4, 512, 512], P('ch', 'seq')
- block_grad: float32 [8, 512, 512], P('seq', 'ch')
All inputs are finite; a program needn't handle non-finite values.
Results may differ from a plain program's by a relative error of at most 0.0072.
Values may be sent and summed in bfloat16 or wider, within the bound.
No kernel may reach another device: no remote copies, remote signals or barrier semaphores. Data moves between devices by JAX's collectives and lax.ppermute only.
A program may use at most 64 MiB of HBM per device.

v0:
```python
import jax
import jax.numpy as jnp
from jax import lax
from jax.sharding import PartitionSpec as P

F32 = jnp.float32
BF16 = jnp.bfloat16
RING_LIMIT = 16


def to_shift_order(x, me, n, axis=0):
    return jnp.take(x, (me + jnp.arange(n)) % n, axis=axis)


def to_source_order(x, me, n, axis=0):
    return jnp.take(x, (me - jnp.arange(n)) % n, axis=axis)


def exchange(pieces, axis_name):
    n = pieces.shape[0]
    if n > RING_LIMIT:
        me = lax.axis_index(axis_name)
        by_target = jnp.take(pieces, (jnp.arange(n) - me) % n, axis=0)
        arrived = lax.all_to_all(by_target, axis_name, 0, 0, tiled=True)
        return to_source_order(arrived, me, n)
    got = [pieces[0]]
    for k in range(1, n):
        got.append(lax.ppermute(pieces[k], axis_name, [(i, (i + k) % n) for i in range(n)]))
    return jnp.stack(got)


def swap(pieces, axis_name):
    return lax.all_to_all(pieces, axis_name, 0, 0, tiled=True)


def split_rows(x, n):
    return x.reshape(n, x.shape[0] // n, *x.shape[1:])


def on_device(
    inputs, gate_in, gate_out, first_blocks, second_blocks, channel_blocks, group_mix, cotangent
):
    n = lax.axis_size("seq")
    m = lax.axis_size("ch")
    s_me = lax.axis_index("seq")
    g_me = lax.axis_index("ch")
    rows, width = inputs.shape
    length_q = first_blocks.shape[1]
    block_width = channel_blocks.shape[1]
    kq = block_width // m

    mix_f = group_mix.astype(F32)
    mix_mine = lax.dynamic_slice_in_dim(mix_f, g_me * kq, kq, 0)
    plus_m = (g_me + jnp.arange(m)) % m
    minus_m = (g_me - jnp.arange(m)) % m
    mix_fwd = jnp.take(jnp.take(mix_mine, minus_m, axis=1), plus_m, axis=2)
    mix_bwd = jnp.take(jnp.take(mix_mine, plus_m, axis=1), minus_m, axis=2)

    second_f = second_blocks.astype(F32)

    upstream = cotangent
    cot_pieces = to_shift_order(upstream.reshape(rows, m, kq), g_me, m, axis=1)
    cot_arrived = exchange(jnp.transpose(cot_pieces, (1, 0, 2)), "ch")
    act_grad_out = jnp.einsum(
        "krq,qpk->prq", cot_arrived.astype(F32), mix_bwd
    ).astype(BF16)
    act_grad_back = to_source_order(exchange(act_grad_out, "ch"), g_me, m)
    act_grad = jnp.transpose(act_grad_back, (1, 0, 2)).reshape(rows, block_width)

    source = inputs.astype(F32)
    slope_in = jax.nn.sigmoid(gate_in * source)
    gated = (source * slope_in).astype(BF16)
    mixed_first = jnp.dot(first_blocks[0], gated, preferred_element_type=F32).astype(BF16)
    first_arrived = swap(split_rows(mixed_first, n), "seq")
    second_out = jnp.einsum(
        "cea,acd->ecd", second_f, first_arrived.astype(F32)
    ).astype(BF16)
    returned = swap(second_out, "seq").reshape(rows, width).astype(F32)
    slope_out = jax.nn.sigmoid(gate_out * source)
    hidden = (source + returned * slope_out).astype(BF16)
    pre_act = jnp.dot(hidden, channel_blocks[0], preferred_element_type=F32)
    activated = jax.nn.gelu(pre_act).astype(BF16)

    act_pieces = to_shift_order(activated.reshape(rows, m, kq), g_me, m, axis=1)
    act_arrived = exchange(jnp.transpose(act_pieces, (1, 0, 2)), "ch")
    added_out = jnp.einsum("krq,qkp->prq", act_arrived.astype(F32), mix_fwd)
    added_back = to_source_order(exchange(added_out, "ch"), g_me, m)
    added = jnp.transpose(added_back, (1, 0, 2)).reshape(rows, block_width)
    outputs = (hidden.astype(F32) + added).astype(BF16)

    pre_grad = jax.vjp(jax.nn.gelu, pre_act)[1](act_grad.astype(F32))[0].astype(BF16)
    back_term = jnp.dot(pre_grad, channel_blocks[0].T, preferred_element_type=F32)
    hidden_grad = (upstream.astype(F32) + back_term).astype(BF16)
    channel_part = jnp.dot(hidden.T, pre_grad, preferred_element_type=F32)
    channel_arrived = swap(split_rows(channel_part, n), "seq")
    channel_grad = jnp.sum(channel_arrived, axis=0)[None]

    grad_flat = hidden_grad.astype(F32)
    gated_grad = (grad_flat * slope_out).astype(BF16)
    grad_arrived = swap(split_rows(gated_grad, n), "seq")
    first_out = jnp.einsum(
        "cea,ecd->acd", second_f, grad_arrived.astype(F32)
    ).astype(BF16)
    first_grad = swap(first_out, "seq").reshape(rows, width)
    block_part = jnp.dot(first_grad, gated.T, preferred_element_type=F32)
    block_arrived = exchange(to_shift_order(split_rows(block_part, m), g_me, m), "ch")
    block_grad = jnp.sum(block_arrived, axis=0)[None]

    spread = jnp.dot(first_blocks[0].T, first_grad, preferred_element_type=F32)
    input_grad = grad_flat + spread * (slope_in + gate_in * source * slope_in * (1.0 - slope_in))
    input_grad = input_grad + grad_flat * returned * slope_out * (1.0 - slope_out) * gate_out
    return (outputs, input_grad.astype(BF16), channel_grad, block_grad)


def solution(mesh):
    placed = (
        P("seq", "ch"),
        P("ch"),
        P("ch"),
        P("seq", None, None),
        P("seq", None, None),
        P("ch", None, None),
        P(),
        P("seq", "ch"),
    )
    return jax.shard_map(
        on_device,
        mesh=mesh,
        in_specs=placed,
        out_specs=(P("seq", "ch"), P("seq", "ch"), P("ch", "seq", None), P("seq", "ch", None)),
        check_vma=False,
    )
```

profile of v0, /device:TPU:0, one launch (start us, length us, event | category | flops | bytes accessed | tf_op | source)
XLA Modules:
  0.0 156.6 jit_solution(11519399410026222417)
XLA Ops:
  0.7 1.3 copy.221
  2.8 0.6 gather_fusion.8
  4.2 0.8 fusion.72
  5.1 5.1 %collective-permute-start.8 = (bf16[512,128]{1,0:T(8,128)(2,1)S(1)}, bf16[512,128]{1,0:T(8,128)(2,1)S(1)}, u32[]{:S(2)}, u32[]{:S(2)}) collective-permute-start(bf16[512,128]{1,0:T(8,128)(2,1)S(1)} %bitcast.149), channel_id=1, source_target_pairs={{0,3},{1,0},{2,1},{3,2},{4,7},{5,4},{6,5},{7,6},{8,11},{9,8},{10,9... | collective-permute-start | bytes 393224 | tf_op jit(solution)/shard_map/ppermute | solution.py:28
  10.7 1.1 collective-permute-start.6
  12.0 2.8 %convolution_convert_fusion.3 = bf16[512,512]{0,1:T(8,128)(2,1)} fusion(bf16[1,512,512]{2,1,0:T(8,128)(2,1)} %param.17, bf16[512,512]{0,1:T(8,128)(2,1)S(1)} %copy.203, f32[512]{0:T(512)S(1)} %copy-done.20), kind=kOutput, calls=%fused_computation.26 | convolution fusion | flops 270532608 | bytes 1574912 | tf_op jit(solution)/shard_map/dot_general | solution.py:73
  14.8 3.7 %all-to-all-start = ((bf16[8,64,512]{2,1,0:T(8,128)(2,1)}), bf16[8,64,512]{2,1,0:T(8,128)(2,1)S(1)}, u32[]{:S(2)}, u32[]{:S(2)}) async-start(bf16[8,64,512]{2,1,0:T(8,128)(2,1)} %bitcast.2), calls=%async_computation | async-start | bytes 1048576 | tf_op jit(solution)/shard_map/all_to_all | solution.py:33
  18.5 0.7 dynamic-slice_convert_fusion
  19.2 0.6 gather_fusion.6
  19.9 0.6 gather_fusion.3
  20.5 0.6 gather_fusion.7
  21.1 0.6 gather_fusion.4
  23.3 1.3 fusion.7
  24.6 3.6 %all-to-all-done = bf16[8,64,512]{2,1,0:T(8,128)(2,1)S(1)} async-done(((bf16[8,64,512]{2,1,0:T(8,128)(2,1)}), bf16[8,64,512]{2,1,0:T(8,128)(2,1)S(1)}, u32[]{:S(2)}, u32[]{:S(2)}) %all-to-all-start) | async-done | bytes 524320 | tf_op jit(solution)/shard_map/all_to_all | solution.py:33
  28.7 0.9 copy.206
  29.7 3.5 %all-to-all-start.1 = ((bf16[8,64,512]{2,1,0:T(8,128)(2,1)}), bf16[8,64,512]{2,1,0:T(8,128)(2,1)S(1)}, u32[]{:S(2)}, u32[]{:S(2)}) async-start(bf16[8,64,512]{2,1,0:T(8,128)(2,1)} %copy.206), calls=%async_computation.1 | async-start | bytes 1048576 | tf_op jit(solution)/shard_map/all_to_all | solution.py:33
  33.2 0.8 fusion.71
  34.1 2.9 %collective-permute-start.11 = (bf16[512,128]{1,0:T(8,128)(2,1)S(1)}, bf16[512,128]{1,0:T(8,128)(2,1)S(1)}, u32[]{:S(2)}, u32[]{:S(2)}) collective-permute-start(bf16[512,128]{1,0:T(8,128)(2,1)S(1)} %bitcast.159), channel_id=1, source_target_pairs={{0,3},{1,0},{2,1},{3,2},{4,7},{5,4},{6,5},{7,6},{8,11},{9,8},{10,9... | collective-permute-start | bytes 393224 | tf_op jit(solution)/shard_map/ppermute | solution.py:28
  37.2 1.2 collective-permute-start.10
  38.5 0.6 collective-permute-start.9
  39.2 0.8 copy.217
  40.0 0.8 collective-permute-done.11
  41.0 9.3 %collective-permute-done.10 = bf16[512,128]{1,0:T(8,128)(2,1)S(1)} collective-permute-done((bf16[512,128]{1,0:T(8,128)(2,1)S(1)}, bf16[512,128]{1,0:T(8,128)(2,1)S(1)}, u32[]{:S(2)}, u32[]{:S(2)}) %collective-permute-start.10) | collective-permute-done | bytes 131104 | tf_op jit(solution)/shard_map/ppermute | solution.py:28
  50.7 1.2 pad_maximum_fusion.1
  52.4 0.6 gather_fusion.1
  53.0 1.0 copy.240
  54.9 1.8 %fusion.30 = bf16[512,512]{0,1:T(8,128)(2,1)S(1)} fusion(bf16[512,512]{0,1:T(8,128)(2,1)} %copy-done.3, f32[512,512]{0,1:T(8,128)S(1)} %copy.207, f32[512]{0:T(512)S(1)} %copy-done.16), kind=kLoop, calls=%fused_computation.55 | loop fusion | flops 2097152 | bytes 2099200 | tf_op jit(solution)/shard_map/convert_element_type | solution.py:80
  56.8 1.2 fusion.20
  58.2 0.7 gather_fusion.5
  59.6 1.4 fusion.73
  61.1 0.8 copy.213
  62.1 1.7 %collective-permute-start.1 = (bf16[512,128]{1,0:T(8,128)(2,1)S(1)}, bf16[512,128]{1,0:T(8,128)(2,1)}, u32[]{:S(2)}, u32[]{:S(2)}) collective-permute-start(bf16[512,128]{1,0:T(8,128)(2,1)S(1)} %bitcast.158), channel_id=1, source_target_pairs={{0,2},{1,3},{2,0},{3,1},{4,6},{5,7},{6,4},{7,5},{8,10},{9,11},{10,... | collective-permute-start | bytes 393224 | tf_op jit(solution)/shard_map/ppermute | solution.py:28
  63.7 0.8 copy.211
  64.6 2.0 %collective-permute-start = (bf16[512,128]{1,0:T(8,128)(2,1)}, bf16[512,128]{1,0:T(8,128)(2,1)}, u32[]{:S(2)}, u32[]{:S(2)}) collective-permute-start(bf16[512,128]{1,0:T(8,128)(2,1)} %bitcast.12), channel_id=1, source_target_pairs={{0,1},{1,2},{2,3},{3,0},{4,5},{5,6},{6,7},{7,4},{8,9},{9,10},{10,1... | collective-permute-start | bytes 393224 | tf_op jit(solution)/shard_map/ppermute | solution.py:28
  66.6 1.4 fusion.21
  68.0 1.0 copy.242
  69.0 4.2 %all-to-all-start.2 = ((bf16[8,64,512]{2,1,0:T(8,128)(2,1)}), bf16[8,64,512]{2,1,0:T(8,128)(2,1)}, u32[]{:S(2)}, u32[]{:S(2)}) async-start(bf16[8,64,512]{2,1,0:T(8,128)(2,1)} %bitcast.49), calls=%async_computation.2 | async-start | bytes 1048576 | tf_op jit(solution)/shard_map/all_to_all | solution.py:33
  73.3 2.6 %collective-permute-done.1 = bf16[512,128]{1,0:T(8,128)(2,1)} collective-permute-done((bf16[512,128]{1,0:T(8,128)(2,1)S(1)}, bf16[512,128]{1,0:T(8,128)(2,1)}, u32[]{:S(2)}, u32[]{:S(2)}) %collective-permute-start.1) | collective-permute-done | bytes 131104 | tf_op jit(solution)/shard_map/ppermute | solution.py:28
  75.9 1.1 copy.215
  77.0 1.1 copy.214
  78.1 2.3 %convolution_bitcast_fusion.1 = f32[4,512,128]{1,0,2:T(4,128)S(1)} fusion(bf16[128,4,4]{1,2,0:T(4,128)(2,1)} %copy.217, bf16[1,512,128]{1,0,2:T(2,128)(2,1)S(1)} %copy.216, bf16[1,512,128]{1,0,2:T(2,128)(2,1)S(1)} %copy.215, bf16[1,512,128]{1,0,2:T(2,128)(2,1)S(1)} %copy.214, bf16[1,512,128]{1,0,2:T(2,128)(2,1)} %get-tuple-element.48), kind=kOutput, calls=%fused_computation.22 | convolution fusion | flops 4194304 | bytes 1576960 | tf_op jit(solution)/shard_map/krq,qkp->prq/dot_general | solution.py:86
  80.5 0.8 fusion.70
  81.4 2.3 %collective-permute-start.3 = (f32[512,128]{0,1:T(8,128)S(1)}, f32[512,128]{0,1:T(8,128)S(1)}, u32[]{:S(2)}, u32[]{:S(2)}) collective-permute-start(f32[512,128]{0,1:T(8,128)S(1)} %bitcast.145), channel_id=1, source_target_pairs={{0,1},{1,2},{2,3},{3,0},{4,5},{5,6},{6,7},{7,4},{8,9},{9,10},{10,1... | collective-permute-start | bytes 786440 | tf_op jit(solution)/shard_map/ppermute | solution.py:28
  83.7 1.4 fusion.74
  85.2 5.1 %collective-permute-done.5 = f32[512,128]{0,1:T(8,128)S(1)} collective-permute-done((f32[512,128]{0,1:T(8,128)S(1)}, f32[512,128]{0,1:T(8,128)S(1)}, u32[]{:S(2)}, u32[]{:S(2)}) %collective-permute-start.5) | collective-permute-done | bytes 262176 | tf_op jit(solution)/shard_map/ppermute | solution.py:28
  90.3 14.2 %collective-permute-done.4 = f32[512,128]{0,1:T(8,128)S(1)} collective-permute-done((f32[512,128]{0,1:T(8,128)S(1)}, f32[512,128]{0,1:T(8,128)S(1)}, u32[]{:S(2)}, u32[]{:S(2)}) %collective-permute-start.4) | collective-permute-done | bytes 262176 | tf_op jit(solution)/shard_map/ppermute | solution.py:28
  104.6 0.6 gather_fusion
  105.2 1.4 fusion.8
  106.7 1.0 copy.245
  107.7 3.9 %all-to-all-start.3 = ((bf16[8,64,512]{2,1,0:T(8,128)(2,1)}), bf16[8,64,512]{2,1,0:T(8,128)(2,1)S(1)}, u32[]{:S(2)}, u32[]{:S(2)}) async-start(bf16[8,64,512]{2,1,0:T(8,128)(2,1)} %copy.245), calls=%async_computation.3 | async-start | bytes 1048576 | tf_op jit(solution)/shard_map/all_to_all | solution.py:33
  112.0 1.0 copy.248
  113.0 8.3 %all-to-all-done.3 = bf16[8,64,512]{2,1,0:T(8,128)(2,1)S(1)} async-done(((bf16[8,64,512]{2,1,0:T(8,128)(2,1)}), bf16[8,64,512]{2,1,0:T(8,128)(2,1)S(1)}, u32[]{:S(2)}, u32[]{:S(2)}) %all-to-all-start.3) | async-done | bytes 524320 | tf_op jit(solution)/shard_map/all_to_all | solution.py:33
  121.3 4.4 %all-to-all-start.4 = ((f32[8,64,512]{2,1,0:T(8,128)}), f32[8,64,512]{2,1,0:T(8,128)}, u32[]{:S(2)}, u32[]{:S(2)}) async-start(f32[8,64,512]{2,1,0:T(8,128)} %bitcast.54), calls=%async_computation.4 | async-start | bytes 2097152 | tf_op jit(solution)/shard_map/all_to_all | solution.py:33
  125.8 0.6 fusion.49
  126.4 0.6 gather_fusion.2
  127.3 0.9 slice_bitcast_fusion.2
  128.2 2.6 %collective-permute-start.13 = (f32[128,512]{1,0:T(8,128)}, f32[128,512]{1,0:T(8,128)}, u32[]{:S(2)}, u32[]{:S(2)}) collective-permute-start(f32[128,512]{1,0:T(8,128)} %get-tuple-element.33), channel_id=1, source_target_pairs={{0,2},{1,3},{2,0},{3,1},{4,6},{5,7},{6,4},{7,5},{8,10},{9,11},{10,... | collective-permute-start | bytes 786440 | tf_op jit(solution)/shard_map/ppermute | solution.py:28
  130.8 2.0 %collective-permute-start.12 = (f32[128,512]{1,0:T(8,128)}, f32[128,512]{1,0:T(8,128)}, u32[]{:S(2)}, u32[]{:S(2)}) collective-permute-start(f32[128,512]{1,0:T(8,128)} %get-tuple-element.31), channel_id=1, source_target_pairs={{0,1},{1,2},{2,3},{3,0},{4,5},{5,6},{6,7},{7,4},{8,9},{9,10},{10,1... | collective-permute-start | bytes 786440 | tf_op jit(solution)/shard_map/ppermute | solution.py:28
  132.8 1.2 fusion.2
  134.0 1.0 copy.249
  135.0 6.1 %all-to-all-done.4 = f32[8,64,512]{2,1,0:T(8,128)} async-done(((f32[8,64,512]{2,1,0:T(8,128)}), f32[8,64,512]{2,1,0:T(8,128)}, u32[]{:S(2)}, u32[]{:S(2)}) %all-to-all-start.4) | async-done | bytes 1048608 | tf_op jit(solution)/shard_map/all_to_all | solution.py:33
  141.2 2.0 %reduce_sum.28 = f32[64,512]{1,0:T(8,128)} reduce(f32[8,64,512]{2,1,0:T(8,128)} %all-to-all-done.4, f32[]{:T(128)} %constant.129.clone.1), dimensions={0}, to_apply=%region_0.0 | reduce | flops 229376 | bytes 1179652 | tf_op jit(solution)/shard_map/reduce_sum | solution.py:96
  143.1 11.6 %collective-permute-done.13 = f32[128,512]{1,0:T(8,128)} collective-permute-done((f32[128,512]{1,0:T(8,128)}, f32[128,512]{1,0:T(8,128)}, u32[]{:S(2)}, u32[]{:S(2)}) %collective-permute-start.13) | collective-permute-done | bytes 262176 | tf_op jit(solution)/shard_map/ppermute | solution.py:28
  154.8 1.8 %fusion.59 = f32[1,128,512]{2,1,0:T(8,128)} fusion(f32[4,128,512]{2,1,0:T(8,128)S(1)} %broadcast_select_fusion, f32[128,512]{1,0:T(8,128)S(1)} %collective-permute-done.14, f32[128,512]{1,0:T(8,128)} %collective-permute-done.13, f32[128,512]{1,0:T(8,128)} %collective-permute-done.12), kind=kLoop, calls=%fused_computation.99 | loop fusion | flops 196608 | bytes 1310720 | tf_op jit(solution)/shard_map/reduce_sum | solution.py:107
  (111 shorter events, 9.2 us)
Async XLA Ops:
  0.6 56.1 %copy-start = (bf16[1,512,512]{2,1,0:T(8,128)(2,1)S(1)}, bf16[1,512,512]{2,1,0:T(8,128)(2,1)}, u32[]{:S(2)}) copy-start(bf16[1,512,512]{2,1,0:T(8,128)(2,1)} %param.19) | copy-start | bytes 1572868
  2.0 0.8 copy-start.6
  4.9 6.8 %copy-start.9 = (bf16[512,512]{1,0:T(8,128)(2,1)S(1)}, bf16[512,512]{1,0:T(8,128)(2,1)}, u32[]{:S(2)}) copy-start(bf16[512,512]{1,0:T(8,128)(2,1)} %param.14) | copy-start | bytes 1572868
  5.1 17.5 %collective-permute-start.8 = (bf16[512,128]{1,0:T(8,128)(2,1)S(1)}, bf16[512,128]{1,0:T(8,128)(2,1)S(1)}, u32[]{:S(2)}, u32[]{:S(2)}) collective-permute-start(bf16[512,128]{1,0:T(8,128)(2,1)S(1)} %bitcast.149), channel_id=1, source_target_pairs={{0,3},{1,0},{2,1},{3,2},{4,7},{5,4},{6,5},{7,6},{8,11},{9,8},{10,9... | collective-permute-start | bytes 393224 | tf_op jit(solution)/shard_map/ppermute | solution.py:28
  10.4 12.5 %collective-permute-start.7 = (bf16[512,128]{1,0:T(8,128)(2,1)S(1)}, bf16[512,128]{1,0:T(8,128)(2,1)S(1)}, u32[]{:S(2)}, u32[]{:S(2)}) collective-permute-start(bf16[512,128]{1,0:T(8,128)(2,1)S(1)} %bitcast.151), channel_id=1, source_target_pairs={{0,2},{1,3},{2,0},{3,1},{4,6},{5,7},{6,4},{7,5},{8,10},{9,11},{10,... | collective-permute-start | bytes 393224 | tf_op jit(solution)/shard_map/ppermute | solution.py:28
  10.7 1.3 copy-start.20
  10.7 12.4 %collective-permute-start.6 = (bf16[512,128]{1,0:T(8,128)(2,1)S(1)}, bf16[512,128]{1,0:T(8,128)(2,1)S(1)}, u32[]{:S(2)}, u32[]{:S(2)}) collective-permute-start(bf16[512,128]{1,0:T(8,128)(2,1)S(1)} %bitcast.153), channel_id=1, source_target_pairs={{0,1},{1,2},{2,3},{3,0},{4,5},{5,6},{6,7},{7,4},{8,9},{9,10},{10,1... | collective-permute-start | bytes 393224 | tf_op jit(solution)/shard_map/ppermute | solution.py:28
  12.0 2.8 %copy-start.3 = (bf16[512,512]{0,1:T(8,128)(2,1)}, bf16[512,512]{0,1:T(8,128)(2,1)S(1)}, u32[]{:S(2)}) copy-start(bf16[512,512]{0,1:T(8,128)(2,1)S(1)} %copy.203) | copy-start | bytes 1572868
  14.8 13.5 %all-to-all-start = ((bf16[8,64,512]{2,1,0:T(8,128)(2,1)}), bf16[8,64,512]{2,1,0:T(8,128)(2,1)S(1)}, u32[]{:S(2)}, u32[]{:S(2)}) async-start(bf16[8,64,512]{2,1,0:T(8,128)(2,1)} %bitcast.2), calls=%async_computation | async-start | bytes 1048576 | tf_op jit(solution)/shard_map/all_to_all | solution.py:33
  18.5 2.5 %copy-start.13 = (pred[4]{0:T(512)(128)(4,1)}, pred[4]{0:T(512)(128)(4,1)S(1)}, u32[]{:S(2)}) copy-start(pred[4]{0:T(512)(128)(4,1)S(1)} %compare_and_fusion.1) | copy-start | bytes 16
  21.8 0.7 copy-start.12
  29.7 24.4 %all-to-all-start.1 = ((bf16[8,64,512]{2,1,0:T(8,128)(2,1)}), bf16[8,64,512]{2,1,0:T(8,128)(2,1)S(1)}, u32[]{:S(2)}, u32[]{:S(2)}) async-start(bf16[8,64,512]{2,1,0:T(8,128)(2,1)} %copy.206), calls=%async_computation.1 | async-start | bytes 1048576 | tf_op jit(solution)/shard_map/all_to_all | solution.py:33
  34.1 6.7 %collective-permute-start.11 = (bf16[512,128]{1,0:T(8,128)(2,1)S(1)}, bf16[512,128]{1,0:T(8,128)(2,1)S(1)}, u32[]{:S(2)}, u32[]{:S(2)}) collective-permute-start(bf16[512,128]{1,0:T(8,128)(2,1)S(1)} %bitcast.159), channel_id=1, source_target_pairs={{0,3},{1,0},{2,1},{3,2},{4,7},{5,4},{6,5},{7,6},{8,11},{9,8},{10,9... | collective-permute-start | bytes 393224 | tf_op jit(solution)/shard_map/ppermute | solution.py:28
  37.2 13.2 %collective-permute-start.10 = (bf16[512,128]{1,0:T(8,128)(2,1)S(1)}, bf16[512,128]{1,0:T(8,128)(2,1)S(1)}, u32[]{:S(2)}, u32[]{:S(2)}) collective-permute-start(bf16[512,128]{1,0:T(8,128)(2,1)S(1)} %bitcast.161), channel_id=1, source_target_pairs={{0,2},{1,3},{2,0},{3,1},{4,6},{5,7},{6,4},{7,5},{8,10},{9,11},{10,... | collective-permute-start | bytes 393224 | tf_op jit(solution)/shard_map/ppermute | solution.py:28
  38.5 12.0 %collective-permute-start.9 = (bf16[512,128]{1,0:T(8,128)(2,1)S(1)}, bf16[512,128]{1,0:T(8,128)(2,1)S(1)}, u32[]{:S(2)}, u32[]{:S(2)}) collective-permute-start(bf16[512,128]{1,0:T(8,128)(2,1)S(1)} %bitcast.163), channel_id=1, source_target_pairs={{0,1},{1,2},{2,3},{3,0},{4,5},{5,6},{6,7},{7,4},{8,9},{9,10},{10,1... | collective-permute-start | bytes 393224 | tf_op jit(solution)/shard_map/ppermute | solution.py:28
  54.2 0.7 copy-start.16
  54.9 1.8 %copy-start.1 = (f32[512,512]{0,1:T(8,128)}, f32[512,512]{0,1:T(8,128)S(1)}, u32[]{:S(2)}) copy-start(f32[512,512]{0,1:T(8,128)S(1)} %copy.207) | copy-start | bytes 3145732
  54.9 1.9 %copy-start.8 = (bf16[4,512,128]{1,2,0:T(8,128)(2,1)S(1)}, bf16[4,512,128]{1,2,0:T(8,128)(2,1)}, u32[]{:S(2)}) copy-start(bf16[4,512,128]{1,2,0:T(8,128)(2,1)} %copy.240) | copy-start | bytes 1572868
  54.9 1.9 %copy-start.14 = (pred[4]{0:T(512)(128)(4,1)S(1)}, pred[4]{0:T(512)(128)(4,1)}, u32[]{:S(2)}) copy-start(pred[4]{0:T(512)(128)(4,1)} %copy-done.13) | copy-start | bytes 16
  61.1 5.5 %copy-start.4 = (bf16[512,512]{0,1:T(8,128)(2,1)S(1)}, bf16[512,512]{0,1:T(8,128)(2,1)}, u32[]{:S(2)}) copy-start(bf16[512,512]{0,1:T(8,128)(2,1)} %copy-done.3) | copy-start | bytes 1572868
  61.1 5.5 %copy-start.7 = (bf16[512,512]{0,1:T(8,128)(2,1)S(1)}, bf16[512,512]{0,1:T(8,128)(2,1)}, u32[]{:S(2)}) copy-start(bf16[512,512]{0,1:T(8,128)(2,1)} %copy-done.6) | copy-start | bytes 1572868
  61.9 11.2 %collective-permute-start.2 = (bf16[512,128]{1,0:T(8,128)(2,1)}, bf16[512,128]{1,0:T(8,128)(2,1)S(1)}, u32[]{:S(2)}, u32[]{:S(2)}) collective-permute-start(bf16[512,128]{1,0:T(8,128)(2,1)} %bitcast.156), channel_id=1, source_target_pairs={{0,3},{1,0},{2,1},{3,2},{4,7},{5,4},{6,5},{7,6},{8,11},{9,8},{10,9... | collective-permute-start | bytes 393224 | tf_op jit(solution)/shard_map/ppermute | solution.py:28
  62.1 13.9 %collective-permute-start.1 = (bf16[512,128]{1,0:T(8,128)(2,1)S(1)}, bf16[512,128]{1,0:T(8,128)(2,1)}, u32[]{:S(2)}, u32[]{:S(2)}) collective-permute-start(bf16[512,128]{1,0:T(8,128)(2,1)S(1)} %bitcast.158), channel_id=1, source_target_pairs={{0,2},{1,3},{2,0},{3,1},{4,6},{5,7},{6,4},{7,5},{8,10},{9,11},{10,... | collective-permute-start | bytes 393224 | tf_op jit(solution)/shard_map/ppermute | solution.py:28
  64.6 2.0 %copy-start.17 = (f32[512]{0:T(512)S(1)}, f32[512]{0:T(512)}, u32[]{:S(2)}) copy-start(f32[512]{0:T(512)} %param.16) | copy-start | bytes 6148
  64.6 12.5 %collective-permute-start = (bf16[512,128]{1,0:T(8,128)(2,1)}, bf16[512,128]{1,0:T(8,128)(2,1)}, u32[]{:S(2)}, u32[]{:S(2)}) collective-permute-start(bf16[512,128]{1,0:T(8,128)(2,1)} %bitcast.12), channel_id=1, source_target_pairs={{0,1},{1,2},{2,3},{3,0},{4,5},{5,6},{6,7},{7,4},{8,9},{9,10},{10,1... | collective-permute-start | bytes 393224 | tf_op jit(solution)/shard_map/ppermute | solution.py:28
  69.0 36.3 %all-to-all-start.2 = ((bf16[8,64,512]{2,1,0:T(8,128)(2,1)}), bf16[8,64,512]{2,1,0:T(8,128)(2,1)}, u32[]{:S(2)}, u32[]{:S(2)}) async-start(bf16[8,64,512]{2,1,0:T(8,128)(2,1)} %bitcast.49), calls=%async_computation.2 | async-start | bytes 1048576 | tf_op jit(solution)/shard_map/all_to_all | solution.py:33
  81.2 9.1 %collective-permute-start.5 = (f32[512,128]{0,1:T(8,128)S(1)}, f32[512,128]{0,1:T(8,128)S(1)}, u32[]{:S(2)}, u32[]{:S(2)}) collective-permute-start(f32[512,128]{0,1:T(8,128)S(1)} %bitcast.143), channel_id=1, source_target_pairs={{0,3},{1,0},{2,1},{3,2},{4,7},{5,4},{6,5},{7,6},{8,11},{9,8},{10,9... | collective-permute-start | bytes 786440 | tf_op jit(solution)/shard_map/ppermute | solution.py:28
  81.3 23.2 %collective-permute-start.4 = (f32[512,128]{0,1:T(8,128)S(1)}, f32[512,128]{0,1:T(8,128)S(1)}, u32[]{:S(2)}, u32[]{:S(2)}) collective-permute-start(f32[512,128]{0,1:T(8,128)S(1)} %bitcast.144), channel_id=1, source_target_pairs={{0,2},{1,3},{2,0},{3,1},{4,6},{5,7},{6,4},{7,5},{8,10},{9,11},{10,... | collective-permute-start | bytes 786440 | tf_op jit(solution)/shard_map/ppermute | solution.py:28
  81.4 23.1 %collective-permute-start.3 = (f32[512,128]{0,1:T(8,128)S(1)}, f32[512,128]{0,1:T(8,128)S(1)}, u32[]{:S(2)}, u32[]{:S(2)}) collective-permute-start(f32[512,128]{0,1:T(8,128)S(1)} %bitcast.145), channel_id=1, source_target_pairs={{0,1},{1,2},{2,3},{3,0},{4,5},{5,6},{6,7},{7,4},{8,9},{9,10},{10,1... | collective-permute-start | bytes 786440 | tf_op jit(solution)/shard_map/ppermute | solution.py:28
  107.6 4.0 %copy-start.15 = (pred[4]{0:T(512)(128)(4,1)S(1)}, pred[4]{0:T(512)(128)(4,1)}, u32[]{:S(2)}) copy-start(pred[4]{0:T(512)(128)(4,1)} %copy-done.13) | copy-start | bytes 16
  107.7 13.7 %all-to-all-start.3 = ((bf16[8,64,512]{2,1,0:T(8,128)(2,1)}), bf16[8,64,512]{2,1,0:T(8,128)(2,1)S(1)}, u32[]{:S(2)}, u32[]{:S(2)}) async-start(bf16[8,64,512]{2,1,0:T(8,128)(2,1)} %copy.245), calls=%async_computation.3 | async-start | bytes 1048576 | tf_op jit(solution)/shard_map/all_to_all | solution.py:33
  121.3 4.4 %copy-start.10 = (bf16[8,64,512]{2,1,0:T(8,128)(2,1)}, bf16[8,64,512]{2,1,0:T(8,128)(2,1)S(1)}, u32[]{:S(2)}) copy-start(bf16[8,64,512]{2,1,0:T(8,128)(2,1)S(1)} %all-to-all-done.3) | copy-start | bytes 1572868
  121.3 4.4 %copy-start.5 = (bf16[512,512]{0,1:T(8,128)(2,1)S(1)}, bf16[512,512]{0,1:T(8,128)(2,1)}, u32[]{:S(2)}) copy-start(bf16[512,512]{0,1:T(8,128)(2,1)} %copy-done.3) | copy-start | bytes 1572868
  121.3 4.4 %copy-start.21 = (f32[512]{0:T(512)S(1)}, f32[512]{0:T(512)}, u32[]{:S(2)}) copy-start(f32[512]{0:T(512)} %param.15) | copy-start | bytes 6148
  121.3 19.8 %all-to-all-start.4 = ((f32[8,64,512]{2,1,0:T(8,128)}), f32[8,64,512]{2,1,0:T(8,128)}, u32[]{:S(2)}, u32[]{:S(2)}) async-start(f32[8,64,512]{2,1,0:T(8,128)} %bitcast.54), calls=%async_computation.4 | async-start | bytes 2097152 | tf_op jit(solution)/shard_map/all_to_all | solution.py:33
  127.0 5.8 %copy-start.19 = (bf16[1,512,512]{2,1,0:T(8,128)(2,1)S(1)}, bf16[1,512,512]{2,1,0:T(8,128)(2,1)}, u32[]{:S(2)}) copy-start(bf16[1,512,512]{2,1,0:T(8,128)(2,1)} %param.17) | copy-start | bytes 1572868
  127.0 5.7 %copy-start.22 = (bf16[512,512]{0,1:T(8,128)(2,1)S(1)}, bf16[512,512]{0,1:T(8,128)(2,1)}, u32[]{:S(2)}) copy-start(bf16[512,512]{0,1:T(8,128)(2,1)} %get-tuple-element.55) | copy-start | bytes 1572868
  127.3 5.5 %copy-start.2 = (f32[512,512]{0,1:T(8,128)S(1)}, f32[512,512]{0,1:T(8,128)}, u32[]{:S(2)}) copy-start(f32[512,512]{0,1:T(8,128)} %copy-done.1) | copy-start | bytes 3145732
  127.3 5.5 %copy-start.11 = (bf16[8,64,512]{2,1,0:T(8,128)(2,1)S(1)}, bf16[8,64,512]{2,1,0:T(8,128)(2,1)}, u32[]{:S(2)}) copy-start(bf16[8,64,512]{2,1,0:T(8,128)(2,1)} %copy-done.10) | copy-start | bytes 1572868
  128.2 14.9 %collective-permute-start.14 = (f32[128,512]{1,0:T(8,128)}, f32[128,512]{1,0:T(8,128)S(1)}, u32[]{:S(2)}, u32[]{:S(2)}) collective-permute-start(f32[128,512]{1,0:T(8,128)} %get-tuple-element.32), channel_id=1, source_target_pairs={{0,3},{1,0},{2,1},{3,2},{4,7},{5,4},{6,5},{7,6},{8,11},{9,8},{10,9... | collective-permute-start | bytes 786440 | tf_op jit(solution)/shard_map/ppermute | solution.py:28
  128.2 26.6 %collective-permute-start.13 = (f32[128,512]{1,0:T(8,128)}, f32[128,512]{1,0:T(8,128)}, u32[]{:S(2)}, u32[]{:S(2)}) collective-permute-start(f32[128,512]{1,0:T(8,128)} %get-tuple-element.33), channel_id=1, source_target_pairs={{0,2},{1,3},{2,0},{3,1},{4,6},{5,7},{6,4},{7,5},{8,10},{9,11},{10,... | collective-permute-start | bytes 786440 | tf_op jit(solution)/shard_map/ppermute | solution.py:28
  130.8 2.0 %copy-start.18 = (f32[512]{0:T(512)S(1)}, f32[512]{0:T(512)}, u32[]{:S(2)}) copy-start(f32[512]{0:T(512)} %param.16) | copy-start | bytes 6148
  130.8 24.0 %collective-permute-start.12 = (f32[128,512]{1,0:T(8,128)}, f32[128,512]{1,0:T(8,128)}, u32[]{:S(2)}, u32[]{:S(2)}) collective-permute-start(f32[128,512]{1,0:T(8,128)} %get-tuple-element.31), channel_id=1, source_target_pairs={{0,1},{1,2},{2,3},{3,0},{4,5},{5,6},{6,7},{7,4},{8,9},{9,10},{10,1... | collective-permute-start | bytes 786440 | tf_op jit(solution)/shard_map/ppermute | solution.py:28
where the time goes:
time: 157 us
  waiting for transfers between devices  61.8 us (39%)
  starting transfers between devices  41.3 us (26%)
  local copies, waits for them, and re-layouts  29.5 us (19%)
  matrix products  14.2 us (9%)
  other arithmetic  8.53 us (5%)
    ppermute x15, waiting for transfers between devices, exchange(): lax.ppermute(pieces[k], axis_name, [(i, (i + k) % n) for i in range(n)])  43.7 us
    ppermute x15, starting transfers between devices, exchange(): lax.ppermute(pieces[k], axis_name, [(i, (i + k) % n) for i in range(n)])  21.6 us
    all_to_all x5, starting transfers between devices, swap(): return lax.all_to_all(pieces, axis_name, 0, 0, tiled=True)  19.7 us
    all_to_all x5, waiting for transfers between devices, swap(): return lax.all_to_all(pieces, axis_name, 0, 0, tiled=True)  18.1 us
    unnamed x55, local copies, waits for them, and re-layouts  5.23 us
    another operation x10, local copies, waits for them, and re-layouts, exchange(): return jnp.stack(got)  3.94 us
    slice x4, local copies, waits for them, and re-layouts, exchange(): got = [pieces[0]]  3.71 us
  transfers between devices with their start and end apart: 20, of which 9 were waited for; matrix products, arithmetic and copies ran while one was open for 22% of the time, Pallas kernels for 0%

commit v1 on v0

--- a/solution.py
+++ b/solution.py
@@ -58,20 +58,21 @@
 
     second_f = second_blocks.astype(F32)
 
+    source = inputs.astype(F32)
+    slope_in = jax.nn.sigmoid(gate_in * source)
+    gated = (source * slope_in).astype(BF16)
+    mixed_first = jnp.dot(first_blocks[0], gated, preferred_element_type=F32).astype(BF16)
+    first_arrived = swap(split_rows(mixed_first, n), "seq")
+
     upstream = cotangent
-    cot_pieces = to_shift_order(upstream.reshape(rows, m, kq), g_me, m, axis=1)
+    upstream_late, first_arrived = lax.optimization_barrier((upstream, first_arrived))
+    cot_pieces = to_shift_order(upstream_late.reshape(rows, m, kq), g_me, m, axis=1)
     cot_arrived = exchange(jnp.transpose(cot_pieces, (1, 0, 2)), "ch")
     act_grad_out = jnp.einsum(
         "krq,qpk->prq", cot_arrived.astype(F32), mix_bwd
     ).astype(BF16)
     act_grad_back = to_source_order(exchange(act_grad_out, "ch"), g_me, m)
     act_grad = jnp.transpose(act_grad_back, (1, 0, 2)).reshape(rows, block_width)
-
-    source = inputs.astype(F32)
-    slope_in = jax.nn.sigmoid(gate_in * source)
-    gated = (source * slope_in).astype(BF16)
-    mixed_first = jnp.dot(first_blocks[0], gated, preferred_element_type=F32).astype(BF16)
-    first_arrived = swap(split_rows(mixed_first, n), "seq")
     second_out = jnp.einsum(
         "cea,acd->ecd", second_f, first_arrived.astype(F32)
     ).astype(BF16)
@@ -83,17 +84,13 @@
 
     act_pieces = to_shift_order(activated.reshape(rows, m, kq), g_me, m, axis=1)
     act_arrived = exchange(jnp.transpose(act_pieces, (1, 0, 2)), "ch")
-    added_out = jnp.einsum("krq,qkp->prq", act_arrived.astype(F32), mix_fwd)
+    added_out = jnp.einsum("krq,qkp->prq", act_arrived.astype(F32), mix_fwd).astype(BF16)
     added_back = to_source_order(exchange(added_out, "ch"), g_me, m)
-    added = jnp.transpose(added_back, (1, 0, 2)).reshape(rows, block_width)
-    outputs = (hidden.astype(F32) + added).astype(BF16)
 
     pre_grad = jax.vjp(jax.nn.gelu, pre_act)[1](act_grad.astype(F32))[0].astype(BF16)
     back_term = jnp.dot(pre_grad, channel_blocks[0].T, preferred_element_type=F32)
     hidden_grad = (upstream.astype(F32) + back_term).astype(BF16)
     channel_part = jnp.dot(hidden.T, pre_grad, preferred_element_type=F32)
-    channel_arrived = swap(split_rows(channel_part, n), "seq")
-    channel_grad = jnp.sum(channel_arrived, axis=0)[None]
 
     grad_flat = hidden_grad.astype(F32)
     gated_grad = (grad_flat * slope_out).astype(BF16)
@@ -102,9 +99,16 @@
         "cea,ecd->acd", second_f, grad_arrived.astype(F32)
     ).astype(BF16)
     first_grad = swap(first_out, "seq").reshape(rows, width)
+    first_grad, added_back, channel_part = lax.optimization_barrier(
+        (first_grad, added_back, channel_part)
+    )
+    added = jnp.transpose(added_back, (1, 0, 2)).reshape(rows, block_width)
+    outputs = (hidden.astype(F32) + added.astype(F32)).astype(BF16)
     block_part = jnp.dot(first_grad, gated.T, preferred_element_type=F32)
     block_arrived = exchange(to_shift_order(split_rows(block_part, m), g_me, m), "ch")
     block_grad = jnp.sum(block_arrived, axis=0)[None]
+    channel_arrived = swap(split_rows(channel_part, n), "seq")
+    channel_grad = jnp.sum(channel_arrived, axis=0)[None]
 
     spread = jnp.dot(first_blocks[0].T, first_grad, preferred_element_type=F32)
     input_grad = grad_flat + spread * (slope_in + gate_in * source * slope_in * (1.0 - slope_in))

time: 157 us -> 164 us (1.045)
  waiting for transfers between devices: 61.8 us -> 39.3 us
  local copies, waits for them, and re-layouts: 29.5 us -> 49.1 us
  other arithmetic: 8.53 us -> 13.1 us
  matrix products: 14.2 us -> 18.1 us
    ppermute x15, waiting for transfers between devices: 43.7 us -> 29.7 us  [exchange(): lax.ppermute(pieces[k], axis_name, [(i, (i + k) % n) for i in range(n)])]
    all_to_all x5, waiting for transfers between devices: 18.1 us -> 9.56 us  [swap(): return lax.all_to_all(pieces, axis_name, 0, 0, tiled=True)]
    another operation x10 -> x14, local copies, waits for them, and re-layouts: 3.94 us -> 11.2 us  [exchange(): return jnp.stack(got)]
    slice x9 -> x12, local copies, waits for them, and re-layouts: 2.91 us -> 7.21 us  [exchange(): pieces[k]]
    unnamed x55 -> x45, local copies, waits for them, and re-layouts: 5.23 us -> 8.27 us
    convert_element_type x0 -> x2, local copies, waits for them, and re-layouts: none -> 2.89 us  [the longest x1 1.55 us: on_device(): outputs = (hidden.astype(F32) + added.astype(F32)).astype(BF16)]
    another operation x2, other arithmetic: 1.29 us -> 3.55 us  [exchange(): return jnp.stack(got)]
    dot_general x1, matrix products: 0.64 us -> 2.74 us  [on_device(): block_part = jnp.dot(first_grad, gated.T, preferred_element_type=F32)]
  transfers between devices with their start and end apart: 20 -> 20, of which waited for: 9 -> 9; matrix products, arithmetic and copies ran while one was open for 22% -> 31% of each run, Pallas kernels for 0% -> 0%
where the time goes in v1:
time: 164 us; the launch traced here: 162 us
  local copies, waits for them, and re-layouts  49.1 us (30%)
  starting transfers between devices  41.5 us (25%)
  waiting for transfers between devices  39.3 us (24%)
  matrix products  18.1 us (11%)
  other arithmetic  13.1 us (8%)
    ppermute x15, waiting for transfers between devices, exchange(): lax.ppermute(pieces[k], axis_name, [(i, (i + k) % n) for i in range(n)])  29.7 us
    all_to_all x5, starting transfers between devices, swap(): return lax.all_to_all(pieces, axis_name, 0, 0, tiled=True)  21.2 us
    ppermute x15, starting transfers between devices, exchange(): lax.ppermute(pieces[k], axis_name, [(i, (i + k) % n) for i in range(n)])  20.3 us
    another operation x14, local copies, waits for them, and re-layouts, exchange(): return jnp.stack(got)  11.2 us
    all_to_all x5, waiting for transfers between devices, swap(): return lax.all_to_all(pieces, axis_name, 0, 0, tiled=True)  9.56 us
    unnamed x45, local copies, waits for them, and re-layouts  8.27 us
    slice x12, local copies, waits for them, and re-layouts, exchange(): pieces[k]  7.21 us
    slice x4, local copies, waits for them, and re-layouts, exchange(): got = [pieces[0]]  4.58 us
  transfers between devices with their start and end apart: 20, of which 9 were waited for; matrix products, arithmetic and copies ran while one was open for 31% of the time, Pallas kernels for 0%

profile of v1, /device:TPU:0, one launch (start us, length us, event | category | flops | bytes accessed | tf_op | source)
XLA Modules:
  0.0 162.4 jit_solution(11878005228788615488)
XLA Ops:
  0.7 1.3 copy.206
  2.0 1.6 convolution_convert_fusion.4
  3.6 5.2 %all-to-all-start = ((bf16[8,64,512]{2,1,0:T(8,128)(2,1)}), bf16[8,64,512]{2,1,0:T(8,128)(2,1)S(1)}, u32[]{:S(2)}, u32[]{:S(2)}) async-start(bf16[8,64,512]{2,1,0:T(8,128)(2,1)} %bitcast.2), calls=%async_computation | async-start | bytes 1048576 | tf_op jit(solution)/shard_map/all_to_all | solution.py:33
  12.0 6.5 %all-to-all-done = bf16[8,64,512]{2,1,0:T(8,128)(2,1)S(1)} async-done(((bf16[8,64,512]{2,1,0:T(8,128)(2,1)}), bf16[8,64,512]{2,1,0:T(8,128)(2,1)S(1)}, u32[]{:S(2)}, u32[]{:S(2)}) %all-to-all-start) | async-done | bytes 524320 | tf_op jit(solution)/shard_map/all_to_all | solution.py:33
  21.7 3.7 %collective-permute-start.2 = (bf16[512,128]{1,0:T(8,128)(2,1)S(1)}, bf16[512,128]{1,0:T(8,128)(2,1)S(1)}, u32[]{:S(2)}, u32[]{:S(2)}) collective-permute-start(bf16[512,128]{1,0:T(8,128)(2,1)S(1)} %bitcast.147), channel_id=1, source_target_pairs={{0,3},{1,0},{2,1},{3,2},{4,7},{5,4},{6,5},{7,6},{8,11},{9,8},{10,9... | collective-permute-start | bytes 393224 | tf_op jit(solution)/shard_map/ppermute | solution.py:28
  25.4 1.0 collective-permute-start.1
  26.5 1.0 copy.211
  27.7 0.8 copy.245
  28.9 3.7 %collective-permute-done = bf16[512,128]{1,0:T(8,128)(2,1)S(1)} collective-permute-done((bf16[512,128]{1,0:T(8,128)(2,1)S(1)}, bf16[512,128]{1,0:T(8,128)(2,1)S(1)}, u32[]{:S(2)}, u32[]{:S(2)}) %collective-permute-start) | collective-permute-done | bytes 131104 | tf_op jit(solution)/shard_map/ppermute | solution.py:28
  32.8 3.1 %collective-permute-done.1 = bf16[512,128]{1,0:T(8,128)(2,1)S(1)} collective-permute-done((bf16[512,128]{1,0:T(8,128)(2,1)S(1)}, bf16[512,128]{1,0:T(8,128)(2,1)S(1)}, u32[]{:S(2)}, u32[]{:S(2)}) %collective-permute-start.1) | collective-permute-done | bytes 131104 | tf_op jit(solution)/shard_map/ppermute | solution.py:28
  36.1 1.3 fusion.7
  38.9 2.3 %collective-permute-start.4 = (bf16[512,128]{1,0:T(8,128)(2,1)S(1)}, bf16[512,128]{1,0:T(8,128)(2,1)S(1)}, u32[]{:S(2)}, u32[]{:S(2)}) collective-permute-start(bf16[512,128]{1,0:T(8,128)(2,1)S(1)} %bitcast.138), channel_id=1, source_target_pairs={{0,2},{1,3},{2,0},{3,1},{4,6},{5,7},{6,4},{7,5},{8,10},{9,11},{10,... | collective-permute-start | bytes 393224 | tf_op jit(solution)/shard_map/ppermute | solution.py:28
  41.2 1.5 collective-permute-start.5
  43.1 0.9 copy.209
  44.1 3.7 %all-to-all-start.1 = ((bf16[8,64,512]{2,1,0:T(8,128)(2,1)}), bf16[8,64,512]{2,1,0:T(8,128)(2,1)S(1)}, u32[]{:S(2)}, u32[]{:S(2)}) async-start(bf16[8,64,512]{2,1,0:T(8,128)(2,1)} %copy.209), calls=%async_computation.1 | async-start | bytes 1048576 | tf_op jit(solution)/shard_map/all_to_all | solution.py:33
  48.0 2.0 %collective-permute-done.4 = bf16[512,128]{1,0:T(8,128)(2,1)S(1)} collective-permute-done((bf16[512,128]{1,0:T(8,128)(2,1)S(1)}, bf16[512,128]{1,0:T(8,128)(2,1)S(1)}, u32[]{:S(2)}, u32[]{:S(2)}) %collective-permute-start.4) | collective-permute-done | bytes 131104 | tf_op jit(solution)/shard_map/ppermute | solution.py:28
  50.4 1.2 pad_maximum_fusion
  52.9 1.3 copy.230
  54.2 3.0 %all-to-all-done.1 = bf16[8,64,512]{2,1,0:T(8,128)(2,1)S(1)} async-done(((bf16[8,64,512]{2,1,0:T(8,128)(2,1)}), bf16[8,64,512]{2,1,0:T(8,128)(2,1)S(1)}, u32[]{:S(2)}, u32[]{:S(2)}) %all-to-all-start.1) | async-done | bytes 524320 | tf_op jit(solution)/shard_map/all_to_all | solution.py:33
  58.1 1.5 fusion.31
  59.6 2.1 %multiply_convert_fusion = (bf16[512,512]{0,1:T(8,128)(2,1)}, bf16[512,512]{0,1:T(8,128)(2,1)}) fusion(f32[512,4,128]{0,2,1:T(8,128)S(1)} %copy-done.6, bf16[512,512]{0,1:T(8,128)(2,1)S(1)} %fusion.31, bf16[1,512,512]{2,1,0:T(8,128)(2,1)S(1)} %copy-done), kind=kOutput, calls=%fused_computation.66 | convolution fusion | flops 274202624 | bytes 3145728 | tf_op jit(solution)/shard_map/dot_general | solution.py:82
  61.7 1.3 copy.237
  64.4 1.4 fusion.69
  68.4 1.4 collective-permute-start.6
  69.8 2.0 %collective-permute-start.7 = (bf16[512,128]{1,0:T(8,128)(2,1)}, bf16[512,128]{1,0:T(8,128)(2,1)}, u32[]{:S(2)}, u32[]{:S(2)}) collective-permute-start(bf16[512,128]{1,0:T(8,128)(2,1)} %bitcast.38), channel_id=1, source_target_pairs={{0,2},{1,3},{2,0},{3,1},{4,6},{5,7},{6,4},{7,5},{8,10},{9,11},{10,... | collective-permute-start | bytes 393224 | tf_op jit(solution)/shard_map/ppermute | solution.py:28
  71.8 2.6 %fusion.22 = (bf16[512,512]{0,1:T(8,128)(2,1)S(1)}, bf16[512,512]{0,1:T(8,128)(2,1)}) fusion(bf16[512,512]{0,1:T(8,128)(2,1)S(1)} %copy-done.2, f32[512]{0:T(512)S(1)} %copy-done.13, bf16[512,512]{0,1:T(8,128)(2,1)} %get-tuple-element.46, bf16[1,512,512]{2,1,0:T(8,128)(2,1)S(1)} %copy-done, bf16[512,512]{0,1:T(8,128)(2,1)} %copy.211), kind=kOutput, calls=%fused_computation.47 | convolution fusion | flops 271319040 | bytes 3147776 | tf_op jit(solution)/shard_map/dot_general | solution.py:91
  74.3 1.0 copy.232
  75.4 3.5 %all-to-all-start.2 = ((bf16[8,64,512]{2,1,0:T(8,128)(2,1)}), bf16[8,64,512]{2,1,0:T(8,128)(2,1)S(1)}, u32[]{:S(2)}, u32[]{:S(2)}) async-start(bf16[8,64,512]{2,1,0:T(8,128)(2,1)} %bitcast.128), calls=%async_computation.2 | async-start | bytes 1048576 | tf_op jit(solution)/shard_map/all_to_all | solution.py:33
  79.5 1.1 copy.244
  80.6 1.8 %copy.242 = bf16[1,512,128]{1,0,2:T(2,128)(2,1)} copy(bf16[1,512,128]{2,1,0:T(8,128)(2,1)} %bitcast.37) | data formatting | bytes 262144 | tf_op jit(solution)/shard_map/stack | solution.py:29
  82.4 1.8 %copy.243 = bf16[1,512,128]{1,0,2:T(2,128)(2,1)} copy(bf16[1,512,128]{2,1,0:T(8,128)(2,1)} %bitcast.39) | data formatting | bytes 262144 | tf_op jit(solution)/shard_map/stack | solution.py:29
  84.2 2.5 %fusion.9 = bf16[4,512,128]{1,0,2:T(4,128)(2,1)S(1)} fusion(bf16[128,4,4]{1,2,0:T(4,128)(2,1)} %copy.245, bf16[1,512,128]{1,0,2:T(2,128)(2,1)S(1)} %copy.244, bf16[1,512,128]{1,0,2:T(2,128)(2,1)} %copy.243, bf16[1,512,128]{1,0,2:T(2,128)(2,1)} %copy.242, bf16[1,512,128]{1,0,2:T(2,128)(2,1)} %get-tuple-element.51), kind=kOutput, calls=%fused_computation.34 | convolution fusion | flops 4194304 | bytes 1052672 | tf_op jit(solution)/shard_map/krq,qkp->prq/dot_general | solution.py:87
  86.7 1.6 %fusion.68 = (bf16[1,512,128]{1,0,2:T(2,128)(2,1)}, bf16[1,512,128]{1,0,2:T(2,128)(2,1)}, bf16[1,512,128]{1,0,2:T(2,128)(2,1)}, bf16[1,512,128]{1,0,2:T(2,128)(2,1)S(1)}) fusion(bf16[4,512,128]{1,0,2:T(4,128)(2,1)S(1)} %fusion.9), kind=kLoop, calls=%fused_computation.130 | loop fusion | bytes 1048576 | tf_op jit(solution)/shard_map/slice | solution.py:26
  88.3 1.7 %copy.248 = bf16[1,512,128]{2,1,0:T(8,128)(2,1)} copy(bf16[1,512,128]{1,0,2:T(2,128)(2,1)} %get-tuple-element.48) | data formatting | bytes 262144 | tf_op jit(solution)/shard_map/slice | solution.py:28
  90.1 1.7 %copy.247 = bf16[1,512,128]{2,1,0:T(8,128)(2,1)} copy(bf16[1,512,128]{1,0,2:T(2,128)(2,1)} %get-tuple-element.49) | data formatting | bytes 262144 | tf_op jit(solution)/shard_map/slice | solution.py:28
  91.8 0.8 copy.246
  92.6 1.0 collective-permute-start.9
  94.2 2.3 %collective-permute-start.11 = (bf16[512,128]{1,0:T(8,128)(2,1)}, bf16[512,128]{1,0:T(8,128)(2,1)S(1)}, u32[]{:S(2)}, u32[]{:S(2)}) collective-permute-start(bf16[512,128]{1,0:T(8,128)(2,1)} %bitcast.132), channel_id=1, source_target_pairs={{0,3},{1,0},{2,1},{3,2},{4,7},{5,4},{6,5},{7,6},{8,11},{9,8},{10,9... | collective-permute-start | bytes 393224 | tf_op jit(solution)/shard_map/ppermute | solution.py:28
  96.9 1.0 copy.235
  97.8 4.5 %all-to-all-start.3 = ((bf16[8,64,512]{2,1,0:T(8,128)(2,1)}), bf16[8,64,512]{2,1,0:T(8,128)(2,1)}, u32[]{:S(2)}, u32[]{:S(2)}) async-start(bf16[8,64,512]{2,1,0:T(8,128)(2,1)} %copy.235), calls=%async_computation.3 | async-start | bytes 1048576 | tf_op jit(solution)/shard_map/all_to_all | solution.py:33
  102.4 1.5 fusion.72
  104.5 1.1 copy.249
  106.3 1.8 %copy.250 = bf16[1,512,128]{1,0,2:T(2,128)(2,1)} copy(bf16[1,512,128]{2,1,0:T(8,128)(2,1)} %bitcast.46) | data formatting | bytes 262144 | tf_op jit(solution)/shard_map/stack | solution.py:29
  108.1 0.9 copy.251
  109.0 2.3 %pad_maximum_fusion.1 = bf16[4,512,128]{1,0,2:T(4,128)(2,1)S(1)} fusion(bf16[1,512,128]{1,0,2:T(2,128)(2,1)} %copy.251, bf16[1,512,128]{1,0,2:T(2,128)(2,1)} %copy.250, bf16[1,512,128]{1,0,2:T(2,128)(2,1)S(1)} %copy.249, bf16[1,512,128]{1,0,2:T(2,128)(2,1)} %get-tuple-element.47), kind=kLoop, calls=%fused_computation.82 | loop fusion | flops 2097152 | bytes 1048576 | tf_op jit(solution)/shard_map/stack | solution.py:29
  111.4 1.2 copy.252
  112.5 1.7 %gather_fusion.8 = bf16[4,512,128]{2,1,0:T(8,128)(2,1)S(1)} fusion(bf16[4,512,128]{2,1,0:T(8,128)(2,1)} %copy.252, s32[1024]{0:T(1024)S(1)} %pad_clamp_fusion.1), kind=kCustom, calls=%fused_computation.7.clone | custom fusion | bytes 1048592 | tf_op jit(solution)/shard_map/jit(_take)/gather | solution.py:16
  114.2 0.9 broadcast_select_fusion.3
  115.2 2.7 %fusion.65 = f32[512,512]{1,0:T(8,128)} fusion(bf16[512,512]{1,0:T(8,128)(2,1)} %bitcast.29, bf16[512,512]{0,1:T(8,128)(2,1)S(1)} %copy-done.2, f32[512]{0:T(512)S(1)} %copy-done.18), kind=kOutput, calls=%fused_computation.129 | convolution fusion | flops 270270464 | bytes 2099200 | tf_op jit(solution)/shard_map/dot_general | solution.py:107
  117.9 3.0 %fusion.2 = bf16[512,512]{0,1:T(8,128)(2,1)} fusion(bf16[512,512]{1,0:T(8,128)(2,1)} %bitcast.29, bf16[512,512]{0,1:T(8,128)(2,1)S(1)} %copy-done.19, bf16[512,512]{0,1:T(8,128)(2,1)S(1)} %copy-done.2, f32[512,512]{0,1:T(8,128)S(1)} %copy.210, bf16[1,512,512]{2,1,0:T(8,128)(2,1)S(1)} %copy-done.16, f32[512]{0:T(512)S(1)} %copy-done.14, f32[512]{0:T(512)S(1)} %copy-done.18), kind=kOutput, calls=%fused_computation.27 | convolution fusion | flops 274464768 | bytes 3674112 | tf_op jit(solution)/shard_map/dot_general | solution.py:113
  120.9 4.4 %all-to-all-start.4 = ((f32[8,64,512]{2,1,0:T(8,128)}), f32[8,64,512]{2,1,0:T(8,128)}, u32[]{:S(2)}, u32[]{:S(2)}) async-start(f32[8,64,512]{2,1,0:T(8,128)} %bitcast.53), calls=%async_computation.4 | async-start | bytes 2097152 | tf_op jit(solution)/shard_map/all_to_all | solution.py:33
  127.0 1.0 convert_bitcast_fusion
  128.2 1.0 copy.256
  129.2 1.6 copy.253
  130.8 0.9 slice_bitcast_fusion.2
  131.7 1.2 collective-permute-start.12
  132.8 2.7 %collective-permute-start.14 = (f32[128,512]{1,0:T(8,128)}, f32[128,512]{1,0:T(8,128)}, u32[]{:S(2)}, u32[]{:S(2)}) collective-permute-start(f32[128,512]{1,0:T(8,128)} %get-tuple-element.43), channel_id=1, source_target_pairs={{0,3},{1,0},{2,1},{3,2},{4,7},{5,4},{6,5},{7,6},{8,11},{9,8},{10,9... | collective-permute-start | bytes 786440 | tf_op jit(solution)/shard_map/ppermute | solution.py:28
  135.5 1.0 fusion.32
  136.5 2.0 %copy.255 = bf16[512,512]{1,0:T(8,128)(2,1)} copy(bf16[512,512]{0,1:T(8,128)(2,1)} %fusion.32) | data formatting | bytes 1048576
  138.5 4.3 %collective-permute-done.12 = f32[128,512]{1,0:T(8,128)S(1)} collective-permute-done((f32[128,512]{1,0:T(8,128)}, f32[128,512]{1,0:T(8,128)S(1)}, u32[]{:S(2)}, u32[]{:S(2)}) %collective-permute-start.12) | collective-permute-done | bytes 262176 | tf_op jit(solution)/shard_map/ppermute | solution.py:28
  142.9 4.5 %collective-permute-done.14 = f32[128,512]{1,0:T(8,128)} collective-permute-done((f32[128,512]{1,0:T(8,128)}, f32[128,512]{1,0:T(8,128)}, u32[]{:S(2)}, u32[]{:S(2)}) %collective-permute-start.14) | collective-permute-done | bytes 262176 | tf_op jit(solution)/shard_map/ppermute | solution.py:28
  147.4 11.3 %collective-permute-done.13 = f32[128,512]{1,0:T(8,128)} collective-permute-done((f32[128,512]{1,0:T(8,128)}, f32[128,512]{1,0:T(8,128)}, u32[]{:S(2)}, u32[]{:S(2)}) %collective-permute-start.13) | collective-permute-done | bytes 262176 | tf_op jit(solution)/shard_map/ppermute | solution.py:28
  158.6 1.8 %fusion.58 = f32[1,128,512]{2,1,0:T(8,128)} fusion(f32[4,128,512]{2,1,0:T(8,128)S(1)} %broadcast_select_fusion, f32[128,512]{1,0:T(8,128)} %collective-permute-done.14, f32[128,512]{1,0:T(8,128)} %collective-permute-done.13, f32[128,512]{1,0:T(8,128)S(1)} %collective-permute-done.12), kind=kLoop, calls=%fused_computation.100 | loop fusion | flops 196608 | bytes 1310720 | tf_op jit(solution)/shard_map/reduce_sum | solution.py:109
  160.4 2.0 %reduce_sum.28 = f32[64,512]{1,0:T(8,128)} reduce(f32[8,64,512]{2,1,0:T(8,128)} %all-to-all-done.4, f32[]{:T(128)} %constant.111.clone.1), dimensions={0}, to_apply=%region_0.5 | reduce | flops 229376 | bytes 1179652 | tf_op jit(solution)/shard_map/reduce_sum | solution.py:111
  (109 shorter events, 20.5 us)
Async XLA Ops:
  0.6 59.0 %copy-start = (bf16[1,512,512]{2,1,0:T(8,128)(2,1)S(1)}, bf16[1,512,512]{2,1,0:T(8,128)(2,1)}, u32[]{:S(2)}) copy-start(bf16[1,512,512]{2,1,0:T(8,128)(2,1)} %param.21) | copy-start | bytes 1572868
  0.6 1.4 copy-start.17
  0.7 1.4 copy-start.15
  2.0 1.6 copy-start.1
  3.6 14.9 %all-to-all-start = ((bf16[8,64,512]{2,1,0:T(8,128)(2,1)}), bf16[8,64,512]{2,1,0:T(8,128)(2,1)S(1)}, u32[]{:S(2)}, u32[]{:S(2)}) async-start(bf16[8,64,512]{2,1,0:T(8,128)(2,1)} %bitcast.2), calls=%async_computation | async-start | bytes 1048576 | tf_op jit(solution)/shard_map/all_to_all | solution.py:33
  9.5 9.0 %copy-start.4 = (bf16[512,512]{1,0:T(8,128)(2,1)S(1)}, bf16[512,512]{1,0:T(8,128)(2,1)}, u32[]{:S(2)}) copy-start(bf16[512,512]{1,0:T(8,128)(2,1)} %param.23) | copy-start | bytes 1572868
  21.7 7.0 %collective-permute-start.2 = (bf16[512,128]{1,0:T(8,128)(2,1)S(1)}, bf16[512,128]{1,0:T(8,128)(2,1)S(1)}, u32[]{:S(2)}, u32[]{:S(2)}) collective-permute-start(bf16[512,128]{1,0:T(8,128)(2,1)S(1)} %bitcast.147), channel_id=1, source_target_pairs={{0,3},{1,0},{2,1},{3,2},{4,7},{5,4},{6,5},{7,6},{8,11},{9,8},{10,9... | collective-permute-start | bytes 393224 | tf_op jit(solution)/shard_map/ppermute | solution.py:28
  25.4 7.2 %collective-permute-start = (bf16[512,128]{1,0:T(8,128)(2,1)S(1)}, bf16[512,128]{1,0:T(8,128)(2,1)S(1)}, u32[]{:S(2)}, u32[]{:S(2)}) collective-permute-start(bf16[512,128]{1,0:T(8,128)(2,1)S(1)} %bitcast.137), channel_id=1, source_target_pairs={{0,1},{1,2},{2,3},{3,0},{4,5},{5,6},{6,7},{7,4},{8,9},{9,10},{10,1... | collective-permute-start | bytes 393224 | tf_op jit(solution)/shard_map/ppermute | solution.py:28
  25.4 10.5 %collective-permute-start.1 = (bf16[512,128]{1,0:T(8,128)(2,1)S(1)}, bf16[512,128]{1,0:T(8,128)(2,1)S(1)}, u32[]{:S(2)}, u32[]{:S(2)}) collective-permute-start(bf16[512,128]{1,0:T(8,128)(2,1)S(1)} %bitcast.133), channel_id=1, source_target_pairs={{0,2},{1,3},{2,0},{3,1},{4,6},{5,7},{6,4},{7,5},{8,10},{9,11},{10,... | collective-permute-start | bytes 393224 | tf_op jit(solution)/shard_map/ppermute | solution.py:28
  27.7 0.8 copy-start.11
  38.8 9.0 %collective-permute-start.3 = (bf16[512,128]{1,0:T(8,128)(2,1)S(1)}, bf16[512,128]{1,0:T(8,128)(2,1)S(1)}, u32[]{:S(2)}, u32[]{:S(2)}) collective-permute-start(bf16[512,128]{1,0:T(8,128)(2,1)S(1)} %bitcast.149), channel_id=1, source_target_pairs={{0,1},{1,2},{2,3},{3,0},{4,5},{5,6},{6,7},{7,4},{8,9},{9,10},{10,1... | collective-permute-start | bytes 393224 | tf_op jit(solution)/shard_map/ppermute | solution.py:28
  38.9 11.2 %collective-permute-start.4 = (bf16[512,128]{1,0:T(8,128)(2,1)S(1)}, bf16[512,128]{1,0:T(8,128)(2,1)S(1)}, u32[]{:S(2)}, u32[]{:S(2)}) collective-permute-start(bf16[512,128]{1,0:T(8,128)(2,1)S(1)} %bitcast.138), channel_id=1, source_target_pairs={{0,2},{1,3},{2,0},{3,1},{4,6},{5,7},{6,4},{7,5},{8,10},{9,11},{10,... | collective-permute-start | bytes 393224 | tf_op jit(solution)/shard_map/ppermute | solution.py:28
  41.2 9.0 %collective-permute-start.5 = (bf16[512,128]{1,0:T(8,128)(2,1)S(1)}, bf16[512,128]{1,0:T(8,128)(2,1)S(1)}, u32[]{:S(2)}, u32[]{:S(2)}) collective-permute-start(bf16[512,128]{1,0:T(8,128)(2,1)S(1)} %bitcast.134), channel_id=1, source_target_pairs={{0,3},{1,0},{2,1},{3,2},{4,7},{5,4},{6,5},{7,6},{8,11},{9,8},{10,9... | collective-permute-start | bytes 393224 | tf_op jit(solution)/shard_map/ppermute | solution.py:28
  44.1 13.2 %all-to-all-start.1 = ((bf16[8,64,512]{2,1,0:T(8,128)(2,1)}), bf16[8,64,512]{2,1,0:T(8,128)(2,1)S(1)}, u32[]{:S(2)}, u32[]{:S(2)}) async-start(bf16[8,64,512]{2,1,0:T(8,128)(2,1)} %copy.209), calls=%async_computation.1 | async-start | bytes 1048576 | tf_op jit(solution)/shard_map/all_to_all | solution.py:33
  57.4 0.7 copy-start.12
  58.1 1.5 copy-start.6
  65.9 5.9 %copy-start.2 = (bf16[512,512]{0,1:T(8,128)(2,1)S(1)}, bf16[512,512]{0,1:T(8,128)(2,1)}, u32[]{:S(2)}) copy-start(bf16[512,512]{0,1:T(8,128)(2,1)} %copy-done.1) | copy-start | bytes 1572868
  67.7 11.2 %collective-permute-start.8 = (bf16[512,128]{1,0:T(8,128)(2,1)S(1)}, bf16[512,128]{1,0:T(8,128)(2,1)S(1)}, u32[]{:S(2)}, u32[]{:S(2)}) collective-permute-start(bf16[512,128]{1,0:T(8,128)(2,1)S(1)} %bitcast.145), channel_id=1, source_target_pairs={{0,3},{1,0},{2,1},{3,2},{4,7},{5,4},{6,5},{7,6},{8,11},{9,8},{10,9... | collective-permute-start | bytes 393224 | tf_op jit(solution)/shard_map/ppermute | solution.py:28
  68.4 3.4 %copy-start.13 = (f32[512]{0:T(512)S(1)}, f32[512]{0:T(512)}, u32[]{:S(2)}) copy-start(f32[512]{0:T(512)} %param.18) | copy-start | bytes 6148
  68.4 12.2 %collective-permute-start.6 = (bf16[512,128]{1,0:T(8,128)(2,1)}, bf16[512,128]{1,0:T(8,128)(2,1)}, u32[]{:S(2)}, u32[]{:S(2)}) collective-permute-start(bf16[512,128]{1,0:T(8,128)(2,1)} %bitcast.36), channel_id=1, source_target_pairs={{0,1},{1,2},{2,3},{3,0},{4,5},{5,6},{6,7},{7,4},{8,9},{9,10},{10,1... | collective-permute-start | bytes 393224 | tf_op jit(solution)/shard_map/ppermute | solution.py:28
  69.8 12.7 %collective-permute-start.7 = (bf16[512,128]{1,0:T(8,128)(2,1)}, bf16[512,128]{1,0:T(8,128)(2,1)}, u32[]{:S(2)}, u32[]{:S(2)}) collective-permute-start(bf16[512,128]{1,0:T(8,128)(2,1)} %bitcast.38), channel_id=1, source_target_pairs={{0,2},{1,3},{2,0},{3,1},{4,6},{5,7},{6,4},{7,5},{8,10},{9,11},{10,... | collective-permute-start | bytes 393224 | tf_op jit(solution)/shard_map/ppermute | solution.py:28
  75.4 21.1 %all-to-all-start.2 = ((bf16[8,64,512]{2,1,0:T(8,128)(2,1)}), bf16[8,64,512]{2,1,0:T(8,128)(2,1)S(1)}, u32[]{:S(2)}, u32[]{:S(2)}) async-start(bf16[8,64,512]{2,1,0:T(8,128)(2,1)} %bitcast.128), calls=%async_computation.2 | async-start | bytes 1048576 | tf_op jit(solution)/shard_map/all_to_all | solution.py:33
  78.9 0.6 copy-start.10
  92.6 11.2 %collective-permute-start.9 = (bf16[512,128]{1,0:T(8,128)(2,1)}, bf16[512,128]{1,0:T(8,128)(2,1)S(1)}, u32[]{:S(2)}, u32[]{:S(2)}) collective-permute-start(bf16[512,128]{1,0:T(8,128)(2,1)} %bitcast.139), channel_id=1, source_target_pairs={{0,1},{1,2},{2,3},{3,0},{4,5},{5,6},{6,7},{7,4},{8,9},{9,10},{10,1... | collective-permute-start | bytes 393224 | tf_op jit(solution)/shard_map/ppermute | solution.py:28
  93.6 12.7 %collective-permute-start.10 = (bf16[512,128]{1,0:T(8,128)(2,1)}, bf16[512,128]{1,0:T(8,128)(2,1)}, u32[]{:S(2)}, u32[]{:S(2)}) collective-permute-start(bf16[512,128]{1,0:T(8,128)(2,1)} %bitcast.135), channel_id=1, source_target_pairs={{0,2},{1,3},{2,0},{3,1},{4,6},{5,7},{6,4},{7,5},{8,10},{9,11},{10,... | collective-permute-start | bytes 393224 | tf_op jit(solution)/shard_map/ppermute | solution.py:28
  94.2 14.0 %collective-permute-start.11 = (bf16[512,128]{1,0:T(8,128)(2,1)}, bf16[512,128]{1,0:T(8,128)(2,1)S(1)}, u32[]{:S(2)}, u32[]{:S(2)}) collective-permute-start(bf16[512,128]{1,0:T(8,128)(2,1)} %bitcast.132), channel_id=1, source_target_pairs={{0,3},{1,0},{2,1},{3,2},{4,7},{5,4},{6,5},{7,6},{8,11},{9,8},{10,9... | collective-permute-start | bytes 393224 | tf_op jit(solution)/shard_map/ppermute | solution.py:28
  97.8 4.5 %copy-start.8 = (bf16[512,512]{0,1:T(8,128)(2,1)S(1)}, bf16[512,512]{0,1:T(8,128)(2,1)}, u32[]{:S(2)}) copy-start(bf16[512,512]{0,1:T(8,128)(2,1)} %get-tuple-element.46) | copy-start | bytes 1572868
  97.8 17.3 %all-to-all-start.3 = ((bf16[8,64,512]{2,1,0:T(8,128)(2,1)}), bf16[8,64,512]{2,1,0:T(8,128)(2,1)}, u32[]{:S(2)}, u32[]{:S(2)}) async-start(bf16[8,64,512]{2,1,0:T(8,128)(2,1)} %copy.235), calls=%async_computation.3 | async-start | bytes 1048576 | tf_op jit(solution)/shard_map/all_to_all | solution.py:33
  103.8 0.7 copy-start.9
  114.2 0.9 copy-start.18
  115.2 2.8 %copy-start.14 = (f32[512]{0:T(512)S(1)}, f32[512]{0:T(512)}, u32[]{:S(2)}) copy-start(f32[512]{0:T(512)} %param.18) | copy-start | bytes 6148
  115.2 2.8 %copy-start.16 = (bf16[1,512,512]{2,1,0:T(8,128)(2,1)S(1)}, bf16[1,512,512]{2,1,0:T(8,128)(2,1)}, u32[]{:S(2)}) copy-start(bf16[1,512,512]{2,1,0:T(8,128)(2,1)} %param.19) | copy-start | bytes 1572868
  115.2 2.8 %copy-start.19 = (bf16[512,512]{0,1:T(8,128)(2,1)S(1)}, bf16[512,512]{0,1:T(8,128)(2,1)}, u32[]{:S(2)}) copy-start(bf16[512,512]{0,1:T(8,128)(2,1)} %get-tuple-element.66) | copy-start | bytes 1572868
  120.9 4.4 %copy-start.5 = (f32[512,512]{1,0:T(8,128)S(1)}, f32[512,512]{1,0:T(8,128)}, u32[]{:S(2)}) copy-start(f32[512,512]{1,0:T(8,128)} %fusion.65) | copy-start | bytes 3145732
  120.9 39.5 %all-to-all-start.4 = ((f32[8,64,512]{2,1,0:T(8,128)}), f32[8,64,512]{2,1,0:T(8,128)}, u32[]{:S(2)}, u32[]{:S(2)}) async-start(f32[8,64,512]{2,1,0:T(8,128)} %bitcast.53), calls=%async_computation.4 | async-start | bytes 2097152 | tf_op jit(solution)/shard_map/all_to_all | solution.py:33
  126.0 1.0 copy-start.3
  127.0 1.2 copy-start.7
  131.7 11.2 %collective-permute-start.12 = (f32[128,512]{1,0:T(8,128)}, f32[128,512]{1,0:T(8,128)S(1)}, u32[]{:S(2)}, u32[]{:S(2)}) collective-permute-start(f32[128,512]{1,0:T(8,128)} %get-tuple-element.42), channel_id=1, source_target_pairs={{0,1},{1,2},{2,3},{3,0},{4,5},{5,6},{6,7},{7,4},{8,9},{9,10},{10,1... | collective-permute-start | bytes 786440 | tf_op jit(solution)/shard_map/ppermute | solution.py:28
  132.8 14.5 %collective-permute-start.14 = (f32[128,512]{1,0:T(8,128)}, f32[128,512]{1,0:T(8,128)}, u32[]{:S(2)}, u32[]{:S(2)}) collective-permute-start(f32[128,512]{1,0:T(8,128)} %get-tuple-element.43), channel_id=1, source_target_pairs={{0,3},{1,0},{2,1},{3,2},{4,7},{5,4},{6,5},{7,6},{8,11},{9,8},{10,9... | collective-permute-start | bytes 786440 | tf_op jit(solution)/shard_map/ppermute | solution.py:28
  135.5 23.1 %collective-permute-start.13 = (f32[128,512]{1,0:T(8,128)}, f32[128,512]{1,0:T(8,128)}, u32[]{:S(2)}, u32[]{:S(2)}) collective-permute-start(f32[128,512]{1,0:T(8,128)} %get-tuple-element.44), channel_id=1, source_target_pairs={{0,2},{1,3},{2,0},{3,1},{4,6},{5,7},{6,4},{7,5},{8,10},{9,11},{10,... | collective-permute-start | bytes 786440 | tf_op jit(solution)/shard_map/ppermute | solution.py:28

commit v2 on v1

--- a/solution.py
+++ b/solution.py
@@ -62,10 +62,9 @@
     slope_in = jax.nn.sigmoid(gate_in * source)
     gated = (source * slope_in).astype(BF16)
     mixed_first = jnp.dot(first_blocks[0], gated, preferred_element_type=F32).astype(BF16)
+    upstream = cotangent
+    upstream_late, mixed_first = lax.optimization_barrier((upstream, mixed_first))
     first_arrived = swap(split_rows(mixed_first, n), "seq")
-
-    upstream = cotangent
-    upstream_late, first_arrived = lax.optimization_barrier((upstream, first_arrived))
     cot_pieces = to_shift_order(upstream_late.reshape(rows, m, kq), g_me, m, axis=1)
     cot_arrived = exchange(jnp.transpose(cot_pieces, (1, 0, 2)), "ch")
     act_grad_out = jnp.einsum(
@@ -105,10 +104,10 @@
     added = jnp.transpose(added_back, (1, 0, 2)).reshape(rows, block_width)
     outputs = (hidden.astype(F32) + added.astype(F32)).astype(BF16)
     block_part = jnp.dot(first_grad, gated.T, preferred_element_type=F32)
-    block_arrived = exchange(to_shift_order(split_rows(block_part, m), g_me, m), "ch")
-    block_grad = jnp.sum(block_arrived, axis=0)[None]
-    channel_arrived = swap(split_rows(channel_part, n), "seq")
-    channel_grad = jnp.sum(channel_arrived, axis=0)[None]
+    block_pieces = to_shift_order(split_rows(block_part, m), g_me, m).astype(BF16)
+    block_grad = jnp.sum(exchange(block_pieces, "ch").astype(F32), axis=0)[None]
+    channel_arrived = swap(split_rows(channel_part, n).astype(BF16), "seq")
+    channel_grad = jnp.sum(channel_arrived.astype(F32), axis=0)[None]
 
     spread = jnp.dot(first_blocks[0].T, first_grad, preferred_element_type=F32)
     input_grad = grad_flat + spread * (slope_in + gate_in * source * slope_in * (1.0 - slope_in))

time: 164 us -> 135 us (0.82)
  waiting for transfers between devices: 39.3 us -> 9.96 us
  starting transfers between devices: 41.5 us -> 45 us
  other arithmetic: 13.1 us -> 11.1 us
    ppermute x15, waiting for transfers between devices: 29.7 us -> 3.32 us  [exchange(): lax.ppermute(pieces[k], axis_name, [(i, (i + k) % n) for i in range(n)])]
    ppermute x15, starting transfers between devices: 20.3 us -> 24.9 us  [exchange(): lax.ppermute(pieces[k], axis_name, [(i, (i + k) % n) for i in range(n)])]
    all_to_all x5, waiting for transfers between devices: 9.56 us -> 6.65 us  [swap(): return lax.all_to_all(pieces, axis_name, 0, 0, tiled=True)]
    convert_element_type x2, other arithmetic: 2 us -> 0.24 us  [on_device(): outputs = (hidden.astype(F32) + added.astype(F32)).astype(BF16)]
    unnamed x45 -> x41, local copies, waits for them, and re-layouts: 8.27 us -> 7.51 us
    slice x4 -> x5, local copies, waits for them, and re-layouts: 4.58 us -> 5.3 us  [exchange(): got = [pieces[0]]]
  transfers between devices with their start and end apart: 20 -> 20, of which waited for: 9 -> 3; matrix products, arithmetic and copies ran while one was open for 31% -> 40% of each run, Pallas kernels for 0% -> 0%
where the time goes in v2:
time: 135 us; the launch traced here: 134 us
  local copies, waits for them, and re-layouts  49.6 us (37%)
  starting transfers between devices  45 us (33%)
  matrix products  16.8 us (12%)
  other arithmetic  11.1 us (8%)
  waiting for transfers between devices  9.96 us (7%)
    ppermute x15, starting transfers between devices, exchange(): lax.ppermute(pieces[k], axis_name, [(i, (i + k) % n) for i in range(n)])  24.9 us
    all_to_all x5, starting transfers between devices, swap(): return lax.all_to_all(pieces, axis_name, 0, 0, tiled=True)  20.2 us
    another operation x14, local copies, waits for them, and re-layouts, exchange(): return jnp.stack(got)  11.2 us
    slice x12, local copies, waits for them, and re-layouts, exchange(): pieces[k]  7.79 us
    unnamed x41, local copies, waits for them, and re-layouts  7.51 us
    all_to_all x5, waiting for transfers between devices, swap(): return lax.all_to_all(pieces, axis_name, 0, 0, tiled=True)  6.65 us
    slice x5, local copies, waits for them, and re-layouts, exchange(): got = [pieces[0]]  5.3 us
    gather x5, local copies, waits for them, and re-layouts, to_shift_order(): return jnp.take(x, (me + jnp.arange(n)) % n, axis=axis)  3.72 us
  transfers between devices with their start and end apart: 20, of which 3 were waited for; matrix products, arithmetic and copies ran while one was open for 40% of the time, Pallas kernels for 0%

profile of v2, /device:TPU:0, one launch (start us, length us, event | category | flops | bytes accessed | tf_op | source)
XLA Modules:
  0.0 133.6 jit_solution(18002511788269225753)
XLA Ops:
  0.7 1.3 copy.210
  5.2 0.8 fusion.71
  6.1 3.1 %collective-permute-start = (bf16[512,128]{1,0:T(8,128)(2,1)S(1)}, bf16[512,128]{1,0:T(8,128)(2,1)S(1)}, u32[]{:S(2)}, u32[]{:S(2)}) collective-permute-start(bf16[512,128]{1,0:T(8,128)(2,1)S(1)} %bitcast.131), channel_id=1, source_target_pairs={{0,1},{1,2},{2,3},{3,0},{4,5},{5,6},{6,7},{7,4},{8,9},{9,10},{10,1... | collective-permute-start | bytes 393224 | tf_op jit(solution)/shard_map/ppermute | solution.py:28
  9.4 2.7 %collective-permute-start.1 = (bf16[512,128]{1,0:T(8,128)(2,1)S(1)}, bf16[512,128]{1,0:T(8,128)(2,1)S(1)}, u32[]{:S(2)}, u32[]{:S(2)}) collective-permute-start(bf16[512,128]{1,0:T(8,128)(2,1)S(1)} %bitcast.133), channel_id=1, source_target_pairs={{0,2},{1,3},{2,0},{3,1},{4,6},{5,7},{6,4},{7,5},{8,10},{9,11},{10,... | collective-permute-start | bytes 393224 | tf_op jit(solution)/shard_map/ppermute | solution.py:28
  12.2 1.4 %collective-permute-start.2 = (bf16[512,128]{1,0:T(8,128)(2,1)S(1)}, bf16[512,128]{1,0:T(8,128)(2,1)S(1)}, u32[]{:S(2)}, u32[]{:S(2)}) collective-permute-start(bf16[512,128]{1,0:T(8,128)(2,1)S(1)} %bitcast.135), channel_id=1, source_target_pairs={{0,3},{1,0},{2,1},{3,2},{4,7},{5,4},{6,5},{7,6},{8,11},{9,8},{10,9... | collective-permute-start | bytes 393224 | tf_op jit(solution)/shard_map/ppermute | solution.py:28
  13.6 1.0 copy.211
  14.6 3.7 %all-to-all-start = ((bf16[8,64,512]{2,1,0:T(8,128)(2,1)}), bf16[8,64,512]{2,1,0:T(8,128)(2,1)S(1)}, u32[]{:S(2)}, u32[]{:S(2)}) async-start(bf16[8,64,512]{2,1,0:T(8,128)(2,1)} %bitcast.2), calls=%async_computation | async-start | bytes 1048576 | tf_op jit(solution)/shard_map/all_to_all | solution.py:33
  21.6 1.0 copy.216
  23.5 0.8 copy.250
  24.9 1.3 %fusion.7 = bf16[4,512,128]{1,0,2:T(4,128)(2,1)S(1)} fusion(bf16[128,4,4]{2,1,0:T(4,128)(2,1)S(1)} %copy.227, bf16[1,512,128]{1,0,2:T(2,128)(2,1)S(1)} %copy.226, bf16[1,512,128]{1,0,2:T(2,128)(2,1)S(1)} %copy.225, bf16[1,512,128]{1,0,2:T(2,128)(2,1)S(1)} %copy.224, bf16[1,512,128]{1,0,2:T(2,128)(2,1)S(1)} %get-tuple-element.60), kind=kOutput, calls=%fused_computation.32 | convolution fusion | flops 4194304 | bytes 1052672 | tf_op jit(solution)/shard_map/krq,qpk->prq/dot_general | solution.py:70
  26.3 0.8 fusion.70
  28.7 2.9 %collective-permute-start.5 = (bf16[512,128]{1,0:T(8,128)(2,1)S(1)}, bf16[512,128]{1,0:T(8,128)(2,1)S(1)}, u32[]{:S(2)}, u32[]{:S(2)}) collective-permute-start(bf16[512,128]{1,0:T(8,128)(2,1)S(1)} %bitcast.145), channel_id=1, source_target_pairs={{0,3},{1,0},{2,1},{3,2},{4,7},{5,4},{6,5},{7,6},{8,11},{9,8},{10,9... | collective-permute-start | bytes 393224 | tf_op jit(solution)/shard_map/ppermute | solution.py:28
  32.1 0.9 copy.214
  33.0 4.2 %all-to-all-start.1 = ((bf16[8,64,512]{2,1,0:T(8,128)(2,1)}), bf16[8,64,512]{2,1,0:T(8,128)(2,1)S(1)}, u32[]{:S(2)}, u32[]{:S(2)}) async-start(bf16[8,64,512]{2,1,0:T(8,128)(2,1)} %copy.214), calls=%async_computation.1 | async-start | bytes 1048576 | tf_op jit(solution)/shard_map/all_to_all | solution.py:33
  37.4 3.3 %collective-permute-done.4 = bf16[512,128]{1,0:T(8,128)(2,1)S(1)} collective-permute-done((bf16[512,128]{1,0:T(8,128)(2,1)S(1)}, bf16[512,128]{1,0:T(8,128)(2,1)S(1)}, u32[]{:S(2)}, u32[]{:S(2)}) %collective-permute-start.4) | collective-permute-done | bytes 131104 | tf_op jit(solution)/shard_map/ppermute | solution.py:28
  41.1 1.2 pad_maximum_fusion
  43.6 1.3 %copy.235 = f32[512,4,128]{0,2,1:T(8,128)} copy(f32[512,4,128]{2,0,1:T(8,128)S(1)} %convert_bitcast_fusion.1) | data formatting | bytes 2097152 | tf_op jit(solution)/shard_map/convert_element_type | solution.py:89
  44.9 2.0 %all-to-all-done.1 = bf16[8,64,512]{2,1,0:T(8,128)(2,1)S(1)} async-done(((bf16[8,64,512]{2,1,0:T(8,128)(2,1)}), bf16[8,64,512]{2,1,0:T(8,128)(2,1)S(1)}, u32[]{:S(2)}, u32[]{:S(2)}) %all-to-all-start.1) | async-done | bytes 524320 | tf_op jit(solution)/shard_map/all_to_all | solution.py:33
  47.8 1.5 %fusion.32 = bf16[512,512]{0,1:T(8,128)(2,1)S(1)} fusion(bf16[512,512]{0,1:T(8,128)(2,1)} %copy-done.1, f32[512,512]{0,1:T(8,128)S(1)} %copy.215, f32[512]{0:T(512)S(1)} %copy-done.10), kind=kLoop, calls=%fused_computation.57 | loop fusion | flops 2097152 | bytes 2099200 | tf_op jit(solution)/shard_map/convert_element_type | solution.py:80
  49.3 2.1 %multiply_convert_fusion = (bf16[512,512]{0,1:T(8,128)(2,1)}, bf16[512,512]{0,1:T(8,128)(2,1)}) fusion(f32[512,4,128]{0,2,1:T(8,128)S(1)} %copy-done.5, bf16[512,512]{0,1:T(8,128)(2,1)S(1)} %fusion.32, bf16[1,512,512]{2,1,0:T(8,128)(2,1)S(1)} %copy-done), kind=kOutput, calls=%fused_computation.70 | convolution fusion | flops 274202624 | bytes 3145728 | tf_op jit(solution)/shard_map/dot_general | solution.py:81
  51.4 1.3 copy.242
  54.1 1.4 %fusion.69 = (bf16[1,512,128]{1,0,2:T(2,128)(2,1)}, bf16[1,512,128]{1,0,2:T(2,128)(2,1)S(1)}, bf16[1,512,128]{1,0,2:T(2,128)(2,1)S(1)}, bf16[1,512,128]{1,0,2:T(2,128)(2,1)S(1)}) fusion(bf16[4,512,128]{1,0,2:T(4,128)(2,1)S(1)} %broadcast_select_fusion), kind=kLoop, calls=%fused_computation.132 | loop fusion | bytes 1048576 | tf_op jit(solution)/shard_map/slice | solution.py:26
  55.6 0.8 copy.244
  56.4 0.8 collective-permute-start.6
  57.2 0.8 copy.245
  58.0 1.2 collective-permute-start.7
  59.2 0.8 copy.246
  60.0 2.9 %collective-permute-start.8 = (bf16[512,128]{1,0:T(8,128)(2,1)}, bf16[512,128]{1,0:T(8,128)(2,1)}, u32[]{:S(2)}, u32[]{:S(2)}) collective-permute-start(bf16[512,128]{1,0:T(8,128)(2,1)} %bitcast.40), channel_id=1, source_target_pairs={{0,3},{1,0},{2,1},{3,2},{4,7},{5,4},{6,5},{7,6},{8,11},{9,8},{10,9... | collective-permute-start | bytes 393224 | tf_op jit(solution)/shard_map/ppermute | solution.py:28
  62.9 2.6 %fusion.23 = (bf16[512,512]{0,1:T(8,128)(2,1)S(1)}, bf16[512,512]{0,1:T(8,128)(2,1)}) fusion(bf16[512,512]{0,1:T(8,128)(2,1)S(1)} %copy-done.2, f32[512]{0:T(512)S(1)} %copy-done.11, bf16[512,512]{0,1:T(8,128)(2,1)} %get-tuple-element.43, bf16[1,512,512]{2,1,0:T(8,128)(2,1)S(1)} %copy-done, bf16[512,512]{0,1:T(8,128)(2,1)} %copy.216), kind=kOutput, calls=%fused_computation.48 | convolution fusion | flops 271319040 | bytes 3147776 | tf_op jit(solution)/shard_map/dot_general | solution.py:90
  65.5 1.0 copy.237
  66.5 3.5 %all-to-all-start.2 = ((bf16[8,64,512]{2,1,0:T(8,128)(2,1)}), bf16[8,64,512]{2,1,0:T(8,128)(2,1)S(1)}, u32[]{:S(2)}, u32[]{:S(2)}) async-start(bf16[8,64,512]{2,1,0:T(8,128)(2,1)} %bitcast.126), calls=%async_computation.2 | async-start | bytes 1048576 | tf_op jit(solution)/shard_map/all_to_all | solution.py:33
  70.7 1.1 copy.247
  71.8 1.8 %copy.248 = bf16[1,512,128]{1,0,2:T(2,128)(2,1)} copy(bf16[1,512,128]{2,1,0:T(8,128)(2,1)} %bitcast.39) | data formatting | bytes 262144 | tf_op jit(solution)/shard_map/stack | solution.py:29
  73.6 1.8 %copy.249 = bf16[1,512,128]{1,0,2:T(2,128)(2,1)} copy(bf16[1,512,128]{2,1,0:T(8,128)(2,1)} %bitcast.41) | data formatting | bytes 262144 | tf_op jit(solution)/shard_map/stack | solution.py:29
  75.3 2.5 %fusion.9 = bf16[4,512,128]{1,0,2:T(4,128)(2,1)S(1)} fusion(bf16[128,4,4]{1,2,0:T(4,128)(2,1)} %copy.250, bf16[1,512,128]{1,0,2:T(2,128)(2,1)} %copy.249, bf16[1,512,128]{1,0,2:T(2,128)(2,1)} %copy.248, bf16[1,512,128]{1,0,2:T(2,128)(2,1)S(1)} %copy.247, bf16[1,512,128]{1,0,2:T(2,128)(2,1)} %get-tuple-element.52), kind=kOutput, calls=%fused_computation.34 | convolution fusion | flops 4194304 | bytes 1052672 | tf_op jit(solution)/shard_map/krq,qkp->prq/dot_general | solution.py:86
  77.9 1.6 %fusion.68 = (bf16[1,512,128]{1,0,2:T(2,128)(2,1)}, bf16[1,512,128]{1,0,2:T(2,128)(2,1)S(1)}, bf16[1,512,128]{1,0,2:T(2,128)(2,1)}, bf16[1,512,128]{1,0,2:T(2,128)(2,1)}) fusion(bf16[4,512,128]{1,0,2:T(4,128)(2,1)S(1)} %fusion.9), kind=kLoop, calls=%fused_computation.131 | loop fusion | bytes 1048576 | tf_op jit(solution)/shard_map/slice | solution.py:26
  79.5 1.7 %copy.251 = bf16[1,512,128]{2,1,0:T(8,128)(2,1)} copy(bf16[1,512,128]{1,0,2:T(2,128)(2,1)} %get-tuple-element.51) | data formatting | bytes 262144 | tf_op jit(solution)/shard_map/slice | solution.py:28
  81.3 1.7 %copy.252 = bf16[1,512,128]{2,1,0:T(8,128)(2,1)} copy(bf16[1,512,128]{1,0,2:T(2,128)(2,1)} %get-tuple-element.50) | data formatting | bytes 262144 | tf_op jit(solution)/shard_map/slice | solution.py:28
  83.1 1.1 collective-permute-start.10
  84.2 0.8 copy.253
  85.0 2.6 %collective-permute-start.11 = (bf16[512,128]{1,0:T(8,128)(2,1)}, bf16[512,128]{1,0:T(8,128)(2,1)S(1)}, u32[]{:S(2)}, u32[]{:S(2)}) collective-permute-start(bf16[512,128]{1,0:T(8,128)(2,1)} %bitcast.139), channel_id=1, source_target_pairs={{0,3},{1,0},{2,1},{3,2},{4,7},{5,4},{6,5},{7,6},{8,11},{9,8},{10,9... | collective-permute-start | bytes 393224 | tf_op jit(solution)/shard_map/ppermute | solution.py:28
  88.0 1.0 copy.240
  89.0 4.5 %all-to-all-start.3 = ((bf16[8,64,512]{2,1,0:T(8,128)(2,1)}), bf16[8,64,512]{2,1,0:T(8,128)(2,1)}, u32[]{:S(2)}, u32[]{:S(2)}) async-start(bf16[8,64,512]{2,1,0:T(8,128)(2,1)} %copy.240), calls=%async_computation.3 | async-start | bytes 1048576 | tf_op jit(solution)/shard_map/all_to_all | solution.py:33
  93.5 1.3 fusion.72
  94.8 1.1 copy.254
  95.9 1.8 %copy.255 = bf16[1,512,128]{1,0,2:T(2,128)(2,1)} copy(bf16[1,512,128]{2,1,0:T(8,128)(2,1)} %bitcast.46) | data formatting | bytes 262144 | tf_op jit(solution)/shard_map/stack | solution.py:29
  97.7 0.9 copy.256
  98.5 2.3 %pad_maximum_fusion.1 = bf16[4,512,128]{1,0,2:T(4,128)(2,1)S(1)} fusion(bf16[1,512,128]{1,0,2:T(2,128)(2,1)} %copy.256, bf16[1,512,128]{1,0,2:T(2,128)(2,1)} %copy.255, bf16[1,512,128]{1,0,2:T(2,128)(2,1)S(1)} %copy.254, bf16[1,512,128]{1,0,2:T(2,128)(2,1)} %get-tuple-element.48), kind=kLoop, calls=%fused_computation.86 | loop fusion | flops 2097152 | bytes 1048576 | tf_op jit(solution)/shard_map/stack | solution.py:29
  100.9 1.2 copy.257
  102.1 1.7 %gather_fusion.8 = bf16[4,512,128]{2,1,0:T(8,128)(2,1)S(1)} fusion(bf16[4,512,128]{2,1,0:T(8,128)(2,1)} %copy.257, s32[1024]{0:T(1024)S(1)} %pad_clamp_fusion.1), kind=kCustom, calls=%fused_computation.7.clone | custom fusion | bytes 1048592 | tf_op jit(solution)/shard_map/jit(_take)/gather | solution.py:16
  103.8 0.9 broadcast_select_fusion.2
  104.7 2.5 %fusion.64 = bf16[512,512]{1,0:T(8,128)(2,1)} fusion(bf16[512,512]{1,0:T(8,128)(2,1)} %bitcast.29, bf16[512,512]{0,1:T(8,128)(2,1)S(1)} %copy-done.2, f32[512]{0:T(512)S(1)} %copy-done.16), kind=kOutput, calls=%fused_computation.129 | convolution fusion | flops 270270464 | bytes 1574912 | tf_op jit(solution)/shard_map/dot_general | solution.py:106
  107.2 1.6 %gather_fusion = bf16[4,128,512]{2,1,0:T(8,128)(2,1)S(1)} fusion(bf16[4,128,512]{2,1,0:T(8,128)(2,1)} %bitcast.129, s32[1024]{0:T(1024)S(1)} %pad_clamp_fusion), kind=kCustom, calls=%fused_computation.8 | custom fusion | bytes 1048592 | tf_op jit(solution)/shard_map/jit(_take)/gather | solution.py:12
  109.0 0.7 fusion.67
  110.3 2.0 %collective-permute-start.13 = (bf16[128,512]{1,0:T(8,128)(2,1)}, bf16[128,512]{1,0:T(8,128)(2,1)S(1)}, u32[]{:S(2)}, u32[]{:S(2)}) collective-permute-start(bf16[128,512]{1,0:T(8,128)(2,1)} %get-tuple-element.46), channel_id=1, source_target_pairs={{0,2},{1,3},{2,0},{3,1},{4,6},{5,7},{6,4},{7,5},{8,10},{9,11},{10,... | collective-permute-start | bytes 393224 | tf_op jit(solution)/shard_map/ppermute | solution.py:28
  112.3 2.4 %collective-permute-start.14 = (bf16[128,512]{1,0:T(8,128)(2,1)}, bf16[128,512]{1,0:T(8,128)(2,1)}, u32[]{:S(2)}, u32[]{:S(2)}) collective-permute-start(bf16[128,512]{1,0:T(8,128)(2,1)} %get-tuple-element.45), channel_id=1, source_target_pairs={{0,3},{1,0},{2,1},{3,2},{4,7},{5,4},{6,5},{7,6},{8,11},{9,8},{10,9... | collective-permute-start | bytes 393224 | tf_op jit(solution)/shard_map/ppermute | solution.py:28
  114.7 3.0 %fusion.2 = bf16[512,512]{0,1:T(8,128)(2,1)} fusion(bf16[512,512]{1,0:T(8,128)(2,1)} %bitcast.29, bf16[512,512]{0,1:T(8,128)(2,1)S(1)} %copy-done.17, bf16[512,512]{0,1:T(8,128)(2,1)S(1)} %copy-done.2, f32[512,512]{0,1:T(8,128)S(1)} %copy.215, bf16[1,512,512]{2,1,0:T(8,128)(2,1)S(1)} %copy-done.14, f32[512]{0:T(512)S(1)} %copy-done.12, f32[512]{0:T(512)S(1)} %copy-done.16), kind=kOutput, calls=%fused_computation.27 | convolution fusion | flops 274464768 | bytes 3674112 | tf_op jit(solution)/shard_map/dot_general | solution.py:112
  117.7 4.3 %all-to-all-start.4 = ((bf16[8,64,512]{2,1,0:T(8,128)(2,1)}), bf16[8,64,512]{2,1,0:T(8,128)(2,1)}, u32[]{:S(2)}, u32[]{:S(2)}) async-start(bf16[8,64,512]{2,1,0:T(8,128)(2,1)} %bitcast.53), calls=%async_computation.4 | async-start | bytes 1048576 | tf_op jit(solution)/shard_map/all_to_all | solution.py:33
  122.6 0.9 copy-done.7
  123.5 1.0 copy.261
  124.5 1.0 copy.260
  125.5 1.7 %convert_reduce_fusion = f32[128,512]{1,0:T(8,128)} fusion(bf16[1,128,512]{2,1,0:T(8,128)(2,1)} %bitcast.62, bf16[1,128,512]{2,1,0:T(8,128)(2,1)S(1)} %bitcast.151, bf16[1,128,512]{2,1,0:T(8,128)(2,1)S(1)} %bitcast.150, bf16[1,128,512]{2,1,0:T(8,128)(2,1)S(1)} %get-tuple-element.44), kind=kLoop, calls=%fused_computation.67 | loop fusion | flops 1245184 | bytes 786432 | tf_op jit(solution)/shard_map/reduce_sum | solution.py:108
  127.2 4.6 %all-to-all-done.4 = bf16[8,64,512]{2,1,0:T(8,128)(2,1)} async-done(((bf16[8,64,512]{2,1,0:T(8,128)(2,1)}), bf16[8,64,512]{2,1,0:T(8,128)(2,1)}, u32[]{:S(2)}, u32[]{:S(2)}) %all-to-all-start.4) | async-done | bytes 524320 | tf_op jit(solution)/shard_map/all_to_all | solution.py:33
  131.8 1.8 %convert_reduce_fusion.1 = f32[64,512]{1,0:T(8,128)} fusion(bf16[8,64,512]{2,1,0:T(8,128)(2,1)} %all-to-all-done.4), kind=kLoop, calls=%fused_computation.69 | loop fusion | flops 491520 | bytes 655360 | tf_op jit(solution)/shard_map/reduce_sum | solution.py:110
  (106 shorter events, 17.0 us)
Async XLA Ops:
  0.6 48.7 %copy-start = (bf16[1,512,512]{2,1,0:T(8,128)(2,1)S(1)}, bf16[1,512,512]{2,1,0:T(8,128)(2,1)}, u32[]{:S(2)}) copy-start(bf16[1,512,512]{2,1,0:T(8,128)(2,1)} %param.21) | copy-start | bytes 1572868
  0.7 1.4 %copy-start.13 = (bf16[1,512,512]{2,1,0:T(8,128)(2,1)S(1)}, bf16[1,512,512]{2,1,0:T(8,128)(2,1)}, u32[]{:S(2)}) copy-start(bf16[1,512,512]{2,1,0:T(8,128)(2,1)} %param.19) | copy-start | bytes 1572868
  0.7 1.4 %copy-start.15 = (f32[512]{0:T(512)S(1)}, f32[512]{0:T(512)}, u32[]{:S(2)}) copy-start(f32[512]{0:T(512)} %param.17) | copy-start | bytes 6148
  2.1 0.8 copy-start.1
  2.1 1.2 copy-start.4
  6.1 18.2 %collective-permute-start = (bf16[512,128]{1,0:T(8,128)(2,1)S(1)}, bf16[512,128]{1,0:T(8,128)(2,1)S(1)}, u32[]{:S(2)}, u32[]{:S(2)}) collective-permute-start(bf16[512,128]{1,0:T(8,128)(2,1)S(1)} %bitcast.131), channel_id=1, source_target_pairs={{0,1},{1,2},{2,3},{3,0},{4,5},{5,6},{6,7},{7,4},{8,9},{9,10},{10,1... | collective-permute-start | bytes 393224 | tf_op jit(solution)/shard_map/ppermute | solution.py:28
  9.4 15.2 %collective-permute-start.1 = (bf16[512,128]{1,0:T(8,128)(2,1)S(1)}, bf16[512,128]{1,0:T(8,128)(2,1)S(1)}, u32[]{:S(2)}, u32[]{:S(2)}) collective-permute-start(bf16[512,128]{1,0:T(8,128)(2,1)S(1)} %bitcast.133), channel_id=1, source_target_pairs={{0,2},{1,3},{2,0},{3,1},{4,6},{5,7},{6,4},{7,5},{8,10},{9,11},{10,... | collective-permute-start | bytes 393224 | tf_op jit(solution)/shard_map/ppermute | solution.py:28
  12.2 12.5 %collective-permute-start.2 = (bf16[512,128]{1,0:T(8,128)(2,1)S(1)}, bf16[512,128]{1,0:T(8,128)(2,1)S(1)}, u32[]{:S(2)}, u32[]{:S(2)}) collective-permute-start(bf16[512,128]{1,0:T(8,128)(2,1)S(1)} %bitcast.135), channel_id=1, source_target_pairs={{0,3},{1,0},{2,1},{3,2},{4,7},{5,4},{6,5},{7,6},{8,11},{9,8},{10,9... | collective-permute-start | bytes 393224 | tf_op jit(solution)/shard_map/ppermute | solution.py:28
  14.6 17.0 %all-to-all-start = ((bf16[8,64,512]{2,1,0:T(8,128)(2,1)}), bf16[8,64,512]{2,1,0:T(8,128)(2,1)S(1)}, u32[]{:S(2)}, u32[]{:S(2)}) async-start(bf16[8,64,512]{2,1,0:T(8,128)(2,1)} %bitcast.2), calls=%async_computation | async-start | bytes 1048576 | tf_op jit(solution)/shard_map/all_to_all | solution.py:33
  22.6 0.7 copy-start.9
  27.2 10.0 %collective-permute-start.3 = (bf16[512,128]{1,0:T(8,128)(2,1)S(1)}, bf16[512,128]{1,0:T(8,128)(2,1)S(1)}, u32[]{:S(2)}, u32[]{:S(2)}) collective-permute-start(bf16[512,128]{1,0:T(8,128)(2,1)S(1)} %bitcast.141), channel_id=1, source_target_pairs={{0,1},{1,2},{2,3},{3,0},{4,5},{5,6},{6,7},{7,4},{8,9},{9,10},{10,1... | collective-permute-start | bytes 393224 | tf_op jit(solution)/shard_map/ppermute | solution.py:28
  28.1 12.6 %collective-permute-start.4 = (bf16[512,128]{1,0:T(8,128)(2,1)S(1)}, bf16[512,128]{1,0:T(8,128)(2,1)S(1)}, u32[]{:S(2)}, u32[]{:S(2)}) collective-permute-start(bf16[512,128]{1,0:T(8,128)(2,1)S(1)} %bitcast.143), channel_id=1, source_target_pairs={{0,2},{1,3},{2,0},{3,1},{4,6},{5,7},{6,4},{7,5},{8,10},{9,11},{10,... | collective-permute-start | bytes 393224 | tf_op jit(solution)/shard_map/ppermute | solution.py:28
  28.7 12.2 %collective-permute-start.5 = (bf16[512,128]{1,0:T(8,128)(2,1)S(1)}, bf16[512,128]{1,0:T(8,128)(2,1)S(1)}, u32[]{:S(2)}, u32[]{:S(2)}) collective-permute-start(bf16[512,128]{1,0:T(8,128)(2,1)S(1)} %bitcast.145), channel_id=1, source_target_pairs={{0,3},{1,0},{2,1},{3,2},{4,7},{5,4},{6,5},{7,6},{8,11},{9,8},{10,9... | collective-permute-start | bytes 393224 | tf_op jit(solution)/shard_map/ppermute | solution.py:28
  33.0 13.9 %all-to-all-start.1 = ((bf16[8,64,512]{2,1,0:T(8,128)(2,1)}), bf16[8,64,512]{2,1,0:T(8,128)(2,1)S(1)}, u32[]{:S(2)}, u32[]{:S(2)}) async-start(bf16[8,64,512]{2,1,0:T(8,128)(2,1)} %copy.214), calls=%async_computation.1 | async-start | bytes 1048576 | tf_op jit(solution)/shard_map/all_to_all | solution.py:33
  47.1 0.7 copy-start.10
  47.8 1.5 %copy-start.5 = (f32[512,4,128]{0,2,1:T(8,128)S(1)}, f32[512,4,128]{0,2,1:T(8,128)}, u32[]{:S(2)}) copy-start(f32[512,4,128]{0,2,1:T(8,128)} %copy.235) | copy-start | bytes 3145732
  55.6 7.4 %copy-start.2 = (bf16[512,512]{0,1:T(8,128)(2,1)S(1)}, bf16[512,512]{0,1:T(8,128)(2,1)}, u32[]{:S(2)}) copy-start(bf16[512,512]{0,1:T(8,128)(2,1)} %copy-done.1) | copy-start | bytes 1572868
  56.4 13.6 %collective-permute-start.6 = (bf16[512,128]{1,0:T(8,128)(2,1)}, bf16[512,128]{1,0:T(8,128)(2,1)S(1)}, u32[]{:S(2)}, u32[]{:S(2)}) collective-permute-start(bf16[512,128]{1,0:T(8,128)(2,1)} %bitcast.147), channel_id=1, source_target_pairs={{0,1},{1,2},{2,3},{3,0},{4,5},{5,6},{6,7},{7,4},{8,9},{9,10},{10,1... | collective-permute-start | bytes 393224 | tf_op jit(solution)/shard_map/ppermute | solution.py:28
  58.0 13.8 %collective-permute-start.7 = (bf16[512,128]{1,0:T(8,128)(2,1)}, bf16[512,128]{1,0:T(8,128)(2,1)}, u32[]{:S(2)}, u32[]{:S(2)}) collective-permute-start(bf16[512,128]{1,0:T(8,128)(2,1)} %bitcast.38), channel_id=1, source_target_pairs={{0,2},{1,3},{2,0},{3,1},{4,6},{5,7},{6,4},{7,5},{8,10},{9,11},{10,... | collective-permute-start | bytes 393224 | tf_op jit(solution)/shard_map/ppermute | solution.py:28
  60.0 2.9 %copy-start.11 = (f32[512]{0:T(512)S(1)}, f32[512]{0:T(512)}, u32[]{:S(2)}) copy-start(f32[512]{0:T(512)} %param.18) | copy-start | bytes 6148
  60.0 13.6 %collective-permute-start.8 = (bf16[512,128]{1,0:T(8,128)(2,1)}, bf16[512,128]{1,0:T(8,128)(2,1)}, u32[]{:S(2)}, u32[]{:S(2)}) collective-permute-start(bf16[512,128]{1,0:T(8,128)(2,1)} %bitcast.40), channel_id=1, source_target_pairs={{0,3},{1,0},{2,1},{3,2},{4,7},{5,4},{6,5},{7,6},{8,11},{9,8},{10,9... | collective-permute-start | bytes 393224 | tf_op jit(solution)/shard_map/ppermute | solution.py:28
  66.5 21.1 %all-to-all-start.2 = ((bf16[8,64,512]{2,1,0:T(8,128)(2,1)}), bf16[8,64,512]{2,1,0:T(8,128)(2,1)S(1)}, u32[]{:S(2)}, u32[]{:S(2)}) async-start(bf16[8,64,512]{2,1,0:T(8,128)(2,1)} %bitcast.126), calls=%async_computation.2 | async-start | bytes 1048576 | tf_op jit(solution)/shard_map/all_to_all | solution.py:33
  70.0 0.7 copy-start.8
  81.2 13.6 %collective-permute-start.9 = (bf16[512,128]{1,0:T(8,128)(2,1)}, bf16[512,128]{1,0:T(8,128)(2,1)}, u32[]{:S(2)}, u32[]{:S(2)}) collective-permute-start(bf16[512,128]{1,0:T(8,128)(2,1)} %bitcast.137), channel_id=1, source_target_pairs={{0,1},{1,2},{2,3},{3,0},{4,5},{5,6},{6,7},{7,4},{8,9},{9,10},{10,1... | collective-permute-start | bytes 393224 | tf_op jit(solution)/shard_map/ppermute | solution.py:28
  83.1 12.8 %collective-permute-start.10 = (bf16[512,128]{1,0:T(8,128)(2,1)}, bf16[512,128]{1,0:T(8,128)(2,1)}, u32[]{:S(2)}, u32[]{:S(2)}) collective-permute-start(bf16[512,128]{1,0:T(8,128)(2,1)} %bitcast.138), channel_id=1, source_target_pairs={{0,2},{1,3},{2,0},{3,1},{4,6},{5,7},{6,4},{7,5},{8,10},{9,11},{10,... | collective-permute-start | bytes 393224 | tf_op jit(solution)/shard_map/ppermute | solution.py:28
  85.0 12.7 %collective-permute-start.11 = (bf16[512,128]{1,0:T(8,128)(2,1)}, bf16[512,128]{1,0:T(8,128)(2,1)S(1)}, u32[]{:S(2)}, u32[]{:S(2)}) collective-permute-start(bf16[512,128]{1,0:T(8,128)(2,1)} %bitcast.139), channel_id=1, source_target_pairs={{0,3},{1,0},{2,1},{3,2},{4,7},{5,4},{6,5},{7,6},{8,11},{9,8},{10,9... | collective-permute-start | bytes 393224 | tf_op jit(solution)/shard_map/ppermute | solution.py:28
  89.0 4.5 %copy-start.6 = (bf16[512,512]{0,1:T(8,128)(2,1)S(1)}, bf16[512,512]{0,1:T(8,128)(2,1)}, u32[]{:S(2)}) copy-start(bf16[512,512]{0,1:T(8,128)(2,1)} %get-tuple-element.43) | copy-start | bytes 1572868
  89.0 15.7 %all-to-all-start.3 = ((bf16[8,64,512]{2,1,0:T(8,128)(2,1)}), bf16[8,64,512]{2,1,0:T(8,128)(2,1)}, u32[]{:S(2)}, u32[]{:S(2)}) async-start(bf16[8,64,512]{2,1,0:T(8,128)(2,1)} %copy.240), calls=%async_computation.3 | async-start | bytes 1048576 | tf_op jit(solution)/shard_map/all_to_all | solution.py:33
  103.7 0.9 copy-start.16
  109.0 5.7 %copy-start.14 = (bf16[1,512,512]{2,1,0:T(8,128)(2,1)S(1)}, bf16[1,512,512]{2,1,0:T(8,128)(2,1)}, u32[]{:S(2)}) copy-start(bf16[1,512,512]{2,1,0:T(8,128)(2,1)} %param.19) | copy-start | bytes 1572868
  109.0 5.7 %copy-start.17 = (bf16[512,512]{0,1:T(8,128)(2,1)S(1)}, bf16[512,512]{0,1:T(8,128)(2,1)}, u32[]{:S(2)}) copy-start(bf16[512,512]{0,1:T(8,128)(2,1)} %get-tuple-element.67) | copy-start | bytes 1572868
  109.8 15.7 %collective-permute-start.12 = (bf16[128,512]{1,0:T(8,128)(2,1)}, bf16[128,512]{1,0:T(8,128)(2,1)S(1)}, u32[]{:S(2)}, u32[]{:S(2)}) collective-permute-start(bf16[128,512]{1,0:T(8,128)(2,1)} %get-tuple-element.47), channel_id=1, source_target_pairs={{0,1},{1,2},{2,3},{3,0},{4,5},{5,6},{6,7},{7,4},{8,9},{9,10},{10,1... | collective-permute-start | bytes 393224 | tf_op jit(solution)/shard_map/ppermute | solution.py:28
  110.3 4.4 %copy-start.12 = (f32[512]{0:T(512)S(1)}, f32[512]{0:T(512)}, u32[]{:S(2)}) copy-start(f32[512]{0:T(512)} %param.18) | copy-start | bytes 6148
  110.3 15.1 %collective-permute-start.13 = (bf16[128,512]{1,0:T(8,128)(2,1)}, bf16[128,512]{1,0:T(8,128)(2,1)S(1)}, u32[]{:S(2)}, u32[]{:S(2)}) collective-permute-start(bf16[128,512]{1,0:T(8,128)(2,1)} %get-tuple-element.46), channel_id=1, source_target_pairs={{0,2},{1,3},{2,0},{3,1},{4,6},{5,7},{6,4},{7,5},{8,10},{9,11},{10,... | collective-permute-start | bytes 393224 | tf_op jit(solution)/shard_map/ppermute | solution.py:28
  112.3 13.2 %collective-permute-start.14 = (bf16[128,512]{1,0:T(8,128)(2,1)}, bf16[128,512]{1,0:T(8,128)(2,1)}, u32[]{:S(2)}, u32[]{:S(2)}) collective-permute-start(bf16[128,512]{1,0:T(8,128)(2,1)} %get-tuple-element.45), channel_id=1, source_target_pairs={{0,3},{1,0},{2,1},{3,2},{4,7},{5,4},{6,5},{7,6},{8,11},{9,8},{10,9... | collective-permute-start | bytes 393224 | tf_op jit(solution)/shard_map/ppermute | solution.py:28
  117.7 4.3 %copy-start.3 = (bf16[4,512,128]{2,1,0:T(8,128)(2,1)S(1)}, bf16[4,512,128]{2,1,0:T(8,128)(2,1)}, u32[]{:S(2)}) copy-start(bf16[4,512,128]{2,1,0:T(8,128)(2,1)} %broadcast_select_fusion.2) | copy-start | bytes 1572868
  117.7 14.1 %all-to-all-start.4 = ((bf16[8,64,512]{2,1,0:T(8,128)(2,1)}), bf16[8,64,512]{2,1,0:T(8,128)(2,1)}, u32[]{:S(2)}, u32[]{:S(2)}) async-start(bf16[8,64,512]{2,1,0:T(8,128)(2,1)} %bitcast.53), calls=%async_computation.4 | async-start | bytes 1048576 | tf_op jit(solution)/shard_map/all_to_all | solution.py:33
  122.4 1.0 copy-start.7

commit v3 on v2

v3 whole, which is shorter than its diff:
```python
import jax
import jax.numpy as jnp
from jax import lax
from jax.sharding import PartitionSpec as P

F32 = jnp.float32
BF16 = jnp.bfloat16


def exchange(pieces, axis_name):
    n = len(pieces)
    got = [pieces[0]]
    for k in range(1, n):
        got.append(lax.ppermute(pieces[k], axis_name, [(i, (i + k) % n) for i in range(n)]))
    return got


def swap(pieces, axis_name):
    return lax.all_to_all(pieces, axis_name, 0, 0, tiled=True)


def split_rows(x, n):
    return x.reshape(n, x.shape[0] // n, *x.shape[1:])


def lane_chunk(x, index, size):
    return lax.dynamic_slice_in_dim(x, index * size, size, axis=1)


def place_chunks(chunks, starts, like):
    out = jnp.zeros(like.shape, like.dtype)
    for chunk, start in zip(chunks, starts):
        out = lax.dynamic_update_slice_in_dim(out, chunk, start, axis=1)
    return out


def on_device(
    inputs, gate_in, gate_out, first_blocks, second_blocks, channel_blocks, group_mix, cotangent
):
    n = lax.axis_size("seq")
    m = lax.axis_size("ch")
    g_me = lax.axis_index("ch")
    rows, width = inputs.shape
    block_width = channel_blocks.shape[1]
    kq = block_width // m
    chunk_of = [(g_me + k) % m for k in range(m)]
    origin_of = [(g_me - k) % m for k in range(m)]

    mix_mine = lax.dynamic_slice_in_dim(group_mix, g_me * kq, kq, 0).astype(F32)

    def coefficient(g, h):
        return lax.dynamic_slice(mix_mine, (0, g, h), (kq, 1, 1)).reshape(1, kq)

    second_f = second_blocks.astype(F32)

    source = inputs.astype(F32)
    slope_in = jax.nn.sigmoid(gate_in * source)
    gated = (source * slope_in).astype(BF16)
    mixed_first = jnp.dot(first_blocks[0], gated, preferred_element_type=F32).astype(BF16)

    upstream = cotangent
    upstream_late, mixed_first = lax.optimization_barrier((upstream, mixed_first))
    cot_arrived = exchange([lane_chunk(upstream_late, t, kq) for t in chunk_of], "ch")
    act_grad_out = [
        sum(
            cot_arrived[k].astype(F32) * coefficient(chunk_of[p], origin_of[k])
            for k in range(m)
        ).astype(BF16)
        for p in range(m)
    ]
    act_grad_back = exchange(act_grad_out, "ch")
    act_grad = place_chunks(act_grad_back, [t * kq for t in origin_of], upstream)

    first_arrived = swap(split_rows(mixed_first, n), "seq")
    second_out = jnp.einsum(
        "cea,acd->ecd", second_f, first_arrived.astype(F32)
    ).astype(BF16)
    returned = swap(second_out, "seq").reshape(rows, width).astype(F32)
    slope_out = jax.nn.sigmoid(gate_out * source)
    hidden = (source + returned * slope_out).astype(BF16)
    pre_act = jnp.dot(hidden, channel_blocks[0], preferred_element_type=F32)
    activated = jax.nn.gelu(pre_act).astype(BF16)

    act_arrived = exchange([lane_chunk(activated, t, kq) for t in chunk_of], "ch")
    added_out = [
        sum(
            act_arrived[k].astype(F32) * coefficient(origin_of[k], chunk_of[p])
            for k in range(m)
        ).astype(BF16)
        for p in range(m)
    ]
    added_back = exchange(added_out, "ch")

    pre_grad = jax.vjp(jax.nn.gelu, pre_act)[1](act_grad.astype(F32))[0].astype(BF16)
    back_term = jnp.dot(pre_grad, channel_blocks[0].T, preferred_element_type=F32)
    hidden_grad = (upstream.astype(F32) + back_term).astype(BF16)
    channel_part = jnp.dot(hidden.T, pre_grad, preferred_element_type=F32)

    grad_flat = hidden_grad.astype(F32)
    gated_grad = (grad_flat * slope_out).astype(BF16)
    grad_arrived = swap(split_rows(gated_grad, n), "seq")
    first_out = jnp.einsum(
        "cea,ecd->acd", second_f, grad_arrived.astype(F32)
    ).astype(BF16)
    first_grad = swap(first_out, "seq").reshape(rows, width)
    first_grad, added_back, channel_part = lax.optimization_barrier(
        (first_grad, added_back, channel_part)
    )
    outputs = place_chunks(
        [
            (lane_chunk(hidden, t, kq).astype(F32) + part.astype(F32)).astype(BF16)
            for t, part in zip(origin_of, added_back)
        ],
        [t * kq for t in origin_of],
        hidden,
    )
    block_part = jnp.dot(first_grad, gated.T, preferred_element_type=F32)
    cq = block_part.shape[0] // m
    block_arrived = exchange(
        [lax.dynamic_slice_in_dim(block_part, t * cq, cq, 0).astype(BF16) for t in chunk_of],
        "ch",
    )
    block_grad = sum(part.astype(F32) for part in block_arrived)[None]
    channel_arrived = swap(split_rows(channel_part, n).astype(BF16), "seq")
    channel_grad = jnp.sum(channel_arrived.astype(F32), axis=0)[None]

    spread = jnp.dot(first_blocks[0].T, first_grad, preferred_element_type=F32)
    input_grad = grad_flat + spread * (slope_in + gate_in * source * slope_in * (1.0 - slope_in))
    input_grad = input_grad + grad_flat * returned * slope_out * (1.0 - slope_out) * gate_out
    return (outputs, input_grad.astype(BF16), channel_grad, block_grad)


def solution(mesh):
    placed = (
        P("seq", "ch"),
        P("ch"),
        P("ch"),
        P("seq", None, None),
        P("seq", None, None),
        P("ch", None, None),
        P(),
        P("seq", "ch"),
    )
    return jax.shard_map(
        on_device,
        mesh=mesh,
        in_specs=placed,
        out_specs=(P("seq", "ch"), P("seq", "ch"), P("ch", "seq", None), P("seq", "ch", None)),
        check_vma=False,
    )
```

time: 135 us -> 98.2 us (0.73)
  local copies, waits for them, and re-layouts: 49.6 us -> 12.9 us
  waiting for transfers between devices: 9.96 us -> 19.5 us
  matrix products: 16.8 us -> 10.3 us
  other arithmetic: 11.1 us -> 8.82 us
    slice x17 -> x0, local copies, waits for them, and re-layouts: 13.1 us -> none  [the longest x12 7.79 us: exchange(): pieces[k]]
    another operation x14 -> x2, local copies, waits for them, and re-layouts: 11.2 us -> 0.07 us  [exchange(): return jnp.stack(got)]
    gather x11 -> x0, local copies, waits for them, and re-layouts: 8.34 us -> none  [the longest x5 3.72 us: to_shift_order(): return jnp.take(x, (me + jnp.arange(n)) % n, axis=axis)]
    all_to_all x5, waiting for transfers between devices: 6.65 us -> 12 us  [swap(): return lax.all_to_all(pieces, axis_name, 0, 0, tiled=True)]
    ppermute x15, waiting for transfers between devices: 3.32 us -> 7.44 us  [exchange(): lax.ppermute(pieces[k], axis_name, [(i, (i + k) % n) for i in range(n)])]
    dot_general x2 -> x0, matrix products: 3.85 us -> none  [the longest x1 2.51 us: on_device(): jnp.einsum('krq,qkp->prq', act_arrived.astype(F32), mix_fwd).astype(BF16)]
    convert_element_type x5 -> x4, other arithmetic: 0.74 us -> 4.42 us  [the longest x2 2.83 us: on_device(): added_out = [sum((act_arrived[k].astype(F32) * coefficient(origin_of[k],...]
    another operation x2 -> x0, other arithmetic: 3.55 us -> none  [exchange(): return jnp.stack(got)]
  transfers between devices with their start and end apart: 20 -> 20, of which waited for: 3 -> 8; matrix products, arithmetic and copies ran while one was open for 40% -> 20% of each run, Pallas kernels for 0% -> 0%
where the time goes in v3:
time: 98.2 us; the launch traced here: 97.3 us
  starting transfers between devices  44.5 us (45%)
  waiting for transfers between devices  19.5 us (20%)
  local copies, waits for them, and re-layouts  12.9 us (13%)
  matrix products  10.3 us (10%)
  other arithmetic  8.82 us (9%)
  between operations  1.24 us (1%)
    ppermute x15, starting transfers between devices, exchange(): lax.ppermute(pieces[k], axis_name, [(i, (i + k) % n) for i in range(n)])  26.3 us
    all_to_all x5, starting transfers between devices, swap(): return lax.all_to_all(pieces, axis_name, 0, 0, tiled=True)  18.2 us
    all_to_all x5, waiting for transfers between devices, swap(): return lax.all_to_all(pieces, axis_name, 0, 0, tiled=True)  12 us
    ppermute x15, waiting for transfers between devices, exchange(): lax.ppermute(pieces[k], axis_name, [(i, (i + k) % n) for i in range(n)])  7.44 us
    unnamed x67, local copies, waits for them, and re-layouts  5.46 us
    dot_general x1, matrix products, on_device(): spread = jnp.dot(first_blocks[0].T, first_grad, preferred_element_type=F32)  3.19 us
    dynamic_update_slice x3, local copies, waits for them, and re-layouts, place_chunks(): out = lax.dynamic_update_slice_in_dim(out, chunk, start, axis=1)  2.87 us
    convert_element_type x2, other arithmetic, on_device(): added_out = [sum((act_arrived[k].astype(F32) * coefficient(origin_of[k],...  2.83 us
  transfers between devices with their start and end apart: 20, of which 8 were waited for; matrix products, arithmetic and copies ran while one was open for 20% of the time, Pallas kernels for 0%

profile of v3, /device:TPU:0, one launch (start us, length us, event | category | flops | bytes accessed | tf_op | source)
XLA Modules:
  0.0 97.3 jit_solution(14563954939628099984)
XLA Ops:
  0.7 0.7 copy-done.29
  1.4 1.8 %fusion.8 = bf16[512,512]{0,1:T(8,128)(2,1)S(1)} fusion(bf16[1,512,512]{2,1,0:T(8,128)(2,1)} %param.11, bf16[512,512]{1,0:T(8,128)(2,1)} %param.8, f32[512]{0:T(512)S(1)} %copy-done.29), kind=kOutput, calls=%fused_computation.25 | convolution fusion | flops 270532608 | bytes 1574912 | tf_op jit(solution)/shard_map/dot_general | solution.py:59
  3.2 0.1 constant_dynamic-slice_fusion.35
  3.3 3.1 %collective-permute-start = (bf16[512,128]{1,0:T(8,128)(2,1)S(1)}, bf16[512,128]{1,0:T(8,128)(2,1)S(1)}, u32[]{:S(2)}, u32[]{:S(2)}) collective-permute-start(bf16[512,128]{1,0:T(8,128)(2,1)S(1)} %get-tuple-element.34), channel_id=1, source_target_pairs={{0,1},{1,2},{2,3},{3,0},{4,5},{5,6},{6,7},{7,4},{8,9},{9,10},{10,1... | collective-permute-start | bytes 393224 | tf_op jit(solution)/shard_map/ppermute | solution.py:14
  6.4 2.6 %collective-permute-start.1 = (bf16[512,128]{1,0:T(8,128)(2,1)S(1)}, bf16[512,128]{1,0:T(8,128)(2,1)S(1)}, u32[]{:S(2)}, u32[]{:S(2)}) collective-permute-start(bf16[512,128]{1,0:T(8,128)(2,1)S(1)} %get-tuple-element.36), channel_id=1, source_target_pairs={{0,2},{1,3},{2,0},{3,1},{4,6},{5,7},{6,4},{7,5},{8,10},{9,11},{10,... | collective-permute-start | bytes 393224 | tf_op jit(solution)/shard_map/ppermute | solution.py:14
  9.0 1.3 %collective-permute-start.2 = (bf16[512,128]{1,0:T(8,128)(2,1)S(1)}, bf16[512,128]{1,0:T(8,128)(2,1)S(1)}, u32[]{:S(2)}, u32[]{:S(2)}) collective-permute-start(bf16[512,128]{1,0:T(8,128)(2,1)S(1)} %get-tuple-element.35), channel_id=1, source_target_pairs={{0,3},{1,0},{2,1},{3,2},{4,7},{5,4},{6,5},{7,6},{8,11},{9,8},{10,9... | collective-permute-start | bytes 393224 | tf_op jit(solution)/shard_map/ppermute | solution.py:14
  10.3 1.0 %copy.25 = bf16[512,512]{1,0:T(8,128)(2,1)} copy(bf16[512,512]{0,1:T(8,128)(2,1)S(1)} %fusion.8) | data formatting | bytes 1048576 | tf_op jit(solution)/shard_map/optimization_barrier | solution.py:62
  11.3 3.7 %all-to-all-start = ((bf16[8,64,512]{2,1,0:T(8,128)(2,1)}), bf16[8,64,512]{2,1,0:T(8,128)(2,1)S(1)}, u32[]{:S(2)}, u32[]{:S(2)}) async-start(bf16[8,64,512]{2,1,0:T(8,128)(2,1)} %bitcast.2), calls=%async_computation | async-start | bytes 1048576 | tf_op jit(solution)/shard_map/all_to_all | solution.py:19
  15.0 0.7 fusion.78
  15.7 0.7 copy-done.14
  16.5 0.1 copy.30
  16.7 0.7 fusion.106
  17.4 0.3 collective-permute-done.1
  17.6 0.9 fusion.56
  18.5 3.3 %collective-permute-start.3 = (bf16[512,128]{1,0:T(8,128)(2,1)}, bf16[512,128]{1,0:T(8,128)(2,1)}, u32[]{:S(2)}, u32[]{:S(2)}) collective-permute-start(bf16[512,128]{1,0:T(8,128)(2,1)} %get-tuple-element.26), channel_id=1, source_target_pairs={{0,1},{1,2},{2,3},{3,0},{4,5},{5,6},{6,7},{7,4},{8,9},{9,10},{10,1... | collective-permute-start | bytes 393224 | tf_op jit(solution)/shard_map/ppermute | solution.py:14
  21.8 1.6 %collective-permute-start.4 = (bf16[512,128]{1,0:T(8,128)(2,1)S(1)}, bf16[512,128]{1,0:T(8,128)(2,1)}, u32[]{:S(2)}, u32[]{:S(2)}) collective-permute-start(bf16[512,128]{1,0:T(8,128)(2,1)S(1)} %get-tuple-element.27), channel_id=1, source_target_pairs={{0,2},{1,3},{2,0},{3,1},{4,6},{5,7},{6,4},{7,5},{8,10},{9,11},{10,... | collective-permute-start | bytes 393224 | tf_op jit(solution)/shard_map/ppermute | solution.py:14
  23.4 0.7 collective-permute-start.5
  24.2 0.6 all-to-all-done
  24.8 0.4 fusion.6
  25.2 0.9 copy.28
  26.2 3.5 %all-to-all-start.1 = ((bf16[8,64,512]{2,1,0:T(8,128)(2,1)}), bf16[8,64,512]{2,1,0:T(8,128)(2,1)S(1)}, u32[]{:S(2)}, u32[]{:S(2)}) async-start(bf16[8,64,512]{2,1,0:T(8,128)(2,1)} %copy.28), calls=%async_computation.1 | async-start | bytes 1048576 | tf_op jit(solution)/shard_map/all_to_all | solution.py:19
  29.7 0.1 fusion.77
  29.9 1.0 %constant_dynamic-update-slice_fusion.2 = bf16[512,512]{1,0:T(8,128)(2,1)S(1)} fusion(bf16[512,512]{1,0:T(8,128)(2,1)S(1)} %fusion.77, bf16[512,128]{1,0:T(8,128)(2,1)} %collective-permute-done.3, s32[]{:T(128)S(6)} %select_n.80), kind=kLoop, calls=%fused_computation.166 | loop fusion | bytes 262148 | tf_op jit(solution)/shard_map/dynamic_update_slice | solution.py:33
  30.9 1.1 %collective-permute-done.4 = bf16[512,128]{1,0:T(8,128)(2,1)} collective-permute-done((bf16[512,128]{1,0:T(8,128)(2,1)S(1)}, bf16[512,128]{1,0:T(8,128)(2,1)}, u32[]{:S(2)}, u32[]{:S(2)}) %collective-permute-start.4) | collective-permute-done | bytes 131104 | tf_op jit(solution)/shard_map/ppermute | solution.py:14
  32.0 0.9 constant_dynamic-update-slice_fusion.1
  33.0 0.9 constant_dynamic-update-slice_fusion
  33.9 5.4 %all-to-all-done.1 = bf16[8,64,512]{2,1,0:T(8,128)(2,1)S(1)} async-done(((bf16[8,64,512]{2,1,0:T(8,128)(2,1)}), bf16[8,64,512]{2,1,0:T(8,128)(2,1)S(1)}, u32[]{:S(2)}, u32[]{:S(2)}) %all-to-all-start.1) | async-done | bytes 524320 | tf_op jit(solution)/shard_map/all_to_all | solution.py:19
  39.4 0.4 fusion.33
  39.8 1.1 %multiply_convert_fusion = (bf16[512,512]{1,0:T(8,128)(2,1)S(1)}, bf16[512,512]{1,0:T(8,128)(2,1)S(1)}) fusion(bf16[512,512]{1,0:T(8,128)(2,1)S(1)} %constant_dynamic-update-slice_fusion, bf16[512,512]{1,0:T(8,128)(2,1)S(1)} %fusion.33, bf16[1,512,512]{2,1,0:T(8,128)(2,1)S(1)} %copy-done), kind=kOutput, calls=%fused_computation.52 | convolution fusion | flops 274464768 | bytes 2621440 | tf_op jit(solution)/shard_map/dot_general | solution.py:81
  40.9 1.6 %fusion.24 = (bf16[512,512]{1,0:T(8,128)(2,1)}, bf16[512,512]{1,0:T(8,128)(2,1)}) fusion(bf16[512,512]{1,0:T(8,128)(2,1)S(1)} %copy-done.4, f32[512]{0:T(512)S(1)} %copy-done.15, bf16[512,512]{1,0:T(8,128)(2,1)S(1)} %get-tuple-element.21, bf16[1,512,512]{2,1,0:T(8,128)(2,1)S(1)} %copy-done, bf16[512,512]{1,0:T(8,128)(2,1)S(1)} %copy-done.1), kind=kOutput, calls=%fused_computation.41 | convolution fusion | flops 271319040 | bytes 3147776 | tf_op jit(solution)/shard_map/dot_general | solution.py:95
  42.5 3.5 %all-to-all-start.2 = ((bf16[8,64,512]{2,1,0:T(8,128)(2,1)}), bf16[8,64,512]{2,1,0:T(8,128)(2,1)S(1)}, u32[]{:S(2)}, u32[]{:S(2)}) async-start(bf16[8,64,512]{2,1,0:T(8,128)(2,1)} %bitcast.22), calls=%async_computation.2 | async-start | bytes 1048576 | tf_op jit(solution)/shard_map/all_to_all | solution.py:19
  46.0 0.1 constant_dynamic-slice_fusion.13
  46.1 1.0 %collective-permute-start.6 = (bf16[512,128]{1,0:T(8,128)(2,1)S(1)}, bf16[512,128]{1,0:T(8,128)(2,1)S(1)}, u32[]{:S(2)}, u32[]{:S(2)}) collective-permute-start(bf16[512,128]{1,0:T(8,128)(2,1)S(1)} %get-tuple-element.33), channel_id=1, source_target_pairs={{0,1},{1,2},{2,3},{3,0},{4,5},{5,6},{6,7},{7,4},{8,9},{9,10},{10,1... | collective-permute-start | bytes 393224 | tf_op jit(solution)/shard_map/ppermute | solution.py:14
  47.1 1.3 %collective-permute-start.7 = (bf16[512,128]{1,0:T(8,128)(2,1)S(1)}, bf16[512,128]{1,0:T(8,128)(2,1)S(1)}, u32[]{:S(2)}, u32[]{:S(2)}) collective-permute-start(bf16[512,128]{1,0:T(8,128)(2,1)S(1)} %get-tuple-element.32), channel_id=1, source_target_pairs={{0,2},{1,3},{2,0},{3,1},{4,6},{5,7},{6,4},{7,5},{8,10},{9,11},{10,... | collective-permute-start | bytes 393224 | tf_op jit(solution)/shard_map/ppermute | solution.py:14
  48.4 1.6 %collective-permute-start.8 = (bf16[512,128]{1,0:T(8,128)(2,1)S(1)}, bf16[512,128]{1,0:T(8,128)(2,1)}, u32[]{:S(2)}, u32[]{:S(2)}) collective-permute-start(bf16[512,128]{1,0:T(8,128)(2,1)S(1)} %get-tuple-element.31), channel_id=1, source_target_pairs={{0,3},{1,0},{2,1},{3,2},{4,7},{5,4},{6,5},{7,6},{8,11},{9,8},{10,9... | collective-permute-start | bytes 393224 | tf_op jit(solution)/shard_map/ppermute | solution.py:14
  50.0 1.3 %fusion.113 = bf16[512,512]{1,0:T(8,128)(2,1)} fusion(bf16[512,512]{1,0:T(8,128)(2,1)S(1)} %fusion.33, bf16[512,512]{1,0:T(8,128)(2,1)S(1)} %copy-done.32), kind=kOutput, calls=%fused_computation.212 | convolution fusion | flops 268435456 | bytes 1572864 | tf_op jit(solution)/shard_map/dot_general | solution.py:97
  51.3 4.4 %all-to-all-done.2 = bf16[8,64,512]{2,1,0:T(8,128)(2,1)S(1)} async-done(((bf16[8,64,512]{2,1,0:T(8,128)(2,1)}), bf16[8,64,512]{2,1,0:T(8,128)(2,1)S(1)}, u32[]{:S(2)}, u32[]{:S(2)}) %all-to-all-start.2) | async-done | bytes 524320 | tf_op jit(solution)/shard_map/all_to_all | solution.py:19
  55.7 0.4 fusion.7
  56.1 0.9 copy.31
  57.1 3.5 %all-to-all-start.3 = ((bf16[8,64,512]{2,1,0:T(8,128)(2,1)}), bf16[8,64,512]{2,1,0:T(8,128)(2,1)S(1)}, u32[]{:S(2)}, u32[]{:S(2)}) async-start(bf16[8,64,512]{2,1,0:T(8,128)(2,1)} %copy.31), calls=%async_computation.3 | async-start | bytes 1048576 | tf_op jit(solution)/shard_map/all_to_all | solution.py:19
  60.7 0.6 copy-done.16
  61.3 1.2 %fusion.72 = (bf16[512,128]{1,0:T(8,128)(2,1)S(1)}, bf16[512,128]{1,0:T(8,128)(2,1)S(1)}, bf16[512,128]{1,0:T(8,128)(2,1)S(1)}) fusion(bf16[512,128]{1,0:T(8,128)(2,1)S(1)} %collective-permute-done.6, bf16[512,128]{1,0:T(8,128)(2,1)S(1)} %collective-permute-done.7, bf16[512,128]{1,0:T(8,128)(2,1)} %collective-permute-done.8, f32[128]{0:T(128)S(1)} %get-tuple-element.38, ...), kind=kLoop, calls=%fused_computation.123 | loop fusion | flops 1835008 | bytes 923652 | tf_op jit(solution)/shard_map/convert_element_type | solution.py:89
  62.5 1.0 collective-permute-start.10
  63.4 3.5 %collective-permute-start.11 = (bf16[512,128]{1,0:T(8,128)(2,1)S(1)}, bf16[512,128]{1,0:T(8,128)(2,1)S(1)}, u32[]{:S(2)}, u32[]{:S(2)}) collective-permute-start(bf16[512,128]{1,0:T(8,128)(2,1)S(1)} %get-tuple-element.22), channel_id=1, source_target_pairs={{0,3},{1,0},{2,1},{3,2},{4,7},{5,4},{6,5},{7,6},{8,11},{9,8},{10,9... | collective-permute-start | bytes 393224 | tf_op jit(solution)/shard_map/ppermute | solution.py:14
  67.0 1.7 %fusion.60 = bf16[512,128]{1,0:T(8,128)(2,1)} fusion(bf16[512,128]{1,0:T(8,128)(2,1)S(1)} %collective-permute-done.6, bf16[512,128]{1,0:T(8,128)(2,1)S(1)} %collective-permute-done.7, bf16[512,128]{1,0:T(8,128)(2,1)} %collective-permute-done.8, f32[128]{0:T(128)S(1)} %copy-done.26, f32[128]{0:T(128)S(1)} %copy-done.27, f32[128]{0:T(128)S(1)} %copy-done.28, ...), kind=kLoop, calls=%fused_computation.111 | loop fusion | flops 786432 | bytes 657412 | tf_op jit(solution)/shard_map/convert_element_type | solution.py:89
  68.6 4.8 %collective-permute-done.10 = bf16[512,128]{1,0:T(8,128)(2,1)S(1)} collective-permute-done((bf16[512,128]{1,0:T(8,128)(2,1)S(1)}, bf16[512,128]{1,0:T(8,128)(2,1)S(1)}, u32[]{:S(2)}, u32[]{:S(2)}) %collective-permute-start.10) | collective-permute-done | bytes 131104 | tf_op jit(solution)/shard_map/ppermute | solution.py:14
  73.4 0.7 copy-done.12
  74.1 0.6 copy-done.10
  74.7 1.3 %collective-permute-done.9 = bf16[512,128]{1,0:T(8,128)(2,1)} collective-permute-done((bf16[512,128]{1,0:T(8,128)(2,1)S(1)}, bf16[512,128]{1,0:T(8,128)(2,1)}, u32[]{:S(2)}, u32[]{:S(2)}) %collective-permute-start.9) | collective-permute-done | bytes 131104 | tf_op jit(solution)/shard_map/ppermute | solution.py:14
  76.0 0.6 fusion.110
  76.6 0.2 copy-done.6
  76.8 0.7 dynamic-slice_convert_fusion.2
  77.5 2.9 %collective-permute-start.12 = (bf16[128,512]{1,0:T(8,128)(2,1)}, bf16[128,512]{1,0:T(8,128)(2,1)S(1)}, u32[]{:S(2)}, u32[]{:S(2)}) collective-permute-start(bf16[128,512]{1,0:T(8,128)(2,1)} %get-tuple-element.28), channel_id=1, source_target_pairs={{0,1},{1,2},{2,3},{3,0},{4,5},{5,6},{6,7},{7,4},{8,9},{9,10},{10,1... | collective-permute-start | bytes 393224 | tf_op jit(solution)/shard_map/ppermute | solution.py:14
  80.4 2.4 %collective-permute-start.14 = (bf16[128,512]{1,0:T(8,128)(2,1)S(1)}, bf16[128,512]{1,0:T(8,128)(2,1)}, u32[]{:S(2)}, u32[]{:S(2)}) collective-permute-start(bf16[128,512]{1,0:T(8,128)(2,1)S(1)} %get-tuple-element.29), channel_id=1, source_target_pairs={{0,3},{1,0},{2,1},{3,2},{4,7},{5,4},{6,5},{7,6},{8,11},{9,8},{10,9... | collective-permute-start | bytes 393224 | tf_op jit(solution)/shard_map/ppermute | solution.py:14
  82.8 4.0 %all-to-all-start.4 = ((bf16[8,64,512]{2,1,0:T(8,128)(2,1)}), bf16[8,64,512]{2,1,0:T(8,128)(2,1)S(1)}, u32[]{:S(2)}, u32[]{:S(2)}) async-start(bf16[8,64,512]{2,1,0:T(8,128)(2,1)} %bitcast.42), calls=%async_computation.4 | async-start | bytes 1048576 | tf_op jit(solution)/shard_map/all_to_all | solution.py:19
  86.8 3.2 %fusion.3 = bf16[512,512]{1,0:T(8,128)(2,1)} fusion(bf16[512,512]{1,0:T(8,128)(2,1)S(1)} %bitcast.112, bf16[512,512]{1,0:T(8,128)(2,1)} %get-tuple-element.69, bf16[512,512]{1,0:T(8,128)(2,1)S(1)} %copy-done.5, bf16[512,512]{1,0:T(8,128)(2,1)S(1)} %bitcast.110, bf16[1,512,512]{2,1,0:T(8,128)(2,1)} %param.11, f32[512]{0:T(512)S(1)} %copy-done.15, ...), kind=kOutput, calls=%fused_computation.20 | convolution fusion | flops 274726912 | bytes 3149824 | tf_op jit(solution)/shard_map/dot_general | solution.py:127
  90.0 0.9 copy-done.9
  91.0 1.0 %fusion.74 = bf16[512,512]{1,0:T(8,128)(2,1)S(1)} fusion(bf16[512,512]{1,0:T(8,128)(2,1)S(1)} %fusion.73, s32[]{:T(128)S(6)} %select_n.80, bf16[512,128]{1,0:T(8,128)(2,1)} %collective-permute-done.9, bf16[512,512]{1,0:T(8,128)(2,1)S(1)} %fusion.33), kind=kLoop, calls=%fused_computation.134 | loop fusion | flops 262144 | bytes 393220 | tf_op jit(solution)/shard_map/dynamic_update_slice | solution.py:33
  92.0 0.1 fusion.75
  92.1 0.8 copy-done.11
  92.9 0.1 fusion.76
  93.0 2.0 %add_bitcast_fusion = f32[1,128,512]{2,1,0:T(8,128)} fusion(bf16[128,512]{1,0:T(8,128)(2,1)} %collective-permute-done.14, bf16[128,512]{1,0:T(8,128)(2,1)} %collective-permute-done.13, bf16[128,512]{1,0:T(8,128)(2,1)S(1)} %collective-permute-done.12, bf16[512,512]{1,0:T(8,128)(2,1)} %copy-done.8, s32[]{:T(128)S(6)} %select_n.64), kind=kLoop, calls=%fused_computation.124 | loop fusion | flops 458752 | bytes 786436 | tf_op jit(solution)/shard_map/broadcast_in_dim | solution.py:123
  95.0 1.6 %all-to-all-done.4 = bf16[8,64,512]{2,1,0:T(8,128)(2,1)S(1)} async-done(((bf16[8,64,512]{2,1,0:T(8,128)(2,1)}), bf16[8,64,512]{2,1,0:T(8,128)(2,1)S(1)}, u32[]{:S(2)}, u32[]{:S(2)}) %all-to-all-start.4) | async-done | bytes 524320 | tf_op jit(solution)/shard_map/all_to_all | solution.py:19
  96.6 0.7 convert_reduce_fusion
  (75 shorter events, 0.3 us)
Async XLA Ops:
  0.6 39.1 %copy-start = (bf16[1,512,512]{2,1,0:T(8,128)(2,1)S(1)}, bf16[1,512,512]{2,1,0:T(8,128)(2,1)}, u32[]{:S(2)}) copy-start(bf16[1,512,512]{2,1,0:T(8,128)(2,1)} %param.13) | copy-start | bytes 1572868
  0.7 0.7 copy-start.29
  1.4 1.8 %copy-start.1 = (bf16[512,512]{1,0:T(8,128)(2,1)S(1)}, bf16[512,512]{1,0:T(8,128)(2,1)}, u32[]{:S(2)}) copy-start(bf16[512,512]{1,0:T(8,128)(2,1)} %param.15) | copy-start | bytes 1572868
  3.3 14.1 %collective-permute-start = (bf16[512,128]{1,0:T(8,128)(2,1)S(1)}, bf16[512,128]{1,0:T(8,128)(2,1)S(1)}, u32[]{:S(2)}, u32[]{:S(2)}) collective-permute-start(bf16[512,128]{1,0:T(8,128)(2,1)S(1)} %get-tuple-element.34), channel_id=1, source_target_pairs={{0,1},{1,2},{2,3},{3,0},{4,5},{5,6},{6,7},{7,4},{8,9},{9,10},{10,1... | collective-permute-start | bytes 393224 | tf_op jit(solution)/shard_map/ppermute | solution.py:14
  6.4 11.2 %collective-permute-start.1 = (bf16[512,128]{1,0:T(8,128)(2,1)S(1)}, bf16[512,128]{1,0:T(8,128)(2,1)S(1)}, u32[]{:S(2)}, u32[]{:S(2)}) collective-permute-start(bf16[512,128]{1,0:T(8,128)(2,1)S(1)} %get-tuple-element.36), channel_id=1, source_target_pairs={{0,2},{1,3},{2,0},{3,1},{4,6},{5,7},{6,4},{7,5},{8,10},{9,11},{10,... | collective-permute-start | bytes 393224 | tf_op jit(solution)/shard_map/ppermute | solution.py:14
  9.0 8.6 %collective-permute-start.2 = (bf16[512,128]{1,0:T(8,128)(2,1)S(1)}, bf16[512,128]{1,0:T(8,128)(2,1)S(1)}, u32[]{:S(2)}, u32[]{:S(2)}) collective-permute-start(bf16[512,128]{1,0:T(8,128)(2,1)S(1)} %get-tuple-element.35), channel_id=1, source_target_pairs={{0,3},{1,0},{2,1},{3,2},{4,7},{5,4},{6,5},{7,6},{8,11},{9,8},{10,9... | collective-permute-start | bytes 393224 | tf_op jit(solution)/shard_map/ppermute | solution.py:14
  11.3 13.5 %all-to-all-start = ((bf16[8,64,512]{2,1,0:T(8,128)(2,1)}), bf16[8,64,512]{2,1,0:T(8,128)(2,1)S(1)}, u32[]{:S(2)}, u32[]{:S(2)}) async-start(bf16[8,64,512]{2,1,0:T(8,128)(2,1)} %bitcast.2), calls=%async_computation | async-start | bytes 1048576 | tf_op jit(solution)/shard_map/all_to_all | solution.py:19
  15.7 0.7 copy-start.14
  18.5 11.4 %collective-permute-start.3 = (bf16[512,128]{1,0:T(8,128)(2,1)}, bf16[512,128]{1,0:T(8,128)(2,1)}, u32[]{:S(2)}, u32[]{:S(2)}) collective-permute-start(bf16[512,128]{1,0:T(8,128)(2,1)} %get-tuple-element.26), channel_id=1, source_target_pairs={{0,1},{1,2},{2,3},{3,0},{4,5},{5,6},{6,7},{7,4},{8,9},{9,10},{10,1... | collective-permute-start | bytes 393224 | tf_op jit(solution)/shard_map/ppermute | solution.py:14
  21.8 10.2 %collective-permute-start.4 = (bf16[512,128]{1,0:T(8,128)(2,1)S(1)}, bf16[512,128]{1,0:T(8,128)(2,1)}, u32[]{:S(2)}, u32[]{:S(2)}) collective-permute-start(bf16[512,128]{1,0:T(8,128)(2,1)S(1)} %get-tuple-element.27), channel_id=1, source_target_pairs={{0,2},{1,3},{2,0},{3,1},{4,6},{5,7},{6,4},{7,5},{8,10},{9,11},{10,... | collective-permute-start | bytes 393224 | tf_op jit(solution)/shard_map/ppermute | solution.py:14
  23.4 9.6 %collective-permute-start.5 = (bf16[512,128]{1,0:T(8,128)(2,1)S(1)}, bf16[512,128]{1,0:T(8,128)(2,1)}, u32[]{:S(2)}, u32[]{:S(2)}) collective-permute-start(bf16[512,128]{1,0:T(8,128)(2,1)S(1)} %get-tuple-element.25), channel_id=1, source_target_pairs={{0,3},{1,0},{2,1},{3,2},{4,7},{5,4},{6,5},{7,6},{8,11},{9,8},{10,9... | collective-permute-start | bytes 393224 | tf_op jit(solution)/shard_map/ppermute | solution.py:14
  26.2 13.2 %all-to-all-start.1 = ((bf16[8,64,512]{2,1,0:T(8,128)(2,1)}), bf16[8,64,512]{2,1,0:T(8,128)(2,1)S(1)}, u32[]{:S(2)}, u32[]{:S(2)}) async-start(bf16[8,64,512]{2,1,0:T(8,128)(2,1)} %copy.28), calls=%async_computation.1 | async-start | bytes 1048576 | tf_op jit(solution)/shard_map/all_to_all | solution.py:19
  29.9 9.5 %copy-start.3 = (bf16[512,512]{1,0:T(8,128)(2,1)S(1)}, bf16[512,512]{1,0:T(8,128)(2,1)}, u32[]{:S(2)}) copy-start(bf16[512,512]{1,0:T(8,128)(2,1)} %param.8) | copy-start | bytes 1572868
  33.0 6.4 %copy-start.15 = (f32[512]{0:T(512)S(1)}, f32[512]{0:T(512)}, u32[]{:S(2)}) copy-start(f32[512]{0:T(512)} %param.10) | copy-start | bytes 6148
  39.8 1.2 %copy-start.4 = (bf16[512,512]{1,0:T(8,128)(2,1)S(1)}, bf16[512,512]{1,0:T(8,128)(2,1)}, u32[]{:S(2)}) copy-start(bf16[512,512]{1,0:T(8,128)(2,1)} %param.8) | copy-start | bytes 1572868
  40.9 1.6 %copy-start.31 = (bf16[512,512]{1,0:T(8,128)(2,1)}, bf16[512,512]{1,0:T(8,128)(2,1)S(1)}, u32[]{:S(2)}) copy-start(bf16[512,512]{1,0:T(8,128)(2,1)S(1)} %get-tuple-element.21) | copy-start | bytes 1572868
  42.5 13.2 %all-to-all-start.2 = ((bf16[8,64,512]{2,1,0:T(8,128)(2,1)}), bf16[8,64,512]{2,1,0:T(8,128)(2,1)S(1)}, u32[]{:S(2)}, u32[]{:S(2)}) async-start(bf16[8,64,512]{2,1,0:T(8,128)(2,1)} %bitcast.22), calls=%async_computation.2 | async-start | bytes 1048576 | tf_op jit(solution)/shard_map/all_to_all | solution.py:19
  46.0 4.0 %copy-start.32 = (bf16[512,512]{1,0:T(8,128)(2,1)S(1)}, bf16[512,512]{1,0:T(8,128)(2,1)}, u32[]{:S(2)}) copy-start(bf16[512,512]{1,0:T(8,128)(2,1)} %copy-done.31) | copy-start | bytes 1572868
  46.1 14.5 %collective-permute-start.6 = (bf16[512,128]{1,0:T(8,128)(2,1)S(1)}, bf16[512,128]{1,0:T(8,128)(2,1)S(1)}, u32[]{:S(2)}, u32[]{:S(2)}) collective-permute-start(bf16[512,128]{1,0:T(8,128)(2,1)S(1)} %get-tuple-element.33), channel_id=1, source_target_pairs={{0,1},{1,2},{2,3},{3,0},{4,5},{5,6},{6,7},{7,4},{8,9},{9,10},{10,1... | collective-permute-start | bytes 393224 | tf_op jit(solution)/shard_map/ppermute | solution.py:14
  47.1 13.5 %collective-permute-start.7 = (bf16[512,128]{1,0:T(8,128)(2,1)S(1)}, bf16[512,128]{1,0:T(8,128)(2,1)S(1)}, u32[]{:S(2)}, u32[]{:S(2)}) collective-permute-start(bf16[512,128]{1,0:T(8,128)(2,1)S(1)} %get-tuple-element.32), channel_id=1, source_target_pairs={{0,2},{1,3},{2,0},{3,1},{4,6},{5,7},{6,4},{7,5},{8,10},{9,11},{10,... | collective-permute-start | bytes 393224 | tf_op jit(solution)/shard_map/ppermute | solution.py:14
  48.4 12.2 %collective-permute-start.8 = (bf16[512,128]{1,0:T(8,128)(2,1)S(1)}, bf16[512,128]{1,0:T(8,128)(2,1)}, u32[]{:S(2)}, u32[]{:S(2)}) collective-permute-start(bf16[512,128]{1,0:T(8,128)(2,1)S(1)} %get-tuple-element.31), channel_id=1, source_target_pairs={{0,3},{1,0},{2,1},{3,2},{4,7},{5,4},{6,5},{7,6},{8,11},{9,8},{10,9... | collective-permute-start | bytes 393224 | tf_op jit(solution)/shard_map/ppermute | solution.py:14
  57.0 3.6 %copy-start.19 = (f32[128]{0:T(128)S(1)}, f32[128]{0:T(128)}, u32[]{:S(2)}) copy-start(f32[128]{0:T(128)} %get-tuple-element.42) | copy-start | bytes 1540
  57.0 3.6 %copy-start.20 = (f32[128]{0:T(128)S(1)}, f32[128]{0:T(128)}, u32[]{:S(2)}) copy-start(f32[128]{0:T(128)} %get-tuple-element.43) | copy-start | bytes 1540
  57.0 3.6 %copy-start.21 = (f32[128]{0:T(128)S(1)}, f32[128]{0:T(128)}, u32[]{:S(2)}) copy-start(f32[128]{0:T(128)} %get-tuple-element.44) | copy-start | bytes 1540
  57.0 3.6 %copy-start.22 = (f32[128]{0:T(128)S(1)}, f32[128]{0:T(128)}, u32[]{:S(2)}) copy-start(f32[128]{0:T(128)} %get-tuple-element.45) | copy-start | bytes 1540
  57.1 3.6 %copy-start.23 = (f32[128]{0:T(128)S(1)}, f32[128]{0:T(128)}, u32[]{:S(2)}) copy-start(f32[128]{0:T(128)} %get-tuple-element.46) | copy-start | bytes 1540
  57.1 3.6 %copy-start.24 = (f32[128]{0:T(128)S(1)}, f32[128]{0:T(128)}, u32[]{:S(2)}) copy-start(f32[128]{0:T(128)} %get-tuple-element.47) | copy-start | bytes 1540
  57.1 3.6 %copy-start.25 = (f32[128]{0:T(128)S(1)}, f32[128]{0:T(128)}, u32[]{:S(2)}) copy-start(f32[128]{0:T(128)} %get-tuple-element.48) | copy-start | bytes 1540
  57.1 18.9 %all-to-all-start.3 = ((bf16[8,64,512]{2,1,0:T(8,128)(2,1)}), bf16[8,64,512]{2,1,0:T(8,128)(2,1)S(1)}, u32[]{:S(2)}, u32[]{:S(2)}) async-start(bf16[8,64,512]{2,1,0:T(8,128)(2,1)} %copy.31), calls=%async_computation.3 | async-start | bytes 1048576 | tf_op jit(solution)/shard_map/all_to_all | solution.py:19
  60.6 0.7 copy-start.16
  60.6 0.6 copy-start.17
  60.7 0.6 copy-start.18
  61.3 5.6 %copy-start.26 = (f32[128]{0:T(128)S(1)}, f32[128]{0:T(128)}, u32[]{:S(2)}) copy-start(f32[128]{0:T(128)} %get-tuple-element.49) | copy-start | bytes 1540
  61.3 5.6 %copy-start.27 = (f32[128]{0:T(128)S(1)}, f32[128]{0:T(128)}, u32[]{:S(2)}) copy-start(f32[128]{0:T(128)} %get-tuple-element.50) | copy-start | bytes 1540
  61.3 5.6 %copy-start.28 = (f32[128]{0:T(128)S(1)}, f32[128]{0:T(128)}, u32[]{:S(2)}) copy-start(f32[128]{0:T(128)} %get-tuple-element.51) | copy-start | bytes 1540
  62.5 13.5 %copy-start.5 = (bf16[512,512]{1,0:T(8,128)(2,1)S(1)}, bf16[512,512]{1,0:T(8,128)(2,1)}, u32[]{:S(2)}) copy-start(bf16[512,512]{1,0:T(8,128)(2,1)} %param.8) | copy-start | bytes 1572868
  62.5 10.9 %collective-permute-start.10 = (bf16[512,128]{1,0:T(8,128)(2,1)S(1)}, bf16[512,128]{1,0:T(8,128)(2,1)S(1)}, u32[]{:S(2)}, u32[]{:S(2)}) collective-permute-start(bf16[512,128]{1,0:T(8,128)(2,1)S(1)} %get-tuple-element.24), channel_id=1, source_target_pairs={{0,2},{1,3},{2,0},{3,1},{4,6},{5,7},{6,4},{7,5},{8,10},{9,11},{10,... | collective-permute-start | bytes 393224 | tf_op jit(solution)/shard_map/ppermute | solution.py:14
  63.4 10.0 %collective-permute-start.11 = (bf16[512,128]{1,0:T(8,128)(2,1)S(1)}, bf16[512,128]{1,0:T(8,128)(2,1)S(1)}, u32[]{:S(2)}, u32[]{:S(2)}) collective-permute-start(bf16[512,128]{1,0:T(8,128)(2,1)S(1)} %get-tuple-element.22), channel_id=1, source_target_pairs={{0,3},{1,0},{2,1},{3,2},{4,7},{5,4},{6,5},{7,6},{8,11},{9,8},{10,9... | collective-permute-start | bytes 393224 | tf_op jit(solution)/shard_map/ppermute | solution.py:14
  66.9 9.0 %collective-permute-start.9 = (bf16[512,128]{1,0:T(8,128)(2,1)S(1)}, bf16[512,128]{1,0:T(8,128)(2,1)}, u32[]{:S(2)}, u32[]{:S(2)}) collective-permute-start(bf16[512,128]{1,0:T(8,128)(2,1)S(1)} %get-tuple-element.23), channel_id=1, source_target_pairs={{0,1},{1,2},{2,3},{3,0},{4,5},{5,6},{6,7},{7,4},{8,9},{9,10},{10,1... | collective-permute-start | bytes 393224 | tf_op jit(solution)/shard_map/ppermute | solution.py:14
  67.0 9.0 %copy-start.30 = (f32[512]{0:T(512)S(1)}, f32[512]{0:T(512)}, u32[]{:S(2)}) copy-start(f32[512]{0:T(512)} %param.9) | copy-start | bytes 6148
  73.4 0.7 copy-start.12
  74.1 0.6 copy-start.10
  76.0 0.8 copy-start.6
  76.8 6.0 %copy-start.8 = (bf16[512,512]{1,0:T(8,128)(2,1)}, bf16[512,512]{1,0:T(8,128)(2,1)S(1)}, u32[]{:S(2)}) copy-start(bf16[512,512]{1,0:T(8,128)(2,1)S(1)} %fusion.110) | copy-start | bytes 1572868
  77.5 15.5 %collective-permute-start.12 = (bf16[128,512]{1,0:T(8,128)(2,1)}, bf16[128,512]{1,0:T(8,128)(2,1)S(1)}, u32[]{:S(2)}, u32[]{:S(2)}) collective-permute-start(bf16[128,512]{1,0:T(8,128)(2,1)} %get-tuple-element.28), channel_id=1, source_target_pairs={{0,1},{1,2},{2,3},{3,0},{4,5},{5,6},{6,7},{7,4},{8,9},{9,10},{10,1... | collective-permute-start | bytes 393224 | tf_op jit(solution)/shard_map/ppermute | solution.py:14
  80.4 12.6 %collective-permute-start.13 = (bf16[128,512]{1,0:T(8,128)(2,1)S(1)}, bf16[128,512]{1,0:T(8,128)(2,1)}, u32[]{:S(2)}, u32[]{:S(2)}) collective-permute-start(bf16[128,512]{1,0:T(8,128)(2,1)S(1)} %get-tuple-element.30), channel_id=1, source_target_pairs={{0,2},{1,3},{2,0},{3,1},{4,6},{5,7},{6,4},{7,5},{8,10},{9,11},{10,... | collective-permute-start | bytes 393224 | tf_op jit(solution)/shard_map/ppermute | solution.py:14
  80.4 12.6 %collective-permute-start.14 = (bf16[128,512]{1,0:T(8,128)(2,1)S(1)}, bf16[128,512]{1,0:T(8,128)(2,1)}, u32[]{:S(2)}, u32[]{:S(2)}) collective-permute-start(bf16[128,512]{1,0:T(8,128)(2,1)S(1)} %get-tuple-element.29), channel_id=1, source_target_pairs={{0,3},{1,0},{2,1},{3,2},{4,7},{5,4},{6,5},{7,6},{8,11},{9,8},{10,9... | collective-permute-start | bytes 393224 | tf_op jit(solution)/shard_map/ppermute | solution.py:14
  82.8 4.0 %copy-start.7 = (bf16[8,64,512]{2,1,0:T(8,128)(2,1)S(1)}, bf16[8,64,512]{2,1,0:T(8,128)(2,1)}, u32[]{:S(2)}) copy-start(bf16[8,64,512]{2,1,0:T(8,128)(2,1)} %copy-done.6) | copy-start | bytes 1572868
  82.8 13.8 %all-to-all-start.4 = ((bf16[8,64,512]{2,1,0:T(8,128)(2,1)}), bf16[8,64,512]{2,1,0:T(8,128)(2,1)S(1)}, u32[]{:S(2)}, u32[]{:S(2)}) async-start(bf16[8,64,512]{2,1,0:T(8,128)(2,1)} %bitcast.42), calls=%async_computation.4 | async-start | bytes 1048576 | tf_op jit(solution)/shard_map/all_to_all | solution.py:19
  90.0 0.9 copy-start.9
  91.0 1.0 %copy-start.13 = (bf16[512,128]{1,0:T(8,128)(2,1)S(1)}, bf16[512,128]{1,0:T(8,128)(2,1)}, u32[]{:S(2)}) copy-start(bf16[512,128]{1,0:T(8,128)(2,1)} %copy-done.12) | copy-start | bytes 393220
  92.0 0.9 copy-start.11
  93.0 4.3 %copy-start.2 = (bf16[512,512]{1,0:T(8,128)(2,1)}, bf16[512,512]{1,0:T(8,128)(2,1)S(1)}, u32[]{:S(2)}) copy-start(bf16[512,512]{1,0:T(8,128)(2,1)S(1)} %fusion.76) | copy-start | bytes 1572868

commit v4 on v3

--- a/solution.py
+++ b/solution.py
@@ -103,9 +103,9 @@
         "cea,ecd->acd", second_f, grad_arrived.astype(F32)
     ).astype(BF16)
     first_grad = swap(first_out, "seq").reshape(rows, width)
-    first_grad, added_back, channel_part = lax.optimization_barrier(
-        (first_grad, added_back, channel_part)
-    )
+    first_grad, channel_part = lax.optimization_barrier((first_grad, channel_part))
+    block_part = jnp.dot(first_grad, gated.T, preferred_element_type=F32)
+    block_part, added_back = lax.optimization_barrier((block_part, added_back))
     outputs = place_chunks(
         [
             (lane_chunk(hidden, t, kq).astype(F32) + part.astype(F32)).astype(BF16)
@@ -114,7 +114,6 @@
         [t * kq for t in origin_of],
         hidden,
     )
-    block_part = jnp.dot(first_grad, gated.T, preferred_element_type=F32)
     cq = block_part.shape[0] // m
     block_arrived = exchange(
         [lax.dynamic_slice_in_dim(block_part, t * cq, cq, 0).astype(BF16) for t in chunk_of],

time: 98.2 us -> 98 us (level)
  other arithmetic: 8.82 us -> 11.3 us
  local copies, waits for them, and re-layouts: 12.9 us -> 10.7 us
    unnamed x67 -> x59, local copies, waits for them, and re-layouts: 5.46 us -> 3.36 us
    dynamic_update_slice x5, other arithmetic: 1.33 us -> 3.1 us  [place_chunks(): out = lax.dynamic_update_slice_in_dim(out, chunk, start, axis=1)]
  transfers between devices with their start and end apart: 20 -> 20, of which waited for: 8 -> 9; matrix products, arithmetic and copies ran while one was open for 20% -> 24% of each run, Pallas kernels for 0% -> 0%
where the time goes in v4:
time: 98 us; the launch traced here: 97.1 us
  starting transfers between devices  44.3 us (45%)
  waiting for transfers between devices  19.3 us (20%)
  other arithmetic  11.3 us (12%)
  local copies, waits for them, and re-layouts  10.7 us (11%)
  matrix products  10.3 us (11%)
  between operations  1.18 us (1%)
    ppermute x15, starting transfers between devices, exchange(): lax.ppermute(pieces[k], axis_name, [(i, (i + k) % n) for i in range(n)])  26.1 us
    all_to_all x5, starting transfers between devices, swap(): return lax.all_to_all(pieces, axis_name, 0, 0, tiled=True)  18.2 us
    all_to_all x5, waiting for transfers between devices, swap(): return lax.all_to_all(pieces, axis_name, 0, 0, tiled=True)  12.1 us
    ppermute x15, waiting for transfers between devices, exchange(): lax.ppermute(pieces[k], axis_name, [(i, (i + k) % n) for i in range(n)])  7.14 us
    convert_element_type x2, other arithmetic, on_device(): added_out = [sum((act_arrived[k].astype(F32) * coefficient(origin_of[k],...  3.51 us
    unnamed x59, local copies, waits for them, and re-layouts  3.36 us
    dot_general x1, matrix products, on_device(): spread = jnp.dot(first_blocks[0].T, first_grad, preferred_element_type=F32)  3.19 us
    dynamic_update_slice x5, other arithmetic, place_chunks(): out = lax.dynamic_update_slice_in_dim(out, chunk, start, axis=1)  3.1 us
  transfers between devices with their start and end apart: 20, of which 9 were waited for; matrix products, arithmetic and copies ran while one was open for 24% of the time, Pallas kernels for 0%

profile of v4, /device:TPU:0, one launch (start us, length us, event | category | flops | bytes accessed | tf_op | source)
XLA Modules:
  0.0 97.1 jit_solution(291595228304784696)
XLA Ops:
  0.7 0.7 copy-done.25
  1.4 1.8 %fusion.8 = bf16[512,512]{0,1:T(8,128)(2,1)S(1)} fusion(bf16[1,512,512]{2,1,0:T(8,128)(2,1)} %param.11, bf16[512,512]{1,0:T(8,128)(2,1)} %param.8, f32[512]{0:T(512)S(1)} %copy-done.25), kind=kOutput, calls=%fused_computation.25 | convolution fusion | flops 270532608 | bytes 1574912 | tf_op jit(solution)/shard_map/dot_general | solution.py:59
  3.2 0.1 constant_dynamic-slice_fusion.35
  3.3 3.1 %collective-permute-start = (bf16[512,128]{1,0:T(8,128)(2,1)S(1)}, bf16[512,128]{1,0:T(8,128)(2,1)S(1)}, u32[]{:S(2)}, u32[]{:S(2)}) collective-permute-start(bf16[512,128]{1,0:T(8,128)(2,1)S(1)} %get-tuple-element.36), channel_id=1, source_target_pairs={{0,1},{1,2},{2,3},{3,0},{4,5},{5,6},{6,7},{7,4},{8,9},{9,10},{10,1... | collective-permute-start | bytes 393224 | tf_op jit(solution)/shard_map/ppermute | solution.py:14
  6.4 2.6 %collective-permute-start.1 = (bf16[512,128]{1,0:T(8,128)(2,1)S(1)}, bf16[512,128]{1,0:T(8,128)(2,1)S(1)}, u32[]{:S(2)}, u32[]{:S(2)}) collective-permute-start(bf16[512,128]{1,0:T(8,128)(2,1)S(1)} %get-tuple-element.38), channel_id=1, source_target_pairs={{0,2},{1,3},{2,0},{3,1},{4,6},{5,7},{6,4},{7,5},{8,10},{9,11},{10,... | collective-permute-start | bytes 393224 | tf_op jit(solution)/shard_map/ppermute | solution.py:14
  9.0 1.3 %collective-permute-start.2 = (bf16[512,128]{1,0:T(8,128)(2,1)S(1)}, bf16[512,128]{1,0:T(8,128)(2,1)S(1)}, u32[]{:S(2)}, u32[]{:S(2)}) collective-permute-start(bf16[512,128]{1,0:T(8,128)(2,1)S(1)} %get-tuple-element.37), channel_id=1, source_target_pairs={{0,3},{1,0},{2,1},{3,2},{4,7},{5,4},{6,5},{7,6},{8,11},{9,8},{10,9... | collective-permute-start | bytes 393224 | tf_op jit(solution)/shard_map/ppermute | solution.py:14
  10.3 1.0 %copy.25 = bf16[512,512]{1,0:T(8,128)(2,1)} copy(bf16[512,512]{0,1:T(8,128)(2,1)S(1)} %fusion.8) | data formatting | bytes 1048576 | tf_op jit(solution)/shard_map/optimization_barrier | solution.py:62
  11.3 3.7 %all-to-all-start = ((bf16[8,64,512]{2,1,0:T(8,128)(2,1)}), bf16[8,64,512]{2,1,0:T(8,128)(2,1)S(1)}, u32[]{:S(2)}, u32[]{:S(2)}) async-start(bf16[8,64,512]{2,1,0:T(8,128)(2,1)} %bitcast.2), calls=%async_computation | async-start | bytes 1048576 | tf_op jit(solution)/shard_map/all_to_all | solution.py:19
  15.0 0.7 fusion.78
  15.7 0.7 copy-done.10
  16.5 0.1 copy.30
  16.7 0.7 fusion.106
  17.4 0.2 collective-permute-done.1
  17.6 0.9 fusion.56
  18.5 3.3 %collective-permute-start.3 = (bf16[512,128]{1,0:T(8,128)(2,1)}, bf16[512,128]{1,0:T(8,128)(2,1)}, u32[]{:S(2)}, u32[]{:S(2)}) collective-permute-start(bf16[512,128]{1,0:T(8,128)(2,1)} %get-tuple-element.28), channel_id=1, source_target_pairs={{0,1},{1,2},{2,3},{3,0},{4,5},{5,6},{6,7},{7,4},{8,9},{9,10},{10,1... | collective-permute-start | bytes 393224 | tf_op jit(solution)/shard_map/ppermute | solution.py:14
  21.8 1.6 %collective-permute-start.4 = (bf16[512,128]{1,0:T(8,128)(2,1)S(1)}, bf16[512,128]{1,0:T(8,128)(2,1)}, u32[]{:S(2)}, u32[]{:S(2)}) collective-permute-start(bf16[512,128]{1,0:T(8,128)(2,1)S(1)} %get-tuple-element.29), channel_id=1, source_target_pairs={{0,2},{1,3},{2,0},{3,1},{4,6},{5,7},{6,4},{7,5},{8,10},{9,11},{10,... | collective-permute-start | bytes 393224 | tf_op jit(solution)/shard_map/ppermute | solution.py:14
  23.4 0.7 collective-permute-start.5
  24.2 0.6 all-to-all-done
  24.8 0.4 fusion.6
  25.2 0.9 copy.28
  26.2 3.5 %all-to-all-start.1 = ((bf16[8,64,512]{2,1,0:T(8,128)(2,1)}), bf16[8,64,512]{2,1,0:T(8,128)(2,1)S(1)}, u32[]{:S(2)}, u32[]{:S(2)}) async-start(bf16[8,64,512]{2,1,0:T(8,128)(2,1)} %copy.28), calls=%async_computation.1 | async-start | bytes 1048576 | tf_op jit(solution)/shard_map/all_to_all | solution.py:19
  29.7 0.1 fusion.77
  29.9 1.0 %constant_dynamic-update-slice_fusion.2 = bf16[512,512]{1,0:T(8,128)(2,1)S(1)} fusion(bf16[512,512]{1,0:T(8,128)(2,1)S(1)} %fusion.77, bf16[512,128]{1,0:T(8,128)(2,1)} %collective-permute-done.3, s32[]{:T(128)S(6)} %select_n.80), kind=kLoop, calls=%fused_computation.166 | loop fusion | bytes 262148 | tf_op jit(solution)/shard_map/dynamic_update_slice | solution.py:33
  30.9 1.1 %collective-permute-done.4 = bf16[512,128]{1,0:T(8,128)(2,1)} collective-permute-done((bf16[512,128]{1,0:T(8,128)(2,1)S(1)}, bf16[512,128]{1,0:T(8,128)(2,1)}, u32[]{:S(2)}, u32[]{:S(2)}) %collective-permute-start.4) | collective-permute-done | bytes 131104 | tf_op jit(solution)/shard_map/ppermute | solution.py:14
  32.0 0.9 constant_dynamic-update-slice_fusion.1
  33.0 0.9 constant_dynamic-update-slice_fusion
  33.9 5.4 %all-to-all-done.1 = bf16[8,64,512]{2,1,0:T(8,128)(2,1)S(1)} async-done(((bf16[8,64,512]{2,1,0:T(8,128)(2,1)}), bf16[8,64,512]{2,1,0:T(8,128)(2,1)S(1)}, u32[]{:S(2)}, u32[]{:S(2)}) %all-to-all-start.1) | async-done | bytes 524320 | tf_op jit(solution)/shard_map/all_to_all | solution.py:19
  39.4 0.4 fusion.33
  39.8 1.1 %multiply_convert_fusion = (bf16[512,512]{1,0:T(8,128)(2,1)S(1)}, bf16[512,512]{1,0:T(8,128)(2,1)S(1)}) fusion(bf16[512,512]{1,0:T(8,128)(2,1)S(1)} %constant_dynamic-update-slice_fusion, bf16[512,512]{1,0:T(8,128)(2,1)S(1)} %fusion.33, bf16[1,512,512]{2,1,0:T(8,128)(2,1)S(1)} %copy-done), kind=kOutput, calls=%fused_computation.52 | convolution fusion | flops 274464768 | bytes 2621440 | tf_op jit(solution)/shard_map/dot_general | solution.py:81
  40.9 1.6 %fusion.24 = (bf16[512,512]{1,0:T(8,128)(2,1)}, bf16[512,512]{1,0:T(8,128)(2,1)}) fusion(bf16[512,512]{1,0:T(8,128)(2,1)S(1)} %copy-done.4, f32[512]{0:T(512)S(1)} %copy-done.11, bf16[512,512]{1,0:T(8,128)(2,1)S(1)} %get-tuple-element.23, bf16[1,512,512]{2,1,0:T(8,128)(2,1)S(1)} %copy-done, bf16[512,512]{1,0:T(8,128)(2,1)S(1)} %copy-done.1), kind=kOutput, calls=%fused_computation.41 | convolution fusion | flops 271319040 | bytes 3147776 | tf_op jit(solution)/shard_map/dot_general | solution.py:95
  42.5 3.5 %all-to-all-start.2 = ((bf16[8,64,512]{2,1,0:T(8,128)(2,1)}), bf16[8,64,512]{2,1,0:T(8,128)(2,1)S(1)}, u32[]{:S(2)}, u32[]{:S(2)}) async-start(bf16[8,64,512]{2,1,0:T(8,128)(2,1)} %bitcast.22), calls=%async_computation.2 | async-start | bytes 1048576 | tf_op jit(solution)/shard_map/all_to_all | solution.py:19
  46.0 0.1 constant_dynamic-slice_fusion.13
  46.1 1.0 %collective-permute-start.6 = (bf16[512,128]{1,0:T(8,128)(2,1)S(1)}, bf16[512,128]{1,0:T(8,128)(2,1)S(1)}, u32[]{:S(2)}, u32[]{:S(2)}) collective-permute-start(bf16[512,128]{1,0:T(8,128)(2,1)S(1)} %get-tuple-element.35), channel_id=1, source_target_pairs={{0,1},{1,2},{2,3},{3,0},{4,5},{5,6},{6,7},{7,4},{8,9},{9,10},{10,1... | collective-permute-start | bytes 393224 | tf_op jit(solution)/shard_map/ppermute | solution.py:14
  47.1 1.3 %collective-permute-start.7 = (bf16[512,128]{1,0:T(8,128)(2,1)S(1)}, bf16[512,128]{1,0:T(8,128)(2,1)S(1)}, u32[]{:S(2)}, u32[]{:S(2)}) collective-permute-start(bf16[512,128]{1,0:T(8,128)(2,1)S(1)} %get-tuple-element.34), channel_id=1, source_target_pairs={{0,2},{1,3},{2,0},{3,1},{4,6},{5,7},{6,4},{7,5},{8,10},{9,11},{10,... | collective-permute-start | bytes 393224 | tf_op jit(solution)/shard_map/ppermute | solution.py:14
  48.4 1.6 %collective-permute-start.8 = (bf16[512,128]{1,0:T(8,128)(2,1)S(1)}, bf16[512,128]{1,0:T(8,128)(2,1)}, u32[]{:S(2)}, u32[]{:S(2)}) collective-permute-start(bf16[512,128]{1,0:T(8,128)(2,1)S(1)} %get-tuple-element.33), channel_id=1, source_target_pairs={{0,3},{1,0},{2,1},{3,2},{4,7},{5,4},{6,5},{7,6},{8,11},{9,8},{10,9... | collective-permute-start | bytes 393224 | tf_op jit(solution)/shard_map/ppermute | solution.py:14
  50.0 1.3 %fusion.113 = bf16[512,512]{1,0:T(8,128)(2,1)} fusion(bf16[512,512]{1,0:T(8,128)(2,1)S(1)} %fusion.33, bf16[512,512]{1,0:T(8,128)(2,1)S(1)} %copy-done.28), kind=kOutput, calls=%fused_computation.212 | convolution fusion | flops 268435456 | bytes 1572864 | tf_op jit(solution)/shard_map/dot_general | solution.py:97
  51.3 4.4 %all-to-all-done.2 = bf16[8,64,512]{2,1,0:T(8,128)(2,1)S(1)} async-done(((bf16[8,64,512]{2,1,0:T(8,128)(2,1)}), bf16[8,64,512]{2,1,0:T(8,128)(2,1)S(1)}, u32[]{:S(2)}, u32[]{:S(2)}) %all-to-all-start.2) | async-done | bytes 524320 | tf_op jit(solution)/shard_map/all_to_all | solution.py:19
  55.7 0.4 fusion.7
  56.1 0.9 copy.31
  57.1 3.5 %all-to-all-start.3 = ((bf16[8,64,512]{2,1,0:T(8,128)(2,1)}), bf16[8,64,512]{2,1,0:T(8,128)(2,1)S(1)}, u32[]{:S(2)}, u32[]{:S(2)}) async-start(bf16[8,64,512]{2,1,0:T(8,128)(2,1)} %copy.31), calls=%async_computation.3 | async-start | bytes 1048576 | tf_op jit(solution)/shard_map/all_to_all | solution.py:19
  60.7 0.6 copy-done.12
  61.3 0.0 copy-done.13
  61.3 1.8 %fusion.72 = (bf16[512,128]{1,0:T(8,128)(2,1)}, bf16[512,128]{1,0:T(8,128)(2,1)}, bf16[512,128]{1,0:T(8,128)(2,1)}) fusion(bf16[512,128]{1,0:T(8,128)(2,1)S(1)} %collective-permute-done.6, bf16[512,128]{1,0:T(8,128)(2,1)S(1)} %collective-permute-done.7, bf16[512,128]{1,0:T(8,128)(2,1)} %collective-permute-done.8, f32[128]{0:T(128)S(1)} %get-tuple-element.40, ...), kind=kLoop, calls=%fused_computation.123 | loop fusion | flops 1835008 | bytes 923652 | tf_op jit(solution)/shard_map/convert_element_type | solution.py:89
  63.2 0.9 collective-permute-start.10
  64.1 3.5 %collective-permute-start.11 = (bf16[512,128]{1,0:T(8,128)(2,1)}, bf16[512,128]{1,0:T(8,128)(2,1)}, u32[]{:S(2)}, u32[]{:S(2)}) collective-permute-start(bf16[512,128]{1,0:T(8,128)(2,1)} %get-tuple-element.24), channel_id=1, source_target_pairs={{0,3},{1,0},{2,1},{3,2},{4,7},{5,4},{6,5},{7,6},{8,11},{9,8},{10,9... | collective-permute-start | bytes 393224 | tf_op jit(solution)/shard_map/ppermute | solution.py:14
  67.6 1.7 %fusion.60 = bf16[512,128]{1,0:T(8,128)(2,1)} fusion(bf16[512,128]{1,0:T(8,128)(2,1)S(1)} %collective-permute-done.6, bf16[512,128]{1,0:T(8,128)(2,1)S(1)} %collective-permute-done.7, bf16[512,128]{1,0:T(8,128)(2,1)} %collective-permute-done.8, f32[128]{0:T(128)S(1)} %copy-done.22, f32[128]{0:T(128)S(1)} %copy-done.23, f32[128]{0:T(128)S(1)} %copy-done.24, ...), kind=kLoop, calls=%fused_computation.111 | loop fusion | flops 786432 | bytes 657412 | tf_op jit(solution)/shard_map/convert_element_type | solution.py:89
  69.3 1.0 %all-to-all-done.3 = bf16[8,64,512]{2,1,0:T(8,128)(2,1)S(1)} async-done(((bf16[8,64,512]{2,1,0:T(8,128)(2,1)}), bf16[8,64,512]{2,1,0:T(8,128)(2,1)S(1)}, u32[]{:S(2)}, u32[]{:S(2)}) %all-to-all-start.3) | async-done | bytes 524320 | tf_op jit(solution)/shard_map/all_to_all | solution.py:19
  70.3 0.6 fusion.110
  70.9 0.2 copy-done.6
  71.1 3.3 %collective-permute-done.10 = bf16[512,128]{1,0:T(8,128)(2,1)} collective-permute-done((bf16[512,128]{1,0:T(8,128)(2,1)}, bf16[512,128]{1,0:T(8,128)(2,1)}, u32[]{:S(2)}, u32[]{:S(2)}) %collective-permute-start.10) | collective-permute-done | bytes 131104 | tf_op jit(solution)/shard_map/ppermute | solution.py:14
  74.3 2.5 %collective-permute-done.9 = bf16[512,128]{1,0:T(8,128)(2,1)} collective-permute-done((bf16[512,128]{1,0:T(8,128)(2,1)}, bf16[512,128]{1,0:T(8,128)(2,1)}, u32[]{:S(2)}, u32[]{:S(2)}) %collective-permute-start.9) | collective-permute-done | bytes 131104 | tf_op jit(solution)/shard_map/ppermute | solution.py:14
  76.8 0.7 dynamic-slice_convert_fusion.2
  77.5 2.4 %collective-permute-start.12 = (bf16[128,512]{1,0:T(8,128)(2,1)}, bf16[128,512]{1,0:T(8,128)(2,1)S(1)}, u32[]{:S(2)}, u32[]{:S(2)}) collective-permute-start(bf16[128,512]{1,0:T(8,128)(2,1)} %get-tuple-element.30), channel_id=1, source_target_pairs={{0,1},{1,2},{2,3},{3,0},{4,5},{5,6},{6,7},{7,4},{8,9},{9,10},{10,1... | collective-permute-start | bytes 393224 | tf_op jit(solution)/shard_map/ppermute | solution.py:14
  79.9 2.8 %collective-permute-start.14 = (bf16[128,512]{1,0:T(8,128)(2,1)S(1)}, bf16[128,512]{1,0:T(8,128)(2,1)}, u32[]{:S(2)}, u32[]{:S(2)}) collective-permute-start(bf16[128,512]{1,0:T(8,128)(2,1)S(1)} %get-tuple-element.31), channel_id=1, source_target_pairs={{0,3},{1,0},{2,1},{3,2},{4,7},{5,4},{6,5},{7,6},{8,11},{9,8},{10,9... | collective-permute-start | bytes 393224 | tf_op jit(solution)/shard_map/ppermute | solution.py:14
  82.7 4.0 %all-to-all-start.4 = ((bf16[8,64,512]{2,1,0:T(8,128)(2,1)}), bf16[8,64,512]{2,1,0:T(8,128)(2,1)S(1)}, u32[]{:S(2)}, u32[]{:S(2)}) async-start(bf16[8,64,512]{2,1,0:T(8,128)(2,1)} %bitcast.42), calls=%async_computation.4 | async-start | bytes 1048576 | tf_op jit(solution)/shard_map/all_to_all | solution.py:19
  86.7 3.2 %fusion.3 = bf16[512,512]{1,0:T(8,128)(2,1)} fusion(bf16[512,512]{1,0:T(8,128)(2,1)S(1)} %bitcast.112, bf16[512,512]{1,0:T(8,128)(2,1)} %get-tuple-element.71, bf16[512,512]{1,0:T(8,128)(2,1)S(1)} %copy-done.5, bf16[512,512]{1,0:T(8,128)(2,1)S(1)} %bitcast.110, bf16[1,512,512]{2,1,0:T(8,128)(2,1)} %param.11, f32[512]{0:T(512)S(1)} %copy-done.11, ...), kind=kOutput, calls=%fused_computation.20 | convolution fusion | flops 274726912 | bytes 3149824 | tf_op jit(solution)/shard_map/dot_general | solution.py:126
  89.9 0.9 copy-done.9
  90.8 0.1 fusion.73
  90.8 1.0 fusion.74
  91.8 1.0 fusion.75
  92.8 1.0 fusion.76
  93.8 2.0 %add_bitcast_fusion = f32[1,128,512]{2,1,0:T(8,128)} fusion(bf16[128,512]{1,0:T(8,128)(2,1)} %collective-permute-done.14, bf16[128,512]{1,0:T(8,128)(2,1)} %collective-permute-done.13, bf16[128,512]{1,0:T(8,128)(2,1)S(1)} %collective-permute-done.12, bf16[512,512]{1,0:T(8,128)(2,1)} %copy-done.8, s32[]{:T(128)S(6)} %select_n.64), kind=kLoop, calls=%fused_computation.124 | loop fusion | flops 458752 | bytes 786436 | tf_op jit(solution)/shard_map/broadcast_in_dim | solution.py:122
  95.7 0.7 all-to-all-done.4
  96.4 0.7 convert_reduce_fusion
  (67 shorter events, 0.2 us)
Async XLA Ops:
  0.6 39.1 %copy-start = (bf16[1,512,512]{2,1,0:T(8,128)(2,1)S(1)}, bf16[1,512,512]{2,1,0:T(8,128)(2,1)}, u32[]{:S(2)}) copy-start(bf16[1,512,512]{2,1,0:T(8,128)(2,1)} %param.13) | copy-start | bytes 1572868
  0.7 0.7 copy-start.25
  1.4 1.8 %copy-start.1 = (bf16[512,512]{1,0:T(8,128)(2,1)S(1)}, bf16[512,512]{1,0:T(8,128)(2,1)}, u32[]{:S(2)}) copy-start(bf16[512,512]{1,0:T(8,128)(2,1)} %param.15) | copy-start | bytes 1572868
  3.3 14.1 %collective-permute-start = (bf16[512,128]{1,0:T(8,128)(2,1)S(1)}, bf16[512,128]{1,0:T(8,128)(2,1)S(1)}, u32[]{:S(2)}, u32[]{:S(2)}) collective-permute-start(bf16[512,128]{1,0:T(8,128)(2,1)S(1)} %get-tuple-element.36), channel_id=1, source_target_pairs={{0,1},{1,2},{2,3},{3,0},{4,5},{5,6},{6,7},{7,4},{8,9},{9,10},{10,1... | collective-permute-start | bytes 393224 | tf_op jit(solution)/shard_map/ppermute | solution.py:14
  6.4 11.2 %collective-permute-start.1 = (bf16[512,128]{1,0:T(8,128)(2,1)S(1)}, bf16[512,128]{1,0:T(8,128)(2,1)S(1)}, u32[]{:S(2)}, u32[]{:S(2)}) collective-permute-start(bf16[512,128]{1,0:T(8,128)(2,1)S(1)} %get-tuple-element.38), channel_id=1, source_target_pairs={{0,2},{1,3},{2,0},{3,1},{4,6},{5,7},{6,4},{7,5},{8,10},{9,11},{10,... | collective-permute-start | bytes 393224 | tf_op jit(solution)/shard_map/ppermute | solution.py:14
  9.0 8.6 %collective-permute-start.2 = (bf16[512,128]{1,0:T(8,128)(2,1)S(1)}, bf16[512,128]{1,0:T(8,128)(2,1)S(1)}, u32[]{:S(2)}, u32[]{:S(2)}) collective-permute-start(bf16[512,128]{1,0:T(8,128)(2,1)S(1)} %get-tuple-element.37), channel_id=1, source_target_pairs={{0,3},{1,0},{2,1},{3,2},{4,7},{5,4},{6,5},{7,6},{8,11},{9,8},{10,9... | collective-permute-start | bytes 393224 | tf_op jit(solution)/shard_map/ppermute | solution.py:14
  11.3 13.5 %all-to-all-start = ((bf16[8,64,512]{2,1,0:T(8,128)(2,1)}), bf16[8,64,512]{2,1,0:T(8,128)(2,1)S(1)}, u32[]{:S(2)}, u32[]{:S(2)}) async-start(bf16[8,64,512]{2,1,0:T(8,128)(2,1)} %bitcast.2), calls=%async_computation | async-start | bytes 1048576 | tf_op jit(solution)/shard_map/all_to_all | solution.py:19
  15.7 0.7 copy-start.10
  18.5 11.4 %collective-permute-start.3 = (bf16[512,128]{1,0:T(8,128)(2,1)}, bf16[512,128]{1,0:T(8,128)(2,1)}, u32[]{:S(2)}, u32[]{:S(2)}) collective-permute-start(bf16[512,128]{1,0:T(8,128)(2,1)} %get-tuple-element.28), channel_id=1, source_target_pairs={{0,1},{1,2},{2,3},{3,0},{4,5},{5,6},{6,7},{7,4},{8,9},{9,10},{10,1... | collective-permute-start | bytes 393224 | tf_op jit(solution)/shard_map/ppermute | solution.py:14
  21.8 10.2 %collective-permute-start.4 = (bf16[512,128]{1,0:T(8,128)(2,1)S(1)}, bf16[512,128]{1,0:T(8,128)(2,1)}, u32[]{:S(2)}, u32[]{:S(2)}) collective-permute-start(bf16[512,128]{1,0:T(8,128)(2,1)S(1)} %get-tuple-element.29), channel_id=1, source_target_pairs={{0,2},{1,3},{2,0},{3,1},{4,6},{5,7},{6,4},{7,5},{8,10},{9,11},{10,... | collective-permute-start | bytes 393224 | tf_op jit(solution)/shard_map/ppermute | solution.py:14
  23.4 9.6 %collective-permute-start.5 = (bf16[512,128]{1,0:T(8,128)(2,1)S(1)}, bf16[512,128]{1,0:T(8,128)(2,1)}, u32[]{:S(2)}, u32[]{:S(2)}) collective-permute-start(bf16[512,128]{1,0:T(8,128)(2,1)S(1)} %get-tuple-element.27), channel_id=1, source_target_pairs={{0,3},{1,0},{2,1},{3,2},{4,7},{5,4},{6,5},{7,6},{8,11},{9,8},{10,9... | collective-permute-start | bytes 393224 | tf_op jit(solution)/shard_map/ppermute | solution.py:14
  26.2 13.2 %all-to-all-start.1 = ((bf16[8,64,512]{2,1,0:T(8,128)(2,1)}), bf16[8,64,512]{2,1,0:T(8,128)(2,1)S(1)}, u32[]{:S(2)}, u32[]{:S(2)}) async-start(bf16[8,64,512]{2,1,0:T(8,128)(2,1)} %copy.28), calls=%async_computation.1 | async-start | bytes 1048576 | tf_op jit(solution)/shard_map/all_to_all | solution.py:19
  29.9 9.5 %copy-start.3 = (bf16[512,512]{1,0:T(8,128)(2,1)S(1)}, bf16[512,512]{1,0:T(8,128)(2,1)}, u32[]{:S(2)}) copy-start(bf16[512,512]{1,0:T(8,128)(2,1)} %param.8) | copy-start | bytes 1572868
  33.0 6.4 %copy-start.11 = (f32[512]{0:T(512)S(1)}, f32[512]{0:T(512)}, u32[]{:S(2)}) copy-start(f32[512]{0:T(512)} %param.10) | copy-start | bytes 6148
  39.8 1.2 %copy-start.4 = (bf16[512,512]{1,0:T(8,128)(2,1)S(1)}, bf16[512,512]{1,0:T(8,128)(2,1)}, u32[]{:S(2)}) copy-start(bf16[512,512]{1,0:T(8,128)(2,1)} %param.8) | copy-start | bytes 1572868
  40.9 1.6 %copy-start.27 = (bf16[512,512]{1,0:T(8,128)(2,1)}, bf16[512,512]{1,0:T(8,128)(2,1)S(1)}, u32[]{:S(2)}) copy-start(bf16[512,512]{1,0:T(8,128)(2,1)S(1)} %get-tuple-element.23) | copy-start | bytes 1572868
  42.5 13.2 %all-to-all-start.2 = ((bf16[8,64,512]{2,1,0:T(8,128)(2,1)}), bf16[8,64,512]{2,1,0:T(8,128)(2,1)S(1)}, u32[]{:S(2)}, u32[]{:S(2)}) async-start(bf16[8,64,512]{2,1,0:T(8,128)(2,1)} %bitcast.22), calls=%async_computation.2 | async-start | bytes 1048576 | tf_op jit(solution)/shard_map/all_to_all | solution.py:19
  46.0 4.0 %copy-start.28 = (bf16[512,512]{1,0:T(8,128)(2,1)S(1)}, bf16[512,512]{1,0:T(8,128)(2,1)}, u32[]{:S(2)}) copy-start(bf16[512,512]{1,0:T(8,128)(2,1)} %copy-done.27) | copy-start | bytes 1572868
  46.1 14.5 %collective-permute-start.6 = (bf16[512,128]{1,0:T(8,128)(2,1)S(1)}, bf16[512,128]{1,0:T(8,128)(2,1)S(1)}, u32[]{:S(2)}, u32[]{:S(2)}) collective-permute-start(bf16[512,128]{1,0:T(8,128)(2,1)S(1)} %get-tuple-element.35), channel_id=1, source_target_pairs={{0,1},{1,2},{2,3},{3,0},{4,5},{5,6},{6,7},{7,4},{8,9},{9,10},{10,1... | collective-permute-start | bytes 393224 | tf_op jit(solution)/shard_map/ppermute | solution.py:14
  47.1 13.5 %collective-permute-start.7 = (bf16[512,128]{1,0:T(8,128)(2,1)S(1)}, bf16[512,128]{1,0:T(8,128)(2,1)S(1)}, u32[]{:S(2)}, u32[]{:S(2)}) collective-permute-start(bf16[512,128]{1,0:T(8,128)(2,1)S(1)} %get-tuple-element.34), channel_id=1, source_target_pairs={{0,2},{1,3},{2,0},{3,1},{4,6},{5,7},{6,4},{7,5},{8,10},{9,11},{10,... | collective-permute-start | bytes 393224 | tf_op jit(solution)/shard_map/ppermute | solution.py:14
  48.4 12.2 %collective-permute-start.8 = (bf16[512,128]{1,0:T(8,128)(2,1)S(1)}, bf16[512,128]{1,0:T(8,128)(2,1)}, u32[]{:S(2)}, u32[]{:S(2)}) collective-permute-start(bf16[512,128]{1,0:T(8,128)(2,1)S(1)} %get-tuple-element.33), channel_id=1, source_target_pairs={{0,3},{1,0},{2,1},{3,2},{4,7},{5,4},{6,5},{7,6},{8,11},{9,8},{10,9... | collective-permute-start | bytes 393224 | tf_op jit(solution)/shard_map/ppermute | solution.py:14
  57.0 3.6 %copy-start.15 = (f32[128]{0:T(128)S(1)}, f32[128]{0:T(128)}, u32[]{:S(2)}) copy-start(f32[128]{0:T(128)} %get-tuple-element.44) | copy-start | bytes 1540
  57.0 3.6 %copy-start.16 = (f32[128]{0:T(128)S(1)}, f32[128]{0:T(128)}, u32[]{:S(2)}) copy-start(f32[128]{0:T(128)} %get-tuple-element.45) | copy-start | bytes 1540
  57.0 3.6 %copy-start.17 = (f32[128]{0:T(128)S(1)}, f32[128]{0:T(128)}, u32[]{:S(2)}) copy-start(f32[128]{0:T(128)} %get-tuple-element.46) | copy-start | bytes 1540
  57.0 3.6 %copy-start.18 = (f32[128]{0:T(128)S(1)}, f32[128]{0:T(128)}, u32[]{:S(2)}) copy-start(f32[128]{0:T(128)} %get-tuple-element.47) | copy-start | bytes 1540
  57.1 3.6 %copy-start.19 = (f32[128]{0:T(128)S(1)}, f32[128]{0:T(128)}, u32[]{:S(2)}) copy-start(f32[128]{0:T(128)} %get-tuple-element.48) | copy-start | bytes 1540
  57.1 3.6 %copy-start.20 = (f32[128]{0:T(128)S(1)}, f32[128]{0:T(128)}, u32[]{:S(2)}) copy-start(f32[128]{0:T(128)} %get-tuple-element.49) | copy-start | bytes 1540
  57.1 3.6 %copy-start.21 = (f32[128]{0:T(128)S(1)}, f32[128]{0:T(128)}, u32[]{:S(2)}) copy-start(f32[128]{0:T(128)} %get-tuple-element.50) | copy-start | bytes 1540
  57.1 13.2 %all-to-all-start.3 = ((bf16[8,64,512]{2,1,0:T(8,128)(2,1)}), bf16[8,64,512]{2,1,0:T(8,128)(2,1)S(1)}, u32[]{:S(2)}, u32[]{:S(2)}) async-start(bf16[8,64,512]{2,1,0:T(8,128)(2,1)} %copy.31), calls=%async_computation.3 | async-start | bytes 1048576 | tf_op jit(solution)/shard_map/all_to_all | solution.py:19
  60.6 0.7 copy-start.12
  60.6 0.7 copy-start.13
  60.7 0.7 copy-start.14
  61.3 6.2 %copy-start.22 = (f32[128]{0:T(128)S(1)}, f32[128]{0:T(128)}, u32[]{:S(2)}) copy-start(f32[128]{0:T(128)} %get-tuple-element.51) | copy-start | bytes 1540
  61.3 6.2 %copy-start.23 = (f32[128]{0:T(128)S(1)}, f32[128]{0:T(128)}, u32[]{:S(2)}) copy-start(f32[128]{0:T(128)} %get-tuple-element.52) | copy-start | bytes 1540
  61.3 6.2 %copy-start.24 = (f32[128]{0:T(128)S(1)}, f32[128]{0:T(128)}, u32[]{:S(2)}) copy-start(f32[128]{0:T(128)} %get-tuple-element.53) | copy-start | bytes 1540
  63.2 7.1 %copy-start.5 = (bf16[512,512]{1,0:T(8,128)(2,1)S(1)}, bf16[512,512]{1,0:T(8,128)(2,1)}, u32[]{:S(2)}) copy-start(bf16[512,512]{1,0:T(8,128)(2,1)} %param.8) | copy-start | bytes 1572868
  63.2 11.2 %collective-permute-start.10 = (bf16[512,128]{1,0:T(8,128)(2,1)}, bf16[512,128]{1,0:T(8,128)(2,1)}, u32[]{:S(2)}, u32[]{:S(2)}) collective-permute-start(bf16[512,128]{1,0:T(8,128)(2,1)} %get-tuple-element.26), channel_id=1, source_target_pairs={{0,2},{1,3},{2,0},{3,1},{4,6},{5,7},{6,4},{7,5},{8,10},{9,11},{10,... | collective-permute-start | bytes 393224 | tf_op jit(solution)/shard_map/ppermute | solution.py:14
  64.1 10.3 %collective-permute-start.11 = (bf16[512,128]{1,0:T(8,128)(2,1)}, bf16[512,128]{1,0:T(8,128)(2,1)}, u32[]{:S(2)}, u32[]{:S(2)}) collective-permute-start(bf16[512,128]{1,0:T(8,128)(2,1)} %get-tuple-element.24), channel_id=1, source_target_pairs={{0,3},{1,0},{2,1},{3,2},{4,7},{5,4},{6,5},{7,6},{8,11},{9,8},{10,9... | collective-permute-start | bytes 393224 | tf_op jit(solution)/shard_map/ppermute | solution.py:14
  67.5 9.3 %collective-permute-start.9 = (bf16[512,128]{1,0:T(8,128)(2,1)}, bf16[512,128]{1,0:T(8,128)(2,1)}, u32[]{:S(2)}, u32[]{:S(2)}) collective-permute-start(bf16[512,128]{1,0:T(8,128)(2,1)} %get-tuple-element.25), channel_id=1, source_target_pairs={{0,1},{1,2},{2,3},{3,0},{4,5},{5,6},{6,7},{7,4},{8,9},{9,10},{10,1... | collective-permute-start | bytes 393224 | tf_op jit(solution)/shard_map/ppermute | solution.py:14
  67.6 2.7 %copy-start.26 = (f32[512]{0:T(512)S(1)}, f32[512]{0:T(512)}, u32[]{:S(2)}) copy-start(f32[512]{0:T(512)} %param.9) | copy-start | bytes 6148
  70.3 0.8 copy-start.6
  71.1 11.6 %copy-start.8 = (bf16[512,512]{1,0:T(8,128)(2,1)}, bf16[512,512]{1,0:T(8,128)(2,1)S(1)}, u32[]{:S(2)}) copy-start(bf16[512,512]{1,0:T(8,128)(2,1)S(1)} %fusion.110) | copy-start | bytes 1572868
  77.5 16.3 %collective-permute-start.12 = (bf16[128,512]{1,0:T(8,128)(2,1)}, bf16[128,512]{1,0:T(8,128)(2,1)S(1)}, u32[]{:S(2)}, u32[]{:S(2)}) collective-permute-start(bf16[128,512]{1,0:T(8,128)(2,1)} %get-tuple-element.30), channel_id=1, source_target_pairs={{0,1},{1,2},{2,3},{3,0},{4,5},{5,6},{6,7},{7,4},{8,9},{9,10},{10,1... | collective-permute-start | bytes 393224 | tf_op jit(solution)/shard_map/ppermute | solution.py:14
  79.9 13.9 %collective-permute-start.13 = (bf16[128,512]{1,0:T(8,128)(2,1)S(1)}, bf16[128,512]{1,0:T(8,128)(2,1)}, u32[]{:S(2)}, u32[]{:S(2)}) collective-permute-start(bf16[128,512]{1,0:T(8,128)(2,1)S(1)} %get-tuple-element.32), channel_id=1, source_target_pairs={{0,2},{1,3},{2,0},{3,1},{4,6},{5,7},{6,4},{7,5},{8,10},{9,11},{10,... | collective-permute-start | bytes 393224 | tf_op jit(solution)/shard_map/ppermute | solution.py:14
  79.9 13.9 %collective-permute-start.14 = (bf16[128,512]{1,0:T(8,128)(2,1)S(1)}, bf16[128,512]{1,0:T(8,128)(2,1)}, u32[]{:S(2)}, u32[]{:S(2)}) collective-permute-start(bf16[128,512]{1,0:T(8,128)(2,1)S(1)} %get-tuple-element.31), channel_id=1, source_target_pairs={{0,3},{1,0},{2,1},{3,2},{4,7},{5,4},{6,5},{7,6},{8,11},{9,8},{10,9... | collective-permute-start | bytes 393224 | tf_op jit(solution)/shard_map/ppermute | solution.py:14
  82.7 4.0 %copy-start.7 = (bf16[8,64,512]{2,1,0:T(8,128)(2,1)S(1)}, bf16[8,64,512]{2,1,0:T(8,128)(2,1)}, u32[]{:S(2)}) copy-start(bf16[8,64,512]{2,1,0:T(8,128)(2,1)} %copy-done.6) | copy-start | bytes 1572868
  82.7 13.8 %all-to-all-start.4 = ((bf16[8,64,512]{2,1,0:T(8,128)(2,1)}), bf16[8,64,512]{2,1,0:T(8,128)(2,1)S(1)}, u32[]{:S(2)}, u32[]{:S(2)}) async-start(bf16[8,64,512]{2,1,0:T(8,128)(2,1)} %bitcast.42), calls=%async_computation.4 | async-start | bytes 1048576 | tf_op jit(solution)/shard_map/all_to_all | solution.py:19
  89.9 0.9 copy-start.9
  93.7 3.4 %copy-start.2 = (bf16[512,512]{1,0:T(8,128)(2,1)}, bf16[512,512]{1,0:T(8,128)(2,1)S(1)}, u32[]{:S(2)}) copy-start(bf16[512,512]{1,0:T(8,128)(2,1)S(1)} %fusion.76) | copy-start | bytes 1572868

commit v5 on v4

--- a/solution.py
+++ b/solution.py
@@ -105,7 +105,13 @@
     first_grad = swap(first_out, "seq").reshape(rows, width)
     first_grad, channel_part = lax.optimization_barrier((first_grad, channel_part))
     block_part = jnp.dot(first_grad, gated.T, preferred_element_type=F32)
-    block_part, added_back = lax.optimization_barrier((block_part, added_back))
+    cq = block_part.shape[0] // m
+    block_arrived = exchange(
+        [lax.dynamic_slice_in_dim(block_part, t * cq, cq, 0).astype(BF16) for t in chunk_of],
+        "ch",
+    )
+    block_arrived, added_back = lax.optimization_barrier((block_arrived, added_back))
+    block_grad = sum(part.astype(F32) for part in block_arrived)[None]
     outputs = place_chunks(
         [
             (lane_chunk(hidden, t, kq).astype(F32) + part.astype(F32)).astype(BF16)
@@ -114,12 +120,6 @@
         [t * kq for t in origin_of],
         hidden,
     )
-    cq = block_part.shape[0] // m
-    block_arrived = exchange(
-        [lax.dynamic_slice_in_dim(block_part, t * cq, cq, 0).astype(BF16) for t in chunk_of],
-        "ch",
-    )
-    block_grad = sum(part.astype(F32) for part in block_arrived)[None]
     channel_arrived = swap(split_rows(channel_part, n).astype(BF16), "seq")
     channel_grad = jnp.sum(channel_arrived.astype(F32), axis=0)[None]
 

time: 98 us -> 94.5 us (0.964)
  starting transfers between devices: 44.3 us -> 42.1 us
  other arithmetic: 11.3 us -> 10.2 us
    ppermute x15, starting transfers between devices: 26.1 us -> 24.2 us  [exchange(): lax.ppermute(pieces[k], axis_name, [(i, (i + k) % n) for i in range(n)])]
    broadcast_in_dim x1, other arithmetic: 1.96 us -> 0.85 us  [on_device(): block_grad = sum((part.astype(F32) for part in block_arrived))[None]]
    unnamed x59 -> x57, local copies, waits for them, and re-layouts: 3.36 us -> 3.35 us
  transfers between devices with their start and end apart: 20 -> 20, of which waited for: 9 -> 7; matrix products, arithmetic and copies ran while one was open for 24% -> 24% of each run, Pallas kernels for 0% -> 0%
where the time goes in v5:
time: 94.5 us; the launch traced here: 93.5 us
  starting transfers between devices  42.1 us (45%)
  waiting for transfers between devices  18.9 us (20%)
  local copies, waits for them, and re-layouts  10.8 us (11%)
  matrix products  10.3 us (11%)
  other arithmetic  10.2 us (11%)
  between operations  1.16 us (1%)
    ppermute x15, starting transfers between devices, exchange(): lax.ppermute(pieces[k], axis_name, [(i, (i + k) % n) for i in range(n)])  24.2 us
    all_to_all x5, starting transfers between devices, swap(): return lax.all_to_all(pieces, axis_name, 0, 0, tiled=True)  17.8 us
    all_to_all x5, waiting for transfers between devices, swap(): return lax.all_to_all(pieces, axis_name, 0, 0, tiled=True)  12.2 us
    ppermute x15, waiting for transfers between devices, exchange(): lax.ppermute(pieces[k], axis_name, [(i, (i + k) % n) for i in range(n)])  6.66 us
    convert_element_type x2, other arithmetic, on_device(): added_out = [sum((act_arrived[k].astype(F32) * coefficient(origin_of[k],...  3.54 us
    unnamed x57, local copies, waits for them, and re-layouts  3.35 us
    dot_general x1, matrix products, on_device(): spread = jnp.dot(first_blocks[0].T, first_grad, preferred_element_type=F32)  3.19 us
    dynamic_update_slice x5, other arithmetic, place_chunks(): out = lax.dynamic_update_slice_in_dim(out, chunk, start, axis=1)  3.1 us
  transfers between devices with their start and end apart: 20, of which 7 were waited for; matrix products, arithmetic and copies ran while one was open for 24% of the time, Pallas kernels for 0%

profile of v5, /device:TPU:0, one launch (start us, length us, event | category | flops | bytes accessed | tf_op | source)
XLA Modules:
  0.0 93.5 jit_solution(12627040718159158922)
XLA Ops:
  0.6 0.0 copy-start
  0.7 0.7 copy-done.24
  1.4 1.8 %fusion.8 = bf16[512,512]{0,1:T(8,128)(2,1)S(1)} fusion(bf16[1,512,512]{2,1,0:T(8,128)(2,1)} %param.11, bf16[512,512]{1,0:T(8,128)(2,1)} %param.8, f32[512]{0:T(512)S(1)} %copy-done.24), kind=kOutput, calls=%fused_computation.25 | convolution fusion | flops 270532608 | bytes 1574912 | tf_op jit(solution)/shard_map/dot_general | solution.py:59
  3.2 0.1 constant_dynamic-slice_fusion.35
  3.3 3.1 %collective-permute-start = (bf16[512,128]{1,0:T(8,128)(2,1)S(1)}, bf16[512,128]{1,0:T(8,128)(2,1)S(1)}, u32[]{:S(2)}, u32[]{:S(2)}) collective-permute-start(bf16[512,128]{1,0:T(8,128)(2,1)S(1)} %get-tuple-element.43), channel_id=1, source_target_pairs={{0,1},{1,2},{2,3},{3,0},{4,5},{5,6},{6,7},{7,4},{8,9},{9,10},{10,1... | collective-permute-start | bytes 393224 | tf_op jit(solution)/shard_map/ppermute | solution.py:14
  6.4 2.6 %collective-permute-start.1 = (bf16[512,128]{1,0:T(8,128)(2,1)S(1)}, bf16[512,128]{1,0:T(8,128)(2,1)S(1)}, u32[]{:S(2)}, u32[]{:S(2)}) collective-permute-start(bf16[512,128]{1,0:T(8,128)(2,1)S(1)} %get-tuple-element.45), channel_id=1, source_target_pairs={{0,2},{1,3},{2,0},{3,1},{4,6},{5,7},{6,4},{7,5},{8,10},{9,11},{10,... | collective-permute-start | bytes 393224 | tf_op jit(solution)/shard_map/ppermute | solution.py:14
  9.0 1.3 %collective-permute-start.2 = (bf16[512,128]{1,0:T(8,128)(2,1)S(1)}, bf16[512,128]{1,0:T(8,128)(2,1)S(1)}, u32[]{:S(2)}, u32[]{:S(2)}) collective-permute-start(bf16[512,128]{1,0:T(8,128)(2,1)S(1)} %get-tuple-element.44), channel_id=1, source_target_pairs={{0,3},{1,0},{2,1},{3,2},{4,7},{5,4},{6,5},{7,6},{8,11},{9,8},{10,9... | collective-permute-start | bytes 393224 | tf_op jit(solution)/shard_map/ppermute | solution.py:14
  10.3 1.0 %copy.25 = bf16[512,512]{1,0:T(8,128)(2,1)} copy(bf16[512,512]{0,1:T(8,128)(2,1)S(1)} %fusion.8) | data formatting | bytes 1048576 | tf_op jit(solution)/shard_map/optimization_barrier | solution.py:62
  11.3 3.7 %all-to-all-start = ((bf16[8,64,512]{2,1,0:T(8,128)(2,1)}), bf16[8,64,512]{2,1,0:T(8,128)(2,1)S(1)}, u32[]{:S(2)}, u32[]{:S(2)}) async-start(bf16[8,64,512]{2,1,0:T(8,128)(2,1)} %bitcast.2), calls=%async_computation | async-start | bytes 1048576 | tf_op jit(solution)/shard_map/all_to_all | solution.py:19
  15.0 0.7 fusion.78
  15.7 0.7 copy-done.9
  16.5 0.1 copy.30
  16.7 0.7 fusion.106
  17.3 0.3 collective-permute-done.1
  17.6 0.9 fusion.56
  18.5 3.3 %collective-permute-start.3 = (bf16[512,128]{1,0:T(8,128)(2,1)}, bf16[512,128]{1,0:T(8,128)(2,1)}, u32[]{:S(2)}, u32[]{:S(2)}) collective-permute-start(bf16[512,128]{1,0:T(8,128)(2,1)} %get-tuple-element.34), channel_id=1, source_target_pairs={{0,1},{1,2},{2,3},{3,0},{4,5},{5,6},{6,7},{7,4},{8,9},{9,10},{10,1... | collective-permute-start | bytes 393224 | tf_op jit(solution)/shard_map/ppermute | solution.py:14
  21.8 1.6 %collective-permute-start.4 = (bf16[512,128]{1,0:T(8,128)(2,1)S(1)}, bf16[512,128]{1,0:T(8,128)(2,1)}, u32[]{:S(2)}, u32[]{:S(2)}) collective-permute-start(bf16[512,128]{1,0:T(8,128)(2,1)S(1)} %get-tuple-element.35), channel_id=1, source_target_pairs={{0,2},{1,3},{2,0},{3,1},{4,6},{5,7},{6,4},{7,5},{8,10},{9,11},{10,... | collective-permute-start | bytes 393224 | tf_op jit(solution)/shard_map/ppermute | solution.py:14
  23.4 0.7 collective-permute-start.5
  24.2 0.6 all-to-all-done
  24.8 0.4 fusion.6
  25.2 0.9 %copy.28 = bf16[8,64,512]{2,1,0:T(8,128)(2,1)} copy(bf16[8,64,512]{2,0,1:T(8,128)(2,1)S(1)} %fusion.6) | data formatting | bytes 1048576 | tf_op jit(solution)/shard_map/convert_element_type | solution.py:77
  26.2 3.5 %all-to-all-start.1 = ((bf16[8,64,512]{2,1,0:T(8,128)(2,1)}), bf16[8,64,512]{2,1,0:T(8,128)(2,1)S(1)}, u32[]{:S(2)}, u32[]{:S(2)}) async-start(bf16[8,64,512]{2,1,0:T(8,128)(2,1)} %copy.28), calls=%async_computation.1 | async-start | bytes 1048576 | tf_op jit(solution)/shard_map/all_to_all | solution.py:19
  29.7 0.1 fusion.77
  29.9 1.0 %constant_dynamic-update-slice_fusion.2 = bf16[512,512]{1,0:T(8,128)(2,1)S(1)} fusion(bf16[512,512]{1,0:T(8,128)(2,1)S(1)} %fusion.77, bf16[512,128]{1,0:T(8,128)(2,1)} %collective-permute-done.3, s32[]{:T(128)S(6)} %select_n.80), kind=kLoop, calls=%fused_computation.166 | loop fusion | bytes 262148 | tf_op jit(solution)/shard_map/dynamic_update_slice | solution.py:33
  30.9 1.1 %collective-permute-done.4 = bf16[512,128]{1,0:T(8,128)(2,1)} collective-permute-done((bf16[512,128]{1,0:T(8,128)(2,1)S(1)}, bf16[512,128]{1,0:T(8,128)(2,1)}, u32[]{:S(2)}, u32[]{:S(2)}) %collective-permute-start.4) | collective-permute-done | bytes 131104 | tf_op jit(solution)/shard_map/ppermute | solution.py:14
  32.0 0.9 %constant_dynamic-update-slice_fusion.1 = bf16[512,512]{1,0:T(8,128)(2,1)S(1)} fusion(bf16[512,512]{1,0:T(8,128)(2,1)S(1)} %constant_dynamic-update-slice_fusion.2, bf16[512,128]{1,0:T(8,128)(2,1)} %collective-permute-done.4, s32[]{:T(128)S(6)} %select_n.82), kind=kLoop, calls=%fused_computation.161 | loop fusion | bytes 262148 | tf_op jit(solution)/shard_map/dynamic_update_slice | solution.py:33
  33.0 0.9 %constant_dynamic-update-slice_fusion = bf16[512,512]{1,0:T(8,128)(2,1)S(1)} fusion(bf16[512,512]{1,0:T(8,128)(2,1)S(1)} %constant_dynamic-update-slice_fusion.1, bf16[512,128]{1,0:T(8,128)(2,1)} %collective-permute-done.5, s32[]{:T(128)S(6)} %select_n.84), kind=kLoop, calls=%fused_computation.156 | loop fusion | bytes 262148 | tf_op jit(solution)/shard_map/dynamic_update_slice | solution.py:33
  33.9 5.4 %all-to-all-done.1 = bf16[8,64,512]{2,1,0:T(8,128)(2,1)S(1)} async-done(((bf16[8,64,512]{2,1,0:T(8,128)(2,1)}), bf16[8,64,512]{2,1,0:T(8,128)(2,1)S(1)}, u32[]{:S(2)}, u32[]{:S(2)}) %all-to-all-start.1) | async-done | bytes 524320 | tf_op jit(solution)/shard_map/all_to_all | solution.py:19
  39.4 0.4 fusion.33
  39.8 1.1 %multiply_convert_fusion = (bf16[512,512]{1,0:T(8,128)(2,1)S(1)}, bf16[512,512]{1,0:T(8,128)(2,1)S(1)}) fusion(bf16[512,512]{1,0:T(8,128)(2,1)S(1)} %constant_dynamic-update-slice_fusion, bf16[512,512]{1,0:T(8,128)(2,1)S(1)} %fusion.33, bf16[1,512,512]{2,1,0:T(8,128)(2,1)S(1)} %copy-done), kind=kOutput, calls=%fused_computation.52 | convolution fusion | flops 274464768 | bytes 2621440 | tf_op jit(solution)/shard_map/dot_general | solution.py:81
  40.9 1.6 %fusion.24 = (bf16[512,512]{1,0:T(8,128)(2,1)}, bf16[512,512]{1,0:T(8,128)(2,1)}) fusion(bf16[512,512]{1,0:T(8,128)(2,1)S(1)} %copy-done.4, f32[512]{0:T(512)S(1)} %copy-done.10, bf16[512,512]{1,0:T(8,128)(2,1)S(1)} %get-tuple-element.29, bf16[1,512,512]{2,1,0:T(8,128)(2,1)S(1)} %copy-done, bf16[512,512]{1,0:T(8,128)(2,1)S(1)} %copy-done.1), kind=kOutput, calls=%fused_computation.41 | convolution fusion | flops 271319040 | bytes 3147776 | tf_op jit(solution)/shard_map/dot_general | solution.py:95
  42.5 3.5 %all-to-all-start.2 = ((bf16[8,64,512]{2,1,0:T(8,128)(2,1)}), bf16[8,64,512]{2,1,0:T(8,128)(2,1)S(1)}, u32[]{:S(2)}, u32[]{:S(2)}) async-start(bf16[8,64,512]{2,1,0:T(8,128)(2,1)} %bitcast.22), calls=%async_computation.2 | async-start | bytes 1048576 | tf_op jit(solution)/shard_map/all_to_all | solution.py:19
  46.0 0.1 constant_dynamic-slice_fusion.13
  46.1 0.5 collective-permute-start.10
  46.6 2.9 %collective-permute-start.11 = (bf16[512,128]{1,0:T(8,128)(2,1)S(1)}, bf16[512,128]{1,0:T(8,128)(2,1)S(1)}, u32[]{:S(2)}, u32[]{:S(2)}) collective-permute-start(bf16[512,128]{1,0:T(8,128)(2,1)S(1)} %get-tuple-element.36), channel_id=1, source_target_pairs={{0,3},{1,0},{2,1},{3,2},{4,7},{5,4},{6,5},{7,6},{8,11},{9,8},{10,9... | collective-permute-start | bytes 393224 | tf_op jit(solution)/shard_map/ppermute | solution.py:14
  49.5 1.3 %fusion.113 = bf16[512,512]{1,0:T(8,128)(2,1)} fusion(bf16[512,512]{1,0:T(8,128)(2,1)S(1)} %fusion.33, bf16[512,512]{1,0:T(8,128)(2,1)S(1)} %copy-done.27), kind=kOutput, calls=%fused_computation.212 | convolution fusion | flops 268435456 | bytes 1572864 | tf_op jit(solution)/shard_map/dot_general | solution.py:97
  50.8 4.9 %all-to-all-done.2 = bf16[8,64,512]{2,1,0:T(8,128)(2,1)S(1)} async-done(((bf16[8,64,512]{2,1,0:T(8,128)(2,1)}), bf16[8,64,512]{2,1,0:T(8,128)(2,1)S(1)}, u32[]{:S(2)}, u32[]{:S(2)}) %all-to-all-start.2) | async-done | bytes 524320 | tf_op jit(solution)/shard_map/all_to_all | solution.py:19
  55.7 0.4 fusion.7
  56.1 0.9 %copy.31 = bf16[8,64,512]{2,1,0:T(8,128)(2,1)} copy(bf16[8,64,512]{2,0,1:T(8,128)(2,1)S(1)} %fusion.7) | data formatting | bytes 1048576 | tf_op jit(solution)/shard_map/convert_element_type | solution.py:104
  57.1 3.5 %all-to-all-start.3 = ((bf16[8,64,512]{2,1,0:T(8,128)(2,1)}), bf16[8,64,512]{2,1,0:T(8,128)(2,1)S(1)}, u32[]{:S(2)}, u32[]{:S(2)}) async-start(bf16[8,64,512]{2,1,0:T(8,128)(2,1)} %copy.31), calls=%async_computation.3 | async-start | bytes 1048576 | tf_op jit(solution)/shard_map/all_to_all | solution.py:19
  60.7 0.6 copy-done.11
  61.3 0.0 copy-done.12
  61.3 1.9 %fusion.72 = (bf16[512,128]{1,0:T(8,128)(2,1)}, bf16[512,128]{1,0:T(8,128)(2,1)}, bf16[512,128]{1,0:T(8,128)(2,1)}) fusion(bf16[512,128]{1,0:T(8,128)(2,1)} %collective-permute-done.9, bf16[512,128]{1,0:T(8,128)(2,1)S(1)} %collective-permute-done.10, bf16[512,128]{1,0:T(8,128)(2,1)S(1)} %collective-permute-done.11, f32[128]{0:T(128)S(1)} %get-tuple-element.47, ...), kind=kLoop, calls=%fused_computation.123 | loop fusion | flops 1835008 | bytes 923652 | tf_op jit(solution)/shard_map/convert_element_type | solution.py:89
  63.2 1.2 %collective-permute-start.12 = (bf16[512,128]{1,0:T(8,128)(2,1)}, bf16[512,128]{1,0:T(8,128)(2,1)}, u32[]{:S(2)}, u32[]{:S(2)}) collective-permute-start(bf16[512,128]{1,0:T(8,128)(2,1)} %get-tuple-element.31), channel_id=1, source_target_pairs={{0,1},{1,2},{2,3},{3,0},{4,5},{5,6},{6,7},{7,4},{8,9},{9,10},{10,1... | collective-permute-start | bytes 393224 | tf_op jit(solution)/shard_map/ppermute | solution.py:14
  64.4 1.1 %collective-permute-start.13 = (bf16[512,128]{1,0:T(8,128)(2,1)}, bf16[512,128]{1,0:T(8,128)(2,1)}, u32[]{:S(2)}, u32[]{:S(2)}) collective-permute-start(bf16[512,128]{1,0:T(8,128)(2,1)} %get-tuple-element.32), channel_id=1, source_target_pairs={{0,2},{1,3},{2,0},{3,1},{4,6},{5,7},{6,4},{7,5},{8,10},{9,11},{10,... | collective-permute-start | bytes 393224 | tf_op jit(solution)/shard_map/ppermute | solution.py:14
  65.5 1.8 %collective-permute-start.14 = (bf16[512,128]{1,0:T(8,128)(2,1)}, bf16[512,128]{1,0:T(8,128)(2,1)}, u32[]{:S(2)}, u32[]{:S(2)}) collective-permute-start(bf16[512,128]{1,0:T(8,128)(2,1)} %get-tuple-element.30), channel_id=1, source_target_pairs={{0,3},{1,0},{2,1},{3,2},{4,7},{5,4},{6,5},{7,6},{8,11},{9,8},{10,9... | collective-permute-start | bytes 393224 | tf_op jit(solution)/shard_map/ppermute | solution.py:14
  67.3 1.7 %fusion.60 = bf16[512,128]{1,0:T(8,128)(2,1)} fusion(bf16[512,128]{1,0:T(8,128)(2,1)} %collective-permute-done.9, bf16[512,128]{1,0:T(8,128)(2,1)S(1)} %collective-permute-done.10, bf16[512,128]{1,0:T(8,128)(2,1)S(1)} %collective-permute-done.11, f32[128]{0:T(128)S(1)} %copy-done.21, f32[128]{0:T(128)S(1)} %copy-done.22, f32[128]{0:T(128)S(1)} %copy-done.23, ...), kind=kLoop, calls=%fused_computation.111 | loop fusion | flops 786432 | bytes 657412 | tf_op jit(solution)/shard_map/convert_element_type | solution.py:89
  69.0 1.3 %all-to-all-done.3 = bf16[8,64,512]{2,1,0:T(8,128)(2,1)S(1)} async-done(((bf16[8,64,512]{2,1,0:T(8,128)(2,1)}), bf16[8,64,512]{2,1,0:T(8,128)(2,1)S(1)}, u32[]{:S(2)}, u32[]{:S(2)}) %all-to-all-start.3) | async-done | bytes 524320 | tf_op jit(solution)/shard_map/all_to_all | solution.py:19
  70.3 0.6 fusion.110
  70.9 0.2 copy-done.6
  71.1 0.8 dynamic-slice_convert_fusion
  71.8 1.0 %collective-permute-start.6 = (bf16[128,512]{1,0:T(8,128)(2,1)}, bf16[128,512]{1,0:T(8,128)(2,1)S(1)}, u32[]{:S(2)}, u32[]{:S(2)}) collective-permute-start(bf16[128,512]{1,0:T(8,128)(2,1)} %get-tuple-element.41), channel_id=1, source_target_pairs={{0,1},{1,2},{2,3},{3,0},{4,5},{5,6},{6,7},{7,4},{8,9},{9,10},{10,1... | collective-permute-start | bytes 393224 | tf_op jit(solution)/shard_map/ppermute | solution.py:14
  72.8 1.3 %collective-permute-start.7 = (bf16[128,512]{1,0:T(8,128)(2,1)}, bf16[128,512]{1,0:T(8,128)(2,1)S(1)}, u32[]{:S(2)}, u32[]{:S(2)}) collective-permute-start(bf16[128,512]{1,0:T(8,128)(2,1)} %get-tuple-element.40), channel_id=1, source_target_pairs={{0,2},{1,3},{2,0},{3,1},{4,6},{5,7},{6,4},{7,5},{8,10},{9,11},{10,... | collective-permute-start | bytes 393224 | tf_op jit(solution)/shard_map/ppermute | solution.py:14
  74.1 3.6 %all-to-all-start.4 = ((bf16[8,64,512]{2,1,0:T(8,128)(2,1)}), bf16[8,64,512]{2,1,0:T(8,128)(2,1)S(1)}, u32[]{:S(2)}, u32[]{:S(2)}) async-start(bf16[8,64,512]{2,1,0:T(8,128)(2,1)} %bitcast.42), calls=%async_computation.4 | async-start | bytes 1048576 | tf_op jit(solution)/shard_map/all_to_all | solution.py:19
  77.7 1.8 %collective-permute-start.8 = (bf16[128,512]{1,0:T(8,128)(2,1)}, bf16[128,512]{1,0:T(8,128)(2,1)S(1)}, u32[]{:S(2)}, u32[]{:S(2)}) collective-permute-start(bf16[128,512]{1,0:T(8,128)(2,1)} %get-tuple-element.39), channel_id=1, source_target_pairs={{0,3},{1,0},{2,1},{3,2},{4,7},{5,4},{6,5},{7,6},{8,11},{9,8},{10,9... | collective-permute-start | bytes 393224 | tf_op jit(solution)/shard_map/ppermute | solution.py:14
  79.5 3.2 %fusion.3 = bf16[512,512]{1,0:T(8,128)(2,1)} fusion(bf16[512,512]{1,0:T(8,128)(2,1)S(1)} %bitcast.112, bf16[512,512]{1,0:T(8,128)(2,1)} %get-tuple-element.78, bf16[512,512]{1,0:T(8,128)(2,1)S(1)} %copy-done.5, bf16[512,512]{1,0:T(8,128)(2,1)S(1)} %bitcast.110, bf16[1,512,512]{2,1,0:T(8,128)(2,1)} %param.11, f32[512]{0:T(512)S(1)} %copy-done.10, ...), kind=kOutput, calls=%fused_computation.20 | convolution fusion | flops 274726912 | bytes 3149824 | tf_op jit(solution)/shard_map/dot_general | solution.py:126
  82.7 5.2 %collective-permute-done.7 = bf16[128,512]{1,0:T(8,128)(2,1)S(1)} collective-permute-done((bf16[128,512]{1,0:T(8,128)(2,1)}, bf16[128,512]{1,0:T(8,128)(2,1)S(1)}, u32[]{:S(2)}, u32[]{:S(2)}) %collective-permute-start.7) | collective-permute-done | bytes 131104 | tf_op jit(solution)/shard_map/ppermute | solution.py:14
  88.0 0.9 copy-done.8
  88.9 0.1 fusion.73
  89.0 1.0 %fusion.74 = bf16[512,512]{1,0:T(8,128)(2,1)S(1)} fusion(bf16[512,512]{1,0:T(8,128)(2,1)S(1)} %fusion.73, s32[]{:T(128)S(6)} %select_n.80, bf16[512,128]{1,0:T(8,128)(2,1)} %collective-permute-done.12, bf16[512,512]{1,0:T(8,128)(2,1)S(1)} %fusion.33), kind=kLoop, calls=%fused_computation.134 | loop fusion | flops 262144 | bytes 393220 | tf_op jit(solution)/shard_map/dynamic_update_slice | solution.py:33
  89.9 1.0 %fusion.75 = bf16[512,512]{1,0:T(8,128)(2,1)S(1)} fusion(bf16[512,512]{1,0:T(8,128)(2,1)S(1)} %fusion.74, s32[]{:T(128)S(6)} %select_n.82, bf16[512,128]{1,0:T(8,128)(2,1)} %collective-permute-done.13, bf16[512,512]{1,0:T(8,128)(2,1)S(1)} %fusion.33), kind=kLoop, calls=%fused_computation.135 | loop fusion | flops 262144 | bytes 393220 | tf_op jit(solution)/shard_map/dynamic_update_slice | solution.py:33
  90.9 1.0 %fusion.76 = bf16[512,512]{1,0:T(8,128)(2,1)S(1)} fusion(bf16[512,512]{1,0:T(8,128)(2,1)S(1)} %fusion.75, s32[]{:T(128)S(6)} %select_n.84, bf16[512,128]{1,0:T(8,128)(2,1)} %collective-permute-done.14, bf16[512,512]{1,0:T(8,128)(2,1)S(1)} %fusion.33), kind=kLoop, calls=%fused_computation.136 | loop fusion | flops 262144 | bytes 393220 | tf_op jit(solution)/shard_map/dynamic_update_slice | solution.py:33
  91.9 0.8 add_bitcast_fusion
  92.7 0.7 convert_reduce_fusion
  (65 shorter events, 0.2 us)
Async XLA Ops:
  0.6 39.1 %copy-start = (bf16[1,512,512]{2,1,0:T(8,128)(2,1)S(1)}, bf16[1,512,512]{2,1,0:T(8,128)(2,1)}, u32[]{:S(2)}) copy-start(bf16[1,512,512]{2,1,0:T(8,128)(2,1)} %param.13) | copy-start | bytes 1572868
  0.7 0.7 copy-start.24
  1.4 1.8 %copy-start.1 = (bf16[512,512]{1,0:T(8,128)(2,1)S(1)}, bf16[512,512]{1,0:T(8,128)(2,1)}, u32[]{:S(2)}) copy-start(bf16[512,512]{1,0:T(8,128)(2,1)} %param.15) | copy-start | bytes 1572868
  3.3 14.0 %collective-permute-start = (bf16[512,128]{1,0:T(8,128)(2,1)S(1)}, bf16[512,128]{1,0:T(8,128)(2,1)S(1)}, u32[]{:S(2)}, u32[]{:S(2)}) collective-permute-start(bf16[512,128]{1,0:T(8,128)(2,1)S(1)} %get-tuple-element.43), channel_id=1, source_target_pairs={{0,1},{1,2},{2,3},{3,0},{4,5},{5,6},{6,7},{7,4},{8,9},{9,10},{10,1... | collective-permute-start | bytes 393224 | tf_op jit(solution)/shard_map/ppermute | solution.py:14
  6.4 11.2 %collective-permute-start.1 = (bf16[512,128]{1,0:T(8,128)(2,1)S(1)}, bf16[512,128]{1,0:T(8,128)(2,1)S(1)}, u32[]{:S(2)}, u32[]{:S(2)}) collective-permute-start(bf16[512,128]{1,0:T(8,128)(2,1)S(1)} %get-tuple-element.45), channel_id=1, source_target_pairs={{0,2},{1,3},{2,0},{3,1},{4,6},{5,7},{6,4},{7,5},{8,10},{9,11},{10,... | collective-permute-start | bytes 393224 | tf_op jit(solution)/shard_map/ppermute | solution.py:14
  9.0 8.6 %collective-permute-start.2 = (bf16[512,128]{1,0:T(8,128)(2,1)S(1)}, bf16[512,128]{1,0:T(8,128)(2,1)S(1)}, u32[]{:S(2)}, u32[]{:S(2)}) collective-permute-start(bf16[512,128]{1,0:T(8,128)(2,1)S(1)} %get-tuple-element.44), channel_id=1, source_target_pairs={{0,3},{1,0},{2,1},{3,2},{4,7},{5,4},{6,5},{7,6},{8,11},{9,8},{10,9... | collective-permute-start | bytes 393224 | tf_op jit(solution)/shard_map/ppermute | solution.py:14
  11.3 13.5 %all-to-all-start = ((bf16[8,64,512]{2,1,0:T(8,128)(2,1)}), bf16[8,64,512]{2,1,0:T(8,128)(2,1)S(1)}, u32[]{:S(2)}, u32[]{:S(2)}) async-start(bf16[8,64,512]{2,1,0:T(8,128)(2,1)} %bitcast.2), calls=%async_computation | async-start | bytes 1048576 | tf_op jit(solution)/shard_map/all_to_all | solution.py:19
  15.7 0.7 copy-start.9
  18.5 11.4 %collective-permute-start.3 = (bf16[512,128]{1,0:T(8,128)(2,1)}, bf16[512,128]{1,0:T(8,128)(2,1)}, u32[]{:S(2)}, u32[]{:S(2)}) collective-permute-start(bf16[512,128]{1,0:T(8,128)(2,1)} %get-tuple-element.34), channel_id=1, source_target_pairs={{0,1},{1,2},{2,3},{3,0},{4,5},{5,6},{6,7},{7,4},{8,9},{9,10},{10,1... | collective-permute-start | bytes 393224 | tf_op jit(solution)/shard_map/ppermute | solution.py:14
  21.8 10.2 %collective-permute-start.4 = (bf16[512,128]{1,0:T(8,128)(2,1)S(1)}, bf16[512,128]{1,0:T(8,128)(2,1)}, u32[]{:S(2)}, u32[]{:S(2)}) collective-permute-start(bf16[512,128]{1,0:T(8,128)(2,1)S(1)} %get-tuple-element.35), channel_id=1, source_target_pairs={{0,2},{1,3},{2,0},{3,1},{4,6},{5,7},{6,4},{7,5},{8,10},{9,11},{10,... | collective-permute-start | bytes 393224 | tf_op jit(solution)/shard_map/ppermute | solution.py:14
  23.4 9.5 %collective-permute-start.5 = (bf16[512,128]{1,0:T(8,128)(2,1)S(1)}, bf16[512,128]{1,0:T(8,128)(2,1)}, u32[]{:S(2)}, u32[]{:S(2)}) collective-permute-start(bf16[512,128]{1,0:T(8,128)(2,1)S(1)} %get-tuple-element.33), channel_id=1, source_target_pairs={{0,3},{1,0},{2,1},{3,2},{4,7},{5,4},{6,5},{7,6},{8,11},{9,8},{10,9... | collective-permute-start | bytes 393224 | tf_op jit(solution)/shard_map/ppermute | solution.py:14
  26.2 13.2 %all-to-all-start.1 = ((bf16[8,64,512]{2,1,0:T(8,128)(2,1)}), bf16[8,64,512]{2,1,0:T(8,128)(2,1)S(1)}, u32[]{:S(2)}, u32[]{:S(2)}) async-start(bf16[8,64,512]{2,1,0:T(8,128)(2,1)} %copy.28), calls=%async_computation.1 | async-start | bytes 1048576 | tf_op jit(solution)/shard_map/all_to_all | solution.py:19
  29.9 9.5 %copy-start.3 = (bf16[512,512]{1,0:T(8,128)(2,1)S(1)}, bf16[512,512]{1,0:T(8,128)(2,1)}, u32[]{:S(2)}) copy-start(bf16[512,512]{1,0:T(8,128)(2,1)} %param.8) | copy-start | bytes 1572868
  32.9 6.4 %copy-start.10 = (f32[512]{0:T(512)S(1)}, f32[512]{0:T(512)}, u32[]{:S(2)}) copy-start(f32[512]{0:T(512)} %param.10) | copy-start | bytes 6148
  39.8 1.2 %copy-start.4 = (bf16[512,512]{1,0:T(8,128)(2,1)S(1)}, bf16[512,512]{1,0:T(8,128)(2,1)}, u32[]{:S(2)}) copy-start(bf16[512,512]{1,0:T(8,128)(2,1)} %param.8) | copy-start | bytes 1572868
  40.9 1.6 %copy-start.26 = (bf16[512,512]{1,0:T(8,128)(2,1)}, bf16[512,512]{1,0:T(8,128)(2,1)S(1)}, u32[]{:S(2)}) copy-start(bf16[512,512]{1,0:T(8,128)(2,1)S(1)} %get-tuple-element.29) | copy-start | bytes 1572868
  42.5 13.2 %all-to-all-start.2 = ((bf16[8,64,512]{2,1,0:T(8,128)(2,1)}), bf16[8,64,512]{2,1,0:T(8,128)(2,1)S(1)}, u32[]{:S(2)}, u32[]{:S(2)}) async-start(bf16[8,64,512]{2,1,0:T(8,128)(2,1)} %bitcast.22), calls=%async_computation.2 | async-start | bytes 1048576 | tf_op jit(solution)/shard_map/all_to_all | solution.py:19
  46.0 3.5 %copy-start.27 = (bf16[512,512]{1,0:T(8,128)(2,1)S(1)}, bf16[512,512]{1,0:T(8,128)(2,1)}, u32[]{:S(2)}) copy-start(bf16[512,512]{1,0:T(8,128)(2,1)} %copy-done.26) | copy-start | bytes 1572868
  46.1 14.5 %collective-permute-start.10 = (bf16[512,128]{1,0:T(8,128)(2,1)S(1)}, bf16[512,128]{1,0:T(8,128)(2,1)S(1)}, u32[]{:S(2)}, u32[]{:S(2)}) collective-permute-start(bf16[512,128]{1,0:T(8,128)(2,1)S(1)} %get-tuple-element.37), channel_id=1, source_target_pairs={{0,2},{1,3},{2,0},{3,1},{4,6},{5,7},{6,4},{7,5},{8,10},{9,11},{10,... | collective-permute-start | bytes 393224 | tf_op jit(solution)/shard_map/ppermute | solution.py:14
  46.6 14.0 %collective-permute-start.11 = (bf16[512,128]{1,0:T(8,128)(2,1)S(1)}, bf16[512,128]{1,0:T(8,128)(2,1)S(1)}, u32[]{:S(2)}, u32[]{:S(2)}) collective-permute-start(bf16[512,128]{1,0:T(8,128)(2,1)S(1)} %get-tuple-element.36), channel_id=1, source_target_pairs={{0,3},{1,0},{2,1},{3,2},{4,7},{5,4},{6,5},{7,6},{8,11},{9,8},{10,9... | collective-permute-start | bytes 393224 | tf_op jit(solution)/shard_map/ppermute | solution.py:14
  49.5 11.1 %collective-permute-start.9 = (bf16[512,128]{1,0:T(8,128)(2,1)S(1)}, bf16[512,128]{1,0:T(8,128)(2,1)}, u32[]{:S(2)}, u32[]{:S(2)}) collective-permute-start(bf16[512,128]{1,0:T(8,128)(2,1)S(1)} %get-tuple-element.38), channel_id=1, source_target_pairs={{0,1},{1,2},{2,3},{3,0},{4,5},{5,6},{6,7},{7,4},{8,9},{9,10},{10,1... | collective-permute-start | bytes 393224 | tf_op jit(solution)/shard_map/ppermute | solution.py:14
  57.0 3.6 %copy-start.14 = (f32[128]{0:T(128)S(1)}, f32[128]{0:T(128)}, u32[]{:S(2)}) copy-start(f32[128]{0:T(128)} %get-tuple-element.51) | copy-start | bytes 1540
  57.0 3.6 %copy-start.15 = (f32[128]{0:T(128)S(1)}, f32[128]{0:T(128)}, u32[]{:S(2)}) copy-start(f32[128]{0:T(128)} %get-tuple-element.52) | copy-start | bytes 1540
  57.0 3.6 %copy-start.16 = (f32[128]{0:T(128)S(1)}, f32[128]{0:T(128)}, u32[]{:S(2)}) copy-start(f32[128]{0:T(128)} %get-tuple-element.53) | copy-start | bytes 1540
  57.0 3.6 %copy-start.17 = (f32[128]{0:T(128)S(1)}, f32[128]{0:T(128)}, u32[]{:S(2)}) copy-start(f32[128]{0:T(128)} %get-tuple-element.54) | copy-start | bytes 1540
  57.1 3.6 %copy-start.18 = (f32[128]{0:T(128)S(1)}, f32[128]{0:T(128)}, u32[]{:S(2)}) copy-start(f32[128]{0:T(128)} %get-tuple-element.55) | copy-start | bytes 1540
  57.1 3.6 %copy-start.19 = (f32[128]{0:T(128)S(1)}, f32[128]{0:T(128)}, u32[]{:S(2)}) copy-start(f32[128]{0:T(128)} %get-tuple-element.56) | copy-start | bytes 1540
  57.1 3.6 %copy-start.20 = (f32[128]{0:T(128)S(1)}, f32[128]{0:T(128)}, u32[]{:S(2)}) copy-start(f32[128]{0:T(128)} %get-tuple-element.57) | copy-start | bytes 1540
  57.1 13.2 %all-to-all-start.3 = ((bf16[8,64,512]{2,1,0:T(8,128)(2,1)}), bf16[8,64,512]{2,1,0:T(8,128)(2,1)S(1)}, u32[]{:S(2)}, u32[]{:S(2)}) async-start(bf16[8,64,512]{2,1,0:T(8,128)(2,1)} %copy.31), calls=%async_computation.3 | async-start | bytes 1048576 | tf_op jit(solution)/shard_map/all_to_all | solution.py:19
  60.6 0.7 copy-start.11
  60.6 0.7 copy-start.12
  60.7 0.7 copy-start.13
  61.3 6.0 %copy-start.21 = (f32[128]{0:T(128)S(1)}, f32[128]{0:T(128)}, u32[]{:S(2)}) copy-start(f32[128]{0:T(128)} %get-tuple-element.58) | copy-start | bytes 1540
  61.3 6.0 %copy-start.22 = (f32[128]{0:T(128)S(1)}, f32[128]{0:T(128)}, u32[]{:S(2)}) copy-start(f32[128]{0:T(128)} %get-tuple-element.59) | copy-start | bytes 1540
  61.3 6.0 %copy-start.23 = (f32[128]{0:T(128)S(1)}, f32[128]{0:T(128)}, u32[]{:S(2)}) copy-start(f32[128]{0:T(128)} %get-tuple-element.60) | copy-start | bytes 1540
  63.2 7.1 %copy-start.5 = (bf16[512,512]{1,0:T(8,128)(2,1)S(1)}, bf16[512,512]{1,0:T(8,128)(2,1)}, u32[]{:S(2)}) copy-start(bf16[512,512]{1,0:T(8,128)(2,1)} %param.8) | copy-start | bytes 1572868
  63.2 14.5 %collective-permute-start.12 = (bf16[512,128]{1,0:T(8,128)(2,1)}, bf16[512,128]{1,0:T(8,128)(2,1)}, u32[]{:S(2)}, u32[]{:S(2)}) collective-permute-start(bf16[512,128]{1,0:T(8,128)(2,1)} %get-tuple-element.31), channel_id=1, source_target_pairs={{0,1},{1,2},{2,3},{3,0},{4,5},{5,6},{6,7},{7,4},{8,9},{9,10},{10,1... | collective-permute-start | bytes 393224 | tf_op jit(solution)/shard_map/ppermute | solution.py:14
  64.4 18.3 %collective-permute-start.13 = (bf16[512,128]{1,0:T(8,128)(2,1)}, bf16[512,128]{1,0:T(8,128)(2,1)}, u32[]{:S(2)}, u32[]{:S(2)}) collective-permute-start(bf16[512,128]{1,0:T(8,128)(2,1)} %get-tuple-element.32), channel_id=1, source_target_pairs={{0,2},{1,3},{2,0},{3,1},{4,6},{5,7},{6,4},{7,5},{8,10},{9,11},{10,... | collective-permute-start | bytes 393224 | tf_op jit(solution)/shard_map/ppermute | solution.py:14
  65.5 17.3 %collective-permute-start.14 = (bf16[512,128]{1,0:T(8,128)(2,1)}, bf16[512,128]{1,0:T(8,128)(2,1)}, u32[]{:S(2)}, u32[]{:S(2)}) collective-permute-start(bf16[512,128]{1,0:T(8,128)(2,1)} %get-tuple-element.30), channel_id=1, source_target_pairs={{0,3},{1,0},{2,1},{3,2},{4,7},{5,4},{6,5},{7,6},{8,11},{9,8},{10,9... | collective-permute-start | bytes 393224 | tf_op jit(solution)/shard_map/ppermute | solution.py:14
  67.3 3.0 %copy-start.25 = (f32[512]{0:T(512)S(1)}, f32[512]{0:T(512)}, u32[]{:S(2)}) copy-start(f32[512]{0:T(512)} %param.9) | copy-start | bytes 6148
  70.3 0.8 copy-start.6
  71.8 10.9 %collective-permute-start.6 = (bf16[128,512]{1,0:T(8,128)(2,1)}, bf16[128,512]{1,0:T(8,128)(2,1)S(1)}, u32[]{:S(2)}, u32[]{:S(2)}) collective-permute-start(bf16[128,512]{1,0:T(8,128)(2,1)} %get-tuple-element.41), channel_id=1, source_target_pairs={{0,1},{1,2},{2,3},{3,0},{4,5},{5,6},{6,7},{7,4},{8,9},{9,10},{10,1... | collective-permute-start | bytes 393224 | tf_op jit(solution)/shard_map/ppermute | solution.py:14
  72.8 15.2 %collective-permute-start.7 = (bf16[128,512]{1,0:T(8,128)(2,1)}, bf16[128,512]{1,0:T(8,128)(2,1)S(1)}, u32[]{:S(2)}, u32[]{:S(2)}) collective-permute-start(bf16[128,512]{1,0:T(8,128)(2,1)} %get-tuple-element.40), channel_id=1, source_target_pairs={{0,2},{1,3},{2,0},{3,1},{4,6},{5,7},{6,4},{7,5},{8,10},{9,11},{10,... | collective-permute-start | bytes 393224 | tf_op jit(solution)/shard_map/ppermute | solution.py:14
  74.1 5.5 %copy-start.7 = (bf16[8,64,512]{2,1,0:T(8,128)(2,1)S(1)}, bf16[8,64,512]{2,1,0:T(8,128)(2,1)}, u32[]{:S(2)}) copy-start(bf16[8,64,512]{2,1,0:T(8,128)(2,1)} %copy-done.6) | copy-start | bytes 1572868
  74.1 18.6 %all-to-all-start.4 = ((bf16[8,64,512]{2,1,0:T(8,128)(2,1)}), bf16[8,64,512]{2,1,0:T(8,128)(2,1)S(1)}, u32[]{:S(2)}, u32[]{:S(2)}) async-start(bf16[8,64,512]{2,1,0:T(8,128)(2,1)} %bitcast.42), calls=%async_computation.4 | async-start | bytes 1048576 | tf_op jit(solution)/shard_map/all_to_all | solution.py:19
  77.7 10.3 %collective-permute-start.8 = (bf16[128,512]{1,0:T(8,128)(2,1)}, bf16[128,512]{1,0:T(8,128)(2,1)S(1)}, u32[]{:S(2)}, u32[]{:S(2)}) collective-permute-start(bf16[128,512]{1,0:T(8,128)(2,1)} %get-tuple-element.39), channel_id=1, source_target_pairs={{0,3},{1,0},{2,1},{3,2},{4,7},{5,4},{6,5},{7,6},{8,11},{9,8},{10,9... | collective-permute-start | bytes 393224 | tf_op jit(solution)/shard_map/ppermute | solution.py:14
  88.0 0.9 copy-start.8
  91.9 1.6 %copy-start.2 = (bf16[512,512]{1,0:T(8,128)(2,1)}, bf16[512,512]{1,0:T(8,128)(2,1)S(1)}, u32[]{:S(2)}) copy-start(bf16[512,512]{1,0:T(8,128)(2,1)S(1)} %fusion.76) | copy-start | bytes 1572868

commit v6 on v5

--- a/solution.py
+++ b/solution.py
@@ -110,7 +110,8 @@
         [lax.dynamic_slice_in_dim(block_part, t * cq, cq, 0).astype(BF16) for t in chunk_of],
         "ch",
     )
-    block_arrived, added_back = lax.optimization_barrier((block_arrived, added_back))
+    first_block, added_back = lax.optimization_barrier((block_arrived[1], added_back))
+    block_arrived[1] = first_block
     block_grad = sum(part.astype(F32) for part in block_arrived)[None]
     outputs = place_chunks(
         [

time: 94.5 us -> 93.2 us (0.986)
  waiting for transfers between devices: 18.9 us -> 17.1 us
    ppermute x15, waiting for transfers between devices: 6.66 us -> 5.63 us  [exchange(): lax.ppermute(pieces[k], axis_name, [(i, (i + k) % n) for i in range(n)])]
    unnamed x57 -> x59, local copies, waits for them, and re-layouts: 3.35 us -> 2.49 us
  transfers between devices with their start and end apart: 20 -> 20, of which waited for: 7 -> 8; matrix products, arithmetic and copies ran while one was open for 24% -> 25% of each run, Pallas kernels for 0% -> 0%
where the time goes in v6:
time: 93.2 us; the launch traced here: 92.3 us
  starting transfers between devices  42.7 us (46%)
  waiting for transfers between devices  17.1 us (18%)
  other arithmetic  11.1 us (12%)
  matrix products  10.3 us (11%)
  local copies, waits for them, and re-layouts  9.92 us (11%)
  between operations  1.17 us (1%)
    ppermute x15, starting transfers between devices, exchange(): lax.ppermute(pieces[k], axis_name, [(i, (i + k) % n) for i in range(n)])  24.9 us
    all_to_all x5, starting transfers between devices, swap(): return lax.all_to_all(pieces, axis_name, 0, 0, tiled=True)  17.8 us
    all_to_all x5, waiting for transfers between devices, swap(): return lax.all_to_all(pieces, axis_name, 0, 0, tiled=True)  11.5 us
    ppermute x15, waiting for transfers between devices, exchange(): lax.ppermute(pieces[k], axis_name, [(i, (i + k) % n) for i in range(n)])  5.63 us
    convert_element_type x2, other arithmetic, on_device(): added_out = [sum((act_arrived[k].astype(F32) * coefficient(origin_of[k],...  3.51 us
    dot_general x1, matrix products, on_device(): spread = jnp.dot(first_blocks[0].T, first_grad, preferred_element_type=F32)  3.19 us
    dynamic_update_slice x5, other arithmetic, place_chunks(): out = lax.dynamic_update_slice_in_dim(out, chunk, start, axis=1)  3.11 us
    dynamic_update_slice x3, local copies, waits for them, and re-layouts, place_chunks(): out = lax.dynamic_update_slice_in_dim(out, chunk, start, axis=1)  2.87 us
  transfers between devices with their start and end apart: 20, of which 8 were waited for; matrix products, arithmetic and copies ran while one was open for 25% of the time, Pallas kernels for 0%

profile of v6, /device:TPU:0, one launch (start us, length us, event | category | flops | bytes accessed | tf_op | source)
XLA Modules:
  0.0 92.3 jit_solution(6809442430410824934)
XLA Ops:
  0.7 0.7 copy-done.25
  1.4 1.8 %fusion.8 = bf16[512,512]{0,1:T(8,128)(2,1)S(1)} fusion(bf16[1,512,512]{2,1,0:T(8,128)(2,1)} %param.11, bf16[512,512]{1,0:T(8,128)(2,1)} %param.8, f32[512]{0:T(512)S(1)} %copy-done.25), kind=kOutput, calls=%fused_computation.25 | convolution fusion | flops 270532608 | bytes 1574912 | tf_op jit(solution)/shard_map/dot_general | solution.py:59
  3.2 0.1 constant_dynamic-slice_fusion.35
  3.3 3.1 %collective-permute-start = (bf16[512,128]{1,0:T(8,128)(2,1)S(1)}, bf16[512,128]{1,0:T(8,128)(2,1)S(1)}, u32[]{:S(2)}, u32[]{:S(2)}) collective-permute-start(bf16[512,128]{1,0:T(8,128)(2,1)S(1)} %get-tuple-element.36), channel_id=1, source_target_pairs={{0,1},{1,2},{2,3},{3,0},{4,5},{5,6},{6,7},{7,4},{8,9},{9,10},{10,1... | collective-permute-start | bytes 393224 | tf_op jit(solution)/shard_map/ppermute | solution.py:14
  6.4 2.6 %collective-permute-start.1 = (bf16[512,128]{1,0:T(8,128)(2,1)S(1)}, bf16[512,128]{1,0:T(8,128)(2,1)S(1)}, u32[]{:S(2)}, u32[]{:S(2)}) collective-permute-start(bf16[512,128]{1,0:T(8,128)(2,1)S(1)} %get-tuple-element.38), channel_id=1, source_target_pairs={{0,2},{1,3},{2,0},{3,1},{4,6},{5,7},{6,4},{7,5},{8,10},{9,11},{10,... | collective-permute-start | bytes 393224 | tf_op jit(solution)/shard_map/ppermute | solution.py:14
  9.0 1.3 %collective-permute-start.2 = (bf16[512,128]{1,0:T(8,128)(2,1)S(1)}, bf16[512,128]{1,0:T(8,128)(2,1)S(1)}, u32[]{:S(2)}, u32[]{:S(2)}) collective-permute-start(bf16[512,128]{1,0:T(8,128)(2,1)S(1)} %get-tuple-element.37), channel_id=1, source_target_pairs={{0,3},{1,0},{2,1},{3,2},{4,7},{5,4},{6,5},{7,6},{8,11},{9,8},{10,9... | collective-permute-start | bytes 393224 | tf_op jit(solution)/shard_map/ppermute | solution.py:14
  10.3 1.0 %copy.25 = bf16[512,512]{1,0:T(8,128)(2,1)} copy(bf16[512,512]{0,1:T(8,128)(2,1)S(1)} %fusion.8) | data formatting | bytes 1048576 | tf_op jit(solution)/shard_map/optimization_barrier | solution.py:62
  11.3 3.7 %all-to-all-start = ((bf16[8,64,512]{2,1,0:T(8,128)(2,1)}), bf16[8,64,512]{2,1,0:T(8,128)(2,1)S(1)}, u32[]{:S(2)}, u32[]{:S(2)}) async-start(bf16[8,64,512]{2,1,0:T(8,128)(2,1)} %bitcast.2), calls=%async_computation | async-start | bytes 1048576 | tf_op jit(solution)/shard_map/all_to_all | solution.py:19
  15.0 0.7 fusion.78
  15.7 0.7 copy-done.10
  16.5 0.1 copy.30
  16.7 0.7 fusion.106
  17.4 0.2 collective-permute-done.1
  17.6 0.9 fusion.56
  18.5 3.3 %collective-permute-start.3 = (bf16[512,128]{1,0:T(8,128)(2,1)}, bf16[512,128]{1,0:T(8,128)(2,1)}, u32[]{:S(2)}, u32[]{:S(2)}) collective-permute-start(bf16[512,128]{1,0:T(8,128)(2,1)} %get-tuple-element.28), channel_id=1, source_target_pairs={{0,1},{1,2},{2,3},{3,0},{4,5},{5,6},{6,7},{7,4},{8,9},{9,10},{10,1... | collective-permute-start | bytes 393224 | tf_op jit(solution)/shard_map/ppermute | solution.py:14
  21.8 1.6 %collective-permute-start.4 = (bf16[512,128]{1,0:T(8,128)(2,1)S(1)}, bf16[512,128]{1,0:T(8,128)(2,1)}, u32[]{:S(2)}, u32[]{:S(2)}) collective-permute-start(bf16[512,128]{1,0:T(8,128)(2,1)S(1)} %get-tuple-element.29), channel_id=1, source_target_pairs={{0,2},{1,3},{2,0},{3,1},{4,6},{5,7},{6,4},{7,5},{8,10},{9,11},{10,... | collective-permute-start | bytes 393224 | tf_op jit(solution)/shard_map/ppermute | solution.py:14
  23.4 0.7 collective-permute-start.5
  24.2 0.6 all-to-all-done
  24.8 0.4 fusion.6
  25.2 0.9 %copy.28 = bf16[8,64,512]{2,1,0:T(8,128)(2,1)} copy(bf16[8,64,512]{2,0,1:T(8,128)(2,1)S(1)} %fusion.6) | data formatting | bytes 1048576 | tf_op jit(solution)/shard_map/convert_element_type | solution.py:77
  26.2 3.5 %all-to-all-start.1 = ((bf16[8,64,512]{2,1,0:T(8,128)(2,1)}), bf16[8,64,512]{2,1,0:T(8,128)(2,1)S(1)}, u32[]{:S(2)}, u32[]{:S(2)}) async-start(bf16[8,64,512]{2,1,0:T(8,128)(2,1)} %copy.28), calls=%async_computation.1 | async-start | bytes 1048576 | tf_op jit(solution)/shard_map/all_to_all | solution.py:19
  29.7 0.1 fusion.77
  29.9 1.0 %constant_dynamic-update-slice_fusion.2 = bf16[512,512]{1,0:T(8,128)(2,1)S(1)} fusion(bf16[512,512]{1,0:T(8,128)(2,1)S(1)} %fusion.77, bf16[512,128]{1,0:T(8,128)(2,1)} %collective-permute-done.3, s32[]{:T(128)S(6)} %select_n.80), kind=kLoop, calls=%fused_computation.166 | loop fusion | bytes 262148 | tf_op jit(solution)/shard_map/dynamic_update_slice | solution.py:33
  30.9 1.1 %collective-permute-done.4 = bf16[512,128]{1,0:T(8,128)(2,1)} collective-permute-done((bf16[512,128]{1,0:T(8,128)(2,1)S(1)}, bf16[512,128]{1,0:T(8,128)(2,1)}, u32[]{:S(2)}, u32[]{:S(2)}) %collective-permute-start.4) | collective-permute-done | bytes 131104 | tf_op jit(solution)/shard_map/ppermute | solution.py:14
  32.0 0.9 %constant_dynamic-update-slice_fusion.1 = bf16[512,512]{1,0:T(8,128)(2,1)S(1)} fusion(bf16[512,512]{1,0:T(8,128)(2,1)S(1)} %constant_dynamic-update-slice_fusion.2, bf16[512,128]{1,0:T(8,128)(2,1)} %collective-permute-done.4, s32[]{:T(128)S(6)} %select_n.82), kind=kLoop, calls=%fused_computation.161 | loop fusion | bytes 262148 | tf_op jit(solution)/shard_map/dynamic_update_slice | solution.py:33
  33.0 0.9 %constant_dynamic-update-slice_fusion = bf16[512,512]{1,0:T(8,128)(2,1)S(1)} fusion(bf16[512,512]{1,0:T(8,128)(2,1)S(1)} %constant_dynamic-update-slice_fusion.1, bf16[512,128]{1,0:T(8,128)(2,1)} %collective-permute-done.5, s32[]{:T(128)S(6)} %select_n.84), kind=kLoop, calls=%fused_computation.156 | loop fusion | bytes 262148 | tf_op jit(solution)/shard_map/dynamic_update_slice | solution.py:33
  33.9 5.4 %all-to-all-done.1 = bf16[8,64,512]{2,1,0:T(8,128)(2,1)S(1)} async-done(((bf16[8,64,512]{2,1,0:T(8,128)(2,1)}), bf16[8,64,512]{2,1,0:T(8,128)(2,1)S(1)}, u32[]{:S(2)}, u32[]{:S(2)}) %all-to-all-start.1) | async-done | bytes 524320 | tf_op jit(solution)/shard_map/all_to_all | solution.py:19
  39.4 0.4 fusion.33
  39.8 1.1 %multiply_convert_fusion = (bf16[512,512]{1,0:T(8,128)(2,1)S(1)}, bf16[512,512]{1,0:T(8,128)(2,1)S(1)}) fusion(bf16[512,512]{1,0:T(8,128)(2,1)S(1)} %constant_dynamic-update-slice_fusion, bf16[512,512]{1,0:T(8,128)(2,1)S(1)} %fusion.33, bf16[1,512,512]{2,1,0:T(8,128)(2,1)S(1)} %copy-done), kind=kOutput, calls=%fused_computation.52 | convolution fusion | flops 274464768 | bytes 2621440 | tf_op jit(solution)/shard_map/dot_general | solution.py:81
  40.9 1.6 %fusion.24 = (bf16[512,512]{1,0:T(8,128)(2,1)}, bf16[512,512]{1,0:T(8,128)(2,1)}) fusion(bf16[512,512]{1,0:T(8,128)(2,1)S(1)} %copy-done.4, f32[512]{0:T(512)S(1)} %copy-done.11, bf16[512,512]{1,0:T(8,128)(2,1)S(1)} %get-tuple-element.23, bf16[1,512,512]{2,1,0:T(8,128)(2,1)S(1)} %copy-done, bf16[512,512]{1,0:T(8,128)(2,1)S(1)} %copy-done.1), kind=kOutput, calls=%fused_computation.41 | convolution fusion | flops 271319040 | bytes 3147776 | tf_op jit(solution)/shard_map/dot_general | solution.py:95
  42.5 3.5 %all-to-all-start.2 = ((bf16[8,64,512]{2,1,0:T(8,128)(2,1)}), bf16[8,64,512]{2,1,0:T(8,128)(2,1)S(1)}, u32[]{:S(2)}, u32[]{:S(2)}) async-start(bf16[8,64,512]{2,1,0:T(8,128)(2,1)} %bitcast.22), calls=%async_computation.2 | async-start | bytes 1048576 | tf_op jit(solution)/shard_map/all_to_all | solution.py:19
  46.0 0.1 constant_dynamic-slice_fusion.13
  46.1 1.0 %collective-permute-start.7 = (bf16[512,128]{1,0:T(8,128)(2,1)S(1)}, bf16[512,128]{1,0:T(8,128)(2,1)S(1)}, u32[]{:S(2)}, u32[]{:S(2)}) collective-permute-start(bf16[512,128]{1,0:T(8,128)(2,1)S(1)} %get-tuple-element.35), channel_id=1, source_target_pairs={{0,1},{1,2},{2,3},{3,0},{4,5},{5,6},{6,7},{7,4},{8,9},{9,10},{10,1... | collective-permute-start | bytes 393224 | tf_op jit(solution)/shard_map/ppermute | solution.py:14
  47.1 1.3 %collective-permute-start.8 = (bf16[512,128]{1,0:T(8,128)(2,1)S(1)}, bf16[512,128]{1,0:T(8,128)(2,1)S(1)}, u32[]{:S(2)}, u32[]{:S(2)}) collective-permute-start(bf16[512,128]{1,0:T(8,128)(2,1)S(1)} %get-tuple-element.34), channel_id=1, source_target_pairs={{0,2},{1,3},{2,0},{3,1},{4,6},{5,7},{6,4},{7,5},{8,10},{9,11},{10,... | collective-permute-start | bytes 393224 | tf_op jit(solution)/shard_map/ppermute | solution.py:14
  48.4 1.6 %collective-permute-start.9 = (bf16[512,128]{1,0:T(8,128)(2,1)S(1)}, bf16[512,128]{1,0:T(8,128)(2,1)}, u32[]{:S(2)}, u32[]{:S(2)}) collective-permute-start(bf16[512,128]{1,0:T(8,128)(2,1)S(1)} %get-tuple-element.33), channel_id=1, source_target_pairs={{0,3},{1,0},{2,1},{3,2},{4,7},{5,4},{6,5},{7,6},{8,11},{9,8},{10,9... | collective-permute-start | bytes 393224 | tf_op jit(solution)/shard_map/ppermute | solution.py:14
  50.0 1.3 %fusion.113 = bf16[512,512]{1,0:T(8,128)(2,1)} fusion(bf16[512,512]{1,0:T(8,128)(2,1)S(1)} %fusion.33, bf16[512,512]{1,0:T(8,128)(2,1)S(1)} %copy-done.28), kind=kOutput, calls=%fused_computation.212 | convolution fusion | flops 268435456 | bytes 1572864 | tf_op jit(solution)/shard_map/dot_general | solution.py:97
  51.3 4.4 %all-to-all-done.2 = bf16[8,64,512]{2,1,0:T(8,128)(2,1)S(1)} async-done(((bf16[8,64,512]{2,1,0:T(8,128)(2,1)}), bf16[8,64,512]{2,1,0:T(8,128)(2,1)S(1)}, u32[]{:S(2)}, u32[]{:S(2)}) %all-to-all-start.2) | async-done | bytes 524320 | tf_op jit(solution)/shard_map/all_to_all | solution.py:19
  55.7 0.4 fusion.7
  56.1 0.9 %copy.31 = bf16[8,64,512]{2,1,0:T(8,128)(2,1)} copy(bf16[8,64,512]{2,0,1:T(8,128)(2,1)S(1)} %fusion.7) | data formatting | bytes 1048576 | tf_op jit(solution)/shard_map/convert_element_type | solution.py:104
  57.1 3.5 %all-to-all-start.3 = ((bf16[8,64,512]{2,1,0:T(8,128)(2,1)}), bf16[8,64,512]{2,1,0:T(8,128)(2,1)S(1)}, u32[]{:S(2)}, u32[]{:S(2)}) async-start(bf16[8,64,512]{2,1,0:T(8,128)(2,1)} %copy.31), calls=%async_computation.3 | async-start | bytes 1048576 | tf_op jit(solution)/shard_map/all_to_all | solution.py:19
  60.7 0.6 copy-done.12
  61.3 0.0 copy-done.13
  61.3 1.8 %fusion.72 = (bf16[512,128]{1,0:T(8,128)(2,1)}, bf16[512,128]{1,0:T(8,128)(2,1)}, bf16[512,128]{1,0:T(8,128)(2,1)}) fusion(bf16[512,128]{1,0:T(8,128)(2,1)S(1)} %collective-permute-done.7, bf16[512,128]{1,0:T(8,128)(2,1)S(1)} %collective-permute-done.8, bf16[512,128]{1,0:T(8,128)(2,1)} %collective-permute-done.9, f32[128]{0:T(128)S(1)} %get-tuple-element.40, ...), kind=kLoop, calls=%fused_computation.123 | loop fusion | flops 1835008 | bytes 923652 | tf_op jit(solution)/shard_map/convert_element_type | solution.py:89
  63.2 2.0 %collective-permute-start.10 = (bf16[512,128]{1,0:T(8,128)(2,1)}, bf16[512,128]{1,0:T(8,128)(2,1)}, u32[]{:S(2)}, u32[]{:S(2)}) collective-permute-start(bf16[512,128]{1,0:T(8,128)(2,1)} %get-tuple-element.25), channel_id=1, source_target_pairs={{0,1},{1,2},{2,3},{3,0},{4,5},{5,6},{6,7},{7,4},{8,9},{9,10},{10,1... | collective-permute-start | bytes 393224 | tf_op jit(solution)/shard_map/ppermute | solution.py:14
  65.2 0.3 collective-permute-start.11
  65.4 2.1 %collective-permute-start.12 = (bf16[512,128]{1,0:T(8,128)(2,1)}, bf16[512,128]{1,0:T(8,128)(2,1)}, u32[]{:S(2)}, u32[]{:S(2)}) collective-permute-start(bf16[512,128]{1,0:T(8,128)(2,1)} %get-tuple-element.24), channel_id=1, source_target_pairs={{0,3},{1,0},{2,1},{3,2},{4,7},{5,4},{6,5},{7,6},{8,11},{9,8},{10,9... | collective-permute-start | bytes 393224 | tf_op jit(solution)/shard_map/ppermute | solution.py:14
  67.6 1.7 %fusion.60 = bf16[512,128]{1,0:T(8,128)(2,1)} fusion(bf16[512,128]{1,0:T(8,128)(2,1)S(1)} %collective-permute-done.7, bf16[512,128]{1,0:T(8,128)(2,1)S(1)} %collective-permute-done.8, bf16[512,128]{1,0:T(8,128)(2,1)} %collective-permute-done.9, f32[128]{0:T(128)S(1)} %copy-done.22, f32[128]{0:T(128)S(1)} %copy-done.23, f32[128]{0:T(128)S(1)} %copy-done.24, ...), kind=kLoop, calls=%fused_computation.111 | loop fusion | flops 786432 | bytes 657412 | tf_op jit(solution)/shard_map/convert_element_type | solution.py:89
  69.2 1.0 %all-to-all-done.3 = bf16[8,64,512]{2,1,0:T(8,128)(2,1)S(1)} async-done(((bf16[8,64,512]{2,1,0:T(8,128)(2,1)}), bf16[8,64,512]{2,1,0:T(8,128)(2,1)S(1)}, u32[]{:S(2)}, u32[]{:S(2)}) %all-to-all-start.3) | async-done | bytes 524320 | tf_op jit(solution)/shard_map/all_to_all | solution.py:19
  70.3 0.6 fusion.110
  70.9 0.2 copy-done.6
  71.1 0.7 dynamic-slice_convert_fusion.1
  71.8 1.0 %collective-permute-start.6 = (bf16[128,512]{1,0:T(8,128)(2,1)}, bf16[128,512]{1,0:T(8,128)(2,1)S(1)}, u32[]{:S(2)}, u32[]{:S(2)}) collective-permute-start(bf16[128,512]{1,0:T(8,128)(2,1)} %get-tuple-element.32), channel_id=1, source_target_pairs={{0,1},{1,2},{2,3},{3,0},{4,5},{5,6},{6,7},{7,4},{8,9},{9,10},{10,1... | collective-permute-start | bytes 393224 | tf_op jit(solution)/shard_map/ppermute | solution.py:14
  72.7 1.3 %collective-permute-start.13 = (bf16[128,512]{1,0:T(8,128)(2,1)S(1)}, bf16[128,512]{1,0:T(8,128)(2,1)}, u32[]{:S(2)}, u32[]{:S(2)}) collective-permute-start(bf16[128,512]{1,0:T(8,128)(2,1)S(1)} %get-tuple-element.30), channel_id=1, source_target_pairs={{0,2},{1,3},{2,0},{3,1},{4,6},{5,7},{6,4},{7,5},{8,10},{9,11},{10,... | collective-permute-start | bytes 393224 | tf_op jit(solution)/shard_map/ppermute | solution.py:14
  74.0 3.6 %all-to-all-start.4 = ((bf16[8,64,512]{2,1,0:T(8,128)(2,1)}), bf16[8,64,512]{2,1,0:T(8,128)(2,1)S(1)}, u32[]{:S(2)}, u32[]{:S(2)}) async-start(bf16[8,64,512]{2,1,0:T(8,128)(2,1)} %bitcast.42), calls=%async_computation.4 | async-start | bytes 1048576 | tf_op jit(solution)/shard_map/all_to_all | solution.py:19
  77.7 3.2 %fusion.3 = bf16[512,512]{1,0:T(8,128)(2,1)} fusion(bf16[512,512]{1,0:T(8,128)(2,1)S(1)} %bitcast.112, bf16[512,512]{1,0:T(8,128)(2,1)} %get-tuple-element.71, bf16[512,512]{1,0:T(8,128)(2,1)S(1)} %copy-done.5, bf16[512,512]{1,0:T(8,128)(2,1)S(1)} %bitcast.110, bf16[1,512,512]{2,1,0:T(8,128)(2,1)} %param.11, f32[512]{0:T(512)S(1)} %copy-done.11, ...), kind=kOutput, calls=%fused_computation.20 | convolution fusion | flops 274726912 | bytes 3149824 | tf_op jit(solution)/shard_map/dot_general | solution.py:127
  80.9 1.7 %collective-permute-start.14 = (bf16[128,512]{1,0:T(8,128)(2,1)S(1)}, bf16[128,512]{1,0:T(8,128)(2,1)S(1)}, u32[]{:S(2)}, u32[]{:S(2)}) collective-permute-start(bf16[128,512]{1,0:T(8,128)(2,1)S(1)} %get-tuple-element.31), channel_id=1, source_target_pairs={{0,3},{1,0},{2,1},{3,2},{4,7},{5,4},{6,5},{7,6},{8,11},{9,8},{10,9... | collective-permute-start | bytes 393224 | tf_op jit(solution)/shard_map/ppermute | solution.py:14
  82.7 0.1 fusion.73
  82.7 1.0 %fusion.74 = bf16[512,512]{1,0:T(8,128)(2,1)S(1)} fusion(bf16[512,512]{1,0:T(8,128)(2,1)S(1)} %fusion.73, s32[]{:T(128)S(6)} %select_n.80, bf16[512,128]{1,0:T(8,128)(2,1)} %collective-permute-done.10, bf16[512,512]{1,0:T(8,128)(2,1)S(1)} %fusion.33), kind=kLoop, calls=%fused_computation.134 | loop fusion | flops 262144 | bytes 393220 | tf_op jit(solution)/shard_map/dynamic_update_slice | solution.py:33
  83.7 1.0 %fusion.75 = bf16[512,512]{1,0:T(8,128)(2,1)S(1)} fusion(bf16[512,512]{1,0:T(8,128)(2,1)S(1)} %fusion.74, s32[]{:T(128)S(6)} %select_n.82, bf16[512,128]{1,0:T(8,128)(2,1)} %collective-permute-done.11, bf16[512,512]{1,0:T(8,128)(2,1)S(1)} %fusion.33), kind=kLoop, calls=%fused_computation.135 | loop fusion | flops 262144 | bytes 393220 | tf_op jit(solution)/shard_map/dynamic_update_slice | solution.py:33
  84.7 1.0 %fusion.76 = bf16[512,512]{1,0:T(8,128)(2,1)S(1)} fusion(bf16[512,512]{1,0:T(8,128)(2,1)S(1)} %fusion.75, s32[]{:T(128)S(6)} %select_n.84, bf16[512,128]{1,0:T(8,128)(2,1)} %collective-permute-done.12, bf16[512,512]{1,0:T(8,128)(2,1)S(1)} %fusion.33), kind=kLoop, calls=%fused_computation.136 | loop fusion | flops 262144 | bytes 393220 | tf_op jit(solution)/shard_map/dynamic_update_slice | solution.py:33
  85.7 2.4 %collective-permute-done.13 = bf16[128,512]{1,0:T(8,128)(2,1)} collective-permute-done((bf16[128,512]{1,0:T(8,128)(2,1)S(1)}, bf16[128,512]{1,0:T(8,128)(2,1)}, u32[]{:S(2)}, u32[]{:S(2)}) %collective-permute-start.13) | collective-permute-done | bytes 131104 | tf_op jit(solution)/shard_map/ppermute | solution.py:14
  88.1 1.8 %collective-permute-done.14 = bf16[128,512]{1,0:T(8,128)(2,1)S(1)} collective-permute-done((bf16[128,512]{1,0:T(8,128)(2,1)S(1)}, bf16[128,512]{1,0:T(8,128)(2,1)S(1)}, u32[]{:S(2)}, u32[]{:S(2)}) %collective-permute-start.14) | collective-permute-done | bytes 131104 | tf_op jit(solution)/shard_map/ppermute | solution.py:14
  89.9 1.7 %add_bitcast_fusion = f32[1,128,512]{2,1,0:T(8,128)} fusion(bf16[128,512]{1,0:T(8,128)(2,1)S(1)} %collective-permute-done.14, bf16[128,512]{1,0:T(8,128)(2,1)} %collective-permute-done.13, bf16[128,512]{1,0:T(8,128)(2,1)S(1)} %collective-permute-done.6, bf16[512,512]{1,0:T(8,128)(2,1)} %copy-done.8, s32[]{:T(128)S(6)} %select_n.64), kind=kLoop, calls=%fused_computation.124 | loop fusion | flops 458752 | bytes 786436 | tf_op jit(solution)/shard_map/broadcast_in_dim | solution.py:115
  91.6 0.7 convert_reduce_fusion
  (67 shorter events, 0.2 us)
Async XLA Ops:
  0.6 39.1 %copy-start = (bf16[1,512,512]{2,1,0:T(8,128)(2,1)S(1)}, bf16[1,512,512]{2,1,0:T(8,128)(2,1)}, u32[]{:S(2)}) copy-start(bf16[1,512,512]{2,1,0:T(8,128)(2,1)} %param.13) | copy-start | bytes 1572868
  0.7 0.7 copy-start.25
  1.4 1.8 %copy-start.1 = (bf16[512,512]{1,0:T(8,128)(2,1)S(1)}, bf16[512,512]{1,0:T(8,128)(2,1)}, u32[]{:S(2)}) copy-start(bf16[512,512]{1,0:T(8,128)(2,1)} %param.15) | copy-start | bytes 1572868
  3.3 14.1 %collective-permute-start = (bf16[512,128]{1,0:T(8,128)(2,1)S(1)}, bf16[512,128]{1,0:T(8,128)(2,1)S(1)}, u32[]{:S(2)}, u32[]{:S(2)}) collective-permute-start(bf16[512,128]{1,0:T(8,128)(2,1)S(1)} %get-tuple-element.36), channel_id=1, source_target_pairs={{0,1},{1,2},{2,3},{3,0},{4,5},{5,6},{6,7},{7,4},{8,9},{9,10},{10,1... | collective-permute-start | bytes 393224 | tf_op jit(solution)/shard_map/ppermute | solution.py:14
  6.4 11.2 %collective-permute-start.1 = (bf16[512,128]{1,0:T(8,128)(2,1)S(1)}, bf16[512,128]{1,0:T(8,128)(2,1)S(1)}, u32[]{:S(2)}, u32[]{:S(2)}) collective-permute-start(bf16[512,128]{1,0:T(8,128)(2,1)S(1)} %get-tuple-element.38), channel_id=1, source_target_pairs={{0,2},{1,3},{2,0},{3,1},{4,6},{5,7},{6,4},{7,5},{8,10},{9,11},{10,... | collective-permute-start | bytes 393224 | tf_op jit(solution)/shard_map/ppermute | solution.py:14
  9.0 8.6 %collective-permute-start.2 = (bf16[512,128]{1,0:T(8,128)(2,1)S(1)}, bf16[512,128]{1,0:T(8,128)(2,1)S(1)}, u32[]{:S(2)}, u32[]{:S(2)}) collective-permute-start(bf16[512,128]{1,0:T(8,128)(2,1)S(1)} %get-tuple-element.37), channel_id=1, source_target_pairs={{0,3},{1,0},{2,1},{3,2},{4,7},{5,4},{6,5},{7,6},{8,11},{9,8},{10,9... | collective-permute-start | bytes 393224 | tf_op jit(solution)/shard_map/ppermute | solution.py:14
  11.3 13.5 %all-to-all-start = ((bf16[8,64,512]{2,1,0:T(8,128)(2,1)}), bf16[8,64,512]{2,1,0:T(8,128)(2,1)S(1)}, u32[]{:S(2)}, u32[]{:S(2)}) async-start(bf16[8,64,512]{2,1,0:T(8,128)(2,1)} %bitcast.2), calls=%async_computation | async-start | bytes 1048576 | tf_op jit(solution)/shard_map/all_to_all | solution.py:19
  15.7 0.7 copy-start.10
  18.5 11.4 %collective-permute-start.3 = (bf16[512,128]{1,0:T(8,128)(2,1)}, bf16[512,128]{1,0:T(8,128)(2,1)}, u32[]{:S(2)}, u32[]{:S(2)}) collective-permute-start(bf16[512,128]{1,0:T(8,128)(2,1)} %get-tuple-element.28), channel_id=1, source_target_pairs={{0,1},{1,2},{2,3},{3,0},{4,5},{5,6},{6,7},{7,4},{8,9},{9,10},{10,1... | collective-permute-start | bytes 393224 | tf_op jit(solution)/shard_map/ppermute | solution.py:14
  21.8 10.2 %collective-permute-start.4 = (bf16[512,128]{1,0:T(8,128)(2,1)S(1)}, bf16[512,128]{1,0:T(8,128)(2,1)}, u32[]{:S(2)}, u32[]{:S(2)}) collective-permute-start(bf16[512,128]{1,0:T(8,128)(2,1)S(1)} %get-tuple-element.29), channel_id=1, source_target_pairs={{0,2},{1,3},{2,0},{3,1},{4,6},{5,7},{6,4},{7,5},{8,10},{9,11},{10,... | collective-permute-start | bytes 393224 | tf_op jit(solution)/shard_map/ppermute | solution.py:14
  23.4 9.6 %collective-permute-start.5 = (bf16[512,128]{1,0:T(8,128)(2,1)S(1)}, bf16[512,128]{1,0:T(8,128)(2,1)}, u32[]{:S(2)}, u32[]{:S(2)}) collective-permute-start(bf16[512,128]{1,0:T(8,128)(2,1)S(1)} %get-tuple-element.27), channel_id=1, source_target_pairs={{0,3},{1,0},{2,1},{3,2},{4,7},{5,4},{6,5},{7,6},{8,11},{9,8},{10,9... | collective-permute-start | bytes 393224 | tf_op jit(solution)/shard_map/ppermute | solution.py:14
  26.2 13.2 %all-to-all-start.1 = ((bf16[8,64,512]{2,1,0:T(8,128)(2,1)}), bf16[8,64,512]{2,1,0:T(8,128)(2,1)S(1)}, u32[]{:S(2)}, u32[]{:S(2)}) async-start(bf16[8,64,512]{2,1,0:T(8,128)(2,1)} %copy.28), calls=%async_computation.1 | async-start | bytes 1048576 | tf_op jit(solution)/shard_map/all_to_all | solution.py:19
  29.9 9.5 %copy-start.3 = (bf16[512,512]{1,0:T(8,128)(2,1)S(1)}, bf16[512,512]{1,0:T(8,128)(2,1)}, u32[]{:S(2)}) copy-start(bf16[512,512]{1,0:T(8,128)(2,1)} %param.8) | copy-start | bytes 1572868
  33.0 6.4 %copy-start.11 = (f32[512]{0:T(512)S(1)}, f32[512]{0:T(512)}, u32[]{:S(2)}) copy-start(f32[512]{0:T(512)} %param.10) | copy-start | bytes 6148
  39.8 1.2 %copy-start.4 = (bf16[512,512]{1,0:T(8,128)(2,1)S(1)}, bf16[512,512]{1,0:T(8,128)(2,1)}, u32[]{:S(2)}) copy-start(bf16[512,512]{1,0:T(8,128)(2,1)} %param.8) | copy-start | bytes 1572868
  40.9 1.6 %copy-start.27 = (bf16[512,512]{1,0:T(8,128)(2,1)}, bf16[512,512]{1,0:T(8,128)(2,1)S(1)}, u32[]{:S(2)}) copy-start(bf16[512,512]{1,0:T(8,128)(2,1)S(1)} %get-tuple-element.23) | copy-start | bytes 1572868
  42.5 13.2 %all-to-all-start.2 = ((bf16[8,64,512]{2,1,0:T(8,128)(2,1)}), bf16[8,64,512]{2,1,0:T(8,128)(2,1)S(1)}, u32[]{:S(2)}, u32[]{:S(2)}) async-start(bf16[8,64,512]{2,1,0:T(8,128)(2,1)} %bitcast.22), calls=%async_computation.2 | async-start | bytes 1048576 | tf_op jit(solution)/shard_map/all_to_all | solution.py:19
  46.0 4.0 %copy-start.28 = (bf16[512,512]{1,0:T(8,128)(2,1)S(1)}, bf16[512,512]{1,0:T(8,128)(2,1)}, u32[]{:S(2)}) copy-start(bf16[512,512]{1,0:T(8,128)(2,1)} %copy-done.27) | copy-start | bytes 1572868
  46.1 14.5 %collective-permute-start.7 = (bf16[512,128]{1,0:T(8,128)(2,1)S(1)}, bf16[512,128]{1,0:T(8,128)(2,1)S(1)}, u32[]{:S(2)}, u32[]{:S(2)}) collective-permute-start(bf16[512,128]{1,0:T(8,128)(2,1)S(1)} %get-tuple-element.35), channel_id=1, source_target_pairs={{0,1},{1,2},{2,3},{3,0},{4,5},{5,6},{6,7},{7,4},{8,9},{9,10},{10,1... | collective-permute-start | bytes 393224 | tf_op jit(solution)/shard_map/ppermute | solution.py:14
  47.1 13.5 %collective-permute-start.8 = (bf16[512,128]{1,0:T(8,128)(2,1)S(1)}, bf16[512,128]{1,0:T(8,128)(2,1)S(1)}, u32[]{:S(2)}, u32[]{:S(2)}) collective-permute-start(bf16[512,128]{1,0:T(8,128)(2,1)S(1)} %get-tuple-element.34), channel_id=1, source_target_pairs={{0,2},{1,3},{2,0},{3,1},{4,6},{5,7},{6,4},{7,5},{8,10},{9,11},{10,... | collective-permute-start | bytes 393224 | tf_op jit(solution)/shard_map/ppermute | solution.py:14
  48.4 12.2 %collective-permute-start.9 = (bf16[512,128]{1,0:T(8,128)(2,1)S(1)}, bf16[512,128]{1,0:T(8,128)(2,1)}, u32[]{:S(2)}, u32[]{:S(2)}) collective-permute-start(bf16[512,128]{1,0:T(8,128)(2,1)S(1)} %get-tuple-element.33), channel_id=1, source_target_pairs={{0,3},{1,0},{2,1},{3,2},{4,7},{5,4},{6,5},{7,6},{8,11},{9,8},{10,9... | collective-permute-start | bytes 393224 | tf_op jit(solution)/shard_map/ppermute | solution.py:14
  57.0 3.6 %copy-start.15 = (f32[128]{0:T(128)S(1)}, f32[128]{0:T(128)}, u32[]{:S(2)}) copy-start(f32[128]{0:T(128)} %get-tuple-element.44) | copy-start | bytes 1540
  57.0 3.6 %copy-start.16 = (f32[128]{0:T(128)S(1)}, f32[128]{0:T(128)}, u32[]{:S(2)}) copy-start(f32[128]{0:T(128)} %get-tuple-element.45) | copy-start | bytes 1540
  57.0 3.6 %copy-start.17 = (f32[128]{0:T(128)S(1)}, f32[128]{0:T(128)}, u32[]{:S(2)}) copy-start(f32[128]{0:T(128)} %get-tuple-element.46) | copy-start | bytes 1540
  57.0 3.6 %copy-start.18 = (f32[128]{0:T(128)S(1)}, f32[128]{0:T(128)}, u32[]{:S(2)}) copy-start(f32[128]{0:T(128)} %get-tuple-element.47) | copy-start | bytes 1540
  57.1 3.6 %copy-start.19 = (f32[128]{0:T(128)S(1)}, f32[128]{0:T(128)}, u32[]{:S(2)}) copy-start(f32[128]{0:T(128)} %get-tuple-element.48) | copy-start | bytes 1540
  57.1 3.6 %copy-start.20 = (f32[128]{0:T(128)S(1)}, f32[128]{0:T(128)}, u32[]{:S(2)}) copy-start(f32[128]{0:T(128)} %get-tuple-element.49) | copy-start | bytes 1540
  57.1 3.6 %copy-start.21 = (f32[128]{0:T(128)S(1)}, f32[128]{0:T(128)}, u32[]{:S(2)}) copy-start(f32[128]{0:T(128)} %get-tuple-element.50) | copy-start | bytes 1540
  57.1 13.2 %all-to-all-start.3 = ((bf16[8,64,512]{2,1,0:T(8,128)(2,1)}), bf16[8,64,512]{2,1,0:T(8,128)(2,1)S(1)}, u32[]{:S(2)}, u32[]{:S(2)}) async-start(bf16[8,64,512]{2,1,0:T(8,128)(2,1)} %copy.31), calls=%async_computation.3 | async-start | bytes 1048576 | tf_op jit(solution)/shard_map/all_to_all | solution.py:19
  60.6 0.7 copy-start.12
  60.6 0.7 copy-start.13
  60.7 0.7 copy-start.14
  61.3 6.2 %copy-start.22 = (f32[128]{0:T(128)S(1)}, f32[128]{0:T(128)}, u32[]{:S(2)}) copy-start(f32[128]{0:T(128)} %get-tuple-element.51) | copy-start | bytes 1540
  61.3 6.2 %copy-start.23 = (f32[128]{0:T(128)S(1)}, f32[128]{0:T(128)}, u32[]{:S(2)}) copy-start(f32[128]{0:T(128)} %get-tuple-element.52) | copy-start | bytes 1540
  61.3 6.2 %copy-start.24 = (f32[128]{0:T(128)S(1)}, f32[128]{0:T(128)}, u32[]{:S(2)}) copy-start(f32[128]{0:T(128)} %get-tuple-element.53) | copy-start | bytes 1540
  63.2 7.1 %copy-start.5 = (bf16[512,512]{1,0:T(8,128)(2,1)S(1)}, bf16[512,512]{1,0:T(8,128)(2,1)}, u32[]{:S(2)}) copy-start(bf16[512,512]{1,0:T(8,128)(2,1)} %param.8) | copy-start | bytes 1572868
  63.2 17.7 %collective-permute-start.10 = (bf16[512,128]{1,0:T(8,128)(2,1)}, bf16[512,128]{1,0:T(8,128)(2,1)}, u32[]{:S(2)}, u32[]{:S(2)}) collective-permute-start(bf16[512,128]{1,0:T(8,128)(2,1)} %get-tuple-element.25), channel_id=1, source_target_pairs={{0,1},{1,2},{2,3},{3,0},{4,5},{5,6},{6,7},{7,4},{8,9},{9,10},{10,1... | collective-permute-start | bytes 393224 | tf_op jit(solution)/shard_map/ppermute | solution.py:14
  65.2 17.4 %collective-permute-start.11 = (bf16[512,128]{1,0:T(8,128)(2,1)}, bf16[512,128]{1,0:T(8,128)(2,1)}, u32[]{:S(2)}, u32[]{:S(2)}) collective-permute-start(bf16[512,128]{1,0:T(8,128)(2,1)} %get-tuple-element.26), channel_id=1, source_target_pairs={{0,2},{1,3},{2,0},{3,1},{4,6},{5,7},{6,4},{7,5},{8,10},{9,11},{10,... | collective-permute-start | bytes 393224 | tf_op jit(solution)/shard_map/ppermute | solution.py:14
  65.4 17.2 %collective-permute-start.12 = (bf16[512,128]{1,0:T(8,128)(2,1)}, bf16[512,128]{1,0:T(8,128)(2,1)}, u32[]{:S(2)}, u32[]{:S(2)}) collective-permute-start(bf16[512,128]{1,0:T(8,128)(2,1)} %get-tuple-element.24), channel_id=1, source_target_pairs={{0,3},{1,0},{2,1},{3,2},{4,7},{5,4},{6,5},{7,6},{8,11},{9,8},{10,9... | collective-permute-start | bytes 393224 | tf_op jit(solution)/shard_map/ppermute | solution.py:14
  67.6 2.7 %copy-start.26 = (f32[512]{0:T(512)S(1)}, f32[512]{0:T(512)}, u32[]{:S(2)}) copy-start(f32[512]{0:T(512)} %param.9) | copy-start | bytes 6148
  70.3 0.8 copy-start.6
  71.1 3.0 %copy-start.8 = (bf16[512,512]{1,0:T(8,128)(2,1)}, bf16[512,512]{1,0:T(8,128)(2,1)S(1)}, u32[]{:S(2)}) copy-start(bf16[512,512]{1,0:T(8,128)(2,1)S(1)} %fusion.110) | copy-start | bytes 1572868
  71.8 10.8 %collective-permute-start.6 = (bf16[128,512]{1,0:T(8,128)(2,1)}, bf16[128,512]{1,0:T(8,128)(2,1)S(1)}, u32[]{:S(2)}, u32[]{:S(2)}) collective-permute-start(bf16[128,512]{1,0:T(8,128)(2,1)} %get-tuple-element.32), channel_id=1, source_target_pairs={{0,1},{1,2},{2,3},{3,0},{4,5},{5,6},{6,7},{7,4},{8,9},{9,10},{10,1... | collective-permute-start | bytes 393224 | tf_op jit(solution)/shard_map/ppermute | solution.py:14
  72.7 15.4 %collective-permute-start.13 = (bf16[128,512]{1,0:T(8,128)(2,1)S(1)}, bf16[128,512]{1,0:T(8,128)(2,1)}, u32[]{:S(2)}, u32[]{:S(2)}) collective-permute-start(bf16[128,512]{1,0:T(8,128)(2,1)S(1)} %get-tuple-element.30), channel_id=1, source_target_pairs={{0,2},{1,3},{2,0},{3,1},{4,6},{5,7},{6,4},{7,5},{8,10},{9,11},{10,... | collective-permute-start | bytes 393224 | tf_op jit(solution)/shard_map/ppermute | solution.py:14
  74.0 3.6 %copy-start.7 = (bf16[8,64,512]{2,1,0:T(8,128)(2,1)S(1)}, bf16[8,64,512]{2,1,0:T(8,128)(2,1)}, u32[]{:S(2)}) copy-start(bf16[8,64,512]{2,1,0:T(8,128)(2,1)} %copy-done.6) | copy-start | bytes 1572868
  74.0 17.6 %all-to-all-start.4 = ((bf16[8,64,512]{2,1,0:T(8,128)(2,1)}), bf16[8,64,512]{2,1,0:T(8,128)(2,1)S(1)}, u32[]{:S(2)}, u32[]{:S(2)}) async-start(bf16[8,64,512]{2,1,0:T(8,128)(2,1)} %bitcast.42), calls=%async_computation.4 | async-start | bytes 1048576 | tf_op jit(solution)/shard_map/all_to_all | solution.py:19
  80.9 1.8 %copy-start.9 = (bf16[512,128]{1,0:T(8,128)(2,1)S(1)}, bf16[512,128]{1,0:T(8,128)(2,1)}, u32[]{:S(2)}) copy-start(bf16[512,128]{1,0:T(8,128)(2,1)} %fusion.60) | copy-start | bytes 393220
  80.9 9.0 %collective-permute-start.14 = (bf16[128,512]{1,0:T(8,128)(2,1)S(1)}, bf16[128,512]{1,0:T(8,128)(2,1)S(1)}, u32[]{:S(2)}, u32[]{:S(2)}) collective-permute-start(bf16[128,512]{1,0:T(8,128)(2,1)S(1)} %get-tuple-element.31), channel_id=1, source_target_pairs={{0,3},{1,0},{2,1},{3,2},{4,7},{5,4},{6,5},{7,6},{8,11},{9,8},{10,9... | collective-permute-start | bytes 393224 | tf_op jit(solution)/shard_map/ppermute | solution.py:14
  85.6 6.7 %copy-start.2 = (bf16[512,512]{1,0:T(8,128)(2,1)}, bf16[512,512]{1,0:T(8,128)(2,1)S(1)}, u32[]{:S(2)}) copy-start(bf16[512,512]{1,0:T(8,128)(2,1)S(1)} %fusion.76) | copy-start | bytes 1572868

commit v7 on v6

--- a/solution.py
+++ b/solution.py
@@ -110,7 +110,9 @@
         [lax.dynamic_slice_in_dim(block_part, t * cq, cq, 0).astype(BF16) for t in chunk_of],
         "ch",
     )
-    first_block, added_back = lax.optimization_barrier((block_arrived[1], added_back))
+    first_block, added_back, first_grad = lax.optimization_barrier(
+        (block_arrived[1], added_back, first_grad)
+    )
     block_arrived[1] = first_block
     block_grad = sum(part.astype(F32) for part in block_arrived)[None]
     outputs = place_chunks(

time: 93.2 us -> 94.5 us (1.014)
  waiting for transfers between devices: 17.1 us -> 19.3 us
  matrix products: 10.3 us -> 9.18 us
    all_to_all x5, waiting for transfers between devices: 11.5 us -> 13.6 us  [swap(): return lax.all_to_all(pieces, axis_name, 0, 0, tiled=True)]
    dot_general x1, matrix products: 3.19 us -> 1.99 us  [on_device(): spread = jnp.dot(first_blocks[0].T, first_grad, preferred_element_type=F32)]
    unnamed x59 -> x63, local copies, waits for them, and re-layouts: 2.49 us -> 2.6 us
  transfers between devices with their start and end apart: 20 -> 20, of which waited for: 8 -> 7; matrix products, arithmetic and copies ran while one was open for 25% -> 24% of each run, Pallas kernels for 0% -> 0%
where the time goes in v7:
time: 94.5 us; the launch traced here: 93.4 us
  starting transfers between devices  42.3 us (45%)
  waiting for transfers between devices  19.3 us (20%)
  local copies, waits for them, and re-layouts  10.8 us (11%)
  other arithmetic  10.6 us (11%)
  matrix products  9.18 us (10%)
  between operations  1.23 us (1%)
    ppermute x15, starting transfers between devices, exchange(): lax.ppermute(pieces[k], axis_name, [(i, (i + k) % n) for i in range(n)])  24.4 us
    all_to_all x5, starting transfers between devices, swap(): return lax.all_to_all(pieces, axis_name, 0, 0, tiled=True)  18 us
    all_to_all x5, waiting for transfers between devices, swap(): return lax.all_to_all(pieces, axis_name, 0, 0, tiled=True)  13.6 us
    ppermute x15, waiting for transfers between devices, exchange(): lax.ppermute(pieces[k], axis_name, [(i, (i + k) % n) for i in range(n)])  5.78 us
    dynamic_update_slice x5, other arithmetic, place_chunks(): out = lax.dynamic_update_slice_in_dim(out, chunk, start, axis=1)  3.25 us
    convert_element_type x2, other arithmetic, on_device(): added_out = [sum((act_arrived[k].astype(F32) * coefficient(origin_of[k],...  2.9 us
    dynamic_update_slice x3, local copies, waits for them, and re-layouts, place_chunks(): out = lax.dynamic_update_slice_in_dim(out, chunk, start, axis=1)  2.87 us
    unnamed x63, local copies, waits for them, and re-layouts  2.6 us
  transfers between devices with their start and end apart: 20, of which 7 were waited for; matrix products, arithmetic and copies ran while one was open for 24% of the time, Pallas kernels for 0%

profile of v7, /device:TPU:0, one launch (start us, length us, event | category | flops | bytes accessed | tf_op | source)
XLA Modules:
  0.0 93.4 jit_solution(15443318085527777961)
XLA Ops:
  0.6 0.0 copy-start
  0.7 0.7 copy-done.26
  1.4 1.8 %fusion.8 = bf16[512,512]{0,1:T(8,128)(2,1)S(1)} fusion(bf16[1,512,512]{2,1,0:T(8,128)(2,1)} %param.11, bf16[512,512]{1,0:T(8,128)(2,1)} %param.8, f32[512]{0:T(512)S(1)} %copy-done.26), kind=kOutput, calls=%fused_computation.25 | convolution fusion | flops 270532608 | bytes 1574912 | tf_op jit(solution)/shard_map/dot_general | solution.py:59
  3.2 0.1 constant_dynamic-slice_fusion.35
  3.3 3.1 %collective-permute-start = (bf16[512,128]{1,0:T(8,128)(2,1)S(1)}, bf16[512,128]{1,0:T(8,128)(2,1)S(1)}, u32[]{:S(2)}, u32[]{:S(2)}) collective-permute-start(bf16[512,128]{1,0:T(8,128)(2,1)S(1)} %get-tuple-element.38), channel_id=1, source_target_pairs={{0,1},{1,2},{2,3},{3,0},{4,5},{5,6},{6,7},{7,4},{8,9},{9,10},{10,1... | collective-permute-start | bytes 393224 | tf_op jit(solution)/shard_map/ppermute | solution.py:14
  6.4 2.6 %collective-permute-start.1 = (bf16[512,128]{1,0:T(8,128)(2,1)S(1)}, bf16[512,128]{1,0:T(8,128)(2,1)S(1)}, u32[]{:S(2)}, u32[]{:S(2)}) collective-permute-start(bf16[512,128]{1,0:T(8,128)(2,1)S(1)} %get-tuple-element.40), channel_id=1, source_target_pairs={{0,2},{1,3},{2,0},{3,1},{4,6},{5,7},{6,4},{7,5},{8,10},{9,11},{10,... | collective-permute-start | bytes 393224 | tf_op jit(solution)/shard_map/ppermute | solution.py:14
  9.0 1.3 %collective-permute-start.2 = (bf16[512,128]{1,0:T(8,128)(2,1)S(1)}, bf16[512,128]{1,0:T(8,128)(2,1)S(1)}, u32[]{:S(2)}, u32[]{:S(2)}) collective-permute-start(bf16[512,128]{1,0:T(8,128)(2,1)S(1)} %get-tuple-element.39), channel_id=1, source_target_pairs={{0,3},{1,0},{2,1},{3,2},{4,7},{5,4},{6,5},{7,6},{8,11},{9,8},{10,9... | collective-permute-start | bytes 393224 | tf_op jit(solution)/shard_map/ppermute | solution.py:14
  10.3 1.0 %copy.25 = bf16[512,512]{1,0:T(8,128)(2,1)} copy(bf16[512,512]{0,1:T(8,128)(2,1)S(1)} %fusion.8) | data formatting | bytes 1048576 | tf_op jit(solution)/shard_map/optimization_barrier | solution.py:62
  11.3 3.7 %all-to-all-start = ((bf16[8,64,512]{2,1,0:T(8,128)(2,1)}), bf16[8,64,512]{2,1,0:T(8,128)(2,1)S(1)}, u32[]{:S(2)}, u32[]{:S(2)}) async-start(bf16[8,64,512]{2,1,0:T(8,128)(2,1)} %bitcast.2), calls=%async_computation | async-start | bytes 1048576 | tf_op jit(solution)/shard_map/all_to_all | solution.py:19
  15.0 0.7 fusion.78
  15.7 0.7 copy-done.10
  16.5 0.1 copy.30
  16.7 0.7 fusion.106
  17.3 0.3 collective-permute-done.1
  17.6 0.9 fusion.56
  18.5 3.3 %collective-permute-start.3 = (bf16[512,128]{1,0:T(8,128)(2,1)}, bf16[512,128]{1,0:T(8,128)(2,1)}, u32[]{:S(2)}, u32[]{:S(2)}) collective-permute-start(bf16[512,128]{1,0:T(8,128)(2,1)} %get-tuple-element.30), channel_id=1, source_target_pairs={{0,1},{1,2},{2,3},{3,0},{4,5},{5,6},{6,7},{7,4},{8,9},{9,10},{10,1... | collective-permute-start | bytes 393224 | tf_op jit(solution)/shard_map/ppermute | solution.py:14
  21.8 1.6 %collective-permute-start.4 = (bf16[512,128]{1,0:T(8,128)(2,1)S(1)}, bf16[512,128]{1,0:T(8,128)(2,1)}, u32[]{:S(2)}, u32[]{:S(2)}) collective-permute-start(bf16[512,128]{1,0:T(8,128)(2,1)S(1)} %get-tuple-element.31), channel_id=1, source_target_pairs={{0,2},{1,3},{2,0},{3,1},{4,6},{5,7},{6,4},{7,5},{8,10},{9,11},{10,... | collective-permute-start | bytes 393224 | tf_op jit(solution)/shard_map/ppermute | solution.py:14
  23.4 0.7 collective-permute-start.5
  24.2 0.6 all-to-all-done
  24.8 0.4 fusion.6
  25.2 0.9 %copy.28 = bf16[8,64,512]{2,1,0:T(8,128)(2,1)} copy(bf16[8,64,512]{2,0,1:T(8,128)(2,1)S(1)} %fusion.6) | data formatting | bytes 1048576 | tf_op jit(solution)/shard_map/convert_element_type | solution.py:77
  26.2 3.5 %all-to-all-start.1 = ((bf16[8,64,512]{2,1,0:T(8,128)(2,1)}), bf16[8,64,512]{2,1,0:T(8,128)(2,1)S(1)}, u32[]{:S(2)}, u32[]{:S(2)}) async-start(bf16[8,64,512]{2,1,0:T(8,128)(2,1)} %copy.28), calls=%async_computation.1 | async-start | bytes 1048576 | tf_op jit(solution)/shard_map/all_to_all | solution.py:19
  29.7 0.1 fusion.77
  29.9 1.0 %constant_dynamic-update-slice_fusion.2 = bf16[512,512]{1,0:T(8,128)(2,1)S(1)} fusion(bf16[512,512]{1,0:T(8,128)(2,1)S(1)} %fusion.77, bf16[512,128]{1,0:T(8,128)(2,1)} %collective-permute-done.3, s32[]{:T(128)S(6)} %select_n.80), kind=kLoop, calls=%fused_computation.166 | loop fusion | bytes 262148 | tf_op jit(solution)/shard_map/dynamic_update_slice | solution.py:33
  30.9 1.1 %collective-permute-done.4 = bf16[512,128]{1,0:T(8,128)(2,1)} collective-permute-done((bf16[512,128]{1,0:T(8,128)(2,1)S(1)}, bf16[512,128]{1,0:T(8,128)(2,1)}, u32[]{:S(2)}, u32[]{:S(2)}) %collective-permute-start.4) | collective-permute-done | bytes 131104 | tf_op jit(solution)/shard_map/ppermute | solution.py:14
  32.0 0.9 %constant_dynamic-update-slice_fusion.1 = bf16[512,512]{1,0:T(8,128)(2,1)S(1)} fusion(bf16[512,512]{1,0:T(8,128)(2,1)S(1)} %constant_dynamic-update-slice_fusion.2, bf16[512,128]{1,0:T(8,128)(2,1)} %collective-permute-done.4, s32[]{:T(128)S(6)} %select_n.82), kind=kLoop, calls=%fused_computation.161 | loop fusion | bytes 262148 | tf_op jit(solution)/shard_map/dynamic_update_slice | solution.py:33
  33.0 0.9 %constant_dynamic-update-slice_fusion = bf16[512,512]{1,0:T(8,128)(2,1)S(1)} fusion(bf16[512,512]{1,0:T(8,128)(2,1)S(1)} %constant_dynamic-update-slice_fusion.1, bf16[512,128]{1,0:T(8,128)(2,1)} %collective-permute-done.5, s32[]{:T(128)S(6)} %select_n.84), kind=kLoop, calls=%fused_computation.156 | loop fusion | bytes 262148 | tf_op jit(solution)/shard_map/dynamic_update_slice | solution.py:33
  33.9 5.4 %all-to-all-done.1 = bf16[8,64,512]{2,1,0:T(8,128)(2,1)S(1)} async-done(((bf16[8,64,512]{2,1,0:T(8,128)(2,1)}), bf16[8,64,512]{2,1,0:T(8,128)(2,1)S(1)}, u32[]{:S(2)}, u32[]{:S(2)}) %all-to-all-start.1) | async-done | bytes 524320 | tf_op jit(solution)/shard_map/all_to_all | solution.py:19
  39.4 0.4 fusion.33
  39.8 1.1 %multiply_convert_fusion = (bf16[512,512]{1,0:T(8,128)(2,1)S(1)}, bf16[512,512]{1,0:T(8,128)(2,1)S(1)}) fusion(bf16[512,512]{1,0:T(8,128)(2,1)S(1)} %constant_dynamic-update-slice_fusion, bf16[512,512]{1,0:T(8,128)(2,1)S(1)} %fusion.33, bf16[1,512,512]{2,1,0:T(8,128)(2,1)S(1)} %copy-done), kind=kOutput, calls=%fused_computation.52 | convolution fusion | flops 274464768 | bytes 2621440 | tf_op jit(solution)/shard_map/dot_general | solution.py:81
  40.9 1.6 %fusion.24 = (bf16[512,512]{1,0:T(8,128)(2,1)}, bf16[512,512]{1,0:T(8,128)(2,1)}) fusion(bf16[512,512]{1,0:T(8,128)(2,1)S(1)} %copy-done.4, f32[512]{0:T(512)S(1)} %copy-done.11, bf16[512,512]{1,0:T(8,128)(2,1)S(1)} %get-tuple-element.25, bf16[1,512,512]{2,1,0:T(8,128)(2,1)S(1)} %copy-done, bf16[512,512]{1,0:T(8,128)(2,1)S(1)} %copy-done.1), kind=kOutput, calls=%fused_computation.41 | convolution fusion | flops 271319040 | bytes 3147776 | tf_op jit(solution)/shard_map/dot_general | solution.py:95
  42.6 3.5 %all-to-all-start.2 = ((bf16[8,64,512]{2,1,0:T(8,128)(2,1)}), bf16[8,64,512]{2,1,0:T(8,128)(2,1)S(1)}, u32[]{:S(2)}, u32[]{:S(2)}) async-start(bf16[8,64,512]{2,1,0:T(8,128)(2,1)} %bitcast.22), calls=%async_computation.2 | async-start | bytes 1048576 | tf_op jit(solution)/shard_map/all_to_all | solution.py:19
  46.1 0.8 constant_dynamic-slice_fusion.13
  46.8 1.0 %collective-permute-start.7 = (bf16[512,128]{1,0:T(8,128)(2,1)}, bf16[512,128]{1,0:T(8,128)(2,1)S(1)}, u32[]{:S(2)}, u32[]{:S(2)}) collective-permute-start(bf16[512,128]{1,0:T(8,128)(2,1)} %get-tuple-element.37), channel_id=1, source_target_pairs={{0,1},{1,2},{2,3},{3,0},{4,5},{5,6},{6,7},{7,4},{8,9},{9,10},{10,1... | collective-permute-start | bytes 393224 | tf_op jit(solution)/shard_map/ppermute | solution.py:14
  47.8 1.3 %collective-permute-start.8 = (bf16[512,128]{1,0:T(8,128)(2,1)}, bf16[512,128]{1,0:T(8,128)(2,1)S(1)}, u32[]{:S(2)}, u32[]{:S(2)}) collective-permute-start(bf16[512,128]{1,0:T(8,128)(2,1)} %get-tuple-element.36), channel_id=1, source_target_pairs={{0,2},{1,3},{2,0},{3,1},{4,6},{5,7},{6,4},{7,5},{8,10},{9,11},{10,... | collective-permute-start | bytes 393224 | tf_op jit(solution)/shard_map/ppermute | solution.py:14
  49.1 1.6 %collective-permute-start.9 = (bf16[512,128]{1,0:T(8,128)(2,1)}, bf16[512,128]{1,0:T(8,128)(2,1)}, u32[]{:S(2)}, u32[]{:S(2)}) collective-permute-start(bf16[512,128]{1,0:T(8,128)(2,1)} %get-tuple-element.35), channel_id=1, source_target_pairs={{0,3},{1,0},{2,1},{3,2},{4,7},{5,4},{6,5},{7,6},{8,11},{9,8},{10,9... | collective-permute-start | bytes 393224 | tf_op jit(solution)/shard_map/ppermute | solution.py:14
  50.7 5.0 %all-to-all-done.2 = bf16[8,64,512]{2,1,0:T(8,128)(2,1)S(1)} async-done(((bf16[8,64,512]{2,1,0:T(8,128)(2,1)}), bf16[8,64,512]{2,1,0:T(8,128)(2,1)S(1)}, u32[]{:S(2)}, u32[]{:S(2)}) %all-to-all-start.2) | async-done | bytes 524320 | tf_op jit(solution)/shard_map/all_to_all | solution.py:19
  55.7 0.4 fusion.7
  56.2 0.9 %copy.31 = bf16[8,64,512]{2,1,0:T(8,128)(2,1)} copy(bf16[8,64,512]{2,0,1:T(8,128)(2,1)S(1)} %fusion.7) | data formatting | bytes 1048576 | tf_op jit(solution)/shard_map/convert_element_type | solution.py:104
  57.1 3.6 %all-to-all-start.3 = ((bf16[8,64,512]{2,1,0:T(8,128)(2,1)}), bf16[8,64,512]{2,1,0:T(8,128)(2,1)S(1)}, u32[]{:S(2)}, u32[]{:S(2)}) async-start(bf16[8,64,512]{2,1,0:T(8,128)(2,1)} %copy.31), calls=%async_computation.3 | async-start | bytes 1048576 | tf_op jit(solution)/shard_map/all_to_all | solution.py:19
  60.9 1.3 %fusion.113 = bf16[512,512]{1,0:T(8,128)(2,1)} fusion(bf16[512,512]{1,0:T(8,128)(2,1)S(1)} %fusion.33, bf16[512,512]{1,0:T(8,128)(2,1)S(1)} %copy-done.29), kind=kOutput, calls=%fused_computation.212 | convolution fusion | flops 268435456 | bytes 1572864 | tf_op jit(solution)/shard_map/dot_general | solution.py:97
  62.2 1.9 %fusion.72 = (bf16[512,128]{1,0:T(8,128)(2,1)}, bf16[512,128]{1,0:T(8,128)(2,1)}, bf16[512,128]{1,0:T(8,128)(2,1)}) fusion(bf16[512,128]{1,0:T(8,128)(2,1)S(1)} %collective-permute-done.7, bf16[512,128]{1,0:T(8,128)(2,1)S(1)} %collective-permute-done.8, bf16[512,128]{1,0:T(8,128)(2,1)} %collective-permute-done.9, f32[128]{0:T(128)S(1)} %get-tuple-element.42, ...), kind=kLoop, calls=%fused_computation.123 | loop fusion | flops 1835008 | bytes 923652 | tf_op jit(solution)/shard_map/convert_element_type | solution.py:89
  64.1 1.4 %collective-permute-start.10 = (bf16[512,128]{1,0:T(8,128)(2,1)}, bf16[512,128]{1,0:T(8,128)(2,1)}, u32[]{:S(2)}, u32[]{:S(2)}) collective-permute-start(bf16[512,128]{1,0:T(8,128)(2,1)} %get-tuple-element.27), channel_id=1, source_target_pairs={{0,1},{1,2},{2,3},{3,0},{4,5},{5,6},{6,7},{7,4},{8,9},{9,10},{10,1... | collective-permute-start | bytes 393224 | tf_op jit(solution)/shard_map/ppermute | solution.py:14
  65.5 0.9 collective-permute-start.11
  66.4 1.6 %collective-permute-start.12 = (bf16[512,128]{1,0:T(8,128)(2,1)}, bf16[512,128]{1,0:T(8,128)(2,1)}, u32[]{:S(2)}, u32[]{:S(2)}) collective-permute-start(bf16[512,128]{1,0:T(8,128)(2,1)} %get-tuple-element.26), channel_id=1, source_target_pairs={{0,3},{1,0},{2,1},{3,2},{4,7},{5,4},{6,5},{7,6},{8,11},{9,8},{10,9... | collective-permute-start | bytes 393224 | tf_op jit(solution)/shard_map/ppermute | solution.py:14
  68.0 2.4 %all-to-all-done.3 = bf16[8,64,512]{2,1,0:T(8,128)(2,1)S(1)} async-done(((bf16[8,64,512]{2,1,0:T(8,128)(2,1)}), bf16[8,64,512]{2,1,0:T(8,128)(2,1)S(1)}, u32[]{:S(2)}, u32[]{:S(2)}) %all-to-all-start.3) | async-done | bytes 524320 | tf_op jit(solution)/shard_map/all_to_all | solution.py:19
  70.4 0.6 fusion.110
  71.0 0.2 copy-done.6
  71.2 0.8 dynamic-slice_convert_fusion.1
  72.0 0.9 %collective-permute-start.6 = (bf16[128,512]{1,0:T(8,128)(2,1)}, bf16[128,512]{1,0:T(8,128)(2,1)}, u32[]{:S(2)}, u32[]{:S(2)}) collective-permute-start(bf16[128,512]{1,0:T(8,128)(2,1)} %get-tuple-element.34), channel_id=1, source_target_pairs={{0,1},{1,2},{2,3},{3,0},{4,5},{5,6},{6,7},{7,4},{8,9},{9,10},{10,1... | collective-permute-start | bytes 393224 | tf_op jit(solution)/shard_map/ppermute | solution.py:14
  73.0 0.6 copy-done.22
  73.6 0.1 copy-done.23
  73.6 1.0 %fusion.60 = bf16[512,128]{1,0:T(8,128)(2,1)S(1)} fusion(bf16[512,128]{1,0:T(8,128)(2,1)S(1)} %collective-permute-done.7, bf16[512,128]{1,0:T(8,128)(2,1)S(1)} %collective-permute-done.8, bf16[512,128]{1,0:T(8,128)(2,1)} %collective-permute-done.9, f32[128]{0:T(128)S(1)} %copy-done.22, f32[128]{0:T(128)S(1)} %copy-done.23, f32[128]{0:T(128)S(1)} %copy-done.24, ...), kind=kLoop, calls=%fused_computation.111 | loop fusion | flops 786432 | bytes 657412 | tf_op jit(solution)/shard_map/convert_element_type | solution.py:89
  74.7 1.4 %collective-permute-start.13 = (bf16[128,512]{1,0:T(8,128)(2,1)}, bf16[128,512]{1,0:T(8,128)(2,1)S(1)}, u32[]{:S(2)}, u32[]{:S(2)}) collective-permute-start(bf16[128,512]{1,0:T(8,128)(2,1)} %get-tuple-element.32), channel_id=1, source_target_pairs={{0,2},{1,3},{2,0},{3,1},{4,6},{5,7},{6,4},{7,5},{8,10},{9,11},{10,... | collective-permute-start | bytes 393224 | tf_op jit(solution)/shard_map/ppermute | solution.py:14
  76.0 3.6 %all-to-all-start.4 = ((bf16[8,64,512]{2,1,0:T(8,128)(2,1)}), bf16[8,64,512]{2,1,0:T(8,128)(2,1)S(1)}, u32[]{:S(2)}, u32[]{:S(2)}) async-start(bf16[8,64,512]{2,1,0:T(8,128)(2,1)} %bitcast.42), calls=%async_computation.4 | async-start | bytes 1048576 | tf_op jit(solution)/shard_map/all_to_all | solution.py:19
  79.7 1.7 %collective-permute-start.14 = (bf16[128,512]{1,0:T(8,128)(2,1)S(1)}, bf16[128,512]{1,0:T(8,128)(2,1)S(1)}, u32[]{:S(2)}, u32[]{:S(2)}) collective-permute-start(bf16[128,512]{1,0:T(8,128)(2,1)S(1)} %copy-done.9), channel_id=1, source_target_pairs={{0,3},{1,0},{2,1},{3,2},{4,7},{5,4},{6,5},{7,6},{8,11},{9,8},{10,9... | collective-permute-start | bytes 393224 | tf_op jit(solution)/shard_map/ppermute | solution.py:14
  81.4 0.1 fusion.73
  81.5 1.0 %fusion.74 = bf16[512,512]{1,0:T(8,128)(2,1)S(1)} fusion(bf16[512,512]{1,0:T(8,128)(2,1)S(1)} %fusion.73, s32[]{:T(128)S(6)} %select_n.80, bf16[512,128]{1,0:T(8,128)(2,1)} %collective-permute-done.10, bf16[512,512]{1,0:T(8,128)(2,1)S(1)} %fusion.33), kind=kLoop, calls=%fused_computation.134 | loop fusion | flops 262144 | bytes 393220 | tf_op jit(solution)/shard_map/dynamic_update_slice | solution.py:33
  82.5 1.0 %fusion.75 = bf16[512,512]{1,0:T(8,128)(2,1)S(1)} fusion(bf16[512,512]{1,0:T(8,128)(2,1)S(1)} %fusion.74, s32[]{:T(128)S(6)} %select_n.82, bf16[512,128]{1,0:T(8,128)(2,1)} %collective-permute-done.11, bf16[512,512]{1,0:T(8,128)(2,1)S(1)} %fusion.33), kind=kLoop, calls=%fused_computation.135 | loop fusion | flops 262144 | bytes 393220 | tf_op jit(solution)/shard_map/dynamic_update_slice | solution.py:33
  83.5 1.1 %fusion.76 = bf16[512,512]{1,0:T(8,128)(2,1)S(1)} fusion(bf16[512,512]{1,0:T(8,128)(2,1)S(1)} %fusion.75, s32[]{:T(128)S(6)} %select_n.84, bf16[512,128]{1,0:T(8,128)(2,1)} %collective-permute-done.12, bf16[512,512]{1,0:T(8,128)(2,1)S(1)} %fusion.33), kind=kLoop, calls=%fused_computation.136 | loop fusion | flops 262144 | bytes 393220 | tf_op jit(solution)/shard_map/dynamic_update_slice | solution.py:33
  84.6 4.4 %collective-permute-done.13 = bf16[128,512]{1,0:T(8,128)(2,1)S(1)} collective-permute-done((bf16[128,512]{1,0:T(8,128)(2,1)}, bf16[128,512]{1,0:T(8,128)(2,1)S(1)}, u32[]{:S(2)}, u32[]{:S(2)}) %collective-permute-start.13) | collective-permute-done | bytes 131104 | tf_op jit(solution)/shard_map/ppermute | solution.py:14
  89.0 1.7 %add_bitcast_fusion = f32[1,128,512]{2,1,0:T(8,128)} fusion(bf16[128,512]{1,0:T(8,128)(2,1)S(1)} %collective-permute-done.14, bf16[128,512]{1,0:T(8,128)(2,1)S(1)} %collective-permute-done.13, bf16[128,512]{1,0:T(8,128)(2,1)} %collective-permute-done.6, bf16[512,512]{1,0:T(8,128)(2,1)} %copy-done.8, s32[]{:T(128)S(6)} %select_n.64), kind=kLoop, calls=%fused_computation.124 | loop fusion | flops 458752 | bytes 786436 | tf_op jit(solution)/shard_map/broadcast_in_dim | solution.py:117
  90.7 2.0 %fusion.3 = bf16[512,512]{1,0:T(8,128)(2,1)} fusion(bf16[512,512]{1,0:T(8,128)(2,1)S(1)} %bitcast.112, bf16[512,512]{1,0:T(8,128)(2,1)S(1)} %copy-done.30, bf16[512,512]{1,0:T(8,128)(2,1)S(1)} %copy-done.5, bf16[512,512]{1,0:T(8,128)(2,1)S(1)} %bitcast.110, bf16[1,512,512]{2,1,0:T(8,128)(2,1)S(1)} %copy-done.25, f32[512]{0:T(512)S(1)} %copy-done.11, ...), kind=kOutput, calls=%fused_computation.20 | convolution fusion | flops 274726912 | bytes 3149824 | tf_op jit(solution)/shard_map/dot_general | solution.py:129
  92.7 0.7 convert_reduce_fusion
  (71 shorter events, 0.2 us)
Async XLA Ops:
  0.6 39.1 %copy-start = (bf16[1,512,512]{2,1,0:T(8,128)(2,1)S(1)}, bf16[1,512,512]{2,1,0:T(8,128)(2,1)}, u32[]{:S(2)}) copy-start(bf16[1,512,512]{2,1,0:T(8,128)(2,1)} %param.13) | copy-start | bytes 1572868
  0.7 0.7 copy-start.26
  1.4 1.8 %copy-start.1 = (bf16[512,512]{1,0:T(8,128)(2,1)S(1)}, bf16[512,512]{1,0:T(8,128)(2,1)}, u32[]{:S(2)}) copy-start(bf16[512,512]{1,0:T(8,128)(2,1)} %param.15) | copy-start | bytes 1572868
  3.3 14.0 %collective-permute-start = (bf16[512,128]{1,0:T(8,128)(2,1)S(1)}, bf16[512,128]{1,0:T(8,128)(2,1)S(1)}, u32[]{:S(2)}, u32[]{:S(2)}) collective-permute-start(bf16[512,128]{1,0:T(8,128)(2,1)S(1)} %get-tuple-element.38), channel_id=1, source_target_pairs={{0,1},{1,2},{2,3},{3,0},{4,5},{5,6},{6,7},{7,4},{8,9},{9,10},{10,1... | collective-permute-start | bytes 393224 | tf_op jit(solution)/shard_map/ppermute | solution.py:14
  6.4 11.2 %collective-permute-start.1 = (bf16[512,128]{1,0:T(8,128)(2,1)S(1)}, bf16[512,128]{1,0:T(8,128)(2,1)S(1)}, u32[]{:S(2)}, u32[]{:S(2)}) collective-permute-start(bf16[512,128]{1,0:T(8,128)(2,1)S(1)} %get-tuple-element.40), channel_id=1, source_target_pairs={{0,2},{1,3},{2,0},{3,1},{4,6},{5,7},{6,4},{7,5},{8,10},{9,11},{10,... | collective-permute-start | bytes 393224 | tf_op jit(solution)/shard_map/ppermute | solution.py:14
  9.0 8.6 %collective-permute-start.2 = (bf16[512,128]{1,0:T(8,128)(2,1)S(1)}, bf16[512,128]{1,0:T(8,128)(2,1)S(1)}, u32[]{:S(2)}, u32[]{:S(2)}) collective-permute-start(bf16[512,128]{1,0:T(8,128)(2,1)S(1)} %get-tuple-element.39), channel_id=1, source_target_pairs={{0,3},{1,0},{2,1},{3,2},{4,7},{5,4},{6,5},{7,6},{8,11},{9,8},{10,9... | collective-permute-start | bytes 393224 | tf_op jit(solution)/shard_map/ppermute | solution.py:14
  11.3 13.5 %all-to-all-start = ((bf16[8,64,512]{2,1,0:T(8,128)(2,1)}), bf16[8,64,512]{2,1,0:T(8,128)(2,1)S(1)}, u32[]{:S(2)}, u32[]{:S(2)}) async-start(bf16[8,64,512]{2,1,0:T(8,128)(2,1)} %bitcast.2), calls=%async_computation | async-start | bytes 1048576 | tf_op jit(solution)/shard_map/all_to_all | solution.py:19
  15.7 0.7 copy-start.10
  18.5 11.4 %collective-permute-start.3 = (bf16[512,128]{1,0:T(8,128)(2,1)}, bf16[512,128]{1,0:T(8,128)(2,1)}, u32[]{:S(2)}, u32[]{:S(2)}) collective-permute-start(bf16[512,128]{1,0:T(8,128)(2,1)} %get-tuple-element.30), channel_id=1, source_target_pairs={{0,1},{1,2},{2,3},{3,0},{4,5},{5,6},{6,7},{7,4},{8,9},{9,10},{10,1... | collective-permute-start | bytes 393224 | tf_op jit(solution)/shard_map/ppermute | solution.py:14
  21.8 10.2 %collective-permute-start.4 = (bf16[512,128]{1,0:T(8,128)(2,1)S(1)}, bf16[512,128]{1,0:T(8,128)(2,1)}, u32[]{:S(2)}, u32[]{:S(2)}) collective-permute-start(bf16[512,128]{1,0:T(8,128)(2,1)S(1)} %get-tuple-element.31), channel_id=1, source_target_pairs={{0,2},{1,3},{2,0},{3,1},{4,6},{5,7},{6,4},{7,5},{8,10},{9,11},{10,... | collective-permute-start | bytes 393224 | tf_op jit(solution)/shard_map/ppermute | solution.py:14
  23.4 9.5 %collective-permute-start.5 = (bf16[512,128]{1,0:T(8,128)(2,1)S(1)}, bf16[512,128]{1,0:T(8,128)(2,1)}, u32[]{:S(2)}, u32[]{:S(2)}) collective-permute-start(bf16[512,128]{1,0:T(8,128)(2,1)S(1)} %get-tuple-element.29), channel_id=1, source_target_pairs={{0,3},{1,0},{2,1},{3,2},{4,7},{5,4},{6,5},{7,6},{8,11},{9,8},{10,9... | collective-permute-start | bytes 393224 | tf_op jit(solution)/shard_map/ppermute | solution.py:14
  26.2 13.2 %all-to-all-start.1 = ((bf16[8,64,512]{2,1,0:T(8,128)(2,1)}), bf16[8,64,512]{2,1,0:T(8,128)(2,1)S(1)}, u32[]{:S(2)}, u32[]{:S(2)}) async-start(bf16[8,64,512]{2,1,0:T(8,128)(2,1)} %copy.28), calls=%async_computation.1 | async-start | bytes 1048576 | tf_op jit(solution)/shard_map/all_to_all | solution.py:19
  29.9 9.5 %copy-start.3 = (bf16[512,512]{1,0:T(8,128)(2,1)S(1)}, bf16[512,512]{1,0:T(8,128)(2,1)}, u32[]{:S(2)}) copy-start(bf16[512,512]{1,0:T(8,128)(2,1)} %param.8) | copy-start | bytes 1572868
  33.0 6.4 %copy-start.11 = (f32[512]{0:T(512)S(1)}, f32[512]{0:T(512)}, u32[]{:S(2)}) copy-start(f32[512]{0:T(512)} %param.10) | copy-start | bytes 6148
  39.8 1.2 %copy-start.4 = (bf16[512,512]{1,0:T(8,128)(2,1)S(1)}, bf16[512,512]{1,0:T(8,128)(2,1)}, u32[]{:S(2)}) copy-start(bf16[512,512]{1,0:T(8,128)(2,1)} %param.8) | copy-start | bytes 1572868
  40.9 1.7 %copy-start.28 = (bf16[512,512]{1,0:T(8,128)(2,1)}, bf16[512,512]{1,0:T(8,128)(2,1)S(1)}, u32[]{:S(2)}) copy-start(bf16[512,512]{1,0:T(8,128)(2,1)S(1)} %get-tuple-element.25) | copy-start | bytes 1572868
  42.6 13.2 %all-to-all-start.2 = ((bf16[8,64,512]{2,1,0:T(8,128)(2,1)}), bf16[8,64,512]{2,1,0:T(8,128)(2,1)S(1)}, u32[]{:S(2)}, u32[]{:S(2)}) async-start(bf16[8,64,512]{2,1,0:T(8,128)(2,1)} %bitcast.22), calls=%async_computation.2 | async-start | bytes 1048576 | tf_op jit(solution)/shard_map/all_to_all | solution.py:19
  46.8 15.3 %collective-permute-start.7 = (bf16[512,128]{1,0:T(8,128)(2,1)}, bf16[512,128]{1,0:T(8,128)(2,1)S(1)}, u32[]{:S(2)}, u32[]{:S(2)}) collective-permute-start(bf16[512,128]{1,0:T(8,128)(2,1)} %get-tuple-element.37), channel_id=1, source_target_pairs={{0,1},{1,2},{2,3},{3,0},{4,5},{5,6},{6,7},{7,4},{8,9},{9,10},{10,1... | collective-permute-start | bytes 393224 | tf_op jit(solution)/shard_map/ppermute | solution.py:14
  47.8 14.3 %collective-permute-start.8 = (bf16[512,128]{1,0:T(8,128)(2,1)}, bf16[512,128]{1,0:T(8,128)(2,1)S(1)}, u32[]{:S(2)}, u32[]{:S(2)}) collective-permute-start(bf16[512,128]{1,0:T(8,128)(2,1)} %get-tuple-element.36), channel_id=1, source_target_pairs={{0,2},{1,3},{2,0},{3,1},{4,6},{5,7},{6,4},{7,5},{8,10},{9,11},{10,... | collective-permute-start | bytes 393224 | tf_op jit(solution)/shard_map/ppermute | solution.py:14
  49.1 13.0 %collective-permute-start.9 = (bf16[512,128]{1,0:T(8,128)(2,1)}, bf16[512,128]{1,0:T(8,128)(2,1)}, u32[]{:S(2)}, u32[]{:S(2)}) collective-permute-start(bf16[512,128]{1,0:T(8,128)(2,1)} %get-tuple-element.35), channel_id=1, source_target_pairs={{0,3},{1,0},{2,1},{3,2},{4,7},{5,4},{6,5},{7,6},{8,11},{9,8},{10,9... | collective-permute-start | bytes 393224 | tf_op jit(solution)/shard_map/ppermute | solution.py:14
  57.1 3.6 %copy-start.29 = (bf16[512,512]{1,0:T(8,128)(2,1)S(1)}, bf16[512,512]{1,0:T(8,128)(2,1)}, u32[]{:S(2)}) copy-start(bf16[512,512]{1,0:T(8,128)(2,1)} %copy-done.28) | copy-start | bytes 1572868
  57.1 13.3 %all-to-all-start.3 = ((bf16[8,64,512]{2,1,0:T(8,128)(2,1)}), bf16[8,64,512]{2,1,0:T(8,128)(2,1)S(1)}, u32[]{:S(2)}, u32[]{:S(2)}) async-start(bf16[8,64,512]{2,1,0:T(8,128)(2,1)} %copy.31), calls=%async_computation.3 | async-start | bytes 1048576 | tf_op jit(solution)/shard_map/all_to_all | solution.py:19
  60.8 1.4 %copy-start.12 = (f32[128]{0:T(128)S(1)}, f32[128]{0:T(128)}, u32[]{:S(2)}) copy-start(f32[128]{0:T(128)} %get-tuple-element.43) | copy-start | bytes 1540
  60.8 1.4 %copy-start.13 = (f32[128]{0:T(128)S(1)}, f32[128]{0:T(128)}, u32[]{:S(2)}) copy-start(f32[128]{0:T(128)} %get-tuple-element.44) | copy-start | bytes 1540
  60.8 1.4 %copy-start.14 = (f32[128]{0:T(128)S(1)}, f32[128]{0:T(128)}, u32[]{:S(2)}) copy-start(f32[128]{0:T(128)} %get-tuple-element.45) | copy-start | bytes 1540
  60.8 1.4 %copy-start.15 = (f32[128]{0:T(128)S(1)}, f32[128]{0:T(128)}, u32[]{:S(2)}) copy-start(f32[128]{0:T(128)} %get-tuple-element.46) | copy-start | bytes 1540
  60.8 1.4 %copy-start.16 = (f32[128]{0:T(128)S(1)}, f32[128]{0:T(128)}, u32[]{:S(2)}) copy-start(f32[128]{0:T(128)} %get-tuple-element.47) | copy-start | bytes 1540
  60.8 1.4 %copy-start.17 = (f32[128]{0:T(128)S(1)}, f32[128]{0:T(128)}, u32[]{:S(2)}) copy-start(f32[128]{0:T(128)} %get-tuple-element.48) | copy-start | bytes 1540
  60.8 1.4 %copy-start.18 = (f32[128]{0:T(128)S(1)}, f32[128]{0:T(128)}, u32[]{:S(2)}) copy-start(f32[128]{0:T(128)} %get-tuple-element.49) | copy-start | bytes 1540
  60.8 1.4 %copy-start.19 = (f32[128]{0:T(128)S(1)}, f32[128]{0:T(128)}, u32[]{:S(2)}) copy-start(f32[128]{0:T(128)} %get-tuple-element.50) | copy-start | bytes 1540
  60.8 1.4 %copy-start.20 = (f32[128]{0:T(128)S(1)}, f32[128]{0:T(128)}, u32[]{:S(2)}) copy-start(f32[128]{0:T(128)} %get-tuple-element.51) | copy-start | bytes 1540
  60.8 1.4 %copy-start.21 = (f32[128]{0:T(128)S(1)}, f32[128]{0:T(128)}, u32[]{:S(2)}) copy-start(f32[128]{0:T(128)} %get-tuple-element.52) | copy-start | bytes 1540
  62.1 8.3 %copy-start.5 = (bf16[512,512]{1,0:T(8,128)(2,1)S(1)}, bf16[512,512]{1,0:T(8,128)(2,1)}, u32[]{:S(2)}) copy-start(bf16[512,512]{1,0:T(8,128)(2,1)} %param.8) | copy-start | bytes 1572868
  64.1 15.5 %collective-permute-start.10 = (bf16[512,128]{1,0:T(8,128)(2,1)}, bf16[512,128]{1,0:T(8,128)(2,1)}, u32[]{:S(2)}, u32[]{:S(2)}) collective-permute-start(bf16[512,128]{1,0:T(8,128)(2,1)} %get-tuple-element.27), channel_id=1, source_target_pairs={{0,1},{1,2},{2,3},{3,0},{4,5},{5,6},{6,7},{7,4},{8,9},{9,10},{10,1... | collective-permute-start | bytes 393224 | tf_op jit(solution)/shard_map/ppermute | solution.py:14
  65.5 4.9 %copy-start.27 = (f32[512]{0:T(512)S(1)}, f32[512]{0:T(512)}, u32[]{:S(2)}) copy-start(f32[512]{0:T(512)} %param.9) | copy-start | bytes 6148
  65.5 15.9 %collective-permute-start.11 = (bf16[512,128]{1,0:T(8,128)(2,1)}, bf16[512,128]{1,0:T(8,128)(2,1)}, u32[]{:S(2)}, u32[]{:S(2)}) collective-permute-start(bf16[512,128]{1,0:T(8,128)(2,1)} %get-tuple-element.28), channel_id=1, source_target_pairs={{0,2},{1,3},{2,0},{3,1},{4,6},{5,7},{6,4},{7,5},{8,10},{9,11},{10,... | collective-permute-start | bytes 393224 | tf_op jit(solution)/shard_map/ppermute | solution.py:14
  66.4 15.0 %collective-permute-start.12 = (bf16[512,128]{1,0:T(8,128)(2,1)}, bf16[512,128]{1,0:T(8,128)(2,1)}, u32[]{:S(2)}, u32[]{:S(2)}) collective-permute-start(bf16[512,128]{1,0:T(8,128)(2,1)} %get-tuple-element.26), channel_id=1, source_target_pairs={{0,3},{1,0},{2,1},{3,2},{4,7},{5,4},{6,5},{7,6},{8,11},{9,8},{10,9... | collective-permute-start | bytes 393224 | tf_op jit(solution)/shard_map/ppermute | solution.py:14
  70.4 0.8 copy-start.6
  71.2 3.4 %copy-start.8 = (bf16[512,512]{1,0:T(8,128)(2,1)}, bf16[512,512]{1,0:T(8,128)(2,1)S(1)}, u32[]{:S(2)}) copy-start(bf16[512,512]{1,0:T(8,128)(2,1)S(1)} %fusion.110) | copy-start | bytes 1572868
  72.0 9.4 %collective-permute-start.6 = (bf16[128,512]{1,0:T(8,128)(2,1)}, bf16[128,512]{1,0:T(8,128)(2,1)}, u32[]{:S(2)}, u32[]{:S(2)}) collective-permute-start(bf16[128,512]{1,0:T(8,128)(2,1)} %get-tuple-element.34), channel_id=1, source_target_pairs={{0,1},{1,2},{2,3},{3,0},{4,5},{5,6},{6,7},{7,4},{8,9},{9,10},{10,1... | collective-permute-start | bytes 393224 | tf_op jit(solution)/shard_map/ppermute | solution.py:14
  73.0 0.6 copy-start.22
  73.0 0.7 copy-start.23
  73.0 0.7 copy-start.24
  74.7 14.3 %collective-permute-start.13 = (bf16[128,512]{1,0:T(8,128)(2,1)}, bf16[128,512]{1,0:T(8,128)(2,1)S(1)}, u32[]{:S(2)}, u32[]{:S(2)}) collective-permute-start(bf16[128,512]{1,0:T(8,128)(2,1)} %get-tuple-element.32), channel_id=1, source_target_pairs={{0,2},{1,3},{2,0},{3,1},{4,6},{5,7},{6,4},{7,5},{8,10},{9,11},{10,... | collective-permute-start | bytes 393224 | tf_op jit(solution)/shard_map/ppermute | solution.py:14
  76.0 3.6 %copy-start.9 = (bf16[128,512]{1,0:T(8,128)(2,1)S(1)}, bf16[128,512]{1,0:T(8,128)(2,1)}, u32[]{:S(2)}) copy-start(bf16[128,512]{1,0:T(8,128)(2,1)} %get-tuple-element.33) | copy-start | bytes 393220
  76.0 16.7 %all-to-all-start.4 = ((bf16[8,64,512]{2,1,0:T(8,128)(2,1)}), bf16[8,64,512]{2,1,0:T(8,128)(2,1)S(1)}, u32[]{:S(2)}, u32[]{:S(2)}) async-start(bf16[8,64,512]{2,1,0:T(8,128)(2,1)} %bitcast.42), calls=%async_computation.4 | async-start | bytes 1048576 | tf_op jit(solution)/shard_map/all_to_all | solution.py:19
  79.7 9.3 %collective-permute-start.14 = (bf16[128,512]{1,0:T(8,128)(2,1)S(1)}, bf16[128,512]{1,0:T(8,128)(2,1)S(1)}, u32[]{:S(2)}, u32[]{:S(2)}) collective-permute-start(bf16[128,512]{1,0:T(8,128)(2,1)S(1)} %copy-done.9), channel_id=1, source_target_pairs={{0,3},{1,0},{2,1},{3,2},{4,7},{5,4},{6,5},{7,6},{8,11},{9,8},{10,9... | collective-permute-start | bytes 393224 | tf_op jit(solution)/shard_map/ppermute | solution.py:14
  82.5 8.2 %copy-start.30 = (bf16[512,512]{1,0:T(8,128)(2,1)S(1)}, bf16[512,512]{1,0:T(8,128)(2,1)}, u32[]{:S(2)}) copy-start(bf16[512,512]{1,0:T(8,128)(2,1)} %get-tuple-element.73) | copy-start | bytes 1572868
  83.5 7.2 %copy-start.7 = (bf16[8,64,512]{2,1,0:T(8,128)(2,1)S(1)}, bf16[8,64,512]{2,1,0:T(8,128)(2,1)}, u32[]{:S(2)}) copy-start(bf16[8,64,512]{2,1,0:T(8,128)(2,1)} %copy-done.6) | copy-start | bytes 1572868
  83.5 7.2 %copy-start.25 = (bf16[1,512,512]{2,1,0:T(8,128)(2,1)S(1)}, bf16[1,512,512]{2,1,0:T(8,128)(2,1)}, u32[]{:S(2)}) copy-start(bf16[1,512,512]{2,1,0:T(8,128)(2,1)} %param.11) | copy-start | bytes 1572868
  84.6 8.1 %copy-start.2 = (bf16[512,512]{1,0:T(8,128)(2,1)}, bf16[512,512]{1,0:T(8,128)(2,1)S(1)}, u32[]{:S(2)}) copy-start(bf16[512,512]{1,0:T(8,128)(2,1)S(1)} %fusion.76) | copy-start | bytes 1572868

commit v8 on v6

--- a/solution.py
+++ b/solution.py
@@ -105,6 +105,8 @@
     first_grad = swap(first_out, "seq").reshape(rows, width)
     first_grad, channel_part = lax.optimization_barrier((first_grad, channel_part))
     block_part = jnp.dot(first_grad, gated.T, preferred_element_type=F32)
+    block_part, early_added = lax.optimization_barrier((block_part, added_back[1]))
+    added_back[1] = early_added
     cq = block_part.shape[0] // m
     block_arrived = exchange(
         [lax.dynamic_slice_in_dim(block_part, t * cq, cq, 0).astype(BF16) for t in chunk_of],

time: 93.2 us -> 98 us (1.052)
  waiting for transfers between devices: 17.1 us -> 20.9 us
  starting transfers between devices: 42.7 us -> 44.3 us
    all_to_all x5, waiting for transfers between devices: 11.5 us -> 13.8 us  [swap(): return lax.all_to_all(pieces, axis_name, 0, 0, tiled=True)]
    ppermute x15, waiting for transfers between devices: 5.63 us -> 7.08 us  [exchange(): lax.ppermute(pieces[k], axis_name, [(i, (i + k) % n) for i in range(n)])]
    ppermute x15, starting transfers between devices: 24.9 us -> 26.1 us  [exchange(): lax.ppermute(pieces[k], axis_name, [(i, (i + k) % n) for i in range(n)])]
    unnamed x59 -> x57, local copies, waits for them, and re-layouts: 2.49 us -> 2.5 us
  transfers between devices with their start and end apart: 20 -> 20, of which waited for: 8 -> 8; matrix products, arithmetic and copies ran while one was open for 25% -> 23% of each run, Pallas kernels for 0% -> 0%
where the time goes in v8:
time: 98 us; the launch traced here: 97.1 us
  starting transfers between devices  44.3 us (45%)
  waiting for transfers between devices  20.9 us (21%)
  other arithmetic  10.5 us (11%)
  matrix products  10.3 us (11%)
  local copies, waits for them, and re-layouts  9.96 us (10%)
  between operations  1.17 us (1%)
    ppermute x15, starting transfers between devices, exchange(): lax.ppermute(pieces[k], axis_name, [(i, (i + k) % n) for i in range(n)])  26.1 us
    all_to_all x5, starting transfers between devices, swap(): return lax.all_to_all(pieces, axis_name, 0, 0, tiled=True)  18.2 us
    all_to_all x5, waiting for transfers between devices, swap(): return lax.all_to_all(pieces, axis_name, 0, 0, tiled=True)  13.8 us
    ppermute x15, waiting for transfers between devices, exchange(): lax.ppermute(pieces[k], axis_name, [(i, (i + k) % n) for i in range(n)])  7.08 us
    convert_element_type x2, other arithmetic, on_device(): added_out = [sum((act_arrived[k].astype(F32) * coefficient(origin_of[k],...  3.52 us
    dot_general x1, matrix products, on_device(): spread = jnp.dot(first_blocks[0].T, first_grad, preferred_element_type=F32)  3.19 us
    dynamic_update_slice x3, local copies, waits for them, and re-layouts, place_chunks(): out = lax.dynamic_update_slice_in_dim(out, chunk, start, axis=1)  2.87 us
    unnamed x57, local copies, waits for them, and re-layouts  2.5 us
  transfers between devices with their start and end apart: 20, of which 8 were waited for; matrix products, arithmetic and copies ran while one was open for 23% of the time, Pallas kernels for 0%

profile of v8, /device:TPU:0, one launch (start us, length us, event | category | flops | bytes accessed | tf_op | source)
XLA Modules:
  0.0 97.1 jit_solution(2769294659575712106)
XLA Ops:
  0.6 0.0 copy-start
  0.7 0.7 copy-done.24
  1.4 1.8 %fusion.8 = bf16[512,512]{0,1:T(8,128)(2,1)S(1)} fusion(bf16[1,512,512]{2,1,0:T(8,128)(2,1)} %param.11, bf16[512,512]{1,0:T(8,128)(2,1)} %param.8, f32[512]{0:T(512)S(1)} %copy-done.24), kind=kOutput, calls=%fused_computation.25 | convolution fusion | flops 270532608 | bytes 1574912 | tf_op jit(solution)/shard_map/dot_general | solution.py:59
  3.2 0.1 constant_dynamic-slice_fusion.35
  3.3 3.1 %collective-permute-start = (bf16[512,128]{1,0:T(8,128)(2,1)S(1)}, bf16[512,128]{1,0:T(8,128)(2,1)S(1)}, u32[]{:S(2)}, u32[]{:S(2)}) collective-permute-start(bf16[512,128]{1,0:T(8,128)(2,1)S(1)} %get-tuple-element.40), channel_id=1, source_target_pairs={{0,1},{1,2},{2,3},{3,0},{4,5},{5,6},{6,7},{7,4},{8,9},{9,10},{10,1... | collective-permute-start | bytes 393224 | tf_op jit(solution)/shard_map/ppermute | solution.py:14
  6.4 2.6 %collective-permute-start.1 = (bf16[512,128]{1,0:T(8,128)(2,1)S(1)}, bf16[512,128]{1,0:T(8,128)(2,1)S(1)}, u32[]{:S(2)}, u32[]{:S(2)}) collective-permute-start(bf16[512,128]{1,0:T(8,128)(2,1)S(1)} %get-tuple-element.42), channel_id=1, source_target_pairs={{0,2},{1,3},{2,0},{3,1},{4,6},{5,7},{6,4},{7,5},{8,10},{9,11},{10,... | collective-permute-start | bytes 393224 | tf_op jit(solution)/shard_map/ppermute | solution.py:14
  9.0 1.3 %collective-permute-start.2 = (bf16[512,128]{1,0:T(8,128)(2,1)S(1)}, bf16[512,128]{1,0:T(8,128)(2,1)S(1)}, u32[]{:S(2)}, u32[]{:S(2)}) collective-permute-start(bf16[512,128]{1,0:T(8,128)(2,1)S(1)} %get-tuple-element.41), channel_id=1, source_target_pairs={{0,3},{1,0},{2,1},{3,2},{4,7},{5,4},{6,5},{7,6},{8,11},{9,8},{10,9... | collective-permute-start | bytes 393224 | tf_op jit(solution)/shard_map/ppermute | solution.py:14
  10.3 1.0 %copy.25 = bf16[512,512]{1,0:T(8,128)(2,1)} copy(bf16[512,512]{0,1:T(8,128)(2,1)S(1)} %fusion.8) | data formatting | bytes 1048576 | tf_op jit(solution)/shard_map/optimization_barrier | solution.py:62
  11.3 3.7 %all-to-all-start = ((bf16[8,64,512]{2,1,0:T(8,128)(2,1)}), bf16[8,64,512]{2,1,0:T(8,128)(2,1)S(1)}, u32[]{:S(2)}, u32[]{:S(2)}) async-start(bf16[8,64,512]{2,1,0:T(8,128)(2,1)} %bitcast.2), calls=%async_computation | async-start | bytes 1048576 | tf_op jit(solution)/shard_map/all_to_all | solution.py:19
  15.0 0.7 fusion.78
  15.7 0.7 copy-done.9
  16.5 0.1 copy.30
  16.7 0.7 fusion.106
  17.4 0.2 collective-permute-done.1
  17.6 0.9 fusion.56
  18.5 3.3 %collective-permute-start.3 = (bf16[512,128]{1,0:T(8,128)(2,1)}, bf16[512,128]{1,0:T(8,128)(2,1)}, u32[]{:S(2)}, u32[]{:S(2)}) collective-permute-start(bf16[512,128]{1,0:T(8,128)(2,1)} %get-tuple-element.32), channel_id=1, source_target_pairs={{0,1},{1,2},{2,3},{3,0},{4,5},{5,6},{6,7},{7,4},{8,9},{9,10},{10,1... | collective-permute-start | bytes 393224 | tf_op jit(solution)/shard_map/ppermute | solution.py:14
  21.8 1.6 %collective-permute-start.4 = (bf16[512,128]{1,0:T(8,128)(2,1)S(1)}, bf16[512,128]{1,0:T(8,128)(2,1)}, u32[]{:S(2)}, u32[]{:S(2)}) collective-permute-start(bf16[512,128]{1,0:T(8,128)(2,1)S(1)} %get-tuple-element.33), channel_id=1, source_target_pairs={{0,2},{1,3},{2,0},{3,1},{4,6},{5,7},{6,4},{7,5},{8,10},{9,11},{10,... | collective-permute-start | bytes 393224 | tf_op jit(solution)/shard_map/ppermute | solution.py:14
  23.4 0.7 collective-permute-start.5
  24.2 0.6 all-to-all-done
  24.8 0.4 fusion.6
  25.2 0.9 copy.28
  26.2 3.5 %all-to-all-start.1 = ((bf16[8,64,512]{2,1,0:T(8,128)(2,1)}), bf16[8,64,512]{2,1,0:T(8,128)(2,1)S(1)}, u32[]{:S(2)}, u32[]{:S(2)}) async-start(bf16[8,64,512]{2,1,0:T(8,128)(2,1)} %copy.28), calls=%async_computation.1 | async-start | bytes 1048576 | tf_op jit(solution)/shard_map/all_to_all | solution.py:19
  29.7 0.1 fusion.77
  29.9 1.0 %constant_dynamic-update-slice_fusion.2 = bf16[512,512]{1,0:T(8,128)(2,1)S(1)} fusion(bf16[512,512]{1,0:T(8,128)(2,1)S(1)} %fusion.77, bf16[512,128]{1,0:T(8,128)(2,1)} %collective-permute-done.3, s32[]{:T(128)S(6)} %select_n.80), kind=kLoop, calls=%fused_computation.166 | loop fusion | bytes 262148 | tf_op jit(solution)/shard_map/dynamic_update_slice | solution.py:33
  30.9 1.1 %collective-permute-done.4 = bf16[512,128]{1,0:T(8,128)(2,1)} collective-permute-done((bf16[512,128]{1,0:T(8,128)(2,1)S(1)}, bf16[512,128]{1,0:T(8,128)(2,1)}, u32[]{:S(2)}, u32[]{:S(2)}) %collective-permute-start.4) | collective-permute-done | bytes 131104 | tf_op jit(solution)/shard_map/ppermute | solution.py:14
  32.0 0.9 constant_dynamic-update-slice_fusion.1
  33.0 0.9 constant_dynamic-update-slice_fusion
  33.9 5.4 %all-to-all-done.1 = bf16[8,64,512]{2,1,0:T(8,128)(2,1)S(1)} async-done(((bf16[8,64,512]{2,1,0:T(8,128)(2,1)}), bf16[8,64,512]{2,1,0:T(8,128)(2,1)S(1)}, u32[]{:S(2)}, u32[]{:S(2)}) %all-to-all-start.1) | async-done | bytes 524320 | tf_op jit(solution)/shard_map/all_to_all | solution.py:19
  39.4 0.4 fusion.33
  39.8 1.1 %multiply_convert_fusion = (bf16[512,512]{1,0:T(8,128)(2,1)S(1)}, bf16[512,512]{1,0:T(8,128)(2,1)S(1)}) fusion(bf16[512,512]{1,0:T(8,128)(2,1)S(1)} %constant_dynamic-update-slice_fusion, bf16[512,512]{1,0:T(8,128)(2,1)S(1)} %fusion.33, bf16[1,512,512]{2,1,0:T(8,128)(2,1)S(1)} %copy-done), kind=kOutput, calls=%fused_computation.52 | convolution fusion | flops 274464768 | bytes 2621440 | tf_op jit(solution)/shard_map/dot_general | solution.py:81
  40.9 1.6 %fusion.24 = (bf16[512,512]{1,0:T(8,128)(2,1)}, bf16[512,512]{1,0:T(8,128)(2,1)}) fusion(bf16[512,512]{1,0:T(8,128)(2,1)S(1)} %copy-done.4, f32[512]{0:T(512)S(1)} %copy-done.10, bf16[512,512]{1,0:T(8,128)(2,1)S(1)} %get-tuple-element.27, bf16[1,512,512]{2,1,0:T(8,128)(2,1)S(1)} %copy-done, bf16[512,512]{1,0:T(8,128)(2,1)S(1)} %copy-done.1), kind=kOutput, calls=%fused_computation.41 | convolution fusion | flops 271319040 | bytes 3147776 | tf_op jit(solution)/shard_map/dot_general | solution.py:95
  42.5 3.5 %all-to-all-start.2 = ((bf16[8,64,512]{2,1,0:T(8,128)(2,1)}), bf16[8,64,512]{2,1,0:T(8,128)(2,1)S(1)}, u32[]{:S(2)}, u32[]{:S(2)}) async-start(bf16[8,64,512]{2,1,0:T(8,128)(2,1)} %bitcast.22), calls=%async_computation.2 | async-start | bytes 1048576 | tf_op jit(solution)/shard_map/all_to_all | solution.py:19
  46.0 0.1 constant_dynamic-slice_fusion.12
  46.1 1.0 %collective-permute-start.6 = (bf16[512,128]{1,0:T(8,128)(2,1)S(1)}, bf16[512,128]{1,0:T(8,128)(2,1)S(1)}, u32[]{:S(2)}, u32[]{:S(2)}) collective-permute-start(bf16[512,128]{1,0:T(8,128)(2,1)S(1)} %get-tuple-element.39), channel_id=1, source_target_pairs={{0,1},{1,2},{2,3},{3,0},{4,5},{5,6},{6,7},{7,4},{8,9},{9,10},{10,1... | collective-permute-start | bytes 393224 | tf_op jit(solution)/shard_map/ppermute | solution.py:14
  47.1 1.3 %collective-permute-start.7 = (bf16[512,128]{1,0:T(8,128)(2,1)S(1)}, bf16[512,128]{1,0:T(8,128)(2,1)S(1)}, u32[]{:S(2)}, u32[]{:S(2)}) collective-permute-start(bf16[512,128]{1,0:T(8,128)(2,1)S(1)} %get-tuple-element.38), channel_id=1, source_target_pairs={{0,2},{1,3},{2,0},{3,1},{4,6},{5,7},{6,4},{7,5},{8,10},{9,11},{10,... | collective-permute-start | bytes 393224 | tf_op jit(solution)/shard_map/ppermute | solution.py:14
  48.4 1.6 %collective-permute-start.8 = (bf16[512,128]{1,0:T(8,128)(2,1)S(1)}, bf16[512,128]{1,0:T(8,128)(2,1)}, u32[]{:S(2)}, u32[]{:S(2)}) collective-permute-start(bf16[512,128]{1,0:T(8,128)(2,1)S(1)} %get-tuple-element.37), channel_id=1, source_target_pairs={{0,3},{1,0},{2,1},{3,2},{4,7},{5,4},{6,5},{7,6},{8,11},{9,8},{10,9... | collective-permute-start | bytes 393224 | tf_op jit(solution)/shard_map/ppermute | solution.py:14
  50.0 1.3 %fusion.113 = bf16[512,512]{1,0:T(8,128)(2,1)} fusion(bf16[512,512]{1,0:T(8,128)(2,1)S(1)} %fusion.33, bf16[512,512]{1,0:T(8,128)(2,1)S(1)} %copy-done.27), kind=kOutput, calls=%fused_computation.212 | convolution fusion | flops 268435456 | bytes 1572864 | tf_op jit(solution)/shard_map/dot_general | solution.py:97
  51.3 4.4 %all-to-all-done.2 = bf16[8,64,512]{2,1,0:T(8,128)(2,1)S(1)} async-done(((bf16[8,64,512]{2,1,0:T(8,128)(2,1)}), bf16[8,64,512]{2,1,0:T(8,128)(2,1)S(1)}, u32[]{:S(2)}, u32[]{:S(2)}) %all-to-all-start.2) | async-done | bytes 524320 | tf_op jit(solution)/shard_map/all_to_all | solution.py:19
  55.7 0.4 fusion.7
  56.1 0.9 copy.31
  57.1 3.5 %all-to-all-start.3 = ((bf16[8,64,512]{2,1,0:T(8,128)(2,1)}), bf16[8,64,512]{2,1,0:T(8,128)(2,1)S(1)}, u32[]{:S(2)}, u32[]{:S(2)}) async-start(bf16[8,64,512]{2,1,0:T(8,128)(2,1)} %copy.31), calls=%async_computation.3 | async-start | bytes 1048576 | tf_op jit(solution)/shard_map/all_to_all | solution.py:19
  60.7 0.6 copy-done.11
  61.3 0.0 copy-done.12
  61.3 1.9 %fusion.72 = (bf16[512,128]{1,0:T(8,128)(2,1)}, bf16[512,128]{1,0:T(8,128)(2,1)S(1)}, bf16[512,128]{1,0:T(8,128)(2,1)}) fusion(bf16[512,128]{1,0:T(8,128)(2,1)S(1)} %collective-permute-done.6, bf16[512,128]{1,0:T(8,128)(2,1)S(1)} %collective-permute-done.7, bf16[512,128]{1,0:T(8,128)(2,1)} %collective-permute-done.8, f32[128]{0:T(128)S(1)} %get-tuple-element.44, ...), kind=kLoop, calls=%fused_computation.123 | loop fusion | flops 1835008 | bytes 923652 | tf_op jit(solution)/shard_map/convert_element_type | solution.py:89
  63.2 0.9 collective-permute-start.11
  64.1 3.5 %collective-permute-start.12 = (bf16[512,128]{1,0:T(8,128)(2,1)}, bf16[512,128]{1,0:T(8,128)(2,1)}, u32[]{:S(2)}, u32[]{:S(2)}) collective-permute-start(bf16[512,128]{1,0:T(8,128)(2,1)} %get-tuple-element.28), channel_id=1, source_target_pairs={{0,3},{1,0},{2,1},{3,2},{4,7},{5,4},{6,5},{7,6},{8,11},{9,8},{10,9... | collective-permute-start | bytes 393224 | tf_op jit(solution)/shard_map/ppermute | solution.py:14
  67.6 1.7 %fusion.60 = bf16[512,128]{1,0:T(8,128)(2,1)} fusion(bf16[512,128]{1,0:T(8,128)(2,1)S(1)} %collective-permute-done.6, bf16[512,128]{1,0:T(8,128)(2,1)S(1)} %collective-permute-done.7, bf16[512,128]{1,0:T(8,128)(2,1)} %collective-permute-done.8, f32[128]{0:T(128)S(1)} %copy-done.20, f32[128]{0:T(128)S(1)} %copy-done.21, f32[128]{0:T(128)S(1)} %copy-done.22, ...), kind=kLoop, calls=%fused_computation.111 | loop fusion | flops 786432 | bytes 657412 | tf_op jit(solution)/shard_map/convert_element_type | solution.py:89
  69.3 1.0 %all-to-all-done.3 = bf16[8,64,512]{2,1,0:T(8,128)(2,1)S(1)} async-done(((bf16[8,64,512]{2,1,0:T(8,128)(2,1)}), bf16[8,64,512]{2,1,0:T(8,128)(2,1)S(1)}, u32[]{:S(2)}, u32[]{:S(2)}) %all-to-all-start.3) | async-done | bytes 524320 | tf_op jit(solution)/shard_map/all_to_all | solution.py:19
  70.3 0.6 fusion.110
  70.8 0.2 copy-done.6
  71.1 5.7 %collective-permute-done.9 = bf16[512,128]{1,0:T(8,128)(2,1)S(1)} collective-permute-done((bf16[512,128]{1,0:T(8,128)(2,1)}, bf16[512,128]{1,0:T(8,128)(2,1)S(1)}, u32[]{:S(2)}, u32[]{:S(2)}) %collective-permute-start.9) | collective-permute-done | bytes 131104 | tf_op jit(solution)/shard_map/ppermute | solution.py:14
  76.7 0.7 dynamic-slice_convert_fusion.1
  77.5 0.4 collective-permute-start.10
  77.9 3.2 %collective-permute-start.13 = (bf16[128,512]{1,0:T(8,128)(2,1)}, bf16[128,512]{1,0:T(8,128)(2,1)}, u32[]{:S(2)}, u32[]{:S(2)}) collective-permute-start(bf16[128,512]{1,0:T(8,128)(2,1)} %get-tuple-element.34), channel_id=1, source_target_pairs={{0,2},{1,3},{2,0},{3,1},{4,6},{5,7},{6,4},{7,5},{8,10},{9,11},{10,... | collective-permute-start | bytes 393224 | tf_op jit(solution)/shard_map/ppermute | solution.py:14
  81.1 1.5 %collective-permute-start.14 = (bf16[128,512]{1,0:T(8,128)(2,1)S(1)}, bf16[128,512]{1,0:T(8,128)(2,1)}, u32[]{:S(2)}, u32[]{:S(2)}) collective-permute-start(bf16[128,512]{1,0:T(8,128)(2,1)S(1)} %get-tuple-element.35), channel_id=1, source_target_pairs={{0,3},{1,0},{2,1},{3,2},{4,7},{5,4},{6,5},{7,6},{8,11},{9,8},{10,9... | collective-permute-start | bytes 393224 | tf_op jit(solution)/shard_map/ppermute | solution.py:14
  82.6 4.0 %all-to-all-start.4 = ((bf16[8,64,512]{2,1,0:T(8,128)(2,1)}), bf16[8,64,512]{2,1,0:T(8,128)(2,1)S(1)}, u32[]{:S(2)}, u32[]{:S(2)}) async-start(bf16[8,64,512]{2,1,0:T(8,128)(2,1)} %bitcast.42), calls=%async_computation.4 | async-start | bytes 1048576 | tf_op jit(solution)/shard_map/all_to_all | solution.py:19
  86.6 3.2 %fusion.3 = bf16[512,512]{1,0:T(8,128)(2,1)} fusion(bf16[512,512]{1,0:T(8,128)(2,1)S(1)} %bitcast.112, bf16[512,512]{1,0:T(8,128)(2,1)} %get-tuple-element.75, bf16[512,512]{1,0:T(8,128)(2,1)S(1)} %copy-done.5, bf16[512,512]{1,0:T(8,128)(2,1)S(1)} %bitcast.110, bf16[1,512,512]{2,1,0:T(8,128)(2,1)} %param.11, f32[512]{0:T(512)S(1)} %copy-done.10, ...), kind=kOutput, calls=%fused_computation.20 | convolution fusion | flops 274726912 | bytes 3149824 | tf_op jit(solution)/shard_map/dot_general | solution.py:129
  89.9 0.1 fusion.73
  90.0 0.1 fusion.74
  90.0 1.0 fusion.75
  91.0 1.0 fusion.76
  92.0 2.0 %add_bitcast_fusion = f32[1,128,512]{2,1,0:T(8,128)} fusion(bf16[128,512]{1,0:T(8,128)(2,1)} %collective-permute-done.14, bf16[128,512]{1,0:T(8,128)(2,1)} %collective-permute-done.13, bf16[128,512]{1,0:T(8,128)(2,1)} %collective-permute-done.10, bf16[512,512]{1,0:T(8,128)(2,1)} %copy-done.8, s32[]{:T(128)S(6)} %select_n.64), kind=kLoop, calls=%fused_computation.124 | loop fusion | flops 458752 | bytes 786436 | tf_op jit(solution)/shard_map/broadcast_in_dim | solution.py:117
  94.0 2.4 %all-to-all-done.4 = bf16[8,64,512]{2,1,0:T(8,128)(2,1)S(1)} async-done(((bf16[8,64,512]{2,1,0:T(8,128)(2,1)}), bf16[8,64,512]{2,1,0:T(8,128)(2,1)S(1)}, u32[]{:S(2)}, u32[]{:S(2)}) %all-to-all-start.4) | async-done | bytes 524320 | tf_op jit(solution)/shard_map/all_to_all | solution.py:19
  96.4 0.7 convert_reduce_fusion
  (65 shorter events, 0.2 us)
Async XLA Ops:
  0.6 39.1 %copy-start = (bf16[1,512,512]{2,1,0:T(8,128)(2,1)S(1)}, bf16[1,512,512]{2,1,0:T(8,128)(2,1)}, u32[]{:S(2)}) copy-start(bf16[1,512,512]{2,1,0:T(8,128)(2,1)} %param.13) | copy-start | bytes 1572868
  0.7 0.7 copy-start.24
  1.4 1.8 %copy-start.1 = (bf16[512,512]{1,0:T(8,128)(2,1)S(1)}, bf16[512,512]{1,0:T(8,128)(2,1)}, u32[]{:S(2)}) copy-start(bf16[512,512]{1,0:T(8,128)(2,1)} %param.15) | copy-start | bytes 1572868
  3.3 14.1 %collective-permute-start = (bf16[512,128]{1,0:T(8,128)(2,1)S(1)}, bf16[512,128]{1,0:T(8,128)(2,1)S(1)}, u32[]{:S(2)}, u32[]{:S(2)}) collective-permute-start(bf16[512,128]{1,0:T(8,128)(2,1)S(1)} %get-tuple-element.40), channel_id=1, source_target_pairs={{0,1},{1,2},{2,3},{3,0},{4,5},{5,6},{6,7},{7,4},{8,9},{9,10},{10,1... | collective-permute-start | bytes 393224 | tf_op jit(solution)/shard_map/ppermute | solution.py:14
  6.4 11.2 %collective-permute-start.1 = (bf16[512,128]{1,0:T(8,128)(2,1)S(1)}, bf16[512,128]{1,0:T(8,128)(2,1)S(1)}, u32[]{:S(2)}, u32[]{:S(2)}) collective-permute-start(bf16[512,128]{1,0:T(8,128)(2,1)S(1)} %get-tuple-element.42), channel_id=1, source_target_pairs={{0,2},{1,3},{2,0},{3,1},{4,6},{5,7},{6,4},{7,5},{8,10},{9,11},{10,... | collective-permute-start | bytes 393224 | tf_op jit(solution)/shard_map/ppermute | solution.py:14
  9.0 8.6 %collective-permute-start.2 = (bf16[512,128]{1,0:T(8,128)(2,1)S(1)}, bf16[512,128]{1,0:T(8,128)(2,1)S(1)}, u32[]{:S(2)}, u32[]{:S(2)}) collective-permute-start(bf16[512,128]{1,0:T(8,128)(2,1)S(1)} %get-tuple-element.41), channel_id=1, source_target_pairs={{0,3},{1,0},{2,1},{3,2},{4,7},{5,4},{6,5},{7,6},{8,11},{9,8},{10,9... | collective-permute-start | bytes 393224 | tf_op jit(solution)/shard_map/ppermute | solution.py:14
  11.3 13.5 %all-to-all-start = ((bf16[8,64,512]{2,1,0:T(8,128)(2,1)}), bf16[8,64,512]{2,1,0:T(8,128)(2,1)S(1)}, u32[]{:S(2)}, u32[]{:S(2)}) async-start(bf16[8,64,512]{2,1,0:T(8,128)(2,1)} %bitcast.2), calls=%async_computation | async-start | bytes 1048576 | tf_op jit(solution)/shard_map/all_to_all | solution.py:19
  15.7 0.7 copy-start.9
  18.5 11.4 %collective-permute-start.3 = (bf16[512,128]{1,0:T(8,128)(2,1)}, bf16[512,128]{1,0:T(8,128)(2,1)}, u32[]{:S(2)}, u32[]{:S(2)}) collective-permute-start(bf16[512,128]{1,0:T(8,128)(2,1)} %get-tuple-element.32), channel_id=1, source_target_pairs={{0,1},{1,2},{2,3},{3,0},{4,5},{5,6},{6,7},{7,4},{8,9},{9,10},{10,1... | collective-permute-start | bytes 393224 | tf_op jit(solution)/shard_map/ppermute | solution.py:14
  21.8 10.2 %collective-permute-start.4 = (bf16[512,128]{1,0:T(8,128)(2,1)S(1)}, bf16[512,128]{1,0:T(8,128)(2,1)}, u32[]{:S(2)}, u32[]{:S(2)}) collective-permute-start(bf16[512,128]{1,0:T(8,128)(2,1)S(1)} %get-tuple-element.33), channel_id=1, source_target_pairs={{0,2},{1,3},{2,0},{3,1},{4,6},{5,7},{6,4},{7,5},{8,10},{9,11},{10,... | collective-permute-start | bytes 393224 | tf_op jit(solution)/shard_map/ppermute | solution.py:14
  23.4 9.6 %collective-permute-start.5 = (bf16[512,128]{1,0:T(8,128)(2,1)S(1)}, bf16[512,128]{1,0:T(8,128)(2,1)}, u32[]{:S(2)}, u32[]{:S(2)}) collective-permute-start(bf16[512,128]{1,0:T(8,128)(2,1)S(1)} %get-tuple-element.31), channel_id=1, source_target_pairs={{0,3},{1,0},{2,1},{3,2},{4,7},{5,4},{6,5},{7,6},{8,11},{9,8},{10,9... | collective-permute-start | bytes 393224 | tf_op jit(solution)/shard_map/ppermute | solution.py:14
  26.2 13.2 %all-to-all-start.1 = ((bf16[8,64,512]{2,1,0:T(8,128)(2,1)}), bf16[8,64,512]{2,1,0:T(8,128)(2,1)S(1)}, u32[]{:S(2)}, u32[]{:S(2)}) async-start(bf16[8,64,512]{2,1,0:T(8,128)(2,1)} %copy.28), calls=%async_computation.1 | async-start | bytes 1048576 | tf_op jit(solution)/shard_map/all_to_all | solution.py:19
  29.9 9.5 %copy-start.3 = (bf16[512,512]{1,0:T(8,128)(2,1)S(1)}, bf16[512,512]{1,0:T(8,128)(2,1)}, u32[]{:S(2)}) copy-start(bf16[512,512]{1,0:T(8,128)(2,1)} %param.8) | copy-start | bytes 1572868
  33.0 6.4 %copy-start.10 = (f32[512]{0:T(512)S(1)}, f32[512]{0:T(512)}, u32[]{:S(2)}) copy-start(f32[512]{0:T(512)} %param.10) | copy-start | bytes 6148
  39.8 1.2 %copy-start.4 = (bf16[512,512]{1,0:T(8,128)(2,1)S(1)}, bf16[512,512]{1,0:T(8,128)(2,1)}, u32[]{:S(2)}) copy-start(bf16[512,512]{1,0:T(8,128)(2,1)} %param.8) | copy-start | bytes 1572868
  40.9 1.6 %copy-start.26 = (bf16[512,512]{1,0:T(8,128)(2,1)}, bf16[512,512]{1,0:T(8,128)(2,1)S(1)}, u32[]{:S(2)}) copy-start(bf16[512,512]{1,0:T(8,128)(2,1)S(1)} %get-tuple-element.27) | copy-start | bytes 1572868
  42.5 13.2 %all-to-all-start.2 = ((bf16[8,64,512]{2,1,0:T(8,128)(2,1)}), bf16[8,64,512]{2,1,0:T(8,128)(2,1)S(1)}, u32[]{:S(2)}, u32[]{:S(2)}) async-start(bf16[8,64,512]{2,1,0:T(8,128)(2,1)} %bitcast.22), calls=%async_computation.2 | async-start | bytes 1048576 | tf_op jit(solution)/shard_map/all_to_all | solution.py:19
  46.0 4.0 %copy-start.27 = (bf16[512,512]{1,0:T(8,128)(2,1)S(1)}, bf16[512,512]{1,0:T(8,128)(2,1)}, u32[]{:S(2)}) copy-start(bf16[512,512]{1,0:T(8,128)(2,1)} %copy-done.26) | copy-start | bytes 1572868
  46.1 14.5 %collective-permute-start.6 = (bf16[512,128]{1,0:T(8,128)(2,1)S(1)}, bf16[512,128]{1,0:T(8,128)(2,1)S(1)}, u32[]{:S(2)}, u32[]{:S(2)}) collective-permute-start(bf16[512,128]{1,0:T(8,128)(2,1)S(1)} %get-tuple-element.39), channel_id=1, source_target_pairs={{0,1},{1,2},{2,3},{3,0},{4,5},{5,6},{6,7},{7,4},{8,9},{9,10},{10,1... | collective-permute-start | bytes 393224 | tf_op jit(solution)/shard_map/ppermute | solution.py:14
  47.1 13.5 %collective-permute-start.7 = (bf16[512,128]{1,0:T(8,128)(2,1)S(1)}, bf16[512,128]{1,0:T(8,128)(2,1)S(1)}, u32[]{:S(2)}, u32[]{:S(2)}) collective-permute-start(bf16[512,128]{1,0:T(8,128)(2,1)S(1)} %get-tuple-element.38), channel_id=1, source_target_pairs={{0,2},{1,3},{2,0},{3,1},{4,6},{5,7},{6,4},{7,5},{8,10},{9,11},{10,... | collective-permute-start | bytes 393224 | tf_op jit(solution)/shard_map/ppermute | solution.py:14
  48.4 12.2 %collective-permute-start.8 = (bf16[512,128]{1,0:T(8,128)(2,1)S(1)}, bf16[512,128]{1,0:T(8,128)(2,1)}, u32[]{:S(2)}, u32[]{:S(2)}) collective-permute-start(bf16[512,128]{1,0:T(8,128)(2,1)S(1)} %get-tuple-element.37), channel_id=1, source_target_pairs={{0,3},{1,0},{2,1},{3,2},{4,7},{5,4},{6,5},{7,6},{8,11},{9,8},{10,9... | collective-permute-start | bytes 393224 | tf_op jit(solution)/shard_map/ppermute | solution.py:14
  57.0 3.6 %copy-start.14 = (f32[128]{0:T(128)S(1)}, f32[128]{0:T(128)}, u32[]{:S(2)}) copy-start(f32[128]{0:T(128)} %get-tuple-element.48) | copy-start | bytes 1540
  57.0 3.6 %copy-start.15 = (f32[128]{0:T(128)S(1)}, f32[128]{0:T(128)}, u32[]{:S(2)}) copy-start(f32[128]{0:T(128)} %get-tuple-element.49) | copy-start | bytes 1540
  57.0 3.6 %copy-start.16 = (f32[128]{0:T(128)S(1)}, f32[128]{0:T(128)}, u32[]{:S(2)}) copy-start(f32[128]{0:T(128)} %get-tuple-element.50) | copy-start | bytes 1540
  57.0 3.6 %copy-start.17 = (f32[128]{0:T(128)S(1)}, f32[128]{0:T(128)}, u32[]{:S(2)}) copy-start(f32[128]{0:T(128)} %get-tuple-element.51) | copy-start | bytes 1540
  57.1 3.6 %copy-start.18 = (f32[128]{0:T(128)S(1)}, f32[128]{0:T(128)}, u32[]{:S(2)}) copy-start(f32[128]{0:T(128)} %get-tuple-element.52) | copy-start | bytes 1540
  57.1 3.6 %copy-start.19 = (f32[128]{0:T(128)S(1)}, f32[128]{0:T(128)}, u32[]{:S(2)}) copy-start(f32[128]{0:T(128)} %get-tuple-element.53) | copy-start | bytes 1540
  57.1 13.2 %all-to-all-start.3 = ((bf16[8,64,512]{2,1,0:T(8,128)(2,1)}), bf16[8,64,512]{2,1,0:T(8,128)(2,1)S(1)}, u32[]{:S(2)}, u32[]{:S(2)}) async-start(bf16[8,64,512]{2,1,0:T(8,128)(2,1)} %copy.31), calls=%async_computation.3 | async-start | bytes 1048576 | tf_op jit(solution)/shard_map/all_to_all | solution.py:19
  60.6 0.7 copy-start.11
  60.6 0.7 copy-start.12
  60.6 0.7 copy-start.13
  61.3 6.3 %copy-start.20 = (f32[128]{0:T(128)S(1)}, f32[128]{0:T(128)}, u32[]{:S(2)}) copy-start(f32[128]{0:T(128)} %get-tuple-element.54) | copy-start | bytes 1540
  61.3 6.3 %copy-start.21 = (f32[128]{0:T(128)S(1)}, f32[128]{0:T(128)}, u32[]{:S(2)}) copy-start(f32[128]{0:T(128)} %get-tuple-element.55) | copy-start | bytes 1540
  61.3 6.3 %copy-start.22 = (f32[128]{0:T(128)S(1)}, f32[128]{0:T(128)}, u32[]{:S(2)}) copy-start(f32[128]{0:T(128)} %get-tuple-element.56) | copy-start | bytes 1540
  61.3 6.3 %copy-start.23 = (f32[128]{0:T(128)S(1)}, f32[128]{0:T(128)}, u32[]{:S(2)}) copy-start(f32[128]{0:T(128)} %get-tuple-element.57) | copy-start | bytes 1540
  63.2 7.1 %copy-start.5 = (bf16[512,512]{1,0:T(8,128)(2,1)S(1)}, bf16[512,512]{1,0:T(8,128)(2,1)}, u32[]{:S(2)}) copy-start(bf16[512,512]{1,0:T(8,128)(2,1)} %param.8) | copy-start | bytes 1572868
  63.2 26.6 %collective-permute-start.11 = (bf16[512,128]{1,0:T(8,128)(2,1)}, bf16[512,128]{1,0:T(8,128)(2,1)}, u32[]{:S(2)}, u32[]{:S(2)}) collective-permute-start(bf16[512,128]{1,0:T(8,128)(2,1)} %get-tuple-element.30), channel_id=1, source_target_pairs={{0,2},{1,3},{2,0},{3,1},{4,6},{5,7},{6,4},{7,5},{8,10},{9,11},{10,... | collective-permute-start | bytes 393224 | tf_op jit(solution)/shard_map/ppermute | solution.py:14
  64.1 25.7 %collective-permute-start.12 = (bf16[512,128]{1,0:T(8,128)(2,1)}, bf16[512,128]{1,0:T(8,128)(2,1)}, u32[]{:S(2)}, u32[]{:S(2)}) collective-permute-start(bf16[512,128]{1,0:T(8,128)(2,1)} %get-tuple-element.28), channel_id=1, source_target_pairs={{0,3},{1,0},{2,1},{3,2},{4,7},{5,4},{6,5},{7,6},{8,11},{9,8},{10,9... | collective-permute-start | bytes 393224 | tf_op jit(solution)/shard_map/ppermute | solution.py:14
  67.6 2.7 %copy-start.25 = (f32[512]{0:T(512)S(1)}, f32[512]{0:T(512)}, u32[]{:S(2)}) copy-start(f32[512]{0:T(512)} %param.9) | copy-start | bytes 6148
  69.3 7.5 %collective-permute-start.9 = (bf16[512,128]{1,0:T(8,128)(2,1)}, bf16[512,128]{1,0:T(8,128)(2,1)S(1)}, u32[]{:S(2)}, u32[]{:S(2)}) collective-permute-start(bf16[512,128]{1,0:T(8,128)(2,1)} %fusion.60), channel_id=1, source_target_pairs={{0,1},{1,2},{2,3},{3,0},{4,5},{5,6},{6,7},{7,4},{8,9},{9,10},{10,1... | collective-permute-start | bytes 393224 | tf_op jit(solution)/shard_map/ppermute | solution.py:14
  70.3 0.8 copy-start.6
  71.1 11.6 %copy-start.8 = (bf16[512,512]{1,0:T(8,128)(2,1)}, bf16[512,512]{1,0:T(8,128)(2,1)S(1)}, u32[]{:S(2)}) copy-start(bf16[512,512]{1,0:T(8,128)(2,1)S(1)} %fusion.110) | copy-start | bytes 1572868
  77.5 12.4 %collective-permute-start.10 = (bf16[128,512]{1,0:T(8,128)(2,1)}, bf16[128,512]{1,0:T(8,128)(2,1)}, u32[]{:S(2)}, u32[]{:S(2)}) collective-permute-start(bf16[128,512]{1,0:T(8,128)(2,1)} %get-tuple-element.36), channel_id=1, source_target_pairs={{0,1},{1,2},{2,3},{3,0},{4,5},{5,6},{6,7},{7,4},{8,9},{9,10},{10,1... | collective-permute-start | bytes 393224 | tf_op jit(solution)/shard_map/ppermute | solution.py:14
  77.9 14.1 %collective-permute-start.13 = (bf16[128,512]{1,0:T(8,128)(2,1)}, bf16[128,512]{1,0:T(8,128)(2,1)}, u32[]{:S(2)}, u32[]{:S(2)}) collective-permute-start(bf16[128,512]{1,0:T(8,128)(2,1)} %get-tuple-element.34), channel_id=1, source_target_pairs={{0,2},{1,3},{2,0},{3,1},{4,6},{5,7},{6,4},{7,5},{8,10},{9,11},{10,... | collective-permute-start | bytes 393224 | tf_op jit(solution)/shard_map/ppermute | solution.py:14
  81.1 10.9 %collective-permute-start.14 = (bf16[128,512]{1,0:T(8,128)(2,1)S(1)}, bf16[128,512]{1,0:T(8,128)(2,1)}, u32[]{:S(2)}, u32[]{:S(2)}) collective-permute-start(bf16[128,512]{1,0:T(8,128)(2,1)S(1)} %get-tuple-element.35), channel_id=1, source_target_pairs={{0,3},{1,0},{2,1},{3,2},{4,7},{5,4},{6,5},{7,6},{8,11},{9,8},{10,9... | collective-permute-start | bytes 393224 | tf_op jit(solution)/shard_map/ppermute | solution.py:14
  82.6 4.0 %copy-start.7 = (bf16[8,64,512]{2,1,0:T(8,128)(2,1)S(1)}, bf16[8,64,512]{2,1,0:T(8,128)(2,1)}, u32[]{:S(2)}) copy-start(bf16[8,64,512]{2,1,0:T(8,128)(2,1)} %copy-done.6) | copy-start | bytes 1572868
  82.6 13.8 %all-to-all-start.4 = ((bf16[8,64,512]{2,1,0:T(8,128)(2,1)}), bf16[8,64,512]{2,1,0:T(8,128)(2,1)S(1)}, u32[]{:S(2)}, u32[]{:S(2)}) async-start(bf16[8,64,512]{2,1,0:T(8,128)(2,1)} %bitcast.42), calls=%async_computation.4 | async-start | bytes 1048576 | tf_op jit(solution)/shard_map/all_to_all | solution.py:19
  92.0 5.1 %copy-start.2 = (bf16[512,512]{1,0:T(8,128)(2,1)}, bf16[512,512]{1,0:T(8,128)(2,1)S(1)}, u32[]{:S(2)}) copy-start(bf16[512,512]{1,0:T(8,128)(2,1)S(1)} %fusion.76) | copy-start | bytes 1572868

commit v9 on v6

--- a/solution.py
+++ b/solution.py
@@ -103,7 +103,11 @@
         "cea,ecd->acd", second_f, grad_arrived.astype(F32)
     ).astype(BF16)
     first_grad = swap(first_out, "seq").reshape(rows, width)
-    first_grad, channel_part = lax.optimization_barrier((first_grad, channel_part))
+    input_scale = slope_in + gate_in * source * slope_in * (1.0 - slope_in)
+    input_base = grad_flat + grad_flat * returned * slope_out * (1.0 - slope_out) * gate_out
+    first_grad, channel_part, input_scale, input_base = lax.optimization_barrier(
+        (first_grad, channel_part, input_scale, input_base)
+    )
     block_part = jnp.dot(first_grad, gated.T, preferred_element_type=F32)
     cq = block_part.shape[0] // m
     block_arrived = exchange(
@@ -125,8 +129,7 @@
     channel_grad = jnp.sum(channel_arrived.astype(F32), axis=0)[None]
 
     spread = jnp.dot(first_blocks[0].T, first_grad, preferred_element_type=F32)
-    input_grad = grad_flat + spread * (slope_in + gate_in * source * slope_in * (1.0 - slope_in))
-    input_grad = input_grad + grad_flat * returned * slope_out * (1.0 - slope_out) * gate_out
+    input_grad = input_base + spread * input_scale
     return (outputs, input_grad.astype(BF16), channel_grad, block_grad)
 
 

time: 93.2 us -> 95.7 us (1.027)
  waiting for transfers between devices: 17.1 us -> 14.5 us
  matrix products: 10.3 us -> 12.4 us
  local copies, waits for them, and re-layouts: 9.92 us -> 11.9 us
  starting transfers between devices: 42.7 us -> 43.8 us
    all_to_all x5, waiting for transfers between devices: 11.5 us -> 9.81 us  [swap(): return lax.all_to_all(pieces, axis_name, 0, 0, tiled=True)]
    unnamed x59 -> x43, local copies, waits for them, and re-layouts: 2.49 us -> 3.67 us
    dot_general x1, matrix products: 0.57 us -> 1.59 us  [on_device(): block_part = jnp.dot(first_grad, gated.T, preferred_element_type=F32)]
  transfers between devices with their start and end apart: 20 -> 20, of which waited for: 8 -> 7; matrix products, arithmetic and copies ran while one was open for 25% -> 26% of each run, Pallas kernels for 0% -> 0%
where the time goes in v9:
time: 95.7 us; the launch traced here: 94.8 us
  starting transfers between devices  43.8 us (46%)
  waiting for transfers between devices  14.5 us (15%)
  matrix products  12.4 us (13%)
  local copies, waits for them, and re-layouts  11.9 us (12%)
  other arithmetic  11.1 us (12%)
  between operations  1.06 us (1%)
    ppermute x15, starting transfers between devices, exchange(): lax.ppermute(pieces[k], axis_name, [(i, (i + k) % n) for i in range(n)])  25.6 us
    all_to_all x5, starting transfers between devices, swap(): return lax.all_to_all(pieces, axis_name, 0, 0, tiled=True)  18.2 us
    all_to_all x5, waiting for transfers between devices, swap(): return lax.all_to_all(pieces, axis_name, 0, 0, tiled=True)  9.81 us
    ppermute x15, waiting for transfers between devices, exchange(): lax.ppermute(pieces[k], axis_name, [(i, (i + k) % n) for i in range(n)])  4.73 us
    unnamed x43, local copies, waits for them, and re-layouts  3.67 us
    convert_element_type x2, other arithmetic, on_device(): added_out = [sum((act_arrived[k].astype(F32) * coefficient(origin_of[k],...  3.53 us
    dynamic_update_slice x5, other arithmetic, place_chunks(): out = lax.dynamic_update_slice_in_dim(out, chunk, start, axis=1)  3.11 us
    dynamic_update_slice x3, local copies, waits for them, and re-layouts, place_chunks(): out = lax.dynamic_update_slice_in_dim(out, chunk, start, axis=1)  2.87 us
  transfers between devices with their start and end apart: 20, of which 7 were waited for; matrix products, arithmetic and copies ran while one was open for 26% of the time, Pallas kernels for 0%

profile of v9, /device:TPU:0, one launch (start us, length us, event | category | flops | bytes accessed | tf_op | source)
XLA Modules:
  0.0 94.8 jit_solution(11330634345437083037)
XLA Ops:
  0.6 0.0 copy-start
  0.7 0.7 copy-done.16
  1.4 1.8 %fusion.8 = bf16[512,512]{0,1:T(8,128)(2,1)S(1)} fusion(bf16[1,512,512]{2,1,0:T(8,128)(2,1)} %param.11, bf16[512,512]{1,0:T(8,128)(2,1)} %param.8, f32[512]{0:T(512)S(1)} %copy-done.16), kind=kOutput, calls=%fused_computation.25 | convolution fusion | flops 270532608 | bytes 1574912 | tf_op jit(solution)/shard_map/dot_general | solution.py:59
  3.2 0.1 constant_dynamic-slice_fusion.35
  3.3 3.1 %collective-permute-start = (bf16[512,128]{1,0:T(8,128)(2,1)S(1)}, bf16[512,128]{1,0:T(8,128)(2,1)S(1)}, u32[]{:S(2)}, u32[]{:S(2)}) collective-permute-start(bf16[512,128]{1,0:T(8,128)(2,1)S(1)} %get-tuple-element.43), channel_id=1, source_target_pairs={{0,1},{1,2},{2,3},{3,0},{4,5},{5,6},{6,7},{7,4},{8,9},{9,10},{10,1... | collective-permute-start | bytes 393224 | tf_op jit(solution)/shard_map/ppermute | solution.py:14
  6.4 2.6 %collective-permute-start.1 = (bf16[512,128]{1,0:T(8,128)(2,1)S(1)}, bf16[512,128]{1,0:T(8,128)(2,1)S(1)}, u32[]{:S(2)}, u32[]{:S(2)}) collective-permute-start(bf16[512,128]{1,0:T(8,128)(2,1)S(1)} %get-tuple-element.45), channel_id=1, source_target_pairs={{0,2},{1,3},{2,0},{3,1},{4,6},{5,7},{6,4},{7,5},{8,10},{9,11},{10,... | collective-permute-start | bytes 393224 | tf_op jit(solution)/shard_map/ppermute | solution.py:14
  9.0 1.3 %collective-permute-start.2 = (bf16[512,128]{1,0:T(8,128)(2,1)S(1)}, bf16[512,128]{1,0:T(8,128)(2,1)S(1)}, u32[]{:S(2)}, u32[]{:S(2)}) collective-permute-start(bf16[512,128]{1,0:T(8,128)(2,1)S(1)} %get-tuple-element.44), channel_id=1, source_target_pairs={{0,3},{1,0},{2,1},{3,2},{4,7},{5,4},{6,5},{7,6},{8,11},{9,8},{10,9... | collective-permute-start | bytes 393224 | tf_op jit(solution)/shard_map/ppermute | solution.py:14
  10.3 1.0 %copy.25 = bf16[512,512]{1,0:T(8,128)(2,1)} copy(bf16[512,512]{0,1:T(8,128)(2,1)S(1)} %fusion.8) | data formatting | bytes 1048576 | tf_op jit(solution)/shard_map/optimization_barrier | solution.py:62
  11.3 3.7 %all-to-all-start = ((bf16[8,64,512]{2,1,0:T(8,128)(2,1)}), bf16[8,64,512]{2,1,0:T(8,128)(2,1)S(1)}, u32[]{:S(2)}, u32[]{:S(2)}) async-start(bf16[8,64,512]{2,1,0:T(8,128)(2,1)} %bitcast.2), calls=%async_computation | async-start | bytes 1048576 | tf_op jit(solution)/shard_map/all_to_all | solution.py:19
  15.0 0.7 fusion.78
  15.7 0.7 copy-done.8
  16.5 0.1 copy.30
  16.7 0.7 fusion.106
  17.4 0.3 collective-permute-done.1
  17.6 0.9 fusion.56
  18.5 3.3 %collective-permute-start.3 = (bf16[512,128]{1,0:T(8,128)(2,1)}, bf16[512,128]{1,0:T(8,128)(2,1)}, u32[]{:S(2)}, u32[]{:S(2)}) collective-permute-start(bf16[512,128]{1,0:T(8,128)(2,1)} %get-tuple-element.34), channel_id=1, source_target_pairs={{0,1},{1,2},{2,3},{3,0},{4,5},{5,6},{6,7},{7,4},{8,9},{9,10},{10,1... | collective-permute-start | bytes 393224 | tf_op jit(solution)/shard_map/ppermute | solution.py:14
  21.8 1.6 %collective-permute-start.4 = (bf16[512,128]{1,0:T(8,128)(2,1)S(1)}, bf16[512,128]{1,0:T(8,128)(2,1)}, u32[]{:S(2)}, u32[]{:S(2)}) collective-permute-start(bf16[512,128]{1,0:T(8,128)(2,1)S(1)} %get-tuple-element.35), channel_id=1, source_target_pairs={{0,2},{1,3},{2,0},{3,1},{4,6},{5,7},{6,4},{7,5},{8,10},{9,11},{10,... | collective-permute-start | bytes 393224 | tf_op jit(solution)/shard_map/ppermute | solution.py:14
  23.4 0.7 collective-permute-start.5
  24.2 0.6 all-to-all-done
  24.8 0.4 fusion.6
  25.2 0.9 %copy.28 = bf16[8,64,512]{2,1,0:T(8,128)(2,1)} copy(bf16[8,64,512]{2,0,1:T(8,128)(2,1)S(1)} %fusion.6) | data formatting | bytes 1048576 | tf_op jit(solution)/shard_map/convert_element_type | solution.py:77
  26.2 3.5 %all-to-all-start.1 = ((bf16[8,64,512]{2,1,0:T(8,128)(2,1)}), bf16[8,64,512]{2,1,0:T(8,128)(2,1)S(1)}, u32[]{:S(2)}, u32[]{:S(2)}) async-start(bf16[8,64,512]{2,1,0:T(8,128)(2,1)} %copy.28), calls=%async_computation.1 | async-start | bytes 1048576 | tf_op jit(solution)/shard_map/all_to_all | solution.py:19
  29.7 0.1 fusion.77
  29.9 1.0 %constant_dynamic-update-slice_fusion.2 = bf16[512,512]{1,0:T(8,128)(2,1)S(1)} fusion(bf16[512,512]{1,0:T(8,128)(2,1)S(1)} %fusion.77, bf16[512,128]{1,0:T(8,128)(2,1)} %collective-permute-done.3, s32[]{:T(128)S(6)} %select_n.80), kind=kLoop, calls=%fused_computation.166 | loop fusion | bytes 262148 | tf_op jit(solution)/shard_map/dynamic_update_slice | solution.py:33
  30.9 1.1 %collective-permute-done.4 = bf16[512,128]{1,0:T(8,128)(2,1)} collective-permute-done((bf16[512,128]{1,0:T(8,128)(2,1)S(1)}, bf16[512,128]{1,0:T(8,128)(2,1)}, u32[]{:S(2)}, u32[]{:S(2)}) %collective-permute-start.4) | collective-permute-done | bytes 131104 | tf_op jit(solution)/shard_map/ppermute | solution.py:14
  32.0 0.9 constant_dynamic-update-slice_fusion.1
  33.0 0.9 constant_dynamic-update-slice_fusion
  33.9 5.4 %all-to-all-done.1 = bf16[8,64,512]{2,1,0:T(8,128)(2,1)S(1)} async-done(((bf16[8,64,512]{2,1,0:T(8,128)(2,1)}), bf16[8,64,512]{2,1,0:T(8,128)(2,1)S(1)}, u32[]{:S(2)}, u32[]{:S(2)}) %all-to-all-start.1) | async-done | bytes 524320 | tf_op jit(solution)/shard_map/all_to_all | solution.py:19
  39.4 0.4 fusion.33
  39.8 1.9 %multiply_convert_fusion = (bf16[512,512]{1,0:T(8,128)(2,1)}, bf16[512,512]{1,0:T(8,128)(2,1)S(1)}) fusion(bf16[512,512]{1,0:T(8,128)(2,1)S(1)} %constant_dynamic-update-slice_fusion, bf16[512,512]{1,0:T(8,128)(2,1)S(1)} %fusion.33, bf16[1,512,512]{2,1,0:T(8,128)(2,1)S(1)} %copy-done), kind=kOutput, calls=%fused_computation.52 | convolution fusion | flops 274464768 | bytes 2621440 | tf_op jit(solution)/shard_map/dot_general | solution.py:81
  41.7 2.3 %convert_add_fusion.1 = (f32[512,512]{1,0:T(8,128)S(1)}, bf16[512,512]{1,0:T(8,128)(2,1)}, f32[512,512]{1,0:T(8,128)}) fusion(bf16[8,64,512]{2,1,0:T(8,128)(2,1)S(1)} %all-to-all-done.1, f32[512]{0:T(512)S(1)} %copy-done.9, bf16[512,512]{1,0:T(8,128)(2,1)S(1)} %copy-done.5, f32[512]{0:T(512)S(1)} %copy-done.17, bf16[512,512]{1,0:T(8,128)(2,1)S(1)} %get-tuple-element.29, ...), kind=kOutput, calls=%fused_computation.4 | convolution fusion | flops 275251200 | bytes 5246976 | tf_op jit(solution)/shard_map/dot_general | solution.py:95
  44.0 3.6 %all-to-all-start.2 = ((bf16[8,64,512]{2,1,0:T(8,128)(2,1)}), bf16[8,64,512]{2,1,0:T(8,128)(2,1)S(1)}, u32[]{:S(2)}, u32[]{:S(2)}) async-start(bf16[8,64,512]{2,1,0:T(8,128)(2,1)} %bitcast.112), calls=%async_computation.2 | async-start | bytes 1048576 | tf_op jit(solution)/shard_map/all_to_all | solution.py:19
  47.7 0.8 constant_dynamic-slice_fusion.13
  48.5 1.0 %collective-permute-start.7 = (bf16[512,128]{1,0:T(8,128)(2,1)}, bf16[512,128]{1,0:T(8,128)(2,1)S(1)}, u32[]{:S(2)}, u32[]{:S(2)}) collective-permute-start(bf16[512,128]{1,0:T(8,128)(2,1)} %get-tuple-element.41), channel_id=1, source_target_pairs={{0,1},{1,2},{2,3},{3,0},{4,5},{5,6},{6,7},{7,4},{8,9},{9,10},{10,1... | collective-permute-start | bytes 393224 | tf_op jit(solution)/shard_map/ppermute | solution.py:14
  49.4 1.3 %collective-permute-start.8 = (bf16[512,128]{1,0:T(8,128)(2,1)}, bf16[512,128]{1,0:T(8,128)(2,1)S(1)}, u32[]{:S(2)}, u32[]{:S(2)}) collective-permute-start(bf16[512,128]{1,0:T(8,128)(2,1)} %get-tuple-element.40), channel_id=1, source_target_pairs={{0,2},{1,3},{2,0},{3,1},{4,6},{5,7},{6,4},{7,5},{8,10},{9,11},{10,... | collective-permute-start | bytes 393224 | tf_op jit(solution)/shard_map/ppermute | solution.py:14
  50.7 1.6 %collective-permute-start.9 = (bf16[512,128]{1,0:T(8,128)(2,1)}, bf16[512,128]{1,0:T(8,128)(2,1)}, u32[]{:S(2)}, u32[]{:S(2)}) collective-permute-start(bf16[512,128]{1,0:T(8,128)(2,1)} %get-tuple-element.39), channel_id=1, source_target_pairs={{0,3},{1,0},{2,1},{3,2},{4,7},{5,4},{6,5},{7,6},{8,11},{9,8},{10,9... | collective-permute-start | bytes 393224 | tf_op jit(solution)/shard_map/ppermute | solution.py:14
  52.3 1.3 %fusion.113 = bf16[512,512]{1,0:T(8,128)(2,1)} fusion(bf16[512,512]{1,0:T(8,128)(2,1)S(1)} %fusion.33, bf16[512,512]{1,0:T(8,128)(2,1)S(1)} %copy-done.20), kind=kOutput, calls=%fused_computation.212 | convolution fusion | flops 268435456 | bytes 1572864 | tf_op jit(solution)/shard_map/dot_general | solution.py:97
  53.6 3.7 %all-to-all-done.2 = bf16[8,64,512]{2,1,0:T(8,128)(2,1)S(1)} async-done(((bf16[8,64,512]{2,1,0:T(8,128)(2,1)}), bf16[8,64,512]{2,1,0:T(8,128)(2,1)S(1)}, u32[]{:S(2)}, u32[]{:S(2)}) %all-to-all-start.2) | async-done | bytes 524320 | tf_op jit(solution)/shard_map/all_to_all | solution.py:19
  57.4 0.4 fusion.7
  57.8 0.9 %copy.31 = bf16[8,64,512]{2,1,0:T(8,128)(2,1)} copy(bf16[8,64,512]{2,0,1:T(8,128)(2,1)S(1)} %fusion.7) | data formatting | bytes 1048576 | tf_op jit(solution)/shard_map/convert_element_type | solution.py:104
  58.7 3.5 %all-to-all-start.3 = ((bf16[8,64,512]{2,1,0:T(8,128)(2,1)}), bf16[8,64,512]{2,1,0:T(8,128)(2,1)S(1)}, u32[]{:S(2)}, u32[]{:S(2)}) async-start(bf16[8,64,512]{2,1,0:T(8,128)(2,1)} %copy.31), calls=%async_computation.3 | async-start | bytes 1048576 | tf_op jit(solution)/shard_map/all_to_all | solution.py:19
  62.3 0.6 copy-done.10
  62.9 1.9 %fusion.72 = (bf16[512,128]{1,0:T(8,128)(2,1)S(1)}, bf16[512,128]{1,0:T(8,128)(2,1)}, bf16[512,128]{1,0:T(8,128)(2,1)}) fusion(bf16[512,128]{1,0:T(8,128)(2,1)S(1)} %collective-permute-done.7, bf16[512,128]{1,0:T(8,128)(2,1)S(1)} %collective-permute-done.8, bf16[512,128]{1,0:T(8,128)(2,1)} %collective-permute-done.9, f32[128]{0:T(128)S(1)} %get-tuple-element.47, ...), kind=kLoop, calls=%fused_computation.123 | loop fusion | flops 1835008 | bytes 923652 | tf_op jit(solution)/shard_map/convert_element_type | solution.py:89
  64.8 2.9 %collective-permute-start.10 = (bf16[512,128]{1,0:T(8,128)(2,1)}, bf16[512,128]{1,0:T(8,128)(2,1)}, u32[]{:S(2)}, u32[]{:S(2)}) collective-permute-start(bf16[512,128]{1,0:T(8,128)(2,1)} %get-tuple-element.31), channel_id=1, source_target_pairs={{0,1},{1,2},{2,3},{3,0},{4,5},{5,6},{6,7},{7,4},{8,9},{9,10},{10,1... | collective-permute-start | bytes 393224 | tf_op jit(solution)/shard_map/ppermute | solution.py:14
  67.7 2.4 %collective-permute-start.12 = (bf16[512,128]{1,0:T(8,128)(2,1)S(1)}, bf16[512,128]{1,0:T(8,128)(2,1)}, u32[]{:S(2)}, u32[]{:S(2)}) collective-permute-start(bf16[512,128]{1,0:T(8,128)(2,1)S(1)} %get-tuple-element.30), channel_id=1, source_target_pairs={{0,3},{1,0},{2,1},{3,2},{4,7},{5,4},{6,5},{7,6},{8,11},{9,8},{10,9... | collective-permute-start | bytes 393224 | tf_op jit(solution)/shard_map/ppermute | solution.py:14
  70.1 0.7 copy-done.13
  70.7 0.0 copy-done.14
  70.8 1.7 %fusion.60 = bf16[512,128]{1,0:T(8,128)(2,1)} fusion(bf16[512,128]{1,0:T(8,128)(2,1)S(1)} %collective-permute-done.7, bf16[512,128]{1,0:T(8,128)(2,1)S(1)} %collective-permute-done.8, bf16[512,128]{1,0:T(8,128)(2,1)} %collective-permute-done.9, f32[128]{0:T(128)S(1)} %copy-done.13, f32[128]{0:T(128)S(1)} %copy-done.14, f32[128]{0:T(128)S(1)} %copy-done.15, ...), kind=kLoop, calls=%fused_computation.111 | loop fusion | flops 786432 | bytes 657412 | tf_op jit(solution)/shard_map/convert_element_type | solution.py:89
  72.4 0.7 copy-done.18
  73.1 1.6 %fusion.110 = bf16[512,512]{1,0:T(8,128)(2,1)S(1)} fusion(bf16[512,512]{1,0:T(8,128)(2,1)S(1)} %bitcast.109, bf16[512,512]{1,0:T(8,128)(2,1)} %param.8, f32[512]{0:T(512)S(1)} %copy-done.18), kind=kOutput, calls=%fused_computation.211 | convolution fusion | flops 270270464 | bytes 1574912 | tf_op jit(solution)/shard_map/dot_general | solution.py:111
  74.7 0.8 dynamic-slice_convert_fusion.1
  75.5 0.4 collective-permute-start.6
  76.0 2.2 %collective-permute-start.13 = (bf16[128,512]{1,0:T(8,128)(2,1)}, bf16[128,512]{1,0:T(8,128)(2,1)}, u32[]{:S(2)}, u32[]{:S(2)}) collective-permute-start(bf16[128,512]{1,0:T(8,128)(2,1)} %get-tuple-element.36), channel_id=1, source_target_pairs={{0,2},{1,3},{2,0},{3,1},{4,6},{5,7},{6,4},{7,5},{8,10},{9,11},{10,... | collective-permute-start | bytes 393224 | tf_op jit(solution)/shard_map/ppermute | solution.py:14
  78.1 3.9 %all-to-all-start.4 = ((bf16[8,64,512]{2,1,0:T(8,128)(2,1)}), bf16[8,64,512]{2,1,0:T(8,128)(2,1)S(1)}, u32[]{:S(2)}, u32[]{:S(2)}) async-start(bf16[8,64,512]{2,1,0:T(8,128)(2,1)} %bitcast.111), calls=%async_computation.4 | async-start | bytes 1048576 | tf_op jit(solution)/shard_map/all_to_all | solution.py:19
  82.0 2.7 %fusion.2 = bf16[512,512]{1,0:T(8,128)(2,1)} fusion(f32[512,512]{1,0:T(8,128)S(1)} %get-tuple-element.22, f32[512,512]{1,0:T(8,128)} %get-tuple-element.23, bf16[512,512]{1,0:T(8,128)(2,1)S(1)} %bitcast.110, bf16[1,512,512]{2,1,0:T(8,128)(2,1)} %param.11), kind=kOutput, calls=%fused_computation.16 | convolution fusion | flops 269221888 | bytes 3670016 | tf_op jit(solution)/shard_map/dot_general | solution.py:131
  84.7 1.2 %collective-permute-start.14 = (bf16[128,512]{1,0:T(8,128)(2,1)S(1)}, bf16[128,512]{1,0:T(8,128)(2,1)S(1)}, u32[]{:S(2)}, u32[]{:S(2)}) collective-permute-start(bf16[128,512]{1,0:T(8,128)(2,1)S(1)} %get-tuple-element.37), channel_id=1, source_target_pairs={{0,3},{1,0},{2,1},{3,2},{4,7},{5,4},{6,5},{7,6},{8,11},{9,8},{10,9... | collective-permute-start | bytes 393224 | tf_op jit(solution)/shard_map/ppermute | solution.py:14
  86.0 0.1 fusion.73
  86.1 1.0 %fusion.74 = bf16[512,512]{1,0:T(8,128)(2,1)S(1)} fusion(bf16[512,512]{1,0:T(8,128)(2,1)S(1)} %fusion.73, s32[]{:T(128)S(6)} %select_n.80, bf16[512,128]{1,0:T(8,128)(2,1)} %collective-permute-done.10, bf16[512,512]{1,0:T(8,128)(2,1)S(1)} %fusion.33), kind=kLoop, calls=%fused_computation.134 | loop fusion | flops 262144 | bytes 393220 | tf_op jit(solution)/shard_map/dynamic_update_slice | solution.py:33
  87.0 1.0 %fusion.75 = bf16[512,512]{1,0:T(8,128)(2,1)S(1)} fusion(bf16[512,512]{1,0:T(8,128)(2,1)S(1)} %fusion.74, s32[]{:T(128)S(6)} %select_n.82, bf16[512,128]{1,0:T(8,128)(2,1)} %collective-permute-done.11, bf16[512,512]{1,0:T(8,128)(2,1)S(1)} %fusion.33), kind=kLoop, calls=%fused_computation.135 | loop fusion | flops 262144 | bytes 393220 | tf_op jit(solution)/shard_map/dynamic_update_slice | solution.py:33
  88.0 1.0 %fusion.76 = bf16[512,512]{1,0:T(8,128)(2,1)S(1)} fusion(bf16[512,512]{1,0:T(8,128)(2,1)S(1)} %fusion.75, s32[]{:T(128)S(6)} %select_n.84, bf16[512,128]{1,0:T(8,128)(2,1)} %collective-permute-done.12, bf16[512,512]{1,0:T(8,128)(2,1)S(1)} %fusion.33), kind=kLoop, calls=%fused_computation.136 | loop fusion | flops 262144 | bytes 393220 | tf_op jit(solution)/shard_map/dynamic_update_slice | solution.py:33
  89.0 0.7 collective-permute-done.13
  89.7 2.6 %collective-permute-done.14 = bf16[128,512]{1,0:T(8,128)(2,1)S(1)} collective-permute-done((bf16[128,512]{1,0:T(8,128)(2,1)S(1)}, bf16[128,512]{1,0:T(8,128)(2,1)S(1)}, u32[]{:S(2)}, u32[]{:S(2)}) %collective-permute-start.14) | collective-permute-done | bytes 131104 | tf_op jit(solution)/shard_map/ppermute | solution.py:14
  92.3 1.7 %add_bitcast_fusion = f32[1,128,512]{2,1,0:T(8,128)} fusion(bf16[128,512]{1,0:T(8,128)(2,1)S(1)} %collective-permute-done.14, bf16[128,512]{1,0:T(8,128)(2,1)} %collective-permute-done.13, bf16[128,512]{1,0:T(8,128)(2,1)S(1)} %collective-permute-done.6, bf16[512,512]{1,0:T(8,128)(2,1)} %copy-done.6, s32[]{:T(128)S(6)} %select_n.64), kind=kLoop, calls=%fused_computation.124 | loop fusion | flops 458752 | bytes 786436 | tf_op jit(solution)/shard_map/broadcast_in_dim | solution.py:119
  94.0 0.7 convert_reduce_fusion
  (51 shorter events, 0.2 us)
Async XLA Ops:
  0.6 39.1 %copy-start = (bf16[1,512,512]{2,1,0:T(8,128)(2,1)S(1)}, bf16[1,512,512]{2,1,0:T(8,128)(2,1)}, u32[]{:S(2)}) copy-start(bf16[1,512,512]{2,1,0:T(8,128)(2,1)} %param.13) | copy-start | bytes 1572868
  0.7 0.7 copy-start.16
  1.4 1.8 %copy-start.1 = (bf16[512,512]{1,0:T(8,128)(2,1)S(1)}, bf16[512,512]{1,0:T(8,128)(2,1)}, u32[]{:S(2)}) copy-start(bf16[512,512]{1,0:T(8,128)(2,1)} %param.15) | copy-start | bytes 1572868
  3.3 14.1 %collective-permute-start = (bf16[512,128]{1,0:T(8,128)(2,1)S(1)}, bf16[512,128]{1,0:T(8,128)(2,1)S(1)}, u32[]{:S(2)}, u32[]{:S(2)}) collective-permute-start(bf16[512,128]{1,0:T(8,128)(2,1)S(1)} %get-tuple-element.43), channel_id=1, source_target_pairs={{0,1},{1,2},{2,3},{3,0},{4,5},{5,6},{6,7},{7,4},{8,9},{9,10},{10,1... | collective-permute-start | bytes 393224 | tf_op jit(solution)/shard_map/ppermute | solution.py:14
  6.4 11.2 %collective-permute-start.1 = (bf16[512,128]{1,0:T(8,128)(2,1)S(1)}, bf16[512,128]{1,0:T(8,128)(2,1)S(1)}, u32[]{:S(2)}, u32[]{:S(2)}) collective-permute-start(bf16[512,128]{1,0:T(8,128)(2,1)S(1)} %get-tuple-element.45), channel_id=1, source_target_pairs={{0,2},{1,3},{2,0},{3,1},{4,6},{5,7},{6,4},{7,5},{8,10},{9,11},{10,... | collective-permute-start | bytes 393224 | tf_op jit(solution)/shard_map/ppermute | solution.py:14
  9.0 8.6 %collective-permute-start.2 = (bf16[512,128]{1,0:T(8,128)(2,1)S(1)}, bf16[512,128]{1,0:T(8,128)(2,1)S(1)}, u32[]{:S(2)}, u32[]{:S(2)}) collective-permute-start(bf16[512,128]{1,0:T(8,128)(2,1)S(1)} %get-tuple-element.44), channel_id=1, source_target_pairs={{0,3},{1,0},{2,1},{3,2},{4,7},{5,4},{6,5},{7,6},{8,11},{9,8},{10,9... | collective-permute-start | bytes 393224 | tf_op jit(solution)/shard_map/ppermute | solution.py:14
  11.3 13.5 %all-to-all-start = ((bf16[8,64,512]{2,1,0:T(8,128)(2,1)}), bf16[8,64,512]{2,1,0:T(8,128)(2,1)S(1)}, u32[]{:S(2)}, u32[]{:S(2)}) async-start(bf16[8,64,512]{2,1,0:T(8,128)(2,1)} %bitcast.2), calls=%async_computation | async-start | bytes 1048576 | tf_op jit(solution)/shard_map/all_to_all | solution.py:19
  15.7 0.7 copy-start.8
  18.5 11.4 %collective-permute-start.3 = (bf16[512,128]{1,0:T(8,128)(2,1)}, bf16[512,128]{1,0:T(8,128)(2,1)}, u32[]{:S(2)}, u32[]{:S(2)}) collective-permute-start(bf16[512,128]{1,0:T(8,128)(2,1)} %get-tuple-element.34), channel_id=1, source_target_pairs={{0,1},{1,2},{2,3},{3,0},{4,5},{5,6},{6,7},{7,4},{8,9},{9,10},{10,1... | collective-permute-start | bytes 393224 | tf_op jit(solution)/shard_map/ppermute | solution.py:14
  21.8 10.2 %collective-permute-start.4 = (bf16[512,128]{1,0:T(8,128)(2,1)S(1)}, bf16[512,128]{1,0:T(8,128)(2,1)}, u32[]{:S(2)}, u32[]{:S(2)}) collective-permute-start(bf16[512,128]{1,0:T(8,128)(2,1)S(1)} %get-tuple-element.35), channel_id=1, source_target_pairs={{0,2},{1,3},{2,0},{3,1},{4,6},{5,7},{6,4},{7,5},{8,10},{9,11},{10,... | collective-permute-start | bytes 393224 | tf_op jit(solution)/shard_map/ppermute | solution.py:14
  23.4 9.5 %collective-permute-start.5 = (bf16[512,128]{1,0:T(8,128)(2,1)S(1)}, bf16[512,128]{1,0:T(8,128)(2,1)}, u32[]{:S(2)}, u32[]{:S(2)}) collective-permute-start(bf16[512,128]{1,0:T(8,128)(2,1)S(1)} %get-tuple-element.33), channel_id=1, source_target_pairs={{0,3},{1,0},{2,1},{3,2},{4,7},{5,4},{6,5},{7,6},{8,11},{9,8},{10,9... | collective-permute-start | bytes 393224 | tf_op jit(solution)/shard_map/ppermute | solution.py:14
  26.2 13.2 %all-to-all-start.1 = ((bf16[8,64,512]{2,1,0:T(8,128)(2,1)}), bf16[8,64,512]{2,1,0:T(8,128)(2,1)S(1)}, u32[]{:S(2)}, u32[]{:S(2)}) async-start(bf16[8,64,512]{2,1,0:T(8,128)(2,1)} %copy.28), calls=%async_computation.1 | async-start | bytes 1048576 | tf_op jit(solution)/shard_map/all_to_all | solution.py:19
  29.9 9.5 %copy-start.4 = (bf16[512,512]{1,0:T(8,128)(2,1)S(1)}, bf16[512,512]{1,0:T(8,128)(2,1)}, u32[]{:S(2)}) copy-start(bf16[512,512]{1,0:T(8,128)(2,1)} %param.8) | copy-start | bytes 1572868
  33.0 6.4 %copy-start.9 = (f32[512]{0:T(512)S(1)}, f32[512]{0:T(512)}, u32[]{:S(2)}) copy-start(f32[512]{0:T(512)} %param.10) | copy-start | bytes 6148
  39.8 1.9 %copy-start.5 = (bf16[512,512]{1,0:T(8,128)(2,1)S(1)}, bf16[512,512]{1,0:T(8,128)(2,1)}, u32[]{:S(2)}) copy-start(bf16[512,512]{1,0:T(8,128)(2,1)} %param.8) | copy-start | bytes 1572868
  39.8 1.9 %copy-start.17 = (f32[512]{0:T(512)S(1)}, f32[512]{0:T(512)}, u32[]{:S(2)}) copy-start(f32[512]{0:T(512)} %param.9) | copy-start | bytes 6148
  41.7 2.3 %copy-start.19 = (bf16[512,512]{1,0:T(8,128)(2,1)}, bf16[512,512]{1,0:T(8,128)(2,1)S(1)}, u32[]{:S(2)}) copy-start(bf16[512,512]{1,0:T(8,128)(2,1)S(1)} %get-tuple-element.29) | copy-start | bytes 1572868
  44.0 3.6 %copy-start.2 = (bf16[512,512]{1,0:T(8,128)(2,1)S(1)}, bf16[512,512]{1,0:T(8,128)(2,1)}, u32[]{:S(2)}) copy-start(bf16[512,512]{1,0:T(8,128)(2,1)} %get-tuple-element.28) | copy-start | bytes 1572868
  44.0 13.3 %all-to-all-start.2 = ((bf16[8,64,512]{2,1,0:T(8,128)(2,1)}), bf16[8,64,512]{2,1,0:T(8,128)(2,1)S(1)}, u32[]{:S(2)}, u32[]{:S(2)}) async-start(bf16[8,64,512]{2,1,0:T(8,128)(2,1)} %bitcast.112), calls=%async_computation.2 | async-start | bytes 1048576 | tf_op jit(solution)/shard_map/all_to_all | solution.py:19
  47.7 4.6 %copy-start.20 = (bf16[512,512]{1,0:T(8,128)(2,1)S(1)}, bf16[512,512]{1,0:T(8,128)(2,1)}, u32[]{:S(2)}) copy-start(bf16[512,512]{1,0:T(8,128)(2,1)} %copy-done.19) | copy-start | bytes 1572868
  48.5 13.8 %collective-permute-start.7 = (bf16[512,128]{1,0:T(8,128)(2,1)}, bf16[512,128]{1,0:T(8,128)(2,1)S(1)}, u32[]{:S(2)}, u32[]{:S(2)}) collective-permute-start(bf16[512,128]{1,0:T(8,128)(2,1)} %get-tuple-element.41), channel_id=1, source_target_pairs={{0,1},{1,2},{2,3},{3,0},{4,5},{5,6},{6,7},{7,4},{8,9},{9,10},{10,1... | collective-permute-start | bytes 393224 | tf_op jit(solution)/shard_map/ppermute | solution.py:14
  49.4 12.8 %collective-permute-start.8 = (bf16[512,128]{1,0:T(8,128)(2,1)}, bf16[512,128]{1,0:T(8,128)(2,1)S(1)}, u32[]{:S(2)}, u32[]{:S(2)}) collective-permute-start(bf16[512,128]{1,0:T(8,128)(2,1)} %get-tuple-element.40), channel_id=1, source_target_pairs={{0,2},{1,3},{2,0},{3,1},{4,6},{5,7},{6,4},{7,5},{8,10},{9,11},{10,... | collective-permute-start | bytes 393224 | tf_op jit(solution)/shard_map/ppermute | solution.py:14
  50.7 11.5 %collective-permute-start.9 = (bf16[512,128]{1,0:T(8,128)(2,1)}, bf16[512,128]{1,0:T(8,128)(2,1)}, u32[]{:S(2)}, u32[]{:S(2)}) collective-permute-start(bf16[512,128]{1,0:T(8,128)(2,1)} %get-tuple-element.39), channel_id=1, source_target_pairs={{0,3},{1,0},{2,1},{3,2},{4,7},{5,4},{6,5},{7,6},{8,11},{9,8},{10,9... | collective-permute-start | bytes 393224 | tf_op jit(solution)/shard_map/ppermute | solution.py:14
  58.7 13.7 %all-to-all-start.3 = ((bf16[8,64,512]{2,1,0:T(8,128)(2,1)}), bf16[8,64,512]{2,1,0:T(8,128)(2,1)S(1)}, u32[]{:S(2)}, u32[]{:S(2)}) async-start(bf16[8,64,512]{2,1,0:T(8,128)(2,1)} %copy.31), calls=%async_computation.3 | async-start | bytes 1048576 | tf_op jit(solution)/shard_map/all_to_all | solution.py:19
  62.2 0.7 copy-start.10
  62.3 0.7 copy-start.11
  62.3 0.7 copy-start.12
  64.8 19.9 %collective-permute-start.10 = (bf16[512,128]{1,0:T(8,128)(2,1)}, bf16[512,128]{1,0:T(8,128)(2,1)}, u32[]{:S(2)}, u32[]{:S(2)}) collective-permute-start(bf16[512,128]{1,0:T(8,128)(2,1)} %get-tuple-element.31), channel_id=1, source_target_pairs={{0,1},{1,2},{2,3},{3,0},{4,5},{5,6},{6,7},{7,4},{8,9},{9,10},{10,1... | collective-permute-start | bytes 393224 | tf_op jit(solution)/shard_map/ppermute | solution.py:14
  67.7 18.2 %collective-permute-start.11 = (bf16[512,128]{1,0:T(8,128)(2,1)}, bf16[512,128]{1,0:T(8,128)(2,1)}, u32[]{:S(2)}, u32[]{:S(2)}) collective-permute-start(bf16[512,128]{1,0:T(8,128)(2,1)} %get-tuple-element.32), channel_id=1, source_target_pairs={{0,2},{1,3},{2,0},{3,1},{4,6},{5,7},{6,4},{7,5},{8,10},{9,11},{10,... | collective-permute-start | bytes 393224 | tf_op jit(solution)/shard_map/ppermute | solution.py:14
  67.7 18.2 %collective-permute-start.12 = (bf16[512,128]{1,0:T(8,128)(2,1)S(1)}, bf16[512,128]{1,0:T(8,128)(2,1)}, u32[]{:S(2)}, u32[]{:S(2)}) collective-permute-start(bf16[512,128]{1,0:T(8,128)(2,1)S(1)} %get-tuple-element.30), channel_id=1, source_target_pairs={{0,3},{1,0},{2,1},{3,2},{4,7},{5,4},{6,5},{7,6},{8,11},{9,8},{10,9... | collective-permute-start | bytes 393224 | tf_op jit(solution)/shard_map/ppermute | solution.py:14
  70.1 0.7 copy-start.13
  70.1 0.7 copy-start.14
  70.1 0.7 copy-start.15
  72.4 0.7 copy-start.18
  74.7 3.4 %copy-start.6 = (bf16[512,512]{1,0:T(8,128)(2,1)}, bf16[512,512]{1,0:T(8,128)(2,1)S(1)}, u32[]{:S(2)}) copy-start(bf16[512,512]{1,0:T(8,128)(2,1)S(1)} %fusion.110) | copy-start | bytes 1572868
  75.5 10.4 %collective-permute-start.6 = (bf16[128,512]{1,0:T(8,128)(2,1)}, bf16[128,512]{1,0:T(8,128)(2,1)S(1)}, u32[]{:S(2)}, u32[]{:S(2)}) collective-permute-start(bf16[128,512]{1,0:T(8,128)(2,1)} %get-tuple-element.38), channel_id=1, source_target_pairs={{0,1},{1,2},{2,3},{3,0},{4,5},{5,6},{6,7},{7,4},{8,9},{9,10},{10,1... | collective-permute-start | bytes 393224 | tf_op jit(solution)/shard_map/ppermute | solution.py:14
  76.0 13.7 %collective-permute-start.13 = (bf16[128,512]{1,0:T(8,128)(2,1)}, bf16[128,512]{1,0:T(8,128)(2,1)}, u32[]{:S(2)}, u32[]{:S(2)}) collective-permute-start(bf16[128,512]{1,0:T(8,128)(2,1)} %get-tuple-element.36), channel_id=1, source_target_pairs={{0,2},{1,3},{2,0},{3,1},{4,6},{5,7},{6,4},{7,5},{8,10},{9,11},{10,... | collective-permute-start | bytes 393224 | tf_op jit(solution)/shard_map/ppermute | solution.py:14
  78.1 15.9 %all-to-all-start.4 = ((bf16[8,64,512]{2,1,0:T(8,128)(2,1)}), bf16[8,64,512]{2,1,0:T(8,128)(2,1)S(1)}, u32[]{:S(2)}, u32[]{:S(2)}) async-start(bf16[8,64,512]{2,1,0:T(8,128)(2,1)} %bitcast.111), calls=%async_computation.4 | async-start | bytes 1048576 | tf_op jit(solution)/shard_map/all_to_all | solution.py:19
  84.7 1.3 %copy-start.7 = (bf16[512,128]{1,0:T(8,128)(2,1)S(1)}, bf16[512,128]{1,0:T(8,128)(2,1)}, u32[]{:S(2)}) copy-start(bf16[512,128]{1,0:T(8,128)(2,1)} %fusion.60) | copy-start | bytes 393220
  84.7 7.6 %collective-permute-start.14 = (bf16[128,512]{1,0:T(8,128)(2,1)S(1)}, bf16[128,512]{1,0:T(8,128)(2,1)S(1)}, u32[]{:S(2)}, u32[]{:S(2)}) collective-permute-start(bf16[128,512]{1,0:T(8,128)(2,1)S(1)} %get-tuple-element.37), channel_id=1, source_target_pairs={{0,3},{1,0},{2,1},{3,2},{4,7},{5,4},{6,5},{7,6},{8,11},{9,8},{10,9... | collective-permute-start | bytes 393224 | tf_op jit(solution)/shard_map/ppermute | solution.py:14
  89.0 5.8 %copy-start.3 = (bf16[512,512]{1,0:T(8,128)(2,1)}, bf16[512,512]{1,0:T(8,128)(2,1)S(1)}, u32[]{:S(2)}) copy-start(bf16[512,512]{1,0:T(8,128)(2,1)S(1)} %fusion.76) | copy-start | bytes 1572868

commit v10 on v6

--- a/solution.py
+++ b/solution.py
@@ -1,6 +1,7 @@
 import jax
 import jax.numpy as jnp
 from jax import lax
+from jax.experimental.layout import Layout, with_layout_constraint
 from jax.sharding import PartitionSpec as P
 
 F32 = jnp.float32
@@ -57,6 +58,7 @@
     slope_in = jax.nn.sigmoid(gate_in * source)
     gated = (source * slope_in).astype(BF16)
     mixed_first = jnp.dot(first_blocks[0], gated, preferred_element_type=F32).astype(BF16)
+    mixed_first = with_layout_constraint(mixed_first, Layout(major_to_minor=(0, 1)))
 
     upstream = cotangent
     upstream_late, mixed_first = lax.optimization_barrier((upstream, mixed_first))

time: 93.2 us -> 93.7 us (level)
  local copies, waits for them, and re-layouts: 9.92 us -> 8.91 us
    ppermute x15, waiting for transfers between devices: 5.63 us -> 6.87 us  [exchange(): lax.ppermute(pieces[k], axis_name, [(i, (i + k) % n) for i in range(n)])]
    optimization_barrier x1 -> x0, local copies, waits for them, and re-layouts: 1 us -> none  [on_device(): lax.optimization_barrier((upstream, mixed_first))]
    all_to_all x5, waiting for transfers between devices: 11.5 us -> 10.5 us  [swap(): return lax.all_to_all(pieces, axis_name, 0, 0, tiled=True)]
  transfers between devices with their start and end apart: 20 -> 20, of which waited for: 8 -> 7; matrix products, arithmetic and copies ran while one was open for 25% -> 24% of each run, Pallas kernels for 0% -> 0%
where the time goes in v10:
time: 93.7 us; the launch traced here: 92.8 us
  starting transfers between devices  43.2 us (46%)
  waiting for transfers between devices  17.4 us (19%)
  matrix products  11.2 us (12%)
  other arithmetic  11.1 us (12%)
  local copies, waits for them, and re-layouts  8.91 us (10%)
  between operations  1.13 us (1%)
    ppermute x15, starting transfers between devices, exchange(): lax.ppermute(pieces[k], axis_name, [(i, (i + k) % n) for i in range(n)])  25.1 us
    all_to_all x5, starting transfers between devices, swap(): return lax.all_to_all(pieces, axis_name, 0, 0, tiled=True)  18.1 us
    all_to_all x5, waiting for transfers between devices, swap(): return lax.all_to_all(pieces, axis_name, 0, 0, tiled=True)  10.5 us
    ppermute x15, waiting for transfers between devices, exchange(): lax.ppermute(pieces[k], axis_name, [(i, (i + k) % n) for i in range(n)])  6.87 us
    convert_element_type x2, other arithmetic, on_device(): added_out = [sum((act_arrived[k].astype(F32) * coefficient(origin_of[k],...  3.51 us
    dot_general x1, matrix products, on_device(): spread = jnp.dot(first_blocks[0].T, first_grad, preferred_element_type=F32)  3.19 us
    dynamic_update_slice x5, other arithmetic, place_chunks(): out = lax.dynamic_update_slice_in_dim(out, chunk, start, axis=1)  3.11 us
    dynamic_update_slice x3, local copies, waits for them, and re-layouts, place_chunks(): out = lax.dynamic_update_slice_in_dim(out, chunk, start, axis=1)  2.87 us
  transfers between devices with their start and end apart: 20, of which 7 were waited for; matrix products, arithmetic and copies ran while one was open for 24% of the time, Pallas kernels for 0%

profile of v10, /device:TPU:0, one launch (start us, length us, event | category | flops | bytes accessed | tf_op | source)
XLA Modules:
  0.0 92.8 jit_solution(16522856905483061984)
XLA Ops:
  0.6 0.0 copy-start
  0.7 0.0 copy-start.25
  0.7 0.7 copy-done.25
  1.4 2.6 %fusion.8 = bf16[512,512]{1,0:T(8,128)(2,1)} fusion(bf16[1,512,512]{2,1,0:T(8,128)(2,1)} %param.11, bf16[512,512]{1,0:T(8,128)(2,1)} %param.8, f32[512]{0:T(512)S(1)} %copy-done.25), kind=kOutput, calls=%fused_computation.25 | convolution fusion | flops 270532608 | bytes 1574912 | tf_op jit(solution)/shard_map/dot_general | solution.py:60
  4.0 0.1 constant_dynamic-slice_fusion.35
  4.1 3.1 %collective-permute-start = (bf16[512,128]{1,0:T(8,128)(2,1)S(1)}, bf16[512,128]{1,0:T(8,128)(2,1)S(1)}, u32[]{:S(2)}, u32[]{:S(2)}) collective-permute-start(bf16[512,128]{1,0:T(8,128)(2,1)S(1)} %get-tuple-element.36), channel_id=1, source_target_pairs={{0,1},{1,2},{2,3},{3,0},{4,5},{5,6},{6,7},{7,4},{8,9},{9,10},{10,1... | collective-permute-start | bytes 393224 | tf_op jit(solution)/shard_map/ppermute | solution.py:15
  7.2 2.6 %collective-permute-start.1 = (bf16[512,128]{1,0:T(8,128)(2,1)S(1)}, bf16[512,128]{1,0:T(8,128)(2,1)S(1)}, u32[]{:S(2)}, u32[]{:S(2)}) collective-permute-start(bf16[512,128]{1,0:T(8,128)(2,1)S(1)} %get-tuple-element.38), channel_id=1, source_target_pairs={{0,2},{1,3},{2,0},{3,1},{4,6},{5,7},{6,4},{7,5},{8,10},{9,11},{10,... | collective-permute-start | bytes 393224 | tf_op jit(solution)/shard_map/ppermute | solution.py:15
  9.8 1.3 %collective-permute-start.2 = (bf16[512,128]{1,0:T(8,128)(2,1)S(1)}, bf16[512,128]{1,0:T(8,128)(2,1)S(1)}, u32[]{:S(2)}, u32[]{:S(2)}) collective-permute-start(bf16[512,128]{1,0:T(8,128)(2,1)S(1)} %get-tuple-element.37), channel_id=1, source_target_pairs={{0,3},{1,0},{2,1},{3,2},{4,7},{5,4},{6,5},{7,6},{8,11},{9,8},{10,9... | collective-permute-start | bytes 393224 | tf_op jit(solution)/shard_map/ppermute | solution.py:15
  11.1 3.7 %all-to-all-start = ((bf16[8,64,512]{2,1,0:T(8,128)(2,1)}), bf16[8,64,512]{2,1,0:T(8,128)(2,1)S(1)}, u32[]{:S(2)}, u32[]{:S(2)}) async-start(bf16[8,64,512]{2,1,0:T(8,128)(2,1)} %bitcast.2), calls=%async_computation | async-start | bytes 1048576 | tf_op jit(solution)/shard_map/all_to_all | solution.py:20
  14.8 0.7 fusion.78
  15.5 0.7 copy-done.10
  16.2 0.1 copy.28
  16.5 0.7 fusion.106
  17.2 1.3 %collective-permute-done.1 = bf16[512,128]{1,0:T(8,128)(2,1)S(1)} collective-permute-done((bf16[512,128]{1,0:T(8,128)(2,1)S(1)}, bf16[512,128]{1,0:T(8,128)(2,1)S(1)}, u32[]{:S(2)}, u32[]{:S(2)}) %collective-permute-start.1) | collective-permute-done | bytes 131104 | tf_op jit(solution)/shard_map/ppermute | solution.py:15
  18.4 0.9 fusion.56
  19.3 3.3 %collective-permute-start.3 = (bf16[512,128]{1,0:T(8,128)(2,1)}, bf16[512,128]{1,0:T(8,128)(2,1)}, u32[]{:S(2)}, u32[]{:S(2)}) collective-permute-start(bf16[512,128]{1,0:T(8,128)(2,1)} %get-tuple-element.28), channel_id=1, source_target_pairs={{0,1},{1,2},{2,3},{3,0},{4,5},{5,6},{6,7},{7,4},{8,9},{9,10},{10,1... | collective-permute-start | bytes 393224 | tf_op jit(solution)/shard_map/ppermute | solution.py:15
  22.6 1.6 %collective-permute-start.4 = (bf16[512,128]{1,0:T(8,128)(2,1)S(1)}, bf16[512,128]{1,0:T(8,128)(2,1)}, u32[]{:S(2)}, u32[]{:S(2)}) collective-permute-start(bf16[512,128]{1,0:T(8,128)(2,1)S(1)} %get-tuple-element.29), channel_id=1, source_target_pairs={{0,2},{1,3},{2,0},{3,1},{4,6},{5,7},{6,4},{7,5},{8,10},{9,11},{10,... | collective-permute-start | bytes 393224 | tf_op jit(solution)/shard_map/ppermute | solution.py:15
  24.2 0.7 collective-permute-start.5
  25.0 0.4 fusion.6
  25.4 0.9 %copy.26 = bf16[8,64,512]{2,1,0:T(8,128)(2,1)} copy(bf16[8,64,512]{2,0,1:T(8,128)(2,1)S(1)} %fusion.6) | data formatting | bytes 1048576 | tf_op jit(solution)/shard_map/convert_element_type | solution.py:79
  26.4 3.7 %all-to-all-start.1 = ((bf16[8,64,512]{2,1,0:T(8,128)(2,1)}), bf16[8,64,512]{2,1,0:T(8,128)(2,1)S(1)}, u32[]{:S(2)}, u32[]{:S(2)}) async-start(bf16[8,64,512]{2,1,0:T(8,128)(2,1)} %copy.26), calls=%async_computation.1 | async-start | bytes 1048576 | tf_op jit(solution)/shard_map/all_to_all | solution.py:20
  30.1 0.1 fusion.77
  30.3 1.0 %constant_dynamic-update-slice_fusion.2 = bf16[512,512]{1,0:T(8,128)(2,1)S(1)} fusion(bf16[512,512]{1,0:T(8,128)(2,1)S(1)} %fusion.77, bf16[512,128]{1,0:T(8,128)(2,1)} %collective-permute-done.3, s32[]{:T(128)S(6)} %select_n.80), kind=kLoop, calls=%fused_computation.166 | loop fusion | bytes 262148 | tf_op jit(solution)/shard_map/dynamic_update_slice | solution.py:34
  31.3 1.4 %collective-permute-done.4 = bf16[512,128]{1,0:T(8,128)(2,1)} collective-permute-done((bf16[512,128]{1,0:T(8,128)(2,1)S(1)}, bf16[512,128]{1,0:T(8,128)(2,1)}, u32[]{:S(2)}, u32[]{:S(2)}) %collective-permute-start.4) | collective-permute-done | bytes 131104 | tf_op jit(solution)/shard_map/ppermute | solution.py:15
  32.6 0.9 %constant_dynamic-update-slice_fusion.1 = bf16[512,512]{1,0:T(8,128)(2,1)S(1)} fusion(bf16[512,512]{1,0:T(8,128)(2,1)S(1)} %constant_dynamic-update-slice_fusion.2, bf16[512,128]{1,0:T(8,128)(2,1)} %collective-permute-done.4, s32[]{:T(128)S(6)} %select_n.82), kind=kLoop, calls=%fused_computation.161 | loop fusion | bytes 262148 | tf_op jit(solution)/shard_map/dynamic_update_slice | solution.py:34
  33.6 0.9 %constant_dynamic-update-slice_fusion = bf16[512,512]{1,0:T(8,128)(2,1)S(1)} fusion(bf16[512,512]{1,0:T(8,128)(2,1)S(1)} %constant_dynamic-update-slice_fusion.1, bf16[512,128]{1,0:T(8,128)(2,1)} %collective-permute-done.5, s32[]{:T(128)S(6)} %select_n.84), kind=kLoop, calls=%fused_computation.156 | loop fusion | bytes 262148 | tf_op jit(solution)/shard_map/dynamic_update_slice | solution.py:34
  34.5 5.3 %all-to-all-done.1 = bf16[8,64,512]{2,1,0:T(8,128)(2,1)S(1)} async-done(((bf16[8,64,512]{2,1,0:T(8,128)(2,1)}), bf16[8,64,512]{2,1,0:T(8,128)(2,1)S(1)}, u32[]{:S(2)}, u32[]{:S(2)}) %all-to-all-start.1) | async-done | bytes 524320 | tf_op jit(solution)/shard_map/all_to_all | solution.py:20
  39.8 0.4 fusion.33
  40.2 1.1 %multiply_convert_fusion = (bf16[512,512]{1,0:T(8,128)(2,1)S(1)}, bf16[512,512]{1,0:T(8,128)(2,1)S(1)}) fusion(bf16[512,512]{1,0:T(8,128)(2,1)S(1)} %constant_dynamic-update-slice_fusion, bf16[512,512]{1,0:T(8,128)(2,1)S(1)} %fusion.33, bf16[1,512,512]{2,1,0:T(8,128)(2,1)S(1)} %copy-done), kind=kOutput, calls=%fused_computation.52 | convolution fusion | flops 274464768 | bytes 2621440 | tf_op jit(solution)/shard_map/dot_general | solution.py:83
  41.4 1.6 %fusion.24 = (bf16[512,512]{1,0:T(8,128)(2,1)}, bf16[512,512]{1,0:T(8,128)(2,1)}) fusion(bf16[512,512]{1,0:T(8,128)(2,1)S(1)} %copy-done.4, f32[512]{0:T(512)S(1)} %copy-done.11, bf16[512,512]{1,0:T(8,128)(2,1)S(1)} %get-tuple-element.23, bf16[1,512,512]{2,1,0:T(8,128)(2,1)S(1)} %copy-done, bf16[512,512]{1,0:T(8,128)(2,1)S(1)} %copy-done.1), kind=kOutput, calls=%fused_computation.41 | convolution fusion | flops 271319040 | bytes 3147776 | tf_op jit(solution)/shard_map/dot_general | solution.py:97
  43.0 3.5 %all-to-all-start.2 = ((bf16[8,64,512]{2,1,0:T(8,128)(2,1)}), bf16[8,64,512]{2,1,0:T(8,128)(2,1)S(1)}, u32[]{:S(2)}, u32[]{:S(2)}) async-start(bf16[8,64,512]{2,1,0:T(8,128)(2,1)} %bitcast.22), calls=%async_computation.2 | async-start | bytes 1048576 | tf_op jit(solution)/shard_map/all_to_all | solution.py:20
  46.5 0.1 constant_dynamic-slice_fusion.13
  46.6 1.4 %collective-permute-start.7 = (bf16[512,128]{1,0:T(8,128)(2,1)S(1)}, bf16[512,128]{1,0:T(8,128)(2,1)S(1)}, u32[]{:S(2)}, u32[]{:S(2)}) collective-permute-start(bf16[512,128]{1,0:T(8,128)(2,1)S(1)} %get-tuple-element.35), channel_id=1, source_target_pairs={{0,1},{1,2},{2,3},{3,0},{4,5},{5,6},{6,7},{7,4},{8,9},{9,10},{10,1... | collective-permute-start | bytes 393224 | tf_op jit(solution)/shard_map/ppermute | solution.py:15
  47.9 1.3 %collective-permute-start.8 = (bf16[512,128]{1,0:T(8,128)(2,1)S(1)}, bf16[512,128]{1,0:T(8,128)(2,1)S(1)}, u32[]{:S(2)}, u32[]{:S(2)}) collective-permute-start(bf16[512,128]{1,0:T(8,128)(2,1)S(1)} %get-tuple-element.34), channel_id=1, source_target_pairs={{0,2},{1,3},{2,0},{3,1},{4,6},{5,7},{6,4},{7,5},{8,10},{9,11},{10,... | collective-permute-start | bytes 393224 | tf_op jit(solution)/shard_map/ppermute | solution.py:15
  49.2 1.2 %collective-permute-start.9 = (bf16[512,128]{1,0:T(8,128)(2,1)S(1)}, bf16[512,128]{1,0:T(8,128)(2,1)}, u32[]{:S(2)}, u32[]{:S(2)}) collective-permute-start(bf16[512,128]{1,0:T(8,128)(2,1)S(1)} %get-tuple-element.33), channel_id=1, source_target_pairs={{0,3},{1,0},{2,1},{3,2},{4,7},{5,4},{6,5},{7,6},{8,11},{9,8},{10,9... | collective-permute-start | bytes 393224 | tf_op jit(solution)/shard_map/ppermute | solution.py:15
  50.5 1.3 %fusion.113 = bf16[512,512]{1,0:T(8,128)(2,1)} fusion(bf16[512,512]{1,0:T(8,128)(2,1)S(1)} %fusion.33, bf16[512,512]{1,0:T(8,128)(2,1)S(1)} %copy-done.28), kind=kOutput, calls=%fused_computation.212 | convolution fusion | flops 268435456 | bytes 1572864 | tf_op jit(solution)/shard_map/dot_general | solution.py:99
  51.8 4.4 %all-to-all-done.2 = bf16[8,64,512]{2,1,0:T(8,128)(2,1)S(1)} async-done(((bf16[8,64,512]{2,1,0:T(8,128)(2,1)}), bf16[8,64,512]{2,1,0:T(8,128)(2,1)S(1)}, u32[]{:S(2)}, u32[]{:S(2)}) %all-to-all-start.2) | async-done | bytes 524320 | tf_op jit(solution)/shard_map/all_to_all | solution.py:20
  56.2 0.4 fusion.7
  56.6 0.9 %copy.29 = bf16[8,64,512]{2,1,0:T(8,128)(2,1)} copy(bf16[8,64,512]{2,0,1:T(8,128)(2,1)S(1)} %fusion.7) | data formatting | bytes 1048576 | tf_op jit(solution)/shard_map/convert_element_type | solution.py:106
  57.6 3.5 %all-to-all-start.3 = ((bf16[8,64,512]{2,1,0:T(8,128)(2,1)}), bf16[8,64,512]{2,1,0:T(8,128)(2,1)S(1)}, u32[]{:S(2)}, u32[]{:S(2)}) async-start(bf16[8,64,512]{2,1,0:T(8,128)(2,1)} %copy.29), calls=%async_computation.3 | async-start | bytes 1048576 | tf_op jit(solution)/shard_map/all_to_all | solution.py:20
  61.2 0.6 copy-done.12
  61.8 0.0 copy-done.13
  61.8 1.8 %fusion.72 = (bf16[512,128]{1,0:T(8,128)(2,1)}, bf16[512,128]{1,0:T(8,128)(2,1)}, bf16[512,128]{1,0:T(8,128)(2,1)}) fusion(bf16[512,128]{1,0:T(8,128)(2,1)S(1)} %collective-permute-done.7, bf16[512,128]{1,0:T(8,128)(2,1)S(1)} %collective-permute-done.8, bf16[512,128]{1,0:T(8,128)(2,1)} %collective-permute-done.9, f32[128]{0:T(128)S(1)} %get-tuple-element.40, ...), kind=kLoop, calls=%fused_computation.123 | loop fusion | flops 1835008 | bytes 923652 | tf_op jit(solution)/shard_map/convert_element_type | solution.py:91
  63.6 2.2 %collective-permute-start.10 = (bf16[512,128]{1,0:T(8,128)(2,1)}, bf16[512,128]{1,0:T(8,128)(2,1)}, u32[]{:S(2)}, u32[]{:S(2)}) collective-permute-start(bf16[512,128]{1,0:T(8,128)(2,1)} %get-tuple-element.25), channel_id=1, source_target_pairs={{0,1},{1,2},{2,3},{3,0},{4,5},{5,6},{6,7},{7,4},{8,9},{9,10},{10,1... | collective-permute-start | bytes 393224 | tf_op jit(solution)/shard_map/ppermute | solution.py:15
  65.9 0.4 collective-permute-start.11
  66.3 2.0 %collective-permute-start.12 = (bf16[512,128]{1,0:T(8,128)(2,1)}, bf16[512,128]{1,0:T(8,128)(2,1)}, u32[]{:S(2)}, u32[]{:S(2)}) collective-permute-start(bf16[512,128]{1,0:T(8,128)(2,1)} %get-tuple-element.24), channel_id=1, source_target_pairs={{0,3},{1,0},{2,1},{3,2},{4,7},{5,4},{6,5},{7,6},{8,11},{9,8},{10,9... | collective-permute-start | bytes 393224 | tf_op jit(solution)/shard_map/ppermute | solution.py:15
  68.3 1.7 %fusion.60 = bf16[512,128]{1,0:T(8,128)(2,1)} fusion(bf16[512,128]{1,0:T(8,128)(2,1)S(1)} %collective-permute-done.7, bf16[512,128]{1,0:T(8,128)(2,1)S(1)} %collective-permute-done.8, bf16[512,128]{1,0:T(8,128)(2,1)} %collective-permute-done.9, f32[128]{0:T(128)S(1)} %copy-done.22, f32[128]{0:T(128)S(1)} %copy-done.23, f32[128]{0:T(128)S(1)} %copy-done.24, ...), kind=kLoop, calls=%fused_computation.111 | loop fusion | flops 786432 | bytes 657412 | tf_op jit(solution)/shard_map/convert_element_type | solution.py:91
  69.9 0.8 all-to-all-done.3
  70.8 0.6 fusion.110
  71.3 0.2 copy-done.6
  71.5 0.7 dynamic-slice_convert_fusion.1
  72.3 1.3 %collective-permute-start.6 = (bf16[128,512]{1,0:T(8,128)(2,1)}, bf16[128,512]{1,0:T(8,128)(2,1)S(1)}, u32[]{:S(2)}, u32[]{:S(2)}) collective-permute-start(bf16[128,512]{1,0:T(8,128)(2,1)} %get-tuple-element.32), channel_id=1, source_target_pairs={{0,1},{1,2},{2,3},{3,0},{4,5},{5,6},{6,7},{7,4},{8,9},{9,10},{10,1... | collective-permute-start | bytes 393224 | tf_op jit(solution)/shard_map/ppermute | solution.py:15
  73.6 1.3 %collective-permute-start.13 = (bf16[128,512]{1,0:T(8,128)(2,1)S(1)}, bf16[128,512]{1,0:T(8,128)(2,1)}, u32[]{:S(2)}, u32[]{:S(2)}) collective-permute-start(bf16[128,512]{1,0:T(8,128)(2,1)S(1)} %get-tuple-element.30), channel_id=1, source_target_pairs={{0,2},{1,3},{2,0},{3,1},{4,6},{5,7},{6,4},{7,5},{8,10},{9,11},{10,... | collective-permute-start | bytes 393224 | tf_op jit(solution)/shard_map/ppermute | solution.py:15
  74.9 3.6 %all-to-all-start.4 = ((bf16[8,64,512]{2,1,0:T(8,128)(2,1)}), bf16[8,64,512]{2,1,0:T(8,128)(2,1)S(1)}, u32[]{:S(2)}, u32[]{:S(2)}) async-start(bf16[8,64,512]{2,1,0:T(8,128)(2,1)} %bitcast.42), calls=%async_computation.4 | async-start | bytes 1048576 | tf_op jit(solution)/shard_map/all_to_all | solution.py:20
  78.5 3.2 %fusion.3 = bf16[512,512]{1,0:T(8,128)(2,1)} fusion(bf16[512,512]{1,0:T(8,128)(2,1)S(1)} %bitcast.112, bf16[512,512]{1,0:T(8,128)(2,1)} %get-tuple-element.71, bf16[512,512]{1,0:T(8,128)(2,1)S(1)} %copy-done.5, bf16[512,512]{1,0:T(8,128)(2,1)S(1)} %bitcast.110, bf16[1,512,512]{2,1,0:T(8,128)(2,1)} %param.11, f32[512]{0:T(512)S(1)} %copy-done.11, ...), kind=kOutput, calls=%fused_computation.20 | convolution fusion | flops 274726912 | bytes 3149824 | tf_op jit(solution)/shard_map/dot_general | solution.py:129
  81.7 1.4 %collective-permute-start.14 = (bf16[128,512]{1,0:T(8,128)(2,1)S(1)}, bf16[128,512]{1,0:T(8,128)(2,1)S(1)}, u32[]{:S(2)}, u32[]{:S(2)}) collective-permute-start(bf16[128,512]{1,0:T(8,128)(2,1)S(1)} %get-tuple-element.31), channel_id=1, source_target_pairs={{0,3},{1,0},{2,1},{3,2},{4,7},{5,4},{6,5},{7,6},{8,11},{9,8},{10,9... | collective-permute-start | bytes 393224 | tf_op jit(solution)/shard_map/ppermute | solution.py:15
  83.1 0.1 fusion.73
  83.2 1.0 %fusion.74 = bf16[512,512]{1,0:T(8,128)(2,1)S(1)} fusion(bf16[512,512]{1,0:T(8,128)(2,1)S(1)} %fusion.73, s32[]{:T(128)S(6)} %select_n.80, bf16[512,128]{1,0:T(8,128)(2,1)} %collective-permute-done.10, bf16[512,512]{1,0:T(8,128)(2,1)S(1)} %fusion.33), kind=kLoop, calls=%fused_computation.134 | loop fusion | flops 262144 | bytes 393220 | tf_op jit(solution)/shard_map/dynamic_update_slice | solution.py:34
  84.2 1.0 %fusion.75 = bf16[512,512]{1,0:T(8,128)(2,1)S(1)} fusion(bf16[512,512]{1,0:T(8,128)(2,1)S(1)} %fusion.74, s32[]{:T(128)S(6)} %select_n.82, bf16[512,128]{1,0:T(8,128)(2,1)} %collective-permute-done.11, bf16[512,512]{1,0:T(8,128)(2,1)S(1)} %fusion.33), kind=kLoop, calls=%fused_computation.135 | loop fusion | flops 262144 | bytes 393220 | tf_op jit(solution)/shard_map/dynamic_update_slice | solution.py:34
  85.2 1.0 %fusion.76 = bf16[512,512]{1,0:T(8,128)(2,1)S(1)} fusion(bf16[512,512]{1,0:T(8,128)(2,1)S(1)} %fusion.75, s32[]{:T(128)S(6)} %select_n.84, bf16[512,128]{1,0:T(8,128)(2,1)} %collective-permute-done.12, bf16[512,512]{1,0:T(8,128)(2,1)S(1)} %fusion.33), kind=kLoop, calls=%fused_computation.136 | loop fusion | flops 262144 | bytes 393220 | tf_op jit(solution)/shard_map/dynamic_update_slice | solution.py:34
  86.1 2.5 %collective-permute-done.13 = bf16[128,512]{1,0:T(8,128)(2,1)} collective-permute-done((bf16[128,512]{1,0:T(8,128)(2,1)S(1)}, bf16[128,512]{1,0:T(8,128)(2,1)}, u32[]{:S(2)}, u32[]{:S(2)}) %collective-permute-start.13) | collective-permute-done | bytes 131104 | tf_op jit(solution)/shard_map/ppermute | solution.py:15
  88.6 1.8 %collective-permute-done.14 = bf16[128,512]{1,0:T(8,128)(2,1)S(1)} collective-permute-done((bf16[128,512]{1,0:T(8,128)(2,1)S(1)}, bf16[128,512]{1,0:T(8,128)(2,1)S(1)}, u32[]{:S(2)}, u32[]{:S(2)}) %collective-permute-start.14) | collective-permute-done | bytes 131104 | tf_op jit(solution)/shard_map/ppermute | solution.py:15
  90.4 1.7 %add_bitcast_fusion = f32[1,128,512]{2,1,0:T(8,128)} fusion(bf16[128,512]{1,0:T(8,128)(2,1)S(1)} %collective-permute-done.14, bf16[128,512]{1,0:T(8,128)(2,1)} %collective-permute-done.13, bf16[128,512]{1,0:T(8,128)(2,1)S(1)} %collective-permute-done.6, bf16[512,512]{1,0:T(8,128)(2,1)} %copy-done.8, s32[]{:T(128)S(6)} %select_n.64), kind=kLoop, calls=%fused_computation.124 | loop fusion | flops 458752 | bytes 786436 | tf_op jit(solution)/shard_map/broadcast_in_dim | solution.py:117
  92.1 0.7 convert_reduce_fusion
  (66 shorter events, 0.2 us)
Async XLA Ops:
  0.6 39.6 %copy-start = (bf16[1,512,512]{2,1,0:T(8,128)(2,1)S(1)}, bf16[1,512,512]{2,1,0:T(8,128)(2,1)}, u32[]{:S(2)}) copy-start(bf16[1,512,512]{2,1,0:T(8,128)(2,1)} %param.13) | copy-start | bytes 1572868
  0.7 0.7 copy-start.25
  1.4 2.6 %copy-start.1 = (bf16[512,512]{1,0:T(8,128)(2,1)S(1)}, bf16[512,512]{1,0:T(8,128)(2,1)}, u32[]{:S(2)}) copy-start(bf16[512,512]{1,0:T(8,128)(2,1)} %param.15) | copy-start | bytes 1572868
  4.1 13.1 %collective-permute-start = (bf16[512,128]{1,0:T(8,128)(2,1)S(1)}, bf16[512,128]{1,0:T(8,128)(2,1)S(1)}, u32[]{:S(2)}, u32[]{:S(2)}) collective-permute-start(bf16[512,128]{1,0:T(8,128)(2,1)S(1)} %get-tuple-element.36), channel_id=1, source_target_pairs={{0,1},{1,2},{2,3},{3,0},{4,5},{5,6},{6,7},{7,4},{8,9},{9,10},{10,1... | collective-permute-start | bytes 393224 | tf_op jit(solution)/shard_map/ppermute | solution.py:15
  7.2 11.2 %collective-permute-start.1 = (bf16[512,128]{1,0:T(8,128)(2,1)S(1)}, bf16[512,128]{1,0:T(8,128)(2,1)S(1)}, u32[]{:S(2)}, u32[]{:S(2)}) collective-permute-start(bf16[512,128]{1,0:T(8,128)(2,1)S(1)} %get-tuple-element.38), channel_id=1, source_target_pairs={{0,2},{1,3},{2,0},{3,1},{4,6},{5,7},{6,4},{7,5},{8,10},{9,11},{10,... | collective-permute-start | bytes 393224 | tf_op jit(solution)/shard_map/ppermute | solution.py:15
  9.8 8.6 %collective-permute-start.2 = (bf16[512,128]{1,0:T(8,128)(2,1)S(1)}, bf16[512,128]{1,0:T(8,128)(2,1)S(1)}, u32[]{:S(2)}, u32[]{:S(2)}) collective-permute-start(bf16[512,128]{1,0:T(8,128)(2,1)S(1)} %get-tuple-element.37), channel_id=1, source_target_pairs={{0,3},{1,0},{2,1},{3,2},{4,7},{5,4},{6,5},{7,6},{8,11},{9,8},{10,9... | collective-permute-start | bytes 393224 | tf_op jit(solution)/shard_map/ppermute | solution.py:15
  11.1 13.8 %all-to-all-start = ((bf16[8,64,512]{2,1,0:T(8,128)(2,1)}), bf16[8,64,512]{2,1,0:T(8,128)(2,1)S(1)}, u32[]{:S(2)}, u32[]{:S(2)}) async-start(bf16[8,64,512]{2,1,0:T(8,128)(2,1)} %bitcast.2), calls=%async_computation | async-start | bytes 1048576 | tf_op jit(solution)/shard_map/all_to_all | solution.py:20
  15.5 0.7 copy-start.10
  19.3 11.0 %collective-permute-start.3 = (bf16[512,128]{1,0:T(8,128)(2,1)}, bf16[512,128]{1,0:T(8,128)(2,1)}, u32[]{:S(2)}, u32[]{:S(2)}) collective-permute-start(bf16[512,128]{1,0:T(8,128)(2,1)} %get-tuple-element.28), channel_id=1, source_target_pairs={{0,1},{1,2},{2,3},{3,0},{4,5},{5,6},{6,7},{7,4},{8,9},{9,10},{10,1... | collective-permute-start | bytes 393224 | tf_op jit(solution)/shard_map/ppermute | solution.py:15
  22.6 10.0 %collective-permute-start.4 = (bf16[512,128]{1,0:T(8,128)(2,1)S(1)}, bf16[512,128]{1,0:T(8,128)(2,1)}, u32[]{:S(2)}, u32[]{:S(2)}) collective-permute-start(bf16[512,128]{1,0:T(8,128)(2,1)S(1)} %get-tuple-element.29), channel_id=1, source_target_pairs={{0,2},{1,3},{2,0},{3,1},{4,6},{5,7},{6,4},{7,5},{8,10},{9,11},{10,... | collective-permute-start | bytes 393224 | tf_op jit(solution)/shard_map/ppermute | solution.py:15
  24.2 9.4 %collective-permute-start.5 = (bf16[512,128]{1,0:T(8,128)(2,1)S(1)}, bf16[512,128]{1,0:T(8,128)(2,1)}, u32[]{:S(2)}, u32[]{:S(2)}) collective-permute-start(bf16[512,128]{1,0:T(8,128)(2,1)S(1)} %get-tuple-element.27), channel_id=1, source_target_pairs={{0,3},{1,0},{2,1},{3,2},{4,7},{5,4},{6,5},{7,6},{8,11},{9,8},{10,9... | collective-permute-start | bytes 393224 | tf_op jit(solution)/shard_map/ppermute | solution.py:15
  26.4 13.5 %all-to-all-start.1 = ((bf16[8,64,512]{2,1,0:T(8,128)(2,1)}), bf16[8,64,512]{2,1,0:T(8,128)(2,1)S(1)}, u32[]{:S(2)}, u32[]{:S(2)}) async-start(bf16[8,64,512]{2,1,0:T(8,128)(2,1)} %copy.26), calls=%async_computation.1 | async-start | bytes 1048576 | tf_op jit(solution)/shard_map/all_to_all | solution.py:20
  30.3 9.6 %copy-start.3 = (bf16[512,512]{1,0:T(8,128)(2,1)S(1)}, bf16[512,512]{1,0:T(8,128)(2,1)}, u32[]{:S(2)}) copy-start(bf16[512,512]{1,0:T(8,128)(2,1)} %param.8) | copy-start | bytes 1572868
  33.6 6.3 %copy-start.11 = (f32[512]{0:T(512)S(1)}, f32[512]{0:T(512)}, u32[]{:S(2)}) copy-start(f32[512]{0:T(512)} %param.10) | copy-start | bytes 6148
  40.2 1.2 %copy-start.4 = (bf16[512,512]{1,0:T(8,128)(2,1)S(1)}, bf16[512,512]{1,0:T(8,128)(2,1)}, u32[]{:S(2)}) copy-start(bf16[512,512]{1,0:T(8,128)(2,1)} %param.8) | copy-start | bytes 1572868
  41.4 1.6 %copy-start.27 = (bf16[512,512]{1,0:T(8,128)(2,1)}, bf16[512,512]{1,0:T(8,128)(2,1)S(1)}, u32[]{:S(2)}) copy-start(bf16[512,512]{1,0:T(8,128)(2,1)S(1)} %get-tuple-element.23) | copy-start | bytes 1572868
  43.0 13.2 %all-to-all-start.2 = ((bf16[8,64,512]{2,1,0:T(8,128)(2,1)}), bf16[8,64,512]{2,1,0:T(8,128)(2,1)S(1)}, u32[]{:S(2)}, u32[]{:S(2)}) async-start(bf16[8,64,512]{2,1,0:T(8,128)(2,1)} %bitcast.22), calls=%async_computation.2 | async-start | bytes 1048576 | tf_op jit(solution)/shard_map/all_to_all | solution.py:20
  46.5 4.0 %copy-start.28 = (bf16[512,512]{1,0:T(8,128)(2,1)S(1)}, bf16[512,512]{1,0:T(8,128)(2,1)}, u32[]{:S(2)}) copy-start(bf16[512,512]{1,0:T(8,128)(2,1)} %copy-done.27) | copy-start | bytes 1572868
  46.6 14.5 %collective-permute-start.7 = (bf16[512,128]{1,0:T(8,128)(2,1)S(1)}, bf16[512,128]{1,0:T(8,128)(2,1)S(1)}, u32[]{:S(2)}, u32[]{:S(2)}) collective-permute-start(bf16[512,128]{1,0:T(8,128)(2,1)S(1)} %get-tuple-element.35), channel_id=1, source_target_pairs={{0,1},{1,2},{2,3},{3,0},{4,5},{5,6},{6,7},{7,4},{8,9},{9,10},{10,1... | collective-permute-start | bytes 393224 | tf_op jit(solution)/shard_map/ppermute | solution.py:15
  47.9 13.1 %collective-permute-start.8 = (bf16[512,128]{1,0:T(8,128)(2,1)S(1)}, bf16[512,128]{1,0:T(8,128)(2,1)S(1)}, u32[]{:S(2)}, u32[]{:S(2)}) collective-permute-start(bf16[512,128]{1,0:T(8,128)(2,1)S(1)} %get-tuple-element.34), channel_id=1, source_target_pairs={{0,2},{1,3},{2,0},{3,1},{4,6},{5,7},{6,4},{7,5},{8,10},{9,11},{10,... | collective-permute-start | bytes 393224 | tf_op jit(solution)/shard_map/ppermute | solution.py:15
  49.2 11.9 %collective-permute-start.9 = (bf16[512,128]{1,0:T(8,128)(2,1)S(1)}, bf16[512,128]{1,0:T(8,128)(2,1)}, u32[]{:S(2)}, u32[]{:S(2)}) collective-permute-start(bf16[512,128]{1,0:T(8,128)(2,1)S(1)} %get-tuple-element.33), channel_id=1, source_target_pairs={{0,3},{1,0},{2,1},{3,2},{4,7},{5,4},{6,5},{7,6},{8,11},{9,8},{10,9... | collective-permute-start | bytes 393224 | tf_op jit(solution)/shard_map/ppermute | solution.py:15
  57.5 3.6 %copy-start.15 = (f32[128]{0:T(128)S(1)}, f32[128]{0:T(128)}, u32[]{:S(2)}) copy-start(f32[128]{0:T(128)} %get-tuple-element.44) | copy-start | bytes 1540
  57.5 3.6 %copy-start.16 = (f32[128]{0:T(128)S(1)}, f32[128]{0:T(128)}, u32[]{:S(2)}) copy-start(f32[128]{0:T(128)} %get-tuple-element.45) | copy-start | bytes 1540
  57.5 3.6 %copy-start.17 = (f32[128]{0:T(128)S(1)}, f32[128]{0:T(128)}, u32[]{:S(2)}) copy-start(f32[128]{0:T(128)} %get-tuple-element.46) | copy-start | bytes 1540
  57.5 3.6 %copy-start.18 = (f32[128]{0:T(128)S(1)}, f32[128]{0:T(128)}, u32[]{:S(2)}) copy-start(f32[128]{0:T(128)} %get-tuple-element.47) | copy-start | bytes 1540
  57.5 3.6 %copy-start.19 = (f32[128]{0:T(128)S(1)}, f32[128]{0:T(128)}, u32[]{:S(2)}) copy-start(f32[128]{0:T(128)} %get-tuple-element.48) | copy-start | bytes 1540
  57.5 3.6 %copy-start.20 = (f32[128]{0:T(128)S(1)}, f32[128]{0:T(128)}, u32[]{:S(2)}) copy-start(f32[128]{0:T(128)} %get-tuple-element.49) | copy-start | bytes 1540
  57.5 3.6 %copy-start.21 = (f32[128]{0:T(128)S(1)}, f32[128]{0:T(128)}, u32[]{:S(2)}) copy-start(f32[128]{0:T(128)} %get-tuple-element.50) | copy-start | bytes 1540
  57.6 13.2 %all-to-all-start.3 = ((bf16[8,64,512]{2,1,0:T(8,128)(2,1)}), bf16[8,64,512]{2,1,0:T(8,128)(2,1)S(1)}, u32[]{:S(2)}, u32[]{:S(2)}) async-start(bf16[8,64,512]{2,1,0:T(8,128)(2,1)} %copy.29), calls=%async_computation.3 | async-start | bytes 1048576 | tf_op jit(solution)/shard_map/all_to_all | solution.py:20
  61.1 0.7 copy-start.12
  61.1 0.7 copy-start.13
  61.1 0.7 copy-start.14
  61.8 6.5 %copy-start.22 = (f32[128]{0:T(128)S(1)}, f32[128]{0:T(128)}, u32[]{:S(2)}) copy-start(f32[128]{0:T(128)} %get-tuple-element.51) | copy-start | bytes 1540
  61.8 6.5 %copy-start.23 = (f32[128]{0:T(128)S(1)}, f32[128]{0:T(128)}, u32[]{:S(2)}) copy-start(f32[128]{0:T(128)} %get-tuple-element.52) | copy-start | bytes 1540
  61.8 6.5 %copy-start.24 = (f32[128]{0:T(128)S(1)}, f32[128]{0:T(128)}, u32[]{:S(2)}) copy-start(f32[128]{0:T(128)} %get-tuple-element.53) | copy-start | bytes 1540
  63.6 7.1 %copy-start.5 = (bf16[512,512]{1,0:T(8,128)(2,1)S(1)}, bf16[512,512]{1,0:T(8,128)(2,1)}, u32[]{:S(2)}) copy-start(bf16[512,512]{1,0:T(8,128)(2,1)} %param.8) | copy-start | bytes 1572868
  63.6 18.1 %collective-permute-start.10 = (bf16[512,128]{1,0:T(8,128)(2,1)}, bf16[512,128]{1,0:T(8,128)(2,1)}, u32[]{:S(2)}, u32[]{:S(2)}) collective-permute-start(bf16[512,128]{1,0:T(8,128)(2,1)} %get-tuple-element.25), channel_id=1, source_target_pairs={{0,1},{1,2},{2,3},{3,0},{4,5},{5,6},{6,7},{7,4},{8,9},{9,10},{10,1... | collective-permute-start | bytes 393224 | tf_op jit(solution)/shard_map/ppermute | solution.py:15
  65.9 17.2 %collective-permute-start.11 = (bf16[512,128]{1,0:T(8,128)(2,1)}, bf16[512,128]{1,0:T(8,128)(2,1)}, u32[]{:S(2)}, u32[]{:S(2)}) collective-permute-start(bf16[512,128]{1,0:T(8,128)(2,1)} %get-tuple-element.26), channel_id=1, source_target_pairs={{0,2},{1,3},{2,0},{3,1},{4,6},{5,7},{6,4},{7,5},{8,10},{9,11},{10,... | collective-permute-start | bytes 393224 | tf_op jit(solution)/shard_map/ppermute | solution.py:15
  66.3 16.8 %collective-permute-start.12 = (bf16[512,128]{1,0:T(8,128)(2,1)}, bf16[512,128]{1,0:T(8,128)(2,1)}, u32[]{:S(2)}, u32[]{:S(2)}) collective-permute-start(bf16[512,128]{1,0:T(8,128)(2,1)} %get-tuple-element.24), channel_id=1, source_target_pairs={{0,3},{1,0},{2,1},{3,2},{4,7},{5,4},{6,5},{7,6},{8,11},{9,8},{10,9... | collective-permute-start | bytes 393224 | tf_op jit(solution)/shard_map/ppermute | solution.py:15
  68.2 2.5 %copy-start.26 = (f32[512]{0:T(512)S(1)}, f32[512]{0:T(512)}, u32[]{:S(2)}) copy-start(f32[512]{0:T(512)} %param.9) | copy-start | bytes 6148
  70.7 0.8 copy-start.6
  71.5 3.3 %copy-start.8 = (bf16[512,512]{1,0:T(8,128)(2,1)}, bf16[512,512]{1,0:T(8,128)(2,1)S(1)}, u32[]{:S(2)}) copy-start(bf16[512,512]{1,0:T(8,128)(2,1)S(1)} %fusion.110) | copy-start | bytes 1572868
  72.3 10.8 %collective-permute-start.6 = (bf16[128,512]{1,0:T(8,128)(2,1)}, bf16[128,512]{1,0:T(8,128)(2,1)S(1)}, u32[]{:S(2)}, u32[]{:S(2)}) collective-permute-start(bf16[128,512]{1,0:T(8,128)(2,1)} %get-tuple-element.32), channel_id=1, source_target_pairs={{0,1},{1,2},{2,3},{3,0},{4,5},{5,6},{6,7},{7,4},{8,9},{9,10},{10,1... | collective-permute-start | bytes 393224 | tf_op jit(solution)/shard_map/ppermute | solution.py:15
  73.6 15.0 %collective-permute-start.13 = (bf16[128,512]{1,0:T(8,128)(2,1)S(1)}, bf16[128,512]{1,0:T(8,128)(2,1)}, u32[]{:S(2)}, u32[]{:S(2)}) collective-permute-start(bf16[128,512]{1,0:T(8,128)(2,1)S(1)} %get-tuple-element.30), channel_id=1, source_target_pairs={{0,2},{1,3},{2,0},{3,1},{4,6},{5,7},{6,4},{7,5},{8,10},{9,11},{10,... | collective-permute-start | bytes 393224 | tf_op jit(solution)/shard_map/ppermute | solution.py:15
  74.9 3.6 %copy-start.7 = (bf16[8,64,512]{2,1,0:T(8,128)(2,1)S(1)}, bf16[8,64,512]{2,1,0:T(8,128)(2,1)}, u32[]{:S(2)}) copy-start(bf16[8,64,512]{2,1,0:T(8,128)(2,1)} %copy-done.6) | copy-start | bytes 1572868
  74.9 17.2 %all-to-all-start.4 = ((bf16[8,64,512]{2,1,0:T(8,128)(2,1)}), bf16[8,64,512]{2,1,0:T(8,128)(2,1)S(1)}, u32[]{:S(2)}, u32[]{:S(2)}) async-start(bf16[8,64,512]{2,1,0:T(8,128)(2,1)} %bitcast.42), calls=%async_computation.4 | async-start | bytes 1048576 | tf_op jit(solution)/shard_map/all_to_all | solution.py:20
  81.7 1.4 %copy-start.9 = (bf16[512,128]{1,0:T(8,128)(2,1)S(1)}, bf16[512,128]{1,0:T(8,128)(2,1)}, u32[]{:S(2)}) copy-start(bf16[512,128]{1,0:T(8,128)(2,1)} %fusion.60) | copy-start | bytes 393220
  81.7 8.7 %collective-permute-start.14 = (bf16[128,512]{1,0:T(8,128)(2,1)S(1)}, bf16[128,512]{1,0:T(8,128)(2,1)S(1)}, u32[]{:S(2)}, u32[]{:S(2)}) collective-permute-start(bf16[128,512]{1,0:T(8,128)(2,1)S(1)} %get-tuple-element.31), channel_id=1, source_target_pairs={{0,3},{1,0},{2,1},{3,2},{4,7},{5,4},{6,5},{7,6},{8,11},{9,8},{10,9... | collective-permute-start | bytes 393224 | tf_op jit(solution)/shard_map/ppermute | solution.py:15
  86.1 6.7 %copy-start.2 = (bf16[512,512]{1,0:T(8,128)(2,1)}, bf16[512,512]{1,0:T(8,128)(2,1)S(1)}, u32[]{:S(2)}) copy-start(bf16[512,512]{1,0:T(8,128)(2,1)S(1)} %fusion.76) | copy-start | bytes 1572868

commit v11 on v7

--- a/solution.py
+++ b/solution.py
@@ -110,7 +110,7 @@
         [lax.dynamic_slice_in_dim(block_part, t * cq, cq, 0).astype(BF16) for t in chunk_of],
         "ch",
     )
-    first_block, added_back, first_grad = lax.optimization_barrier(
+    first_block, added_back, spread_source = lax.optimization_barrier(
         (block_arrived[1], added_back, first_grad)
     )
     block_arrived[1] = first_block
@@ -126,7 +126,7 @@
     channel_arrived = swap(split_rows(channel_part, n).astype(BF16), "seq")
     channel_grad = jnp.sum(channel_arrived.astype(F32), axis=0)[None]
 
-    spread = jnp.dot(first_blocks[0].T, first_grad, preferred_element_type=F32)
+    spread = jnp.dot(first_blocks[0].T, spread_source, preferred_element_type=F32)
     input_grad = grad_flat + spread * (slope_in + gate_in * source * slope_in * (1.0 - slope_in))
     input_grad = input_grad + grad_flat * returned * slope_out * (1.0 - slope_out) * gate_out
     return (outputs, input_grad.astype(BF16), channel_grad, block_grad)

time: 94.5 us -> 94.5 us (level)
  no operation moved by 1% of the time
where the time goes in v11:
time: 94.5 us; the launch traced here: 93.4 us
  starting transfers between devices  42.3 us (45%)
  waiting for transfers between devices  19.3 us (20%)
  local copies, waits for them, and re-layouts  10.8 us (11%)
  other arithmetic  10.6 us (11%)
  matrix products  9.18 us (10%)
  between operations  1.23 us (1%)
    ppermute x15, starting transfers between devices, exchange(): lax.ppermute(pieces[k], axis_name, [(i, (i + k) % n) for i in range(n)])  24.4 us
    all_to_all x5, starting transfers between devices, swap(): return lax.all_to_all(pieces, axis_name, 0, 0, tiled=True)  18 us
    all_to_all x5, waiting for transfers between devices, swap(): return lax.all_to_all(pieces, axis_name, 0, 0, tiled=True)  13.6 us
    ppermute x15, waiting for transfers between devices, exchange(): lax.ppermute(pieces[k], axis_name, [(i, (i + k) % n) for i in range(n)])  5.78 us
    dynamic_update_slice x5, other arithmetic, place_chunks(): out = lax.dynamic_update_slice_in_dim(out, chunk, start, axis=1)  3.25 us
    convert_element_type x2, other arithmetic, on_device(): added_out = [sum((act_arrived[k].astype(F32) * coefficient(origin_of[k],...  2.9 us
    dynamic_update_slice x3, local copies, waits for them, and re-layouts, place_chunks(): out = lax.dynamic_update_slice_in_dim(out, chunk, start, axis=1)  2.87 us
    unnamed x63, local copies, waits for them, and re-layouts  2.6 us
  transfers between devices with their start and end apart: 20, of which 7 were waited for; matrix products, arithmetic and copies ran while one was open for 24% of the time, Pallas kernels for 0%

profile of v11, /device:TPU:0, one launch (start us, length us, event | category | flops | bytes accessed | tf_op | source)
XLA Modules:
  0.0 93.4 jit_solution(15443318085527777961)
XLA Ops:
  0.6 0.0 copy-start
  0.7 0.7 copy-done.26
  1.4 1.8 %fusion.8 = bf16[512,512]{0,1:T(8,128)(2,1)S(1)} fusion(bf16[1,512,512]{2,1,0:T(8,128)(2,1)} %param.11, bf16[512,512]{1,0:T(8,128)(2,1)} %param.8, f32[512]{0:T(512)S(1)} %copy-done.26), kind=kOutput, calls=%fused_computation.25 | convolution fusion | flops 270532608 | bytes 1574912 | tf_op jit(solution)/shard_map/dot_general | solution.py:59
  3.2 0.1 constant_dynamic-slice_fusion.35
  3.3 3.1 %collective-permute-start = (bf16[512,128]{1,0:T(8,128)(2,1)S(1)}, bf16[512,128]{1,0:T(8,128)(2,1)S(1)}, u32[]{:S(2)}, u32[]{:S(2)}) collective-permute-start(bf16[512,128]{1,0:T(8,128)(2,1)S(1)} %get-tuple-element.38), channel_id=1, source_target_pairs={{0,1},{1,2},{2,3},{3,0},{4,5},{5,6},{6,7},{7,4},{8,9},{9,10},{10,1... | collective-permute-start | bytes 393224 | tf_op jit(solution)/shard_map/ppermute | solution.py:14
  6.4 2.6 %collective-permute-start.1 = (bf16[512,128]{1,0:T(8,128)(2,1)S(1)}, bf16[512,128]{1,0:T(8,128)(2,1)S(1)}, u32[]{:S(2)}, u32[]{:S(2)}) collective-permute-start(bf16[512,128]{1,0:T(8,128)(2,1)S(1)} %get-tuple-element.40), channel_id=1, source_target_pairs={{0,2},{1,3},{2,0},{3,1},{4,6},{5,7},{6,4},{7,5},{8,10},{9,11},{10,... | collective-permute-start | bytes 393224 | tf_op jit(solution)/shard_map/ppermute | solution.py:14
  9.0 1.3 %collective-permute-start.2 = (bf16[512,128]{1,0:T(8,128)(2,1)S(1)}, bf16[512,128]{1,0:T(8,128)(2,1)S(1)}, u32[]{:S(2)}, u32[]{:S(2)}) collective-permute-start(bf16[512,128]{1,0:T(8,128)(2,1)S(1)} %get-tuple-element.39), channel_id=1, source_target_pairs={{0,3},{1,0},{2,1},{3,2},{4,7},{5,4},{6,5},{7,6},{8,11},{9,8},{10,9... | collective-permute-start | bytes 393224 | tf_op jit(solution)/shard_map/ppermute | solution.py:14
  10.3 1.0 %copy.25 = bf16[512,512]{1,0:T(8,128)(2,1)} copy(bf16[512,512]{0,1:T(8,128)(2,1)S(1)} %fusion.8) | data formatting | bytes 1048576 | tf_op jit(solution)/shard_map/optimization_barrier | solution.py:62
  11.3 3.7 %all-to-all-start = ((bf16[8,64,512]{2,1,0:T(8,128)(2,1)}), bf16[8,64,512]{2,1,0:T(8,128)(2,1)S(1)}, u32[]{:S(2)}, u32[]{:S(2)}) async-start(bf16[8,64,512]{2,1,0:T(8,128)(2,1)} %bitcast.2), calls=%async_computation | async-start | bytes 1048576 | tf_op jit(solution)/shard_map/all_to_all | solution.py:19
  15.0 0.7 fusion.78
  15.7 0.7 copy-done.10
  16.5 0.1 copy.30
  16.7 0.7 fusion.106
  17.3 0.3 collective-permute-done.1
  17.6 0.9 fusion.56
  18.5 3.3 %collective-permute-start.3 = (bf16[512,128]{1,0:T(8,128)(2,1)}, bf16[512,128]{1,0:T(8,128)(2,1)}, u32[]{:S(2)}, u32[]{:S(2)}) collective-permute-start(bf16[512,128]{1,0:T(8,128)(2,1)} %get-tuple-element.30), channel_id=1, source_target_pairs={{0,1},{1,2},{2,3},{3,0},{4,5},{5,6},{6,7},{7,4},{8,9},{9,10},{10,1... | collective-permute-start | bytes 393224 | tf_op jit(solution)/shard_map/ppermute | solution.py:14
  21.8 1.6 %collective-permute-start.4 = (bf16[512,128]{1,0:T(8,128)(2,1)S(1)}, bf16[512,128]{1,0:T(8,128)(2,1)}, u32[]{:S(2)}, u32[]{:S(2)}) collective-permute-start(bf16[512,128]{1,0:T(8,128)(2,1)S(1)} %get-tuple-element.31), channel_id=1, source_target_pairs={{0,2},{1,3},{2,0},{3,1},{4,6},{5,7},{6,4},{7,5},{8,10},{9,11},{10,... | collective-permute-start | bytes 393224 | tf_op jit(solution)/shard_map/ppermute | solution.py:14
  23.4 0.7 collective-permute-start.5
  24.2 0.6 all-to-all-done
  24.8 0.4 fusion.6
  25.2 0.9 %copy.28 = bf16[8,64,512]{2,1,0:T(8,128)(2,1)} copy(bf16[8,64,512]{2,0,1:T(8,128)(2,1)S(1)} %fusion.6) | data formatting | bytes 1048576 | tf_op jit(solution)/shard_map/convert_element_type | solution.py:77
  26.2 3.5 %all-to-all-start.1 = ((bf16[8,64,512]{2,1,0:T(8,128)(2,1)}), bf16[8,64,512]{2,1,0:T(8,128)(2,1)S(1)}, u32[]{:S(2)}, u32[]{:S(2)}) async-start(bf16[8,64,512]{2,1,0:T(8,128)(2,1)} %copy.28), calls=%async_computation.1 | async-start | bytes 1048576 | tf_op jit(solution)/shard_map/all_to_all | solution.py:19
  29.7 0.1 fusion.77
  29.9 1.0 %constant_dynamic-update-slice_fusion.2 = bf16[512,512]{1,0:T(8,128)(2,1)S(1)} fusion(bf16[512,512]{1,0:T(8,128)(2,1)S(1)} %fusion.77, bf16[512,128]{1,0:T(8,128)(2,1)} %collective-permute-done.3, s32[]{:T(128)S(6)} %select_n.80), kind=kLoop, calls=%fused_computation.166 | loop fusion | bytes 262148 | tf_op jit(solution)/shard_map/dynamic_update_slice | solution.py:33
  30.9 1.1 %collective-permute-done.4 = bf16[512,128]{1,0:T(8,128)(2,1)} collective-permute-done((bf16[512,128]{1,0:T(8,128)(2,1)S(1)}, bf16[512,128]{1,0:T(8,128)(2,1)}, u32[]{:S(2)}, u32[]{:S(2)}) %collective-permute-start.4) | collective-permute-done | bytes 131104 | tf_op jit(solution)/shard_map/ppermute | solution.py:14
  32.0 0.9 %constant_dynamic-update-slice_fusion.1 = bf16[512,512]{1,0:T(8,128)(2,1)S(1)} fusion(bf16[512,512]{1,0:T(8,128)(2,1)S(1)} %constant_dynamic-update-slice_fusion.2, bf16[512,128]{1,0:T(8,128)(2,1)} %collective-permute-done.4, s32[]{:T(128)S(6)} %select_n.82), kind=kLoop, calls=%fused_computation.161 | loop fusion | bytes 262148 | tf_op jit(solution)/shard_map/dynamic_update_slice | solution.py:33
  33.0 0.9 %constant_dynamic-update-slice_fusion = bf16[512,512]{1,0:T(8,128)(2,1)S(1)} fusion(bf16[512,512]{1,0:T(8,128)(2,1)S(1)} %constant_dynamic-update-slice_fusion.1, bf16[512,128]{1,0:T(8,128)(2,1)} %collective-permute-done.5, s32[]{:T(128)S(6)} %select_n.84), kind=kLoop, calls=%fused_computation.156 | loop fusion | bytes 262148 | tf_op jit(solution)/shard_map/dynamic_update_slice | solution.py:33
  33.9 5.4 %all-to-all-done.1 = bf16[8,64,512]{2,1,0:T(8,128)(2,1)S(1)} async-done(((bf16[8,64,512]{2,1,0:T(8,128)(2,1)}), bf16[8,64,512]{2,1,0:T(8,128)(2,1)S(1)}, u32[]{:S(2)}, u32[]{:S(2)}) %all-to-all-start.1) | async-done | bytes 524320 | tf_op jit(solution)/shard_map/all_to_all | solution.py:19
  39.4 0.4 fusion.33
  39.8 1.1 %multiply_convert_fusion = (bf16[512,512]{1,0:T(8,128)(2,1)S(1)}, bf16[512,512]{1,0:T(8,128)(2,1)S(1)}) fusion(bf16[512,512]{1,0:T(8,128)(2,1)S(1)} %constant_dynamic-update-slice_fusion, bf16[512,512]{1,0:T(8,128)(2,1)S(1)} %fusion.33, bf16[1,512,512]{2,1,0:T(8,128)(2,1)S(1)} %copy-done), kind=kOutput, calls=%fused_computation.52 | convolution fusion | flops 274464768 | bytes 2621440 | tf_op jit(solution)/shard_map/dot_general | solution.py:81
  40.9 1.6 %fusion.24 = (bf16[512,512]{1,0:T(8,128)(2,1)}, bf16[512,512]{1,0:T(8,128)(2,1)}) fusion(bf16[512,512]{1,0:T(8,128)(2,1)S(1)} %copy-done.4, f32[512]{0:T(512)S(1)} %copy-done.11, bf16[512,512]{1,0:T(8,128)(2,1)S(1)} %get-tuple-element.25, bf16[1,512,512]{2,1,0:T(8,128)(2,1)S(1)} %copy-done, bf16[512,512]{1,0:T(8,128)(2,1)S(1)} %copy-done.1), kind=kOutput, calls=%fused_computation.41 | convolution fusion | flops 271319040 | bytes 3147776 | tf_op jit(solution)/shard_map/dot_general | solution.py:95
  42.6 3.5 %all-to-all-start.2 = ((bf16[8,64,512]{2,1,0:T(8,128)(2,1)}), bf16[8,64,512]{2,1,0:T(8,128)(2,1)S(1)}, u32[]{:S(2)}, u32[]{:S(2)}) async-start(bf16[8,64,512]{2,1,0:T(8,128)(2,1)} %bitcast.22), calls=%async_computation.2 | async-start | bytes 1048576 | tf_op jit(solution)/shard_map/all_to_all | solution.py:19
  46.1 0.8 constant_dynamic-slice_fusion.13
  46.8 1.0 %collective-permute-start.7 = (bf16[512,128]{1,0:T(8,128)(2,1)}, bf16[512,128]{1,0:T(8,128)(2,1)S(1)}, u32[]{:S(2)}, u32[]{:S(2)}) collective-permute-start(bf16[512,128]{1,0:T(8,128)(2,1)} %get-tuple-element.37), channel_id=1, source_target_pairs={{0,1},{1,2},{2,3},{3,0},{4,5},{5,6},{6,7},{7,4},{8,9},{9,10},{10,1... | collective-permute-start | bytes 393224 | tf_op jit(solution)/shard_map/ppermute | solution.py:14
  47.8 1.3 %collective-permute-start.8 = (bf16[512,128]{1,0:T(8,128)(2,1)}, bf16[512,128]{1,0:T(8,128)(2,1)S(1)}, u32[]{:S(2)}, u32[]{:S(2)}) collective-permute-start(bf16[512,128]{1,0:T(8,128)(2,1)} %get-tuple-element.36), channel_id=1, source_target_pairs={{0,2},{1,3},{2,0},{3,1},{4,6},{5,7},{6,4},{7,5},{8,10},{9,11},{10,... | collective-permute-start | bytes 393224 | tf_op jit(solution)/shard_map/ppermute | solution.py:14
  49.1 1.6 %collective-permute-start.9 = (bf16[512,128]{1,0:T(8,128)(2,1)}, bf16[512,128]{1,0:T(8,128)(2,1)}, u32[]{:S(2)}, u32[]{:S(2)}) collective-permute-start(bf16[512,128]{1,0:T(8,128)(2,1)} %get-tuple-element.35), channel_id=1, source_target_pairs={{0,3},{1,0},{2,1},{3,2},{4,7},{5,4},{6,5},{7,6},{8,11},{9,8},{10,9... | collective-permute-start | bytes 393224 | tf_op jit(solution)/shard_map/ppermute | solution.py:14
  50.7 5.0 %all-to-all-done.2 = bf16[8,64,512]{2,1,0:T(8,128)(2,1)S(1)} async-done(((bf16[8,64,512]{2,1,0:T(8,128)(2,1)}), bf16[8,64,512]{2,1,0:T(8,128)(2,1)S(1)}, u32[]{:S(2)}, u32[]{:S(2)}) %all-to-all-start.2) | async-done | bytes 524320 | tf_op jit(solution)/shard_map/all_to_all | solution.py:19
  55.7 0.4 fusion.7
  56.2 0.9 %copy.31 = bf16[8,64,512]{2,1,0:T(8,128)(2,1)} copy(bf16[8,64,512]{2,0,1:T(8,128)(2,1)S(1)} %fusion.7) | data formatting | bytes 1048576 | tf_op jit(solution)/shard_map/convert_element_type | solution.py:104
  57.1 3.6 %all-to-all-start.3 = ((bf16[8,64,512]{2,1,0:T(8,128)(2,1)}), bf16[8,64,512]{2,1,0:T(8,128)(2,1)S(1)}, u32[]{:S(2)}, u32[]{:S(2)}) async-start(bf16[8,64,512]{2,1,0:T(8,128)(2,1)} %copy.31), calls=%async_computation.3 | async-start | bytes 1048576 | tf_op jit(solution)/shard_map/all_to_all | solution.py:19
  60.9 1.3 %fusion.113 = bf16[512,512]{1,0:T(8,128)(2,1)} fusion(bf16[512,512]{1,0:T(8,128)(2,1)S(1)} %fusion.33, bf16[512,512]{1,0:T(8,128)(2,1)S(1)} %copy-done.29), kind=kOutput, calls=%fused_computation.212 | convolution fusion | flops 268435456 | bytes 1572864 | tf_op jit(solution)/shard_map/dot_general | solution.py:97
  62.2 1.9 %fusion.72 = (bf16[512,128]{1,0:T(8,128)(2,1)}, bf16[512,128]{1,0:T(8,128)(2,1)}, bf16[512,128]{1,0:T(8,128)(2,1)}) fusion(bf16[512,128]{1,0:T(8,128)(2,1)S(1)} %collective-permute-done.7, bf16[512,128]{1,0:T(8,128)(2,1)S(1)} %collective-permute-done.8, bf16[512,128]{1,0:T(8,128)(2,1)} %collective-permute-done.9, f32[128]{0:T(128)S(1)} %get-tuple-element.42, ...), kind=kLoop, calls=%fused_computation.123 | loop fusion | flops 1835008 | bytes 923652 | tf_op jit(solution)/shard_map/convert_element_type | solution.py:89
  64.1 1.4 %collective-permute-start.10 = (bf16[512,128]{1,0:T(8,128)(2,1)}, bf16[512,128]{1,0:T(8,128)(2,1)}, u32[]{:S(2)}, u32[]{:S(2)}) collective-permute-start(bf16[512,128]{1,0:T(8,128)(2,1)} %get-tuple-element.27), channel_id=1, source_target_pairs={{0,1},{1,2},{2,3},{3,0},{4,5},{5,6},{6,7},{7,4},{8,9},{9,10},{10,1... | collective-permute-start | bytes 393224 | tf_op jit(solution)/shard_map/ppermute | solution.py:14
  65.5 0.9 collective-permute-start.11
  66.4 1.6 %collective-permute-start.12 = (bf16[512,128]{1,0:T(8,128)(2,1)}, bf16[512,128]{1,0:T(8,128)(2,1)}, u32[]{:S(2)}, u32[]{:S(2)}) collective-permute-start(bf16[512,128]{1,0:T(8,128)(2,1)} %get-tuple-element.26), channel_id=1, source_target_pairs={{0,3},{1,0},{2,1},{3,2},{4,7},{5,4},{6,5},{7,6},{8,11},{9,8},{10,9... | collective-permute-start | bytes 393224 | tf_op jit(solution)/shard_map/ppermute | solution.py:14
  68.0 2.4 %all-to-all-done.3 = bf16[8,64,512]{2,1,0:T(8,128)(2,1)S(1)} async-done(((bf16[8,64,512]{2,1,0:T(8,128)(2,1)}), bf16[8,64,512]{2,1,0:T(8,128)(2,1)S(1)}, u32[]{:S(2)}, u32[]{:S(2)}) %all-to-all-start.3) | async-done | bytes 524320 | tf_op jit(solution)/shard_map/all_to_all | solution.py:19
  70.4 0.6 fusion.110
  71.0 0.2 copy-done.6
  71.2 0.8 dynamic-slice_convert_fusion.1
  72.0 0.9 %collective-permute-start.6 = (bf16[128,512]{1,0:T(8,128)(2,1)}, bf16[128,512]{1,0:T(8,128)(2,1)}, u32[]{:S(2)}, u32[]{:S(2)}) collective-permute-start(bf16[128,512]{1,0:T(8,128)(2,1)} %get-tuple-element.34), channel_id=1, source_target_pairs={{0,1},{1,2},{2,3},{3,0},{4,5},{5,6},{6,7},{7,4},{8,9},{9,10},{10,1... | collective-permute-start | bytes 393224 | tf_op jit(solution)/shard_map/ppermute | solution.py:14
  73.0 0.6 copy-done.22
  73.6 0.1 copy-done.23
  73.6 1.0 %fusion.60 = bf16[512,128]{1,0:T(8,128)(2,1)S(1)} fusion(bf16[512,128]{1,0:T(8,128)(2,1)S(1)} %collective-permute-done.7, bf16[512,128]{1,0:T(8,128)(2,1)S(1)} %collective-permute-done.8, bf16[512,128]{1,0:T(8,128)(2,1)} %collective-permute-done.9, f32[128]{0:T(128)S(1)} %copy-done.22, f32[128]{0:T(128)S(1)} %copy-done.23, f32[128]{0:T(128)S(1)} %copy-done.24, ...), kind=kLoop, calls=%fused_computation.111 | loop fusion | flops 786432 | bytes 657412 | tf_op jit(solution)/shard_map/convert_element_type | solution.py:89
  74.7 1.4 %collective-permute-start.13 = (bf16[128,512]{1,0:T(8,128)(2,1)}, bf16[128,512]{1,0:T(8,128)(2,1)S(1)}, u32[]{:S(2)}, u32[]{:S(2)}) collective-permute-start(bf16[128,512]{1,0:T(8,128)(2,1)} %get-tuple-element.32), channel_id=1, source_target_pairs={{0,2},{1,3},{2,0},{3,1},{4,6},{5,7},{6,4},{7,5},{8,10},{9,11},{10,... | collective-permute-start | bytes 393224 | tf_op jit(solution)/shard_map/ppermute | solution.py:14
  76.0 3.6 %all-to-all-start.4 = ((bf16[8,64,512]{2,1,0:T(8,128)(2,1)}), bf16[8,64,512]{2,1,0:T(8,128)(2,1)S(1)}, u32[]{:S(2)}, u32[]{:S(2)}) async-start(bf16[8,64,512]{2,1,0:T(8,128)(2,1)} %bitcast.42), calls=%async_computation.4 | async-start | bytes 1048576 | tf_op jit(solution)/shard_map/all_to_all | solution.py:19
  79.7 1.7 %collective-permute-start.14 = (bf16[128,512]{1,0:T(8,128)(2,1)S(1)}, bf16[128,512]{1,0:T(8,128)(2,1)S(1)}, u32[]{:S(2)}, u32[]{:S(2)}) collective-permute-start(bf16[128,512]{1,0:T(8,128)(2,1)S(1)} %copy-done.9), channel_id=1, source_target_pairs={{0,3},{1,0},{2,1},{3,2},{4,7},{5,4},{6,5},{7,6},{8,11},{9,8},{10,9... | collective-permute-start | bytes 393224 | tf_op jit(solution)/shard_map/ppermute | solution.py:14
  81.4 0.1 fusion.73
  81.5 1.0 %fusion.74 = bf16[512,512]{1,0:T(8,128)(2,1)S(1)} fusion(bf16[512,512]{1,0:T(8,128)(2,1)S(1)} %fusion.73, s32[]{:T(128)S(6)} %select_n.80, bf16[512,128]{1,0:T(8,128)(2,1)} %collective-permute-done.10, bf16[512,512]{1,0:T(8,128)(2,1)S(1)} %fusion.33), kind=kLoop, calls=%fused_computation.134 | loop fusion | flops 262144 | bytes 393220 | tf_op jit(solution)/shard_map/dynamic_update_slice | solution.py:33
  82.5 1.0 %fusion.75 = bf16[512,512]{1,0:T(8,128)(2,1)S(1)} fusion(bf16[512,512]{1,0:T(8,128)(2,1)S(1)} %fusion.74, s32[]{:T(128)S(6)} %select_n.82, bf16[512,128]{1,0:T(8,128)(2,1)} %collective-permute-done.11, bf16[512,512]{1,0:T(8,128)(2,1)S(1)} %fusion.33), kind=kLoop, calls=%fused_computation.135 | loop fusion | flops 262144 | bytes 393220 | tf_op jit(solution)/shard_map/dynamic_update_slice | solution.py:33
  83.5 1.1 %fusion.76 = bf16[512,512]{1,0:T(8,128)(2,1)S(1)} fusion(bf16[512,512]{1,0:T(8,128)(2,1)S(1)} %fusion.75, s32[]{:T(128)S(6)} %select_n.84, bf16[512,128]{1,0:T(8,128)(2,1)} %collective-permute-done.12, bf16[512,512]{1,0:T(8,128)(2,1)S(1)} %fusion.33), kind=kLoop, calls=%fused_computation.136 | loop fusion | flops 262144 | bytes 393220 | tf_op jit(solution)/shard_map/dynamic_update_slice | solution.py:33
  84.6 4.4 %collective-permute-done.13 = bf16[128,512]{1,0:T(8,128)(2,1)S(1)} collective-permute-done((bf16[128,512]{1,0:T(8,128)(2,1)}, bf16[128,512]{1,0:T(8,128)(2,1)S(1)}, u32[]{:S(2)}, u32[]{:S(2)}) %collective-permute-start.13) | collective-permute-done | bytes 131104 | tf_op jit(solution)/shard_map/ppermute | solution.py:14
  89.0 1.7 %add_bitcast_fusion = f32[1,128,512]{2,1,0:T(8,128)} fusion(bf16[128,512]{1,0:T(8,128)(2,1)S(1)} %collective-permute-done.14, bf16[128,512]{1,0:T(8,128)(2,1)S(1)} %collective-permute-done.13, bf16[128,512]{1,0:T(8,128)(2,1)} %collective-permute-done.6, bf16[512,512]{1,0:T(8,128)(2,1)} %copy-done.8, s32[]{:T(128)S(6)} %select_n.64), kind=kLoop, calls=%fused_computation.124 | loop fusion | flops 458752 | bytes 786436 | tf_op jit(solution)/shard_map/broadcast_in_dim | solution.py:117
  90.7 2.0 %fusion.3 = bf16[512,512]{1,0:T(8,128)(2,1)} fusion(bf16[512,512]{1,0:T(8,128)(2,1)S(1)} %bitcast.112, bf16[512,512]{1,0:T(8,128)(2,1)S(1)} %copy-done.30, bf16[512,512]{1,0:T(8,128)(2,1)S(1)} %copy-done.5, bf16[512,512]{1,0:T(8,128)(2,1)S(1)} %bitcast.110, bf16[1,512,512]{2,1,0:T(8,128)(2,1)S(1)} %copy-done.25, f32[512]{0:T(512)S(1)} %copy-done.11, ...), kind=kOutput, calls=%fused_computation.20 | convolution fusion | flops 274726912 | bytes 3149824 | tf_op jit(solution)/shard_map/dot_general | solution.py:129
  92.7 0.7 convert_reduce_fusion
  (71 shorter events, 0.2 us)
Async XLA Ops:
  0.6 39.1 %copy-start = (bf16[1,512,512]{2,1,0:T(8,128)(2,1)S(1)}, bf16[1,512,512]{2,1,0:T(8,128)(2,1)}, u32[]{:S(2)}) copy-start(bf16[1,512,512]{2,1,0:T(8,128)(2,1)} %param.13) | copy-start | bytes 1572868
  0.7 0.7 copy-start.26
  1.4 1.8 %copy-start.1 = (bf16[512,512]{1,0:T(8,128)(2,1)S(1)}, bf16[512,512]{1,0:T(8,128)(2,1)}, u32[]{:S(2)}) copy-start(bf16[512,512]{1,0:T(8,128)(2,1)} %param.15) | copy-start | bytes 1572868
  3.3 14.0 %collective-permute-start = (bf16[512,128]{1,0:T(8,128)(2,1)S(1)}, bf16[512,128]{1,0:T(8,128)(2,1)S(1)}, u32[]{:S(2)}, u32[]{:S(2)}) collective-permute-start(bf16[512,128]{1,0:T(8,128)(2,1)S(1)} %get-tuple-element.38), channel_id=1, source_target_pairs={{0,1},{1,2},{2,3},{3,0},{4,5},{5,6},{6,7},{7,4},{8,9},{9,10},{10,1... | collective-permute-start | bytes 393224 | tf_op jit(solution)/shard_map/ppermute | solution.py:14
  6.4 11.2 %collective-permute-start.1 = (bf16[512,128]{1,0:T(8,128)(2,1)S(1)}, bf16[512,128]{1,0:T(8,128)(2,1)S(1)}, u32[]{:S(2)}, u32[]{:S(2)}) collective-permute-start(bf16[512,128]{1,0:T(8,128)(2,1)S(1)} %get-tuple-element.40), channel_id=1, source_target_pairs={{0,2},{1,3},{2,0},{3,1},{4,6},{5,7},{6,4},{7,5},{8,10},{9,11},{10,... | collective-permute-start | bytes 393224 | tf_op jit(solution)/shard_map/ppermute | solution.py:14
  9.0 8.6 %collective-permute-start.2 = (bf16[512,128]{1,0:T(8,128)(2,1)S(1)}, bf16[512,128]{1,0:T(8,128)(2,1)S(1)}, u32[]{:S(2)}, u32[]{:S(2)}) collective-permute-start(bf16[512,128]{1,0:T(8,128)(2,1)S(1)} %get-tuple-element.39), channel_id=1, source_target_pairs={{0,3},{1,0},{2,1},{3,2},{4,7},{5,4},{6,5},{7,6},{8,11},{9,8},{10,9... | collective-permute-start | bytes 393224 | tf_op jit(solution)/shard_map/ppermute | solution.py:14
  11.3 13.5 %all-to-all-start = ((bf16[8,64,512]{2,1,0:T(8,128)(2,1)}), bf16[8,64,512]{2,1,0:T(8,128)(2,1)S(1)}, u32[]{:S(2)}, u32[]{:S(2)}) async-start(bf16[8,64,512]{2,1,0:T(8,128)(2,1)} %bitcast.2), calls=%async_computation | async-start | bytes 1048576 | tf_op jit(solution)/shard_map/all_to_all | solution.py:19
  15.7 0.7 copy-start.10
  18.5 11.4 %collective-permute-start.3 = (bf16[512,128]{1,0:T(8,128)(2,1)}, bf16[512,128]{1,0:T(8,128)(2,1)}, u32[]{:S(2)}, u32[]{:S(2)}) collective-permute-start(bf16[512,128]{1,0:T(8,128)(2,1)} %get-tuple-element.30), channel_id=1, source_target_pairs={{0,1},{1,2},{2,3},{3,0},{4,5},{5,6},{6,7},{7,4},{8,9},{9,10},{10,1... | collective-permute-start | bytes 393224 | tf_op jit(solution)/shard_map/ppermute | solution.py:14
  21.8 10.2 %collective-permute-start.4 = (bf16[512,128]{1,0:T(8,128)(2,1)S(1)}, bf16[512,128]{1,0:T(8,128)(2,1)}, u32[]{:S(2)}, u32[]{:S(2)}) collective-permute-start(bf16[512,128]{1,0:T(8,128)(2,1)S(1)} %get-tuple-element.31), channel_id=1, source_target_pairs={{0,2},{1,3},{2,0},{3,1},{4,6},{5,7},{6,4},{7,5},{8,10},{9,11},{10,... | collective-permute-start | bytes 393224 | tf_op jit(solution)/shard_map/ppermute | solution.py:14
  23.4 9.5 %collective-permute-start.5 = (bf16[512,128]{1,0:T(8,128)(2,1)S(1)}, bf16[512,128]{1,0:T(8,128)(2,1)}, u32[]{:S(2)}, u32[]{:S(2)}) collective-permute-start(bf16[512,128]{1,0:T(8,128)(2,1)S(1)} %get-tuple-element.29), channel_id=1, source_target_pairs={{0,3},{1,0},{2,1},{3,2},{4,7},{5,4},{6,5},{7,6},{8,11},{9,8},{10,9... | collective-permute-start | bytes 393224 | tf_op jit(solution)/shard_map/ppermute | solution.py:14
  26.2 13.2 %all-to-all-start.1 = ((bf16[8,64,512]{2,1,0:T(8,128)(2,1)}), bf16[8,64,512]{2,1,0:T(8,128)(2,1)S(1)}, u32[]{:S(2)}, u32[]{:S(2)}) async-start(bf16[8,64,512]{2,1,0:T(8,128)(2,1)} %copy.28), calls=%async_computation.1 | async-start | bytes 1048576 | tf_op jit(solution)/shard_map/all_to_all | solution.py:19
  29.9 9.5 %copy-start.3 = (bf16[512,512]{1,0:T(8,128)(2,1)S(1)}, bf16[512,512]{1,0:T(8,128)(2,1)}, u32[]{:S(2)}) copy-start(bf16[512,512]{1,0:T(8,128)(2,1)} %param.8) | copy-start | bytes 1572868
  33.0 6.4 %copy-start.11 = (f32[512]{0:T(512)S(1)}, f32[512]{0:T(512)}, u32[]{:S(2)}) copy-start(f32[512]{0:T(512)} %param.10) | copy-start | bytes 6148
  39.8 1.2 %copy-start.4 = (bf16[512,512]{1,0:T(8,128)(2,1)S(1)}, bf16[512,512]{1,0:T(8,128)(2,1)}, u32[]{:S(2)}) copy-start(bf16[512,512]{1,0:T(8,128)(2,1)} %param.8) | copy-start | bytes 1572868
  40.9 1.7 %copy-start.28 = (bf16[512,512]{1,0:T(8,128)(2,1)}, bf16[512,512]{1,0:T(8,128)(2,1)S(1)}, u32[]{:S(2)}) copy-start(bf16[512,512]{1,0:T(8,128)(2,1)S(1)} %get-tuple-element.25) | copy-start | bytes 1572868
  42.6 13.2 %all-to-all-start.2 = ((bf16[8,64,512]{2,1,0:T(8,128)(2,1)}), bf16[8,64,512]{2,1,0:T(8,128)(2,1)S(1)}, u32[]{:S(2)}, u32[]{:S(2)}) async-start(bf16[8,64,512]{2,1,0:T(8,128)(2,1)} %bitcast.22), calls=%async_computation.2 | async-start | bytes 1048576 | tf_op jit(solution)/shard_map/all_to_all | solution.py:19
  46.8 15.3 %collective-permute-start.7 = (bf16[512,128]{1,0:T(8,128)(2,1)}, bf16[512,128]{1,0:T(8,128)(2,1)S(1)}, u32[]{:S(2)}, u32[]{:S(2)}) collective-permute-start(bf16[512,128]{1,0:T(8,128)(2,1)} %get-tuple-element.37), channel_id=1, source_target_pairs={{0,1},{1,2},{2,3},{3,0},{4,5},{5,6},{6,7},{7,4},{8,9},{9,10},{10,1... | collective-permute-start | bytes 393224 | tf_op jit(solution)/shard_map/ppermute | solution.py:14
  47.8 14.3 %collective-permute-start.8 = (bf16[512,128]{1,0:T(8,128)(2,1)}, bf16[512,128]{1,0:T(8,128)(2,1)S(1)}, u32[]{:S(2)}, u32[]{:S(2)}) collective-permute-start(bf16[512,128]{1,0:T(8,128)(2,1)} %get-tuple-element.36), channel_id=1, source_target_pairs={{0,2},{1,3},{2,0},{3,1},{4,6},{5,7},{6,4},{7,5},{8,10},{9,11},{10,... | collective-permute-start | bytes 393224 | tf_op jit(solution)/shard_map/ppermute | solution.py:14
  49.1 13.0 %collective-permute-start.9 = (bf16[512,128]{1,0:T(8,128)(2,1)}, bf16[512,128]{1,0:T(8,128)(2,1)}, u32[]{:S(2)}, u32[]{:S(2)}) collective-permute-start(bf16[512,128]{1,0:T(8,128)(2,1)} %get-tuple-element.35), channel_id=1, source_target_pairs={{0,3},{1,0},{2,1},{3,2},{4,7},{5,4},{6,5},{7,6},{8,11},{9,8},{10,9... | collective-permute-start | bytes 393224 | tf_op jit(solution)/shard_map/ppermute | solution.py:14
  57.1 3.6 %copy-start.29 = (bf16[512,512]{1,0:T(8,128)(2,1)S(1)}, bf16[512,512]{1,0:T(8,128)(2,1)}, u32[]{:S(2)}) copy-start(bf16[512,512]{1,0:T(8,128)(2,1)} %copy-done.28) | copy-start | bytes 1572868
  57.1 13.3 %all-to-all-start.3 = ((bf16[8,64,512]{2,1,0:T(8,128)(2,1)}), bf16[8,64,512]{2,1,0:T(8,128)(2,1)S(1)}, u32[]{:S(2)}, u32[]{:S(2)}) async-start(bf16[8,64,512]{2,1,0:T(8,128)(2,1)} %copy.31), calls=%async_computation.3 | async-start | bytes 1048576 | tf_op jit(solution)/shard_map/all_to_all | solution.py:19
  60.8 1.4 %copy-start.12 = (f32[128]{0:T(128)S(1)}, f32[128]{0:T(128)}, u32[]{:S(2)}) copy-start(f32[128]{0:T(128)} %get-tuple-element.43) | copy-start | bytes 1540
  60.8 1.4 %copy-start.13 = (f32[128]{0:T(128)S(1)}, f32[128]{0:T(128)}, u32[]{:S(2)}) copy-start(f32[128]{0:T(128)} %get-tuple-element.44) | copy-start | bytes 1540
  60.8 1.4 %copy-start.14 = (f32[128]{0:T(128)S(1)}, f32[128]{0:T(128)}, u32[]{:S(2)}) copy-start(f32[128]{0:T(128)} %get-tuple-element.45) | copy-start | bytes 1540
  60.8 1.4 %copy-start.15 = (f32[128]{0:T(128)S(1)}, f32[128]{0:T(128)}, u32[]{:S(2)}) copy-start(f32[128]{0:T(128)} %get-tuple-element.46) | copy-start | bytes 1540
  60.8 1.4 %copy-start.16 = (f32[128]{0:T(128)S(1)}, f32[128]{0:T(128)}, u32[]{:S(2)}) copy-start(f32[128]{0:T(128)} %get-tuple-element.47) | copy-start | bytes 1540
  60.8 1.4 %copy-start.17 = (f32[128]{0:T(128)S(1)}, f32[128]{0:T(128)}, u32[]{:S(2)}) copy-start(f32[128]{0:T(128)} %get-tuple-element.48) | copy-start | bytes 1540
  60.8 1.4 %copy-start.18 = (f32[128]{0:T(128)S(1)}, f32[128]{0:T(128)}, u32[]{:S(2)}) copy-start(f32[128]{0:T(128)} %get-tuple-element.49) | copy-start | bytes 1540
  60.8 1.4 %copy-start.19 = (f32[128]{0:T(128)S(1)}, f32[128]{0:T(128)}, u32[]{:S(2)}) copy-start(f32[128]{0:T(128)} %get-tuple-element.50) | copy-start | bytes 1540
  60.8 1.4 %copy-start.20 = (f32[128]{0:T(128)S(1)}, f32[128]{0:T(128)}, u32[]{:S(2)}) copy-start(f32[128]{0:T(128)} %get-tuple-element.51) | copy-start | bytes 1540
  60.8 1.4 %copy-start.21 = (f32[128]{0:T(128)S(1)}, f32[128]{0:T(128)}, u32[]{:S(2)}) copy-start(f32[128]{0:T(128)} %get-tuple-element.52) | copy-start | bytes 1540
  62.1 8.3 %copy-start.5 = (bf16[512,512]{1,0:T(8,128)(2,1)S(1)}, bf16[512,512]{1,0:T(8,128)(2,1)}, u32[]{:S(2)}) copy-start(bf16[512,512]{1,0:T(8,128)(2,1)} %param.8) | copy-start | bytes 1572868
  64.1 15.5 %collective-permute-start.10 = (bf16[512,128]{1,0:T(8,128)(2,1)}, bf16[512,128]{1,0:T(8,128)(2,1)}, u32[]{:S(2)}, u32[]{:S(2)}) collective-permute-start(bf16[512,128]{1,0:T(8,128)(2,1)} %get-tuple-element.27), channel_id=1, source_target_pairs={{0,1},{1,2},{2,3},{3,0},{4,5},{5,6},{6,7},{7,4},{8,9},{9,10},{10,1... | collective-permute-start | bytes 393224 | tf_op jit(solution)/shard_map/ppermute | solution.py:14
  65.5 4.9 %copy-start.27 = (f32[512]{0:T(512)S(1)}, f32[512]{0:T(512)}, u32[]{:S(2)}) copy-start(f32[512]{0:T(512)} %param.9) | copy-start | bytes 6148
  65.5 15.9 %collective-permute-start.11 = (bf16[512,128]{1,0:T(8,128)(2,1)}, bf16[512,128]{1,0:T(8,128)(2,1)}, u32[]{:S(2)}, u32[]{:S(2)}) collective-permute-start(bf16[512,128]{1,0:T(8,128)(2,1)} %get-tuple-element.28), channel_id=1, source_target_pairs={{0,2},{1,3},{2,0},{3,1},{4,6},{5,7},{6,4},{7,5},{8,10},{9,11},{10,... | collective-permute-start | bytes 393224 | tf_op jit(solution)/shard_map/ppermute | solution.py:14
  66.4 15.0 %collective-permute-start.12 = (bf16[512,128]{1,0:T(8,128)(2,1)}, bf16[512,128]{1,0:T(8,128)(2,1)}, u32[]{:S(2)}, u32[]{:S(2)}) collective-permute-start(bf16[512,128]{1,0:T(8,128)(2,1)} %get-tuple-element.26), channel_id=1, source_target_pairs={{0,3},{1,0},{2,1},{3,2},{4,7},{5,4},{6,5},{7,6},{8,11},{9,8},{10,9... | collective-permute-start | bytes 393224 | tf_op jit(solution)/shard_map/ppermute | solution.py:14
  70.4 0.8 copy-start.6
  71.2 3.4 %copy-start.8 = (bf16[512,512]{1,0:T(8,128)(2,1)}, bf16[512,512]{1,0:T(8,128)(2,1)S(1)}, u32[]{:S(2)}) copy-start(bf16[512,512]{1,0:T(8,128)(2,1)S(1)} %fusion.110) | copy-start | bytes 1572868
  72.0 9.4 %collective-permute-start.6 = (bf16[128,512]{1,0:T(8,128)(2,1)}, bf16[128,512]{1,0:T(8,128)(2,1)}, u32[]{:S(2)}, u32[]{:S(2)}) collective-permute-start(bf16[128,512]{1,0:T(8,128)(2,1)} %get-tuple-element.34), channel_id=1, source_target_pairs={{0,1},{1,2},{2,3},{3,0},{4,5},{5,6},{6,7},{7,4},{8,9},{9,10},{10,1... | collective-permute-start | bytes 393224 | tf_op jit(solution)/shard_map/ppermute | solution.py:14
  73.0 0.6 copy-start.22
  73.0 0.7 copy-start.23
  73.0 0.7 copy-start.24
  74.7 14.3 %collective-permute-start.13 = (bf16[128,512]{1,0:T(8,128)(2,1)}, bf16[128,512]{1,0:T(8,128)(2,1)S(1)}, u32[]{:S(2)}, u32[]{:S(2)}) collective-permute-start(bf16[128,512]{1,0:T(8,128)(2,1)} %get-tuple-element.32), channel_id=1, source_target_pairs={{0,2},{1,3},{2,0},{3,1},{4,6},{5,7},{6,4},{7,5},{8,10},{9,11},{10,... | collective-permute-start | bytes 393224 | tf_op jit(solution)/shard_map/ppermute | solution.py:14
  76.0 3.6 %copy-start.9 = (bf16[128,512]{1,0:T(8,128)(2,1)S(1)}, bf16[128,512]{1,0:T(8,128)(2,1)}, u32[]{:S(2)}) copy-start(bf16[128,512]{1,0:T(8,128)(2,1)} %get-tuple-element.33) | copy-start | bytes 393220
  76.0 16.7 %all-to-all-start.4 = ((bf16[8,64,512]{2,1,0:T(8,128)(2,1)}), bf16[8,64,512]{2,1,0:T(8,128)(2,1)S(1)}, u32[]{:S(2)}, u32[]{:S(2)}) async-start(bf16[8,64,512]{2,1,0:T(8,128)(2,1)} %bitcast.42), calls=%async_computation.4 | async-start | bytes 1048576 | tf_op jit(solution)/shard_map/all_to_all | solution.py:19
  79.7 9.3 %collective-permute-start.14 = (bf16[128,512]{1,0:T(8,128)(2,1)S(1)}, bf16[128,512]{1,0:T(8,128)(2,1)S(1)}, u32[]{:S(2)}, u32[]{:S(2)}) collective-permute-start(bf16[128,512]{1,0:T(8,128)(2,1)S(1)} %copy-done.9), channel_id=1, source_target_pairs={{0,3},{1,0},{2,1},{3,2},{4,7},{5,4},{6,5},{7,6},{8,11},{9,8},{10,9... | collective-permute-start | bytes 393224 | tf_op jit(solution)/shard_map/ppermute | solution.py:14
  82.5 8.2 %copy-start.30 = (bf16[512,512]{1,0:T(8,128)(2,1)S(1)}, bf16[512,512]{1,0:T(8,128)(2,1)}, u32[]{:S(2)}) copy-start(bf16[512,512]{1,0:T(8,128)(2,1)} %get-tuple-element.73) | copy-start | bytes 1572868
  83.5 7.2 %copy-start.7 = (bf16[8,64,512]{2,1,0:T(8,128)(2,1)S(1)}, bf16[8,64,512]{2,1,0:T(8,128)(2,1)}, u32[]{:S(2)}) copy-start(bf16[8,64,512]{2,1,0:T(8,128)(2,1)} %copy-done.6) | copy-start | bytes 1572868
  83.5 7.2 %copy-start.25 = (bf16[1,512,512]{2,1,0:T(8,128)(2,1)S(1)}, bf16[1,512,512]{2,1,0:T(8,128)(2,1)}, u32[]{:S(2)}) copy-start(bf16[1,512,512]{2,1,0:T(8,128)(2,1)} %param.11) | copy-start | bytes 1572868
  84.6 8.1 %copy-start.2 = (bf16[512,512]{1,0:T(8,128)(2,1)}, bf16[512,512]{1,0:T(8,128)(2,1)S(1)}, u32[]{:S(2)}) copy-start(bf16[512,512]{1,0:T(8,128)(2,1)S(1)} %fusion.76) | copy-start | bytes 1572868

commit v12 on v6

--- a/solution.py
+++ b/solution.py
@@ -112,7 +112,6 @@
     )
     first_block, added_back = lax.optimization_barrier((block_arrived[1], added_back))
     block_arrived[1] = first_block
-    block_grad = sum(part.astype(F32) for part in block_arrived)[None]
     outputs = place_chunks(
         [
             (lane_chunk(hidden, t, kq).astype(F32) + part.astype(F32)).astype(BF16)
@@ -123,6 +122,9 @@
     )
     channel_arrived = swap(split_rows(channel_part, n).astype(BF16), "seq")
     channel_grad = jnp.sum(channel_arrived.astype(F32), axis=0)[None]
+    late_blocks, channel_grad = lax.optimization_barrier((block_arrived[2:], channel_grad))
+    block_arrived[2:] = late_blocks
+    block_grad = sum(part.astype(F32) for part in block_arrived)[None]
 
     spread = jnp.dot(first_blocks[0].T, first_grad, preferred_element_type=F32)
     input_grad = grad_flat + spread * (slope_in + gate_in * source * slope_in * (1.0 - slope_in))

time: 93.2 us -> 99.7 us (1.070)
  waiting for transfers between devices: 17.1 us -> 27.3 us
  starting transfers between devices: 42.7 us -> 39.4 us
  matrix products: 10.3 us -> 9.14 us
  local copies, waits for them, and re-layouts: 9.92 us -> 11 us
    ppermute x15, waiting for transfers between devices: 5.63 us -> 23.3 us  [exchange(): lax.ppermute(pieces[k], axis_name, [(i, (i + k) % n) for i in range(n)])]
    all_to_all x5, waiting for transfers between devices: 11.5 us -> 3.99 us  [swap(): return lax.all_to_all(pieces, axis_name, 0, 0, tiled=True)]
    ppermute x15, starting transfers between devices: 24.9 us -> 19.2 us  [exchange(): lax.ppermute(pieces[k], axis_name, [(i, (i + k) % n) for i in range(n)])]
    all_to_all x5, starting transfers between devices: 17.8 us -> 20.2 us  [swap(): return lax.all_to_all(pieces, axis_name, 0, 0, tiled=True)]
    dot_general x1, matrix products: 3.19 us -> 1.99 us  [on_device(): spread = jnp.dot(first_blocks[0].T, first_grad, preferred_element_type=F32)]
    unnamed x59 -> x61, local copies, waits for them, and re-layouts: 2.49 us -> 3.66 us
  transfers between devices with their start and end apart: 20 -> 20, of which waited for: 8 -> 10; matrix products, arithmetic and copies ran while one was open for 25% -> 20% of each run, Pallas kernels for 0% -> 0%
where the time goes in v12:
time: 99.7 us; the launch traced here: 98.8 us
  starting transfers between devices  39.4 us (40%)
  waiting for transfers between devices  27.3 us (27%)
  local copies, waits for them, and re-layouts  11 us (11%)
  other arithmetic  11 us (11%)
  matrix products  9.14 us (9%)
  between operations  1.05 us (1%)
    ppermute x15, waiting for transfers between devices, exchange(): lax.ppermute(pieces[k], axis_name, [(i, (i + k) % n) for i in range(n)])  23.3 us
    all_to_all x5, starting transfers between devices, swap(): return lax.all_to_all(pieces, axis_name, 0, 0, tiled=True)  20.2 us
    ppermute x15, starting transfers between devices, exchange(): lax.ppermute(pieces[k], axis_name, [(i, (i + k) % n) for i in range(n)])  19.2 us
    all_to_all x5, waiting for transfers between devices, swap(): return lax.all_to_all(pieces, axis_name, 0, 0, tiled=True)  3.99 us
    unnamed x61, local copies, waits for them, and re-layouts  3.66 us
    convert_element_type x2, other arithmetic, on_device(): added_out = [sum((act_arrived[k].astype(F32) * coefficient(origin_of[k],...  3.49 us
    dynamic_update_slice x5, other arithmetic, place_chunks(): out = lax.dynamic_update_slice_in_dim(out, chunk, start, axis=1)  3.1 us
    dynamic_update_slice x3, local copies, waits for them, and re-layouts, place_chunks(): out = lax.dynamic_update_slice_in_dim(out, chunk, start, axis=1)  2.81 us
  transfers between devices with their start and end apart: 20, of which 10 were waited for; matrix products, arithmetic and copies ran while one was open for 20% of the time, Pallas kernels for 0%

profile of v12, /device:TPU:0, one launch (start us, length us, event | category | flops | bytes accessed | tf_op | source)
XLA Modules:
  0.0 98.8 jit_solution(2060123216216718009)
XLA Ops:
  0.6 1.8 %fusion.8 = bf16[512,512]{0,1:T(8,128)(2,1)S(1)} fusion(bf16[1,512,512]{2,1,0:T(8,128)(2,1)} %param.11, bf16[512,512]{1,0:T(8,128)(2,1)} %param.8, f32[512]{0:T(512)} %param.9), kind=kOutput, calls=%fused_computation.25 | convolution fusion | flops 270532608 | bytes 1574912 | tf_op jit(solution)/shard_map/dot_general | solution.py:59
  2.4 1.0 %copy.25 = bf16[512,512]{1,0:T(8,128)(2,1)} copy(bf16[512,512]{0,1:T(8,128)(2,1)S(1)} %fusion.8) | data formatting | bytes 1048576 | tf_op jit(solution)/shard_map/optimization_barrier | solution.py:62
  3.4 5.3 %all-to-all-start = ((bf16[8,64,512]{2,1,0:T(8,128)(2,1)}), bf16[8,64,512]{2,1,0:T(8,128)(2,1)S(1)}, u32[]{:S(2)}, u32[]{:S(2)}) async-start(bf16[8,64,512]{2,1,0:T(8,128)(2,1)} %bitcast.2), calls=%async_computation | async-start | bytes 1048576 | tf_op jit(solution)/shard_map/all_to_all | solution.py:19
  8.7 0.1 constant_dynamic-slice_fusion.35
  8.8 1.6 %collective-permute-start = (bf16[512,128]{1,0:T(8,128)(2,1)S(1)}, bf16[512,128]{1,0:T(8,128)(2,1)S(1)}, u32[]{:S(2)}, u32[]{:S(2)}) collective-permute-start(bf16[512,128]{1,0:T(8,128)(2,1)S(1)} %get-tuple-element.42), channel_id=1, source_target_pairs={{0,1},{1,2},{2,3},{3,0},{4,5},{5,6},{6,7},{7,4},{8,9},{9,10},{10,1... | collective-permute-start | bytes 393224 | tf_op jit(solution)/shard_map/ppermute | solution.py:14
  10.5 2.2 %collective-permute-start.2 = (bf16[512,128]{1,0:T(8,128)(2,1)S(1)}, bf16[512,128]{1,0:T(8,128)(2,1)S(1)}, u32[]{:S(2)}, u32[]{:S(2)}) collective-permute-start(bf16[512,128]{1,0:T(8,128)(2,1)S(1)} %get-tuple-element.43), channel_id=1, source_target_pairs={{0,3},{1,0},{2,1},{3,2},{4,7},{5,4},{6,5},{7,6},{8,11},{9,8},{10,9... | collective-permute-start | bytes 393224 | tf_op jit(solution)/shard_map/ppermute | solution.py:14
  12.7 0.8 collective-permute-start.1
  13.5 0.7 fusion.78
  14.2 0.7 copy-done.10
  14.9 0.1 copy.30
  15.1 0.7 fusion.106
  15.8 1.2 %collective-permute-done = bf16[512,128]{1,0:T(8,128)(2,1)S(1)} collective-permute-done((bf16[512,128]{1,0:T(8,128)(2,1)S(1)}, bf16[512,128]{1,0:T(8,128)(2,1)S(1)}, u32[]{:S(2)}, u32[]{:S(2)}) %collective-permute-start) | collective-permute-done | bytes 131104 | tf_op jit(solution)/shard_map/ppermute | solution.py:14
  17.0 1.9 %collective-permute-done.2 = bf16[512,128]{1,0:T(8,128)(2,1)S(1)} collective-permute-done((bf16[512,128]{1,0:T(8,128)(2,1)S(1)}, bf16[512,128]{1,0:T(8,128)(2,1)S(1)}, u32[]{:S(2)}, u32[]{:S(2)}) %collective-permute-start.2) | collective-permute-done | bytes 131104 | tf_op jit(solution)/shard_map/ppermute | solution.py:14
  18.9 6.2 %collective-permute-done.1 = bf16[512,128]{1,0:T(8,128)(2,1)S(1)} collective-permute-done((bf16[512,128]{1,0:T(8,128)(2,1)S(1)}, bf16[512,128]{1,0:T(8,128)(2,1)S(1)}, u32[]{:S(2)}, u32[]{:S(2)}) %collective-permute-start.1) | collective-permute-done | bytes 131104 | tf_op jit(solution)/shard_map/ppermute | solution.py:14
  25.1 0.9 fusion.56
  26.0 1.6 %collective-permute-start.5 = (bf16[512,128]{1,0:T(8,128)(2,1)S(1)}, bf16[512,128]{1,0:T(8,128)(2,1)}, u32[]{:S(2)}, u32[]{:S(2)}) collective-permute-start(bf16[512,128]{1,0:T(8,128)(2,1)S(1)} %get-tuple-element.33), channel_id=1, source_target_pairs={{0,3},{1,0},{2,1},{3,2},{4,7},{5,4},{6,5},{7,6},{8,11},{9,8},{10,9... | collective-permute-start | bytes 393224 | tf_op jit(solution)/shard_map/ppermute | solution.py:14
  27.6 0.4 collective-permute-start.3
  28.0 0.2 collective-permute-start.4
  28.2 0.4 fusion.6
  28.6 0.9 copy.28
  29.5 3.8 %all-to-all-start.1 = ((bf16[8,64,512]{2,1,0:T(8,128)(2,1)}), bf16[8,64,512]{2,1,0:T(8,128)(2,1)S(1)}, u32[]{:S(2)}, u32[]{:S(2)}) async-start(bf16[8,64,512]{2,1,0:T(8,128)(2,1)} %copy.28), calls=%async_computation.1 | async-start | bytes 1048576 | tf_op jit(solution)/shard_map/all_to_all | solution.py:19
  33.4 0.1 fusion.77
  33.6 2.5 %collective-permute-done.3 = bf16[512,128]{1,0:T(8,128)(2,1)} collective-permute-done((bf16[512,128]{1,0:T(8,128)(2,1)}, bf16[512,128]{1,0:T(8,128)(2,1)}, u32[]{:S(2)}, u32[]{:S(2)}) %collective-permute-start.3) | collective-permute-done | bytes 131104 | tf_op jit(solution)/shard_map/ppermute | solution.py:14
  36.1 0.9 constant_dynamic-update-slice_fusion.2
  37.0 2.5 %collective-permute-done.4 = bf16[512,128]{1,0:T(8,128)(2,1)} collective-permute-done((bf16[512,128]{1,0:T(8,128)(2,1)S(1)}, bf16[512,128]{1,0:T(8,128)(2,1)}, u32[]{:S(2)}, u32[]{:S(2)}) %collective-permute-start.4) | collective-permute-done | bytes 131104 | tf_op jit(solution)/shard_map/ppermute | solution.py:14
  39.5 0.9 constant_dynamic-update-slice_fusion.1
  40.5 0.9 constant_dynamic-update-slice_fusion
  41.5 1.7 %all-to-all-done.1 = bf16[8,64,512]{2,1,0:T(8,128)(2,1)S(1)} async-done(((bf16[8,64,512]{2,1,0:T(8,128)(2,1)}), bf16[8,64,512]{2,1,0:T(8,128)(2,1)S(1)}, u32[]{:S(2)}, u32[]{:S(2)}) %all-to-all-start.1) | async-done | bytes 524320 | tf_op jit(solution)/shard_map/all_to_all | solution.py:19
  43.1 0.4 fusion.33
  43.6 1.1 %multiply_convert_fusion = (bf16[512,512]{1,0:T(8,128)(2,1)S(1)}, bf16[512,512]{1,0:T(8,128)(2,1)S(1)}) fusion(bf16[512,512]{1,0:T(8,128)(2,1)S(1)} %constant_dynamic-update-slice_fusion, bf16[512,512]{1,0:T(8,128)(2,1)S(1)} %fusion.33, bf16[1,512,512]{2,1,0:T(8,128)(2,1)S(1)} %copy-done), kind=kOutput, calls=%fused_computation.52 | convolution fusion | flops 274464768 | bytes 2621440 | tf_op jit(solution)/shard_map/dot_general | solution.py:81
  44.7 1.6 %fusion.24 = (bf16[512,512]{1,0:T(8,128)(2,1)}, bf16[512,512]{1,0:T(8,128)(2,1)}) fusion(bf16[512,512]{1,0:T(8,128)(2,1)S(1)} %copy-done.4, f32[512]{0:T(512)S(1)} %copy-done.11, bf16[512,512]{1,0:T(8,128)(2,1)S(1)} %get-tuple-element.29, bf16[1,512,512]{2,1,0:T(8,128)(2,1)S(1)} %copy-done, bf16[512,512]{1,0:T(8,128)(2,1)S(1)} %copy-done.1), kind=kOutput, calls=%fused_computation.41 | convolution fusion | flops 271319040 | bytes 3147776 | tf_op jit(solution)/shard_map/dot_general | solution.py:95
  46.3 3.5 %all-to-all-start.2 = ((bf16[8,64,512]{2,1,0:T(8,128)(2,1)}), bf16[8,64,512]{2,1,0:T(8,128)(2,1)S(1)}, u32[]{:S(2)}, u32[]{:S(2)}) async-start(bf16[8,64,512]{2,1,0:T(8,128)(2,1)} %bitcast.22), calls=%async_computation.2 | async-start | bytes 1048576 | tf_op jit(solution)/shard_map/all_to_all | solution.py:19
  49.8 0.8 constant_dynamic-slice_fusion.13
  50.6 3.3 %collective-permute-start.9 = (bf16[512,128]{1,0:T(8,128)(2,1)}, bf16[512,128]{1,0:T(8,128)(2,1)S(1)}, u32[]{:S(2)}, u32[]{:S(2)}) collective-permute-start(bf16[512,128]{1,0:T(8,128)(2,1)} %get-tuple-element.39), channel_id=1, source_target_pairs={{0,3},{1,0},{2,1},{3,2},{4,7},{5,4},{6,5},{7,6},{8,11},{9,8},{10,9... | collective-permute-start | bytes 393224 | tf_op jit(solution)/shard_map/ppermute | solution.py:14
  53.9 2.0 %collective-permute-start.8 = (bf16[512,128]{1,0:T(8,128)(2,1)}, bf16[512,128]{1,0:T(8,128)(2,1)S(1)}, u32[]{:S(2)}, u32[]{:S(2)}) collective-permute-start(bf16[512,128]{1,0:T(8,128)(2,1)} %get-tuple-element.40), channel_id=1, source_target_pairs={{0,2},{1,3},{2,0},{3,1},{4,6},{5,7},{6,4},{7,5},{8,10},{9,11},{10,... | collective-permute-start | bytes 393224 | tf_op jit(solution)/shard_map/ppermute | solution.py:14
  55.9 1.3 %fusion.113 = bf16[512,512]{1,0:T(8,128)(2,1)} fusion(bf16[512,512]{1,0:T(8,128)(2,1)S(1)} %fusion.33, bf16[512,512]{1,0:T(8,128)(2,1)S(1)} %copy-done.28), kind=kOutput, calls=%fused_computation.212 | convolution fusion | flops 268435456 | bytes 1572864 | tf_op jit(solution)/shard_map/dot_general | solution.py:97
  57.2 2.3 %all-to-all-done.2 = bf16[8,64,512]{2,1,0:T(8,128)(2,1)S(1)} async-done(((bf16[8,64,512]{2,1,0:T(8,128)(2,1)}), bf16[8,64,512]{2,1,0:T(8,128)(2,1)S(1)}, u32[]{:S(2)}, u32[]{:S(2)}) %all-to-all-start.2) | async-done | bytes 524320 | tf_op jit(solution)/shard_map/all_to_all | solution.py:19
  59.5 0.4 fusion.7
  59.9 0.9 copy.31
  60.9 3.5 %all-to-all-start.3 = ((bf16[8,64,512]{2,1,0:T(8,128)(2,1)}), bf16[8,64,512]{2,1,0:T(8,128)(2,1)S(1)}, u32[]{:S(2)}, u32[]{:S(2)}) async-start(bf16[8,64,512]{2,1,0:T(8,128)(2,1)} %copy.31), calls=%async_computation.3 | async-start | bytes 1048576 | tf_op jit(solution)/shard_map/all_to_all | solution.py:19
  64.4 3.9 %collective-permute-done.8 = bf16[512,128]{1,0:T(8,128)(2,1)S(1)} collective-permute-done((bf16[512,128]{1,0:T(8,128)(2,1)}, bf16[512,128]{1,0:T(8,128)(2,1)S(1)}, u32[]{:S(2)}, u32[]{:S(2)}) %collective-permute-start.8) | collective-permute-done | bytes 131104 | tf_op jit(solution)/shard_map/ppermute | solution.py:14
  68.3 0.5 copy-done.12
  68.9 0.1 copy-done.13
  68.9 1.8 %fusion.72 = (bf16[512,128]{1,0:T(8,128)(2,1)}, bf16[512,128]{1,0:T(8,128)(2,1)}, bf16[512,128]{1,0:T(8,128)(2,1)}) fusion(bf16[512,128]{1,0:T(8,128)(2,1)} %collective-permute-done.7, bf16[512,128]{1,0:T(8,128)(2,1)S(1)} %collective-permute-done.8, bf16[512,128]{1,0:T(8,128)(2,1)S(1)} %collective-permute-done.9, f32[128]{0:T(128)S(1)} %get-tuple-element.46, ...), kind=kLoop, calls=%fused_computation.123 | loop fusion | flops 1835008 | bytes 923652 | tf_op jit(solution)/shard_map/convert_element_type | solution.py:89
  70.8 2.0 %collective-permute-start.10 = (bf16[512,128]{1,0:T(8,128)(2,1)}, bf16[512,128]{1,0:T(8,128)(2,1)}, u32[]{:S(2)}, u32[]{:S(2)}) collective-permute-start(bf16[512,128]{1,0:T(8,128)(2,1)} %get-tuple-element.31), channel_id=1, source_target_pairs={{0,1},{1,2},{2,3},{3,0},{4,5},{5,6},{6,7},{7,4},{8,9},{9,10},{10,1... | collective-permute-start | bytes 393224 | tf_op jit(solution)/shard_map/ppermute | solution.py:14
  72.8 0.8 collective-permute-start.11
  73.6 0.6 copy-done.22
  74.3 1.7 %fusion.60 = bf16[512,128]{1,0:T(8,128)(2,1)} fusion(bf16[512,128]{1,0:T(8,128)(2,1)} %collective-permute-done.7, bf16[512,128]{1,0:T(8,128)(2,1)S(1)} %collective-permute-done.8, bf16[512,128]{1,0:T(8,128)(2,1)S(1)} %collective-permute-done.9, f32[128]{0:T(128)S(1)} %copy-done.22, f32[128]{0:T(128)S(1)} %copy-done.23, f32[128]{0:T(128)S(1)} %copy-done.24, ...), kind=kLoop, calls=%fused_computation.111 | loop fusion | flops 786432 | bytes 657412 | tf_op jit(solution)/shard_map/convert_element_type | solution.py:89
  76.0 4.0 %all-to-all-start.4 = ((bf16[8,64,512]{2,1,0:T(8,128)(2,1)}), bf16[8,64,512]{2,1,0:T(8,128)(2,1)S(1)}, u32[]{:S(2)}, u32[]{:S(2)}) async-start(bf16[8,64,512]{2,1,0:T(8,128)(2,1)} %bitcast.42), calls=%async_computation.4 | async-start | bytes 1048576 | tf_op jit(solution)/shard_map/all_to_all | solution.py:19
  80.0 0.6 fusion.110
  80.6 0.8 copy-done.6
  81.4 1.9 %collective-permute-start.14 = (bf16[128,512]{1,0:T(8,128)(2,1)S(1)}, bf16[128,512]{1,0:T(8,128)(2,1)S(1)}, u32[]{:S(2)}, u32[]{:S(2)}) collective-permute-start(bf16[128,512]{1,0:T(8,128)(2,1)S(1)} %get-tuple-element.36), channel_id=1, source_target_pairs={{0,3},{1,0},{2,1},{3,2},{4,7},{5,4},{6,5},{7,6},{8,11},{9,8},{10,9... | collective-permute-start | bytes 393224 | tf_op jit(solution)/shard_map/ppermute | solution.py:14
  83.2 0.2 collective-permute-start.6
  83.5 2.0 %fusion.3 = bf16[512,512]{1,0:T(8,128)(2,1)} fusion(bf16[512,512]{1,0:T(8,128)(2,1)S(1)} %bitcast.112, bf16[512,512]{1,0:T(8,128)(2,1)S(1)} %copy-done.29, bf16[512,512]{1,0:T(8,128)(2,1)S(1)} %copy-done.5, bf16[512,512]{1,0:T(8,128)(2,1)S(1)} %bitcast.110, bf16[1,512,512]{2,1,0:T(8,128)(2,1)S(1)} %copy-done.25, f32[512]{0:T(512)S(1)} %copy-done.11, ...), kind=kOutput, calls=%fused_computation.20 | convolution fusion | flops 274726912 | bytes 3149824 | tf_op jit(solution)/shard_map/dot_general | solution.py:129
  85.5 2.1 %collective-permute-start.13 = (bf16[128,512]{1,0:T(8,128)(2,1)S(1)}, bf16[128,512]{1,0:T(8,128)(2,1)S(1)}, u32[]{:S(2)}, u32[]{:S(2)}) collective-permute-start(bf16[128,512]{1,0:T(8,128)(2,1)S(1)} %get-tuple-element.37), channel_id=1, source_target_pairs={{0,2},{1,3},{2,0},{3,1},{4,6},{5,7},{6,4},{7,5},{8,10},{9,11},{10,... | collective-permute-start | bytes 393224 | tf_op jit(solution)/shard_map/ppermute | solution.py:14
  87.6 4.6 %collective-permute-done.6 = bf16[128,512]{1,0:T(8,128)(2,1)S(1)} collective-permute-done((bf16[128,512]{1,0:T(8,128)(2,1)S(1)}, bf16[128,512]{1,0:T(8,128)(2,1)S(1)}, u32[]{:S(2)}, u32[]{:S(2)}) %collective-permute-start.6) | collective-permute-done | bytes 131104 | tf_op jit(solution)/shard_map/ppermute | solution.py:14
  92.3 0.6 copy-done.8
  92.9 0.1 fusion.73
  92.9 1.0 fusion.74
  93.9 1.0 fusion.75
  94.9 1.0 fusion.76
  95.9 0.7 convert_reduce_fusion
  96.6 0.6 collective-permute-done.13
  97.2 1.7 %add_bitcast_fusion = f32[1,128,512]{2,1,0:T(8,128)} fusion(bf16[128,512]{1,0:T(8,128)(2,1)S(1)} %collective-permute-done.14, bf16[128,512]{1,0:T(8,128)(2,1)S(1)} %collective-permute-done.13, bf16[128,512]{1,0:T(8,128)(2,1)S(1)} %copy-done.9, bf16[512,512]{1,0:T(8,128)(2,1)} %copy-done.6, s32[]{:T(128)S(6)} %select_n.64), kind=kLoop, calls=%fused_computation.124 | loop fusion | flops 458752 | bytes 786436 | tf_op jit(solution)/shard_map/broadcast_in_dim | solution.py:127
  (69 shorter events, 0.3 us)
Async XLA Ops:
  0.6 42.9 %copy-start = (bf16[1,512,512]{2,1,0:T(8,128)(2,1)S(1)}, bf16[1,512,512]{2,1,0:T(8,128)(2,1)}, u32[]{:S(2)}) copy-start(bf16[1,512,512]{2,1,0:T(8,128)(2,1)} %param.13) | copy-start | bytes 1572868
  3.4 5.3 %copy-start.1 = (bf16[512,512]{1,0:T(8,128)(2,1)S(1)}, bf16[512,512]{1,0:T(8,128)(2,1)}, u32[]{:S(2)}) copy-start(bf16[512,512]{1,0:T(8,128)(2,1)} %param.15) | copy-start | bytes 1572868
  3.4 24.7 %all-to-all-start = ((bf16[8,64,512]{2,1,0:T(8,128)(2,1)}), bf16[8,64,512]{2,1,0:T(8,128)(2,1)S(1)}, u32[]{:S(2)}, u32[]{:S(2)}) async-start(bf16[8,64,512]{2,1,0:T(8,128)(2,1)} %bitcast.2), calls=%async_computation | async-start | bytes 1048576 | tf_op jit(solution)/shard_map/all_to_all | solution.py:19
  8.8 8.2 %collective-permute-start = (bf16[512,128]{1,0:T(8,128)(2,1)S(1)}, bf16[512,128]{1,0:T(8,128)(2,1)S(1)}, u32[]{:S(2)}, u32[]{:S(2)}) collective-permute-start(bf16[512,128]{1,0:T(8,128)(2,1)S(1)} %get-tuple-element.42), channel_id=1, source_target_pairs={{0,1},{1,2},{2,3},{3,0},{4,5},{5,6},{6,7},{7,4},{8,9},{9,10},{10,1... | collective-permute-start | bytes 393224 | tf_op jit(solution)/shard_map/ppermute | solution.py:14
  10.5 8.4 %collective-permute-start.2 = (bf16[512,128]{1,0:T(8,128)(2,1)S(1)}, bf16[512,128]{1,0:T(8,128)(2,1)S(1)}, u32[]{:S(2)}, u32[]{:S(2)}) collective-permute-start(bf16[512,128]{1,0:T(8,128)(2,1)S(1)} %get-tuple-element.43), channel_id=1, source_target_pairs={{0,3},{1,0},{2,1},{3,2},{4,7},{5,4},{6,5},{7,6},{8,11},{9,8},{10,9... | collective-permute-start | bytes 393224 | tf_op jit(solution)/shard_map/ppermute | solution.py:14
  12.7 12.4 %collective-permute-start.1 = (bf16[512,128]{1,0:T(8,128)(2,1)S(1)}, bf16[512,128]{1,0:T(8,128)(2,1)S(1)}, u32[]{:S(2)}, u32[]{:S(2)}) collective-permute-start(bf16[512,128]{1,0:T(8,128)(2,1)S(1)} %get-tuple-element.44), channel_id=1, source_target_pairs={{0,2},{1,3},{2,0},{3,1},{4,6},{5,7},{6,4},{7,5},{8,10},{9,11},{10,... | collective-permute-start | bytes 393224 | tf_op jit(solution)/shard_map/ppermute | solution.py:14
  14.2 0.7 copy-start.10
  26.0 14.5 %collective-permute-start.5 = (bf16[512,128]{1,0:T(8,128)(2,1)S(1)}, bf16[512,128]{1,0:T(8,128)(2,1)}, u32[]{:S(2)}, u32[]{:S(2)}) collective-permute-start(bf16[512,128]{1,0:T(8,128)(2,1)S(1)} %get-tuple-element.33), channel_id=1, source_target_pairs={{0,3},{1,0},{2,1},{3,2},{4,7},{5,4},{6,5},{7,6},{8,11},{9,8},{10,9... | collective-permute-start | bytes 393224 | tf_op jit(solution)/shard_map/ppermute | solution.py:14
  27.6 8.5 %collective-permute-start.3 = (bf16[512,128]{1,0:T(8,128)(2,1)}, bf16[512,128]{1,0:T(8,128)(2,1)}, u32[]{:S(2)}, u32[]{:S(2)}) collective-permute-start(bf16[512,128]{1,0:T(8,128)(2,1)} %get-tuple-element.34), channel_id=1, source_target_pairs={{0,1},{1,2},{2,3},{3,0},{4,5},{5,6},{6,7},{7,4},{8,9},{9,10},{10,1... | collective-permute-start | bytes 393224 | tf_op jit(solution)/shard_map/ppermute | solution.py:14
  28.0 11.6 %collective-permute-start.4 = (bf16[512,128]{1,0:T(8,128)(2,1)S(1)}, bf16[512,128]{1,0:T(8,128)(2,1)}, u32[]{:S(2)}, u32[]{:S(2)}) collective-permute-start(bf16[512,128]{1,0:T(8,128)(2,1)S(1)} %get-tuple-element.35), channel_id=1, source_target_pairs={{0,2},{1,3},{2,0},{3,1},{4,6},{5,7},{6,4},{7,5},{8,10},{9,11},{10,... | collective-permute-start | bytes 393224 | tf_op jit(solution)/shard_map/ppermute | solution.py:14
  29.5 13.6 %all-to-all-start.1 = ((bf16[8,64,512]{2,1,0:T(8,128)(2,1)}), bf16[8,64,512]{2,1,0:T(8,128)(2,1)S(1)}, u32[]{:S(2)}, u32[]{:S(2)}) async-start(bf16[8,64,512]{2,1,0:T(8,128)(2,1)} %copy.28), calls=%async_computation.1 | async-start | bytes 1048576 | tf_op jit(solution)/shard_map/all_to_all | solution.py:19
  33.6 9.6 %copy-start.3 = (bf16[512,512]{1,0:T(8,128)(2,1)S(1)}, bf16[512,512]{1,0:T(8,128)(2,1)}, u32[]{:S(2)}) copy-start(bf16[512,512]{1,0:T(8,128)(2,1)} %param.8) | copy-start | bytes 1572868
  40.5 2.7 %copy-start.11 = (f32[512]{0:T(512)S(1)}, f32[512]{0:T(512)}, u32[]{:S(2)}) copy-start(f32[512]{0:T(512)} %param.10) | copy-start | bytes 6148
  43.5 1.2 %copy-start.4 = (bf16[512,512]{1,0:T(8,128)(2,1)S(1)}, bf16[512,512]{1,0:T(8,128)(2,1)}, u32[]{:S(2)}) copy-start(bf16[512,512]{1,0:T(8,128)(2,1)} %param.8) | copy-start | bytes 1572868
  44.7 1.6 %copy-start.27 = (bf16[512,512]{1,0:T(8,128)(2,1)}, bf16[512,512]{1,0:T(8,128)(2,1)S(1)}, u32[]{:S(2)}) copy-start(bf16[512,512]{1,0:T(8,128)(2,1)S(1)} %get-tuple-element.29) | copy-start | bytes 1572868
  46.3 13.2 %all-to-all-start.2 = ((bf16[8,64,512]{2,1,0:T(8,128)(2,1)}), bf16[8,64,512]{2,1,0:T(8,128)(2,1)S(1)}, u32[]{:S(2)}, u32[]{:S(2)}) async-start(bf16[8,64,512]{2,1,0:T(8,128)(2,1)} %bitcast.22), calls=%async_computation.2 | async-start | bytes 1048576 | tf_op jit(solution)/shard_map/all_to_all | solution.py:19
  49.8 6.1 %copy-start.28 = (bf16[512,512]{1,0:T(8,128)(2,1)S(1)}, bf16[512,512]{1,0:T(8,128)(2,1)}, u32[]{:S(2)}) copy-start(bf16[512,512]{1,0:T(8,128)(2,1)} %copy-done.27) | copy-start | bytes 1572868
  50.6 13.8 %collective-permute-start.9 = (bf16[512,128]{1,0:T(8,128)(2,1)}, bf16[512,128]{1,0:T(8,128)(2,1)S(1)}, u32[]{:S(2)}, u32[]{:S(2)}) collective-permute-start(bf16[512,128]{1,0:T(8,128)(2,1)} %get-tuple-element.39), channel_id=1, source_target_pairs={{0,3},{1,0},{2,1},{3,2},{4,7},{5,4},{6,5},{7,6},{8,11},{9,8},{10,9... | collective-permute-start | bytes 393224 | tf_op jit(solution)/shard_map/ppermute | solution.py:14
  53.9 14.4 %collective-permute-start.8 = (bf16[512,128]{1,0:T(8,128)(2,1)}, bf16[512,128]{1,0:T(8,128)(2,1)S(1)}, u32[]{:S(2)}, u32[]{:S(2)}) collective-permute-start(bf16[512,128]{1,0:T(8,128)(2,1)} %get-tuple-element.40), channel_id=1, source_target_pairs={{0,2},{1,3},{2,0},{3,1},{4,6},{5,7},{6,4},{7,5},{8,10},{9,11},{10,... | collective-permute-start | bytes 393224 | tf_op jit(solution)/shard_map/ppermute | solution.py:14
  55.9 12.4 %collective-permute-start.7 = (bf16[512,128]{1,0:T(8,128)(2,1)}, bf16[512,128]{1,0:T(8,128)(2,1)}, u32[]{:S(2)}, u32[]{:S(2)}) collective-permute-start(bf16[512,128]{1,0:T(8,128)(2,1)} %get-tuple-element.41), channel_id=1, source_target_pairs={{0,1},{1,2},{2,3},{3,0},{4,5},{5,6},{6,7},{7,4},{8,9},{9,10},{10,1... | collective-permute-start | bytes 393224 | tf_op jit(solution)/shard_map/ppermute | solution.py:14
  60.8 7.4 %copy-start.15 = (f32[128]{0:T(128)S(1)}, f32[128]{0:T(128)}, u32[]{:S(2)}) copy-start(f32[128]{0:T(128)} %get-tuple-element.50) | copy-start | bytes 1540
  60.8 7.5 %copy-start.16 = (f32[128]{0:T(128)S(1)}, f32[128]{0:T(128)}, u32[]{:S(2)}) copy-start(f32[128]{0:T(128)} %get-tuple-element.51) | copy-start | bytes 1540
  60.8 7.5 %copy-start.17 = (f32[128]{0:T(128)S(1)}, f32[128]{0:T(128)}, u32[]{:S(2)}) copy-start(f32[128]{0:T(128)} %get-tuple-element.52) | copy-start | bytes 1540
  60.8 7.5 %copy-start.18 = (f32[128]{0:T(128)S(1)}, f32[128]{0:T(128)}, u32[]{:S(2)}) copy-start(f32[128]{0:T(128)} %get-tuple-element.53) | copy-start | bytes 1540
  60.8 7.5 %copy-start.19 = (f32[128]{0:T(128)S(1)}, f32[128]{0:T(128)}, u32[]{:S(2)}) copy-start(f32[128]{0:T(128)} %get-tuple-element.54) | copy-start | bytes 1540
  60.8 7.5 %copy-start.20 = (f32[128]{0:T(128)S(1)}, f32[128]{0:T(128)}, u32[]{:S(2)}) copy-start(f32[128]{0:T(128)} %get-tuple-element.55) | copy-start | bytes 1540
  60.9 7.5 %copy-start.21 = (f32[128]{0:T(128)S(1)}, f32[128]{0:T(128)}, u32[]{:S(2)}) copy-start(f32[128]{0:T(128)} %get-tuple-element.56) | copy-start | bytes 1540
  60.9 15.1 %all-to-all-start.3 = ((bf16[8,64,512]{2,1,0:T(8,128)(2,1)}), bf16[8,64,512]{2,1,0:T(8,128)(2,1)S(1)}, u32[]{:S(2)}, u32[]{:S(2)}) async-start(bf16[8,64,512]{2,1,0:T(8,128)(2,1)} %copy.31), calls=%async_computation.3 | async-start | bytes 1048576 | tf_op jit(solution)/shard_map/all_to_all | solution.py:19
  68.3 0.6 copy-start.12
  68.3 0.7 copy-start.13
  68.3 0.7 copy-start.14
  70.8 14.7 %collective-permute-start.12 = (bf16[512,128]{1,0:T(8,128)(2,1)}, bf16[512,128]{1,0:T(8,128)(2,1)}, u32[]{:S(2)}, u32[]{:S(2)}) collective-permute-start(bf16[512,128]{1,0:T(8,128)(2,1)} %get-tuple-element.30), channel_id=1, source_target_pairs={{0,3},{1,0},{2,1},{3,2},{4,7},{5,4},{6,5},{7,6},{8,11},{9,8},{10,9... | collective-permute-start | bytes 393224 | tf_op jit(solution)/shard_map/ppermute | solution.py:14
  70.8 16.8 %collective-permute-start.10 = (bf16[512,128]{1,0:T(8,128)(2,1)}, bf16[512,128]{1,0:T(8,128)(2,1)}, u32[]{:S(2)}, u32[]{:S(2)}) collective-permute-start(bf16[512,128]{1,0:T(8,128)(2,1)} %get-tuple-element.31), channel_id=1, source_target_pairs={{0,1},{1,2},{2,3},{3,0},{4,5},{5,6},{6,7},{7,4},{8,9},{9,10},{10,1... | collective-permute-start | bytes 393224 | tf_op jit(solution)/shard_map/ppermute | solution.py:14
  72.8 14.8 %collective-permute-start.11 = (bf16[512,128]{1,0:T(8,128)(2,1)}, bf16[512,128]{1,0:T(8,128)(2,1)}, u32[]{:S(2)}, u32[]{:S(2)}) collective-permute-start(bf16[512,128]{1,0:T(8,128)(2,1)} %get-tuple-element.32), channel_id=1, source_target_pairs={{0,2},{1,3},{2,0},{3,1},{4,6},{5,7},{6,4},{7,5},{8,10},{9,11},{10,... | collective-permute-start | bytes 393224 | tf_op jit(solution)/shard_map/ppermute | solution.py:14
  73.6 0.6 copy-start.22
  73.6 0.7 copy-start.23
  73.6 0.7 copy-start.24
  76.0 4.0 %copy-start.5 = (bf16[512,512]{1,0:T(8,128)(2,1)S(1)}, bf16[512,512]{1,0:T(8,128)(2,1)}, u32[]{:S(2)}) copy-start(bf16[512,512]{1,0:T(8,128)(2,1)} %param.8) | copy-start | bytes 1572868
  76.0 4.0 %copy-start.26 = (f32[512]{0:T(512)S(1)}, f32[512]{0:T(512)}, u32[]{:S(2)}) copy-start(f32[512]{0:T(512)} %param.9) | copy-start | bytes 6148
  76.0 19.9 %all-to-all-start.4 = ((bf16[8,64,512]{2,1,0:T(8,128)(2,1)}), bf16[8,64,512]{2,1,0:T(8,128)(2,1)S(1)}, u32[]{:S(2)}, u32[]{:S(2)}) async-start(bf16[8,64,512]{2,1,0:T(8,128)(2,1)} %bitcast.42), calls=%async_computation.4 | async-start | bytes 1048576 | tf_op jit(solution)/shard_map/all_to_all | solution.py:19
  80.0 3.5 %copy-start.29 = (bf16[512,512]{1,0:T(8,128)(2,1)S(1)}, bf16[512,512]{1,0:T(8,128)(2,1)}, u32[]{:S(2)}) copy-start(bf16[512,512]{1,0:T(8,128)(2,1)} %get-tuple-element.77) | copy-start | bytes 1572868
  80.6 0.8 copy-start.6
  81.4 2.1 %copy-start.25 = (bf16[1,512,512]{2,1,0:T(8,128)(2,1)S(1)}, bf16[1,512,512]{2,1,0:T(8,128)(2,1)}, u32[]{:S(2)}) copy-start(bf16[1,512,512]{2,1,0:T(8,128)(2,1)} %param.11) | copy-start | bytes 1572868
  81.4 15.2 %collective-permute-start.14 = (bf16[128,512]{1,0:T(8,128)(2,1)S(1)}, bf16[128,512]{1,0:T(8,128)(2,1)S(1)}, u32[]{:S(2)}, u32[]{:S(2)}) collective-permute-start(bf16[128,512]{1,0:T(8,128)(2,1)S(1)} %get-tuple-element.36), channel_id=1, source_target_pairs={{0,3},{1,0},{2,1},{3,2},{4,7},{5,4},{6,5},{7,6},{8,11},{9,8},{10,9... | collective-permute-start | bytes 393224 | tf_op jit(solution)/shard_map/ppermute | solution.py:14
  83.2 9.0 %collective-permute-start.6 = (bf16[128,512]{1,0:T(8,128)(2,1)S(1)}, bf16[128,512]{1,0:T(8,128)(2,1)S(1)}, u32[]{:S(2)}, u32[]{:S(2)}) collective-permute-start(bf16[128,512]{1,0:T(8,128)(2,1)S(1)} %get-tuple-element.38), channel_id=1, source_target_pairs={{0,1},{1,2},{2,3},{3,0},{4,5},{5,6},{6,7},{7,4},{8,9},{9,10},{10,1... | collective-permute-start | bytes 393224 | tf_op jit(solution)/shard_map/ppermute | solution.py:14
  85.5 7.4 %copy-start.7 = (bf16[512,128]{1,0:T(8,128)(2,1)S(1)}, bf16[512,128]{1,0:T(8,128)(2,1)}, u32[]{:S(2)}) copy-start(bf16[512,128]{1,0:T(8,128)(2,1)} %fusion.60) | copy-start | bytes 393220
  85.5 11.7 %collective-permute-start.13 = (bf16[128,512]{1,0:T(8,128)(2,1)S(1)}, bf16[128,512]{1,0:T(8,128)(2,1)S(1)}, u32[]{:S(2)}, u32[]{:S(2)}) collective-permute-start(bf16[128,512]{1,0:T(8,128)(2,1)S(1)} %get-tuple-element.37), channel_id=1, source_target_pairs={{0,2},{1,3},{2,0},{3,1},{4,6},{5,7},{6,4},{7,5},{8,10},{9,11},{10,... | collective-permute-start | bytes 393224 | tf_op jit(solution)/shard_map/ppermute | solution.py:14
  92.2 0.7 copy-start.8
  95.8 3.0 %copy-start.2 = (bf16[512,512]{1,0:T(8,128)(2,1)}, bf16[512,512]{1,0:T(8,128)(2,1)S(1)}, u32[]{:S(2)}) copy-start(bf16[512,512]{1,0:T(8,128)(2,1)S(1)} %fusion.76) | copy-start | bytes 1572868
  95.9 1.3 %copy-start.9 = (bf16[128,512]{1,0:T(8,128)(2,1)S(1)}, bf16[128,512]{1,0:T(8,128)(2,1)}, u32[]{:S(2)}) copy-start(bf16[128,512]{1,0:T(8,128)(2,1)} %copy-done.8) | copy-start | bytes 393220

commit v13 on v6

--- a/solution.py
+++ b/solution.py
@@ -51,7 +51,10 @@
     def coefficient(g, h):
         return lax.dynamic_slice(mix_mine, (0, g, h), (kq, 1, 1)).reshape(1, kq)
 
-    second_f = second_blocks.astype(F32)
+    cq_seq = second_blocks.shape[0]
+    diagonal = jnp.eye(cq_seq, dtype=BF16)
+    seq_mix = (jnp.transpose(second_blocks, (1, 0, 2))[:, :, :, None] * diagonal[None, :, None, :])
+    seq_mix = seq_mix.reshape(n * cq_seq, n * cq_seq)
 
     source = inputs.astype(F32)
     slope_in = jax.nn.sigmoid(gate_in * source)
@@ -72,9 +75,9 @@
     act_grad = place_chunks(act_grad_back, [t * kq for t in origin_of], upstream)
 
     first_arrived = swap(split_rows(mixed_first, n), "seq")
-    second_out = jnp.einsum(
-        "cea,acd->ecd", second_f, first_arrived.astype(F32)
-    ).astype(BF16)
+    second_out = jnp.dot(
+        seq_mix, first_arrived.reshape(rows, width), preferred_element_type=F32
+    ).astype(BF16).reshape(n, cq_seq, width)
     returned = swap(second_out, "seq").reshape(rows, width).astype(F32)
     slope_out = jax.nn.sigmoid(gate_out * source)
     hidden = (source + returned * slope_out).astype(BF16)
@@ -99,9 +102,9 @@
     grad_flat = hidden_grad.astype(F32)
     gated_grad = (grad_flat * slope_out).astype(BF16)
     grad_arrived = swap(split_rows(gated_grad, n), "seq")
-    first_out = jnp.einsum(
-        "cea,ecd->acd", second_f, grad_arrived.astype(F32)
-    ).astype(BF16)
+    first_out = jnp.dot(
+        seq_mix.T, grad_arrived.reshape(rows, width), preferred_element_type=F32
+    ).astype(BF16).reshape(n, cq_seq, width)
     first_grad = swap(first_out, "seq").reshape(rows, width)
     first_grad, channel_part = lax.optimization_barrier((first_grad, channel_part))
     block_part = jnp.dot(first_grad, gated.T, preferred_element_type=F32)

time: 93.2 us -> 93.9 us (level)
  waiting for transfers between devices: 17.1 us -> 15.1 us
  matrix products: 10.3 us -> 12 us
  local copies, waits for them, and re-layouts: 9.92 us -> 11.2 us
  other arithmetic: 11.1 us -> 9.95 us
    all_to_all x5, waiting for transfers between devices: 11.5 us -> 8.56 us  [swap(): return lax.all_to_all(pieces, axis_name, 0, 0, tiled=True)]
    convert_element_type x2 -> x0, local copies, waits for them, and re-layouts: 1.9 us -> none  [the longest x1 0.95 us: on_device(): first_out = jnp.einsum('cea,ecd->acd', second_f, grad_arrived.astype(F32)...]
    convert_element_type x2, other arithmetic: 3.51 us -> 1.72 us  [on_device(): added_out = [sum((act_arrived[k].astype(F32) * coefficient(origin_of[k],...]
    dot_general x2, matrix products: 0.84 us -> 2.48 us  [the longest x1 1.25 us: on_device(): jnp.dot(seq_mix.T, grad_arrived.reshape(rows, width), preferred_element_t...]
    dynamic_slice x2, local copies, waits for them, and re-layouts: 0.16 us -> 1.55 us  [lane_chunk(): return lax.dynamic_slice_in_dim(x, index * size, size, axis=1)]
    unnamed x59 -> x60, local copies, waits for them, and re-layouts: 2.49 us -> 3.53 us
    ppermute x15, starting transfers between devices: 24.9 us -> 25.9 us  [exchange(): lax.ppermute(pieces[k], axis_name, [(i, (i + k) % n) for i in range(n)])]
  transfers between devices with their start and end apart: 20 -> 20, of which waited for: 8 -> 7; matrix products, arithmetic and copies ran while one was open for 25% -> 25% of each run, Pallas kernels for 0% -> 0%
where the time goes in v13:
time: 93.9 us; the launch traced here: 93 us
  starting transfers between devices  43.6 us (46%)
  waiting for transfers between devices  15.1 us (16%)
  matrix products  12 us (13%)
  local copies, waits for them, and re-layouts  11.2 us (12%)
  other arithmetic  9.95 us (11%)
  between operations  1.2 us (1%)
    ppermute x15, starting transfers between devices, exchange(): lax.ppermute(pieces[k], axis_name, [(i, (i + k) % n) for i in range(n)])  25.9 us
    all_to_all x5, starting transfers between devices, swap(): return lax.all_to_all(pieces, axis_name, 0, 0, tiled=True)  17.7 us
    all_to_all x5, waiting for transfers between devices, swap(): return lax.all_to_all(pieces, axis_name, 0, 0, tiled=True)  8.56 us
    ppermute x15, waiting for transfers between devices, exchange(): lax.ppermute(pieces[k], axis_name, [(i, (i + k) % n) for i in range(n)])  6.52 us
    unnamed x60, local copies, waits for them, and re-layouts  3.53 us
    dot_general x1, matrix products, on_device(): spread = jnp.dot(first_blocks[0].T, first_grad, preferred_element_type=F32)  3.19 us
    dynamic_update_slice x5, other arithmetic, place_chunks(): out = lax.dynamic_update_slice_in_dim(out, chunk, start, axis=1)  3.11 us
    dynamic_update_slice x3, local copies, waits for them, and re-layouts, place_chunks(): out = lax.dynamic_update_slice_in_dim(out, chunk, start, axis=1)  2.87 us
  transfers between devices with their start and end apart: 20, of which 7 were waited for; matrix products, arithmetic and copies ran while one was open for 25% of the time, Pallas kernels for 0%

profile of v13, /device:TPU:0, one launch (start us, length us, event | category | flops | bytes accessed | tf_op | source)
XLA Modules:
  0.0 93.0 jit_solution(3749769621997538348)
XLA Ops:
  0.7 0.7 copy-done.26
  1.4 1.8 %fusion.6 = bf16[512,512]{0,1:T(8,128)(2,1)S(1)} fusion(bf16[1,512,512]{2,1,0:T(8,128)(2,1)} %param.11, bf16[512,512]{1,0:T(8,128)(2,1)} %param.8, f32[512]{0:T(512)S(1)} %copy-done.26), kind=kOutput, calls=%fused_computation.23 | convolution fusion | flops 270532608 | bytes 1574912 | tf_op jit(solution)/shard_map/dot_general | solution.py:62
  3.2 0.8 constant_dynamic-slice_fusion.35
  4.0 3.0 %collective-permute-start = (bf16[512,128]{1,0:T(8,128)(2,1)}, bf16[512,128]{1,0:T(8,128)(2,1)S(1)}, u32[]{:S(2)}, u32[]{:S(2)}) collective-permute-start(bf16[512,128]{1,0:T(8,128)(2,1)} %get-tuple-element.36), channel_id=1, source_target_pairs={{0,1},{1,2},{2,3},{3,0},{4,5},{5,6},{6,7},{7,4},{8,9},{9,10},{10,1... | collective-permute-start | bytes 393224 | tf_op jit(solution)/shard_map/ppermute | solution.py:14
  7.0 2.6 %collective-permute-start.1 = (bf16[512,128]{1,0:T(8,128)(2,1)}, bf16[512,128]{1,0:T(8,128)(2,1)S(1)}, u32[]{:S(2)}, u32[]{:S(2)}) collective-permute-start(bf16[512,128]{1,0:T(8,128)(2,1)} %get-tuple-element.38), channel_id=1, source_target_pairs={{0,2},{1,3},{2,0},{3,1},{4,6},{5,7},{6,4},{7,5},{8,10},{9,11},{10,... | collective-permute-start | bytes 393224 | tf_op jit(solution)/shard_map/ppermute | solution.py:14
  9.6 1.3 %collective-permute-start.2 = (bf16[512,128]{1,0:T(8,128)(2,1)}, bf16[512,128]{1,0:T(8,128)(2,1)S(1)}, u32[]{:S(2)}, u32[]{:S(2)}) collective-permute-start(bf16[512,128]{1,0:T(8,128)(2,1)} %get-tuple-element.37), channel_id=1, source_target_pairs={{0,3},{1,0},{2,1},{3,2},{4,7},{5,4},{6,5},{7,6},{8,11},{9,8},{10,9... | collective-permute-start | bytes 393224 | tf_op jit(solution)/shard_map/ppermute | solution.py:14
  11.0 1.0 %copy.15 = bf16[512,512]{1,0:T(8,128)(2,1)} copy(bf16[512,512]{0,1:T(8,128)(2,1)S(1)} %fusion.6) | data formatting | bytes 1048576 | tf_op jit(solution)/shard_map/optimization_barrier | solution.py:65
  12.0 3.7 %all-to-all-start = ((bf16[8,64,512]{2,1,0:T(8,128)(2,1)}), bf16[8,64,512]{2,1,0:T(8,128)(2,1)S(1)}, u32[]{:S(2)}, u32[]{:S(2)}) async-start(bf16[8,64,512]{2,1,0:T(8,128)(2,1)} %bitcast.3), calls=%async_computation | async-start | bytes 1048576 | tf_op jit(solution)/shard_map/all_to_all | solution.py:19
  15.7 0.7 copy-done.10
  16.4 0.1 copy.14
  16.5 0.6 broadcast_multiply_fusion
  17.1 0.7 fusion.75
  17.8 0.6 mul.487
  18.5 0.7 fusion.103
  19.2 1.0 %fusion.52 = (bf16[512,128]{1,0:T(8,128)(2,1)}, bf16[512,128]{1,0:T(8,128)(2,1)}, bf16[512,128]{1,0:T(8,128)(2,1)}) fusion(bf16[512,128]{1,0:T(8,128)(2,1)S(1)} %collective-permute-done, bf16[512,128]{1,0:T(8,128)(2,1)S(1)} %collective-permute-done.1, bf16[512,128]{1,0:T(8,128)(2,1)S(1)} %collective-permute-done.2, f32[128]{0:T(128)S(1)} %get-tuple-element.54, ...), kind=kLoop, calls=%fused_computation.104 | loop fusion | flops 1835008 | bytes 923652 | tf_op jit(solution)/shard_map/convert_element_type | solution.py:71
  20.2 2.5 %collective-permute-start.3 = (bf16[512,128]{1,0:T(8,128)(2,1)}, bf16[512,128]{1,0:T(8,128)(2,1)}, u32[]{:S(2)}, u32[]{:S(2)}) collective-permute-start(bf16[512,128]{1,0:T(8,128)(2,1)} %get-tuple-element.28), channel_id=1, source_target_pairs={{0,1},{1,2},{2,3},{3,0},{4,5},{5,6},{6,7},{7,4},{8,9},{9,10},{10,1... | collective-permute-start | bytes 393224 | tf_op jit(solution)/shard_map/ppermute | solution.py:14
  22.7 1.6 %collective-permute-start.4 = (bf16[512,128]{1,0:T(8,128)(2,1)}, bf16[512,128]{1,0:T(8,128)(2,1)}, u32[]{:S(2)}, u32[]{:S(2)}) collective-permute-start(bf16[512,128]{1,0:T(8,128)(2,1)} %get-tuple-element.29), channel_id=1, source_target_pairs={{0,2},{1,3},{2,0},{3,1},{4,6},{5,7},{6,4},{7,5},{8,10},{9,11},{10,... | collective-permute-start | bytes 393224 | tf_op jit(solution)/shard_map/ppermute | solution.py:14
  24.3 0.7 collective-permute-start.5
  25.1 0.4 all-to-all-done
  25.4 1.2 %convolution_convert_fusion.1 = bf16[512,512]{1,0:T(8,128)(2,1)} fusion(bf16[512,512]{1,0:T(8,128)(2,1)S(1)} %mul.487, bf16[512,512]{1,0:T(8,128)(2,1)S(1)} %bitcast.115), kind=kOutput, calls=%fused_computation.17 | convolution fusion | flops 268697600 | bytes 1572864 | tf_op jit(solution)/shard_map/dot_general | solution.py:78
  26.7 3.5 %all-to-all-start.1 = ((bf16[8,64,512]{2,1,0:T(8,128)(2,1)}), bf16[8,64,512]{2,1,0:T(8,128)(2,1)S(1)}, u32[]{:S(2)}, u32[]{:S(2)}) async-start(bf16[8,64,512]{2,1,0:T(8,128)(2,1)} %bitcast.5), calls=%async_computation.1 | async-start | bytes 1048576 | tf_op jit(solution)/shard_map/all_to_all | solution.py:19
  30.2 0.1 fusion.73
  30.4 1.0 %constant_dynamic-update-slice_fusion.2 = bf16[512,512]{1,0:T(8,128)(2,1)S(1)} fusion(bf16[512,512]{1,0:T(8,128)(2,1)S(1)} %fusion.73, bf16[512,128]{1,0:T(8,128)(2,1)} %collective-permute-done.3, s32[]{:T(128)S(6)} %select_n.80), kind=kLoop, calls=%fused_computation.165 | loop fusion | bytes 262148 | tf_op jit(solution)/shard_map/dynamic_update_slice | solution.py:33
  31.4 2.6 %collective-permute-done.4 = bf16[512,128]{1,0:T(8,128)(2,1)} collective-permute-done((bf16[512,128]{1,0:T(8,128)(2,1)}, bf16[512,128]{1,0:T(8,128)(2,1)}, u32[]{:S(2)}, u32[]{:S(2)}) %collective-permute-start.4) | collective-permute-done | bytes 131104 | tf_op jit(solution)/shard_map/ppermute | solution.py:14
  34.0 0.9 %constant_dynamic-update-slice_fusion.1 = bf16[512,512]{1,0:T(8,128)(2,1)S(1)} fusion(bf16[512,512]{1,0:T(8,128)(2,1)S(1)} %constant_dynamic-update-slice_fusion.2, bf16[512,128]{1,0:T(8,128)(2,1)} %collective-permute-done.4, s32[]{:T(128)S(6)} %select_n.82), kind=kLoop, calls=%fused_computation.160 | loop fusion | bytes 262148 | tf_op jit(solution)/shard_map/dynamic_update_slice | solution.py:33
  34.9 0.9 %constant_dynamic-update-slice_fusion = bf16[512,512]{1,0:T(8,128)(2,1)S(1)} fusion(bf16[512,512]{1,0:T(8,128)(2,1)S(1)} %constant_dynamic-update-slice_fusion.1, bf16[512,128]{1,0:T(8,128)(2,1)} %collective-permute-done.5, s32[]{:T(128)S(6)} %select_n.84), kind=kLoop, calls=%fused_computation.155 | loop fusion | bytes 262148 | tf_op jit(solution)/shard_map/dynamic_update_slice | solution.py:33
  35.9 0.8 copy-done.2
  36.7 3.2 %all-to-all-done.1 = bf16[8,64,512]{2,1,0:T(8,128)(2,1)S(1)} async-done(((bf16[8,64,512]{2,1,0:T(8,128)(2,1)}), bf16[8,64,512]{2,1,0:T(8,128)(2,1)S(1)}, u32[]{:S(2)}, u32[]{:S(2)}) %all-to-all-start.1) | async-done | bytes 524320 | tf_op jit(solution)/shard_map/all_to_all | solution.py:19
  39.8 0.4 fusion.31
  40.2 0.6 copy-done.3
  40.9 1.1 %multiply_convert_fusion = (bf16[512,512]{1,0:T(8,128)(2,1)S(1)}, bf16[512,512]{1,0:T(8,128)(2,1)S(1)}) fusion(bf16[512,512]{1,0:T(8,128)(2,1)S(1)} %copy-done.3, bf16[512,512]{1,0:T(8,128)(2,1)S(1)} %fusion.31, bf16[1,512,512]{2,1,0:T(8,128)(2,1)S(1)} %copy-done), kind=kOutput, calls=%fused_computation.50 | convolution fusion | flops 274464768 | bytes 2621440 | tf_op jit(solution)/shard_map/dot_general | solution.py:84
  42.0 1.6 %fusion.22 = (bf16[512,512]{1,0:T(8,128)(2,1)}, bf16[512,512]{1,0:T(8,128)(2,1)}) fusion(bf16[512,512]{1,0:T(8,128)(2,1)S(1)} %copy-done.6, f32[512]{0:T(512)S(1)} %copy-done.11, bf16[512,512]{1,0:T(8,128)(2,1)S(1)} %get-tuple-element.23, bf16[1,512,512]{2,1,0:T(8,128)(2,1)S(1)} %copy-done, bf16[512,512]{1,0:T(8,128)(2,1)S(1)} %copy-done.1), kind=kOutput, calls=%fused_computation.39 | convolution fusion | flops 271319040 | bytes 3147776 | tf_op jit(solution)/shard_map/dot_general | solution.py:98
  43.6 3.5 %all-to-all-start.2 = ((bf16[8,64,512]{2,1,0:T(8,128)(2,1)}), bf16[8,64,512]{2,1,0:T(8,128)(2,1)S(1)}, u32[]{:S(2)}, u32[]{:S(2)}) async-start(bf16[8,64,512]{2,1,0:T(8,128)(2,1)} %bitcast.121), calls=%async_computation.2 | async-start | bytes 1048576 | tf_op jit(solution)/shard_map/all_to_all | solution.py:19
  47.1 0.8 constant_dynamic-slice_fusion.13
  47.9 1.2 %collective-permute-start.7 = (bf16[512,128]{1,0:T(8,128)(2,1)}, bf16[512,128]{1,0:T(8,128)(2,1)S(1)}, u32[]{:S(2)}, u32[]{:S(2)}) collective-permute-start(bf16[512,128]{1,0:T(8,128)(2,1)} %get-tuple-element.35), channel_id=1, source_target_pairs={{0,1},{1,2},{2,3},{3,0},{4,5},{5,6},{6,7},{7,4},{8,9},{9,10},{10,1... | collective-permute-start | bytes 393224 | tf_op jit(solution)/shard_map/ppermute | solution.py:14
  49.1 1.3 %collective-permute-start.8 = (bf16[512,128]{1,0:T(8,128)(2,1)}, bf16[512,128]{1,0:T(8,128)(2,1)S(1)}, u32[]{:S(2)}, u32[]{:S(2)}) collective-permute-start(bf16[512,128]{1,0:T(8,128)(2,1)} %get-tuple-element.34), channel_id=1, source_target_pairs={{0,2},{1,3},{2,0},{3,1},{4,6},{5,7},{6,4},{7,5},{8,10},{9,11},{10,... | collective-permute-start | bytes 393224 | tf_op jit(solution)/shard_map/ppermute | solution.py:14
  50.4 1.8 %collective-permute-start.9 = (bf16[512,128]{1,0:T(8,128)(2,1)}, bf16[512,128]{1,0:T(8,128)(2,1)S(1)}, u32[]{:S(2)}, u32[]{:S(2)}) collective-permute-start(bf16[512,128]{1,0:T(8,128)(2,1)} %get-tuple-element.33), channel_id=1, source_target_pairs={{0,3},{1,0},{2,1},{3,2},{4,7},{5,4},{6,5},{7,6},{8,11},{9,8},{10,9... | collective-permute-start | bytes 393224 | tf_op jit(solution)/shard_map/ppermute | solution.py:14
  52.2 1.3 %fusion.110 = bf16[512,512]{1,0:T(8,128)(2,1)} fusion(bf16[512,512]{1,0:T(8,128)(2,1)S(1)} %fusion.31, bf16[512,512]{1,0:T(8,128)(2,1)S(1)} %copy-done.29), kind=kOutput, calls=%fused_computation.211 | convolution fusion | flops 268435456 | bytes 1572864 | tf_op jit(solution)/shard_map/dot_general | solution.py:100
  53.5 3.3 %all-to-all-done.2 = bf16[8,64,512]{2,1,0:T(8,128)(2,1)S(1)} async-done(((bf16[8,64,512]{2,1,0:T(8,128)(2,1)}), bf16[8,64,512]{2,1,0:T(8,128)(2,1)S(1)}, u32[]{:S(2)}, u32[]{:S(2)}) %all-to-all-start.2) | async-done | bytes 524320 | tf_op jit(solution)/shard_map/all_to_all | solution.py:19
  56.8 1.3 %convolution_convert_fusion = bf16[512,512]{1,0:T(8,128)(2,1)} fusion(bf16[512,512]{1,0:T(8,128)(2,1)S(1)} %mul.487, bf16[512,512]{1,0:T(8,128)(2,1)S(1)} %bitcast.120), kind=kOutput, calls=%fused_computation.16 | convolution fusion | flops 268697600 | bytes 1572864 | tf_op jit(solution)/shard_map/dot_general | solution.py:105
  58.1 3.5 %all-to-all-start.3 = ((bf16[8,64,512]{2,1,0:T(8,128)(2,1)}), bf16[8,64,512]{2,1,0:T(8,128)(2,1)S(1)}, u32[]{:S(2)}, u32[]{:S(2)}) async-start(bf16[8,64,512]{2,1,0:T(8,128)(2,1)} %bitcast.119), calls=%async_computation.3 | async-start | bytes 1048576 | tf_op jit(solution)/shard_map/all_to_all | solution.py:19
  61.8 0.5 copy-done.12
  62.3 0.0 copy-done.13
  62.3 0.9 %fusion.68 = (bf16[512,128]{1,0:T(8,128)(2,1)}, bf16[512,128]{1,0:T(8,128)(2,1)}, bf16[512,128]{1,0:T(8,128)(2,1)}) fusion(bf16[512,128]{1,0:T(8,128)(2,1)S(1)} %collective-permute-done.7, bf16[512,128]{1,0:T(8,128)(2,1)S(1)} %collective-permute-done.8, bf16[512,128]{1,0:T(8,128)(2,1)S(1)} %collective-permute-done.9, f32[128]{0:T(128)S(1)} %copy-done.12, ...), kind=kLoop, calls=%fused_computation.120 | loop fusion | flops 1835008 | bytes 923652 | tf_op jit(solution)/shard_map/convert_element_type | solution.py:92
  63.3 3.1 %collective-permute-start.10 = (bf16[512,128]{1,0:T(8,128)(2,1)}, bf16[512,128]{1,0:T(8,128)(2,1)}, u32[]{:S(2)}, u32[]{:S(2)}) collective-permute-start(bf16[512,128]{1,0:T(8,128)(2,1)} %get-tuple-element.25), channel_id=1, source_target_pairs={{0,1},{1,2},{2,3},{3,0},{4,5},{5,6},{6,7},{7,4},{8,9},{9,10},{10,1... | collective-permute-start | bytes 393224 | tf_op jit(solution)/shard_map/ppermute | solution.py:14
  66.4 0.5 collective-permute-start.11
  66.8 1.9 %collective-permute-start.12 = (bf16[512,128]{1,0:T(8,128)(2,1)}, bf16[512,128]{1,0:T(8,128)(2,1)}, u32[]{:S(2)}, u32[]{:S(2)}) collective-permute-start(bf16[512,128]{1,0:T(8,128)(2,1)} %get-tuple-element.24), channel_id=1, source_target_pairs={{0,3},{1,0},{2,1},{3,2},{4,7},{5,4},{6,5},{7,6},{8,11},{9,8},{10,9... | collective-permute-start | bytes 393224 | tf_op jit(solution)/shard_map/ppermute | solution.py:14
  68.7 0.8 fusion.56
  69.5 1.8 %all-to-all-done.3 = bf16[8,64,512]{2,1,0:T(8,128)(2,1)S(1)} async-done(((bf16[8,64,512]{2,1,0:T(8,128)(2,1)}), bf16[8,64,512]{2,1,0:T(8,128)(2,1)S(1)}, u32[]{:S(2)}, u32[]{:S(2)}) %all-to-all-start.3) | async-done | bytes 524320 | tf_op jit(solution)/shard_map/all_to_all | solution.py:19
  71.3 0.6 fusion.107
  71.9 0.8 dynamic-slice_convert_fusion.1
  72.6 1.2 %collective-permute-start.6 = (bf16[128,512]{1,0:T(8,128)(2,1)}, bf16[128,512]{1,0:T(8,128)(2,1)S(1)}, u32[]{:S(2)}, u32[]{:S(2)}) collective-permute-start(bf16[128,512]{1,0:T(8,128)(2,1)} %get-tuple-element.32), channel_id=1, source_target_pairs={{0,1},{1,2},{2,3},{3,0},{4,5},{5,6},{6,7},{7,4},{8,9},{9,10},{10,1... | collective-permute-start | bytes 393224 | tf_op jit(solution)/shard_map/ppermute | solution.py:14
  73.8 1.3 %collective-permute-start.13 = (bf16[128,512]{1,0:T(8,128)(2,1)S(1)}, bf16[128,512]{1,0:T(8,128)(2,1)}, u32[]{:S(2)}, u32[]{:S(2)}) collective-permute-start(bf16[128,512]{1,0:T(8,128)(2,1)S(1)} %get-tuple-element.30), channel_id=1, source_target_pairs={{0,2},{1,3},{2,0},{3,1},{4,6},{5,7},{6,4},{7,5},{8,10},{9,11},{10,... | collective-permute-start | bytes 393224 | tf_op jit(solution)/shard_map/ppermute | solution.py:14
  75.1 3.5 %all-to-all-start.4 = ((bf16[8,64,512]{2,1,0:T(8,128)(2,1)}), bf16[8,64,512]{2,1,0:T(8,128)(2,1)S(1)}, u32[]{:S(2)}, u32[]{:S(2)}) async-start(bf16[8,64,512]{2,1,0:T(8,128)(2,1)} %bitcast.45), calls=%async_computation.4 | async-start | bytes 1048576 | tf_op jit(solution)/shard_map/all_to_all | solution.py:19
  78.6 3.2 %fusion.3 = bf16[512,512]{1,0:T(8,128)(2,1)} fusion(bf16[512,512]{1,0:T(8,128)(2,1)S(1)} %bitcast.118, bf16[512,512]{1,0:T(8,128)(2,1)} %get-tuple-element.71, bf16[512,512]{1,0:T(8,128)(2,1)S(1)} %copy-done.7, bf16[512,512]{1,0:T(8,128)(2,1)S(1)} %bitcast.116, bf16[1,512,512]{2,1,0:T(8,128)(2,1)} %param.11, f32[512]{0:T(512)S(1)} %copy-done.11, ...), kind=kOutput, calls=%fused_computation.20 | convolution fusion | flops 274726912 | bytes 3149824 | tf_op jit(solution)/shard_map/dot_general | solution.py:130
  81.8 1.8 %collective-permute-start.14 = (bf16[128,512]{1,0:T(8,128)(2,1)S(1)}, bf16[128,512]{1,0:T(8,128)(2,1)S(1)}, u32[]{:S(2)}, u32[]{:S(2)}) collective-permute-start(bf16[128,512]{1,0:T(8,128)(2,1)S(1)} %get-tuple-element.31), channel_id=1, source_target_pairs={{0,3},{1,0},{2,1},{3,2},{4,7},{5,4},{6,5},{7,6},{8,11},{9,8},{10,9... | collective-permute-start | bytes 393224 | tf_op jit(solution)/shard_map/ppermute | solution.py:14
  83.7 0.1 fusion.69
  83.8 1.0 %fusion.70 = bf16[512,512]{1,0:T(8,128)(2,1)S(1)} fusion(bf16[512,512]{1,0:T(8,128)(2,1)S(1)} %fusion.69, s32[]{:T(128)S(6)} %select_n.80, bf16[512,128]{1,0:T(8,128)(2,1)} %collective-permute-done.10, bf16[512,512]{1,0:T(8,128)(2,1)S(1)} %fusion.31), kind=kLoop, calls=%fused_computation.131 | loop fusion | flops 262144 | bytes 393220 | tf_op jit(solution)/shard_map/dynamic_update_slice | solution.py:33
  84.7 1.0 %fusion.71 = bf16[512,512]{1,0:T(8,128)(2,1)S(1)} fusion(bf16[512,512]{1,0:T(8,128)(2,1)S(1)} %fusion.70, s32[]{:T(128)S(6)} %select_n.82, bf16[512,128]{1,0:T(8,128)(2,1)} %collective-permute-done.11, bf16[512,512]{1,0:T(8,128)(2,1)S(1)} %fusion.31), kind=kLoop, calls=%fused_computation.132 | loop fusion | flops 262144 | bytes 393220 | tf_op jit(solution)/shard_map/dynamic_update_slice | solution.py:33
  85.7 1.0 %fusion.72 = bf16[512,512]{1,0:T(8,128)(2,1)S(1)} fusion(bf16[512,512]{1,0:T(8,128)(2,1)S(1)} %fusion.71, s32[]{:T(128)S(6)} %select_n.84, bf16[512,128]{1,0:T(8,128)(2,1)} %collective-permute-done.12, bf16[512,512]{1,0:T(8,128)(2,1)S(1)} %fusion.31), kind=kLoop, calls=%fused_computation.133 | loop fusion | flops 262144 | bytes 393220 | tf_op jit(solution)/shard_map/dynamic_update_slice | solution.py:33
  86.7 1.5 %collective-permute-done.13 = bf16[128,512]{1,0:T(8,128)(2,1)} collective-permute-done((bf16[128,512]{1,0:T(8,128)(2,1)S(1)}, bf16[128,512]{1,0:T(8,128)(2,1)}, u32[]{:S(2)}, u32[]{:S(2)}) %collective-permute-start.13) | collective-permute-done | bytes 131104 | tf_op jit(solution)/shard_map/ppermute | solution.py:14
  88.2 2.4 %collective-permute-done.14 = bf16[128,512]{1,0:T(8,128)(2,1)S(1)} collective-permute-done((bf16[128,512]{1,0:T(8,128)(2,1)S(1)}, bf16[128,512]{1,0:T(8,128)(2,1)S(1)}, u32[]{:S(2)}, u32[]{:S(2)}) %collective-permute-start.14) | collective-permute-done | bytes 131104 | tf_op jit(solution)/shard_map/ppermute | solution.py:14
  90.6 1.7 %add_bitcast_fusion = f32[1,128,512]{2,1,0:T(8,128)} fusion(bf16[128,512]{1,0:T(8,128)(2,1)S(1)} %collective-permute-done.14, bf16[128,512]{1,0:T(8,128)(2,1)} %collective-permute-done.13, bf16[128,512]{1,0:T(8,128)(2,1)S(1)} %collective-permute-done.6, bf16[512,512]{1,0:T(8,128)(2,1)} %copy-done.8, s32[]{:T(128)S(6)} %select_n.64), kind=kLoop, calls=%fused_computation.121 | loop fusion | flops 458752 | bytes 786436 | tf_op jit(solution)/shard_map/broadcast_in_dim | solution.py:118
  92.3 0.7 convert_reduce_fusion
  (70 shorter events, 0.2 us)
Async XLA Ops:
  0.6 39.6 %copy-start = (bf16[1,512,512]{2,1,0:T(8,128)(2,1)S(1)}, bf16[1,512,512]{2,1,0:T(8,128)(2,1)}, u32[]{:S(2)}) copy-start(bf16[1,512,512]{2,1,0:T(8,128)(2,1)} %param.13) | copy-start | bytes 1572868
  0.7 0.7 copy-start.26
  1.4 1.8 %copy-start.1 = (bf16[512,512]{1,0:T(8,128)(2,1)S(1)}, bf16[512,512]{1,0:T(8,128)(2,1)}, u32[]{:S(2)}) copy-start(bf16[512,512]{1,0:T(8,128)(2,1)} %param.15) | copy-start | bytes 1572868
  4.0 15.2 %collective-permute-start = (bf16[512,128]{1,0:T(8,128)(2,1)}, bf16[512,128]{1,0:T(8,128)(2,1)S(1)}, u32[]{:S(2)}, u32[]{:S(2)}) collective-permute-start(bf16[512,128]{1,0:T(8,128)(2,1)} %get-tuple-element.36), channel_id=1, source_target_pairs={{0,1},{1,2},{2,3},{3,0},{4,5},{5,6},{6,7},{7,4},{8,9},{9,10},{10,1... | collective-permute-start | bytes 393224 | tf_op jit(solution)/shard_map/ppermute | solution.py:14
  7.0 12.2 %collective-permute-start.1 = (bf16[512,128]{1,0:T(8,128)(2,1)}, bf16[512,128]{1,0:T(8,128)(2,1)S(1)}, u32[]{:S(2)}, u32[]{:S(2)}) collective-permute-start(bf16[512,128]{1,0:T(8,128)(2,1)} %get-tuple-element.38), channel_id=1, source_target_pairs={{0,2},{1,3},{2,0},{3,1},{4,6},{5,7},{6,4},{7,5},{8,10},{9,11},{10,... | collective-permute-start | bytes 393224 | tf_op jit(solution)/shard_map/ppermute | solution.py:14
  9.6 9.6 %collective-permute-start.2 = (bf16[512,128]{1,0:T(8,128)(2,1)}, bf16[512,128]{1,0:T(8,128)(2,1)S(1)}, u32[]{:S(2)}, u32[]{:S(2)}) collective-permute-start(bf16[512,128]{1,0:T(8,128)(2,1)} %get-tuple-element.37), channel_id=1, source_target_pairs={{0,3},{1,0},{2,1},{3,2},{4,7},{5,4},{6,5},{7,6},{8,11},{9,8},{10,9... | collective-permute-start | bytes 393224 | tf_op jit(solution)/shard_map/ppermute | solution.py:14
  12.0 13.5 %all-to-all-start = ((bf16[8,64,512]{2,1,0:T(8,128)(2,1)}), bf16[8,64,512]{2,1,0:T(8,128)(2,1)S(1)}, u32[]{:S(2)}, u32[]{:S(2)}) async-start(bf16[8,64,512]{2,1,0:T(8,128)(2,1)} %bitcast.3), calls=%async_computation | async-start | bytes 1048576 | tf_op jit(solution)/shard_map/all_to_all | solution.py:19
  15.7 0.7 copy-start.10
  20.2 10.2 %collective-permute-start.3 = (bf16[512,128]{1,0:T(8,128)(2,1)}, bf16[512,128]{1,0:T(8,128)(2,1)}, u32[]{:S(2)}, u32[]{:S(2)}) collective-permute-start(bf16[512,128]{1,0:T(8,128)(2,1)} %get-tuple-element.28), channel_id=1, source_target_pairs={{0,1},{1,2},{2,3},{3,0},{4,5},{5,6},{6,7},{7,4},{8,9},{9,10},{10,1... | collective-permute-start | bytes 393224 | tf_op jit(solution)/shard_map/ppermute | solution.py:14
  22.7 11.3 %collective-permute-start.4 = (bf16[512,128]{1,0:T(8,128)(2,1)}, bf16[512,128]{1,0:T(8,128)(2,1)}, u32[]{:S(2)}, u32[]{:S(2)}) collective-permute-start(bf16[512,128]{1,0:T(8,128)(2,1)} %get-tuple-element.29), channel_id=1, source_target_pairs={{0,2},{1,3},{2,0},{3,1},{4,6},{5,7},{6,4},{7,5},{8,10},{9,11},{10,... | collective-permute-start | bytes 393224 | tf_op jit(solution)/shard_map/ppermute | solution.py:14
  24.3 10.6 %collective-permute-start.5 = (bf16[512,128]{1,0:T(8,128)(2,1)}, bf16[512,128]{1,0:T(8,128)(2,1)}, u32[]{:S(2)}, u32[]{:S(2)}) collective-permute-start(bf16[512,128]{1,0:T(8,128)(2,1)} %get-tuple-element.27), channel_id=1, source_target_pairs={{0,3},{1,0},{2,1},{3,2},{4,7},{5,4},{6,5},{7,6},{8,11},{9,8},{10,9... | collective-permute-start | bytes 393224 | tf_op jit(solution)/shard_map/ppermute | solution.py:14
  26.7 13.2 %all-to-all-start.1 = ((bf16[8,64,512]{2,1,0:T(8,128)(2,1)}), bf16[8,64,512]{2,1,0:T(8,128)(2,1)S(1)}, u32[]{:S(2)}, u32[]{:S(2)}) async-start(bf16[8,64,512]{2,1,0:T(8,128)(2,1)} %bitcast.5), calls=%async_computation.1 | async-start | bytes 1048576 | tf_op jit(solution)/shard_map/all_to_all | solution.py:19
  30.4 9.5 %copy-start.5 = (bf16[512,512]{1,0:T(8,128)(2,1)S(1)}, bf16[512,512]{1,0:T(8,128)(2,1)}, u32[]{:S(2)}) copy-start(bf16[512,512]{1,0:T(8,128)(2,1)} %param.8) | copy-start | bytes 1572868
  34.9 4.9 %copy-start.11 = (f32[512]{0:T(512)S(1)}, f32[512]{0:T(512)}, u32[]{:S(2)}) copy-start(f32[512]{0:T(512)} %param.10) | copy-start | bytes 6148
  35.9 0.8 copy-start.2
  39.8 1.0 %copy-start.3 = (bf16[512,512]{1,0:T(8,128)(2,1)S(1)}, bf16[512,512]{1,0:T(8,128)(2,1)}, u32[]{:S(2)}) copy-start(bf16[512,512]{1,0:T(8,128)(2,1)} %copy-done.2) | copy-start | bytes 1572868
  40.9 1.1 %copy-start.6 = (bf16[512,512]{1,0:T(8,128)(2,1)S(1)}, bf16[512,512]{1,0:T(8,128)(2,1)}, u32[]{:S(2)}) copy-start(bf16[512,512]{1,0:T(8,128)(2,1)} %param.8) | copy-start | bytes 1572868
  42.0 1.6 %copy-start.28 = (bf16[512,512]{1,0:T(8,128)(2,1)}, bf16[512,512]{1,0:T(8,128)(2,1)S(1)}, u32[]{:S(2)}) copy-start(bf16[512,512]{1,0:T(8,128)(2,1)S(1)} %get-tuple-element.23) | copy-start | bytes 1572868
  43.6 13.2 %all-to-all-start.2 = ((bf16[8,64,512]{2,1,0:T(8,128)(2,1)}), bf16[8,64,512]{2,1,0:T(8,128)(2,1)S(1)}, u32[]{:S(2)}, u32[]{:S(2)}) async-start(bf16[8,64,512]{2,1,0:T(8,128)(2,1)} %bitcast.121), calls=%async_computation.2 | async-start | bytes 1048576 | tf_op jit(solution)/shard_map/all_to_all | solution.py:19
  47.1 5.1 %copy-start.29 = (bf16[512,512]{1,0:T(8,128)(2,1)S(1)}, bf16[512,512]{1,0:T(8,128)(2,1)}, u32[]{:S(2)}) copy-start(bf16[512,512]{1,0:T(8,128)(2,1)} %copy-done.28) | copy-start | bytes 1572868
  47.9 13.7 %collective-permute-start.7 = (bf16[512,128]{1,0:T(8,128)(2,1)}, bf16[512,128]{1,0:T(8,128)(2,1)S(1)}, u32[]{:S(2)}, u32[]{:S(2)}) collective-permute-start(bf16[512,128]{1,0:T(8,128)(2,1)} %get-tuple-element.35), channel_id=1, source_target_pairs={{0,1},{1,2},{2,3},{3,0},{4,5},{5,6},{6,7},{7,4},{8,9},{9,10},{10,1... | collective-permute-start | bytes 393224 | tf_op jit(solution)/shard_map/ppermute | solution.py:14
  49.1 12.5 %collective-permute-start.8 = (bf16[512,128]{1,0:T(8,128)(2,1)}, bf16[512,128]{1,0:T(8,128)(2,1)S(1)}, u32[]{:S(2)}, u32[]{:S(2)}) collective-permute-start(bf16[512,128]{1,0:T(8,128)(2,1)} %get-tuple-element.34), channel_id=1, source_target_pairs={{0,2},{1,3},{2,0},{3,1},{4,6},{5,7},{6,4},{7,5},{8,10},{9,11},{10,... | collective-permute-start | bytes 393224 | tf_op jit(solution)/shard_map/ppermute | solution.py:14
  50.4 11.2 %collective-permute-start.9 = (bf16[512,128]{1,0:T(8,128)(2,1)}, bf16[512,128]{1,0:T(8,128)(2,1)S(1)}, u32[]{:S(2)}, u32[]{:S(2)}) collective-permute-start(bf16[512,128]{1,0:T(8,128)(2,1)} %get-tuple-element.33), channel_id=1, source_target_pairs={{0,3},{1,0},{2,1},{3,2},{4,7},{5,4},{6,5},{7,6},{8,11},{9,8},{10,9... | collective-permute-start | bytes 393224 | tf_op jit(solution)/shard_map/ppermute | solution.py:14
  58.0 3.6 %copy-start.15 = (f32[128]{0:T(128)S(1)}, f32[128]{0:T(128)}, u32[]{:S(2)}) copy-start(f32[128]{0:T(128)} %get-tuple-element.43) | copy-start | bytes 1540
  58.1 3.6 %copy-start.16 = (f32[128]{0:T(128)S(1)}, f32[128]{0:T(128)}, u32[]{:S(2)}) copy-start(f32[128]{0:T(128)} %get-tuple-element.44) | copy-start | bytes 1540
  58.1 3.6 %copy-start.17 = (f32[128]{0:T(128)S(1)}, f32[128]{0:T(128)}, u32[]{:S(2)}) copy-start(f32[128]{0:T(128)} %get-tuple-element.45) | copy-start | bytes 1540
  58.1 3.7 %copy-start.18 = (f32[128]{0:T(128)S(1)}, f32[128]{0:T(128)}, u32[]{:S(2)}) copy-start(f32[128]{0:T(128)} %get-tuple-element.46) | copy-start | bytes 1540
  58.1 3.7 %copy-start.19 = (f32[128]{0:T(128)S(1)}, f32[128]{0:T(128)}, u32[]{:S(2)}) copy-start(f32[128]{0:T(128)} %get-tuple-element.47) | copy-start | bytes 1540
  58.1 3.7 %copy-start.20 = (f32[128]{0:T(128)S(1)}, f32[128]{0:T(128)}, u32[]{:S(2)}) copy-start(f32[128]{0:T(128)} %get-tuple-element.48) | copy-start | bytes 1540
  58.1 3.7 %copy-start.21 = (f32[128]{0:T(128)S(1)}, f32[128]{0:T(128)}, u32[]{:S(2)}) copy-start(f32[128]{0:T(128)} %get-tuple-element.49) | copy-start | bytes 1540
  58.1 3.7 %copy-start.22 = (f32[128]{0:T(128)S(1)}, f32[128]{0:T(128)}, u32[]{:S(2)}) copy-start(f32[128]{0:T(128)} %get-tuple-element.50) | copy-start | bytes 1540
  58.1 13.2 %all-to-all-start.3 = ((bf16[8,64,512]{2,1,0:T(8,128)(2,1)}), bf16[8,64,512]{2,1,0:T(8,128)(2,1)S(1)}, u32[]{:S(2)}, u32[]{:S(2)}) async-start(bf16[8,64,512]{2,1,0:T(8,128)(2,1)} %bitcast.119), calls=%async_computation.3 | async-start | bytes 1048576 | tf_op jit(solution)/shard_map/all_to_all | solution.py:19
  61.6 0.6 copy-start.12
  61.7 0.7 copy-start.13
  61.7 0.7 copy-start.14
  62.3 6.4 %copy-start.23 = (f32[128]{0:T(128)S(1)}, f32[128]{0:T(128)}, u32[]{:S(2)}) copy-start(f32[128]{0:T(128)} %get-tuple-element.51) | copy-start | bytes 1540
  62.3 6.4 %copy-start.24 = (f32[128]{0:T(128)S(1)}, f32[128]{0:T(128)}, u32[]{:S(2)}) copy-start(f32[128]{0:T(128)} %get-tuple-element.52) | copy-start | bytes 1540
  62.3 6.4 %copy-start.25 = (f32[128]{0:T(128)S(1)}, f32[128]{0:T(128)}, u32[]{:S(2)}) copy-start(f32[128]{0:T(128)} %get-tuple-element.53) | copy-start | bytes 1540
  63.3 8.0 %copy-start.7 = (bf16[512,512]{1,0:T(8,128)(2,1)S(1)}, bf16[512,512]{1,0:T(8,128)(2,1)}, u32[]{:S(2)}) copy-start(bf16[512,512]{1,0:T(8,128)(2,1)} %param.8) | copy-start | bytes 1572868
  63.3 18.5 %collective-permute-start.10 = (bf16[512,128]{1,0:T(8,128)(2,1)}, bf16[512,128]{1,0:T(8,128)(2,1)}, u32[]{:S(2)}, u32[]{:S(2)}) collective-permute-start(bf16[512,128]{1,0:T(8,128)(2,1)} %get-tuple-element.25), channel_id=1, source_target_pairs={{0,1},{1,2},{2,3},{3,0},{4,5},{5,6},{6,7},{7,4},{8,9},{9,10},{10,1... | collective-permute-start | bytes 393224 | tf_op jit(solution)/shard_map/ppermute | solution.py:14
  66.4 17.3 %collective-permute-start.11 = (bf16[512,128]{1,0:T(8,128)(2,1)}, bf16[512,128]{1,0:T(8,128)(2,1)}, u32[]{:S(2)}, u32[]{:S(2)}) collective-permute-start(bf16[512,128]{1,0:T(8,128)(2,1)} %get-tuple-element.26), channel_id=1, source_target_pairs={{0,2},{1,3},{2,0},{3,1},{4,6},{5,7},{6,4},{7,5},{8,10},{9,11},{10,... | collective-permute-start | bytes 393224 | tf_op jit(solution)/shard_map/ppermute | solution.py:14
  66.8 16.8 %collective-permute-start.12 = (bf16[512,128]{1,0:T(8,128)(2,1)}, bf16[512,128]{1,0:T(8,128)(2,1)}, u32[]{:S(2)}, u32[]{:S(2)}) collective-permute-start(bf16[512,128]{1,0:T(8,128)(2,1)} %get-tuple-element.24), channel_id=1, source_target_pairs={{0,3},{1,0},{2,1},{3,2},{4,7},{5,4},{6,5},{7,6},{8,11},{9,8},{10,9... | collective-permute-start | bytes 393224 | tf_op jit(solution)/shard_map/ppermute | solution.py:14
  68.7 2.6 %copy-start.27 = (f32[512]{0:T(512)S(1)}, f32[512]{0:T(512)}, u32[]{:S(2)}) copy-start(f32[512]{0:T(512)} %param.9) | copy-start | bytes 6148
  71.9 3.3 %copy-start.8 = (bf16[512,512]{1,0:T(8,128)(2,1)}, bf16[512,512]{1,0:T(8,128)(2,1)S(1)}, u32[]{:S(2)}) copy-start(bf16[512,512]{1,0:T(8,128)(2,1)S(1)} %fusion.107) | copy-start | bytes 1572868
  72.6 11.0 %collective-permute-start.6 = (bf16[128,512]{1,0:T(8,128)(2,1)}, bf16[128,512]{1,0:T(8,128)(2,1)S(1)}, u32[]{:S(2)}, u32[]{:S(2)}) collective-permute-start(bf16[128,512]{1,0:T(8,128)(2,1)} %get-tuple-element.32), channel_id=1, source_target_pairs={{0,1},{1,2},{2,3},{3,0},{4,5},{5,6},{6,7},{7,4},{8,9},{9,10},{10,1... | collective-permute-start | bytes 393224 | tf_op jit(solution)/shard_map/ppermute | solution.py:14
  73.8 14.4 %collective-permute-start.13 = (bf16[128,512]{1,0:T(8,128)(2,1)S(1)}, bf16[128,512]{1,0:T(8,128)(2,1)}, u32[]{:S(2)}, u32[]{:S(2)}) collective-permute-start(bf16[128,512]{1,0:T(8,128)(2,1)S(1)} %get-tuple-element.30), channel_id=1, source_target_pairs={{0,2},{1,3},{2,0},{3,1},{4,6},{5,7},{6,4},{7,5},{8,10},{9,11},{10,... | collective-permute-start | bytes 393224 | tf_op jit(solution)/shard_map/ppermute | solution.py:14
  75.1 17.2 %all-to-all-start.4 = ((bf16[8,64,512]{2,1,0:T(8,128)(2,1)}), bf16[8,64,512]{2,1,0:T(8,128)(2,1)S(1)}, u32[]{:S(2)}, u32[]{:S(2)}) async-start(bf16[8,64,512]{2,1,0:T(8,128)(2,1)} %bitcast.45), calls=%async_computation.4 | async-start | bytes 1048576 | tf_op jit(solution)/shard_map/all_to_all | solution.py:19
  81.8 1.9 %copy-start.9 = (bf16[512,128]{1,0:T(8,128)(2,1)S(1)}, bf16[512,128]{1,0:T(8,128)(2,1)}, u32[]{:S(2)}) copy-start(bf16[512,128]{1,0:T(8,128)(2,1)} %fusion.56) | copy-start | bytes 393220
  81.8 8.8 %collective-permute-start.14 = (bf16[128,512]{1,0:T(8,128)(2,1)S(1)}, bf16[128,512]{1,0:T(8,128)(2,1)S(1)}, u32[]{:S(2)}, u32[]{:S(2)}) collective-permute-start(bf16[128,512]{1,0:T(8,128)(2,1)S(1)} %get-tuple-element.31), channel_id=1, source_target_pairs={{0,3},{1,0},{2,1},{3,2},{4,7},{5,4},{6,5},{7,6},{8,11},{9,8},{10,9... | collective-permute-start | bytes 393224 | tf_op jit(solution)/shard_map/ppermute | solution.py:14
  86.7 6.4 %copy-start.4 = (bf16[512,512]{1,0:T(8,128)(2,1)}, bf16[512,512]{1,0:T(8,128)(2,1)S(1)}, u32[]{:S(2)}) copy-start(bf16[512,512]{1,0:T(8,128)(2,1)S(1)} %fusion.72) | copy-start | bytes 1572868

commit v14 on v13

--- a/solution.py
+++ b/solution.py
@@ -1,6 +1,7 @@
 import jax
 import jax.numpy as jnp
 from jax import lax
+from jax.experimental.layout import Layout, with_layout_constraint
 from jax.sharding import PartitionSpec as P
 
 F32 = jnp.float32
@@ -53,13 +54,15 @@
 
     cq_seq = second_blocks.shape[0]
     diagonal = jnp.eye(cq_seq, dtype=BF16)
-    seq_mix = (jnp.transpose(second_blocks, (1, 0, 2))[:, :, :, None] * diagonal[None, :, None, :])
-    seq_mix = seq_mix.reshape(n * cq_seq, n * cq_seq)
 
     source = inputs.astype(F32)
     slope_in = jax.nn.sigmoid(gate_in * source)
     gated = (source * slope_in).astype(BF16)
     mixed_first = jnp.dot(first_blocks[0], gated, preferred_element_type=F32).astype(BF16)
+    mixed_first = with_layout_constraint(mixed_first, Layout(major_to_minor=(0, 1)))
+    second_late, mixed_first = lax.optimization_barrier((second_blocks, mixed_first))
+    seq_mix = (jnp.transpose(second_late, (1, 0, 2))[:, :, :, None] * diagonal[None, :, None, :])
+    seq_mix = seq_mix.reshape(n * cq_seq, n * cq_seq)
 
     upstream = cotangent
     upstream_late, mixed_first = lax.optimization_barrier((upstream, mixed_first))

time: 93.9 us -> 94.6 us (level)
  local copies, waits for them, and re-layouts: 11.2 us -> 10.2 us
    all_to_all x5, waiting for transfers between devices: 8.56 us -> 9.66 us  [swap(): return lax.all_to_all(pieces, axis_name, 0, 0, tiled=True)]
    optimization_barrier x1 -> x0, local copies, waits for them, and re-layouts: 1 us -> none  [on_device(): lax.optimization_barrier((upstream, mixed_first))]
  transfers between devices with their start and end apart: 20 -> 20, of which waited for: 7 -> 7; matrix products, arithmetic and copies ran while one was open for 25% -> 24% of each run, Pallas kernels for 0% -> 0%
where the time goes in v14:
time: 94.6 us; the launch traced here: 93.8 us
  starting transfers between devices  43.6 us (46%)
  waiting for transfers between devices  16 us (17%)
  matrix products  12.8 us (14%)
  local copies, waits for them, and re-layouts  10.2 us (11%)
  other arithmetic  9.94 us (11%)
  between operations  1.14 us (1%)
    ppermute x15, starting transfers between devices, exchange(): lax.ppermute(pieces[k], axis_name, [(i, (i + k) % n) for i in range(n)])  25.7 us
    all_to_all x5, starting transfers between devices, swap(): return lax.all_to_all(pieces, axis_name, 0, 0, tiled=True)  17.9 us
    all_to_all x5, waiting for transfers between devices, swap(): return lax.all_to_all(pieces, axis_name, 0, 0, tiled=True)  9.66 us
    ppermute x15, waiting for transfers between devices, exchange(): lax.ppermute(pieces[k], axis_name, [(i, (i + k) % n) for i in range(n)])  6.36 us
    unnamed x60, local copies, waits for them, and re-layouts  3.53 us
    dot_general x1, matrix products, on_device(): spread = jnp.dot(first_blocks[0].T, first_grad, preferred_element_type=F32)  3.19 us
    dynamic_update_slice x5, other arithmetic, place_chunks(): out = lax.dynamic_update_slice_in_dim(out, chunk, start, axis=1)  3.11 us
    dynamic_update_slice x3, local copies, waits for them, and re-layouts, place_chunks(): out = lax.dynamic_update_slice_in_dim(out, chunk, start, axis=1)  2.87 us
  transfers between devices with their start and end apart: 20, of which 7 were waited for; matrix products, arithmetic and copies ran while one was open for 24% of the time, Pallas kernels for 0%

profile of v14, /device:TPU:0, one launch (start us, length us, event | category | flops | bytes accessed | tf_op | source)
XLA Modules:
  0.0 93.8 jit_solution(10001748262157749330)
XLA Ops:
  0.6 0.0 copy-start
  0.7 0.7 copy-done.26
  1.4 2.6 %fusion.6 = bf16[512,512]{1,0:T(8,128)(2,1)} fusion(bf16[1,512,512]{2,1,0:T(8,128)(2,1)} %param.11, bf16[512,512]{1,0:T(8,128)(2,1)} %param.8, f32[512]{0:T(512)S(1)} %copy-done.26), kind=kOutput, calls=%fused_computation.23 | convolution fusion | flops 270532608 | bytes 1574912 | tf_op jit(solution)/shard_map/dot_general | solution.py:61
  4.0 0.8 constant_dynamic-slice_fusion.35
  4.8 3.0 %collective-permute-start = (bf16[512,128]{1,0:T(8,128)(2,1)}, bf16[512,128]{1,0:T(8,128)(2,1)S(1)}, u32[]{:S(2)}, u32[]{:S(2)}) collective-permute-start(bf16[512,128]{1,0:T(8,128)(2,1)} %get-tuple-element.40), channel_id=1, source_target_pairs={{0,1},{1,2},{2,3},{3,0},{4,5},{5,6},{6,7},{7,4},{8,9},{9,10},{10,1... | collective-permute-start | bytes 393224 | tf_op jit(solution)/shard_map/ppermute | solution.py:15
  7.8 2.6 %collective-permute-start.1 = (bf16[512,128]{1,0:T(8,128)(2,1)}, bf16[512,128]{1,0:T(8,128)(2,1)S(1)}, u32[]{:S(2)}, u32[]{:S(2)}) collective-permute-start(bf16[512,128]{1,0:T(8,128)(2,1)} %get-tuple-element.42), channel_id=1, source_target_pairs={{0,2},{1,3},{2,0},{3,1},{4,6},{5,7},{6,4},{7,5},{8,10},{9,11},{10,... | collective-permute-start | bytes 393224 | tf_op jit(solution)/shard_map/ppermute | solution.py:15
  10.4 1.3 %collective-permute-start.2 = (bf16[512,128]{1,0:T(8,128)(2,1)}, bf16[512,128]{1,0:T(8,128)(2,1)S(1)}, u32[]{:S(2)}, u32[]{:S(2)}) collective-permute-start(bf16[512,128]{1,0:T(8,128)(2,1)} %get-tuple-element.41), channel_id=1, source_target_pairs={{0,3},{1,0},{2,1},{3,2},{4,7},{5,4},{6,5},{7,6},{8,11},{9,8},{10,9... | collective-permute-start | bytes 393224 | tf_op jit(solution)/shard_map/ppermute | solution.py:15
  11.8 3.7 %all-to-all-start = ((bf16[8,64,512]{2,1,0:T(8,128)(2,1)}), bf16[8,64,512]{2,1,0:T(8,128)(2,1)S(1)}, u32[]{:S(2)}, u32[]{:S(2)}) async-start(bf16[8,64,512]{2,1,0:T(8,128)(2,1)} %bitcast.3), calls=%async_computation | async-start | bytes 1048576 | tf_op jit(solution)/shard_map/all_to_all | solution.py:20
  15.5 0.7 copy-done.10
  16.2 0.1 copy.12
  16.3 0.6 broadcast_multiply_fusion
  16.9 0.7 fusion.75
  17.6 0.6 mul.490
  18.3 0.7 fusion.103
  19.0 0.2 collective-permute-done.1
  19.3 1.0 %fusion.52 = (bf16[512,128]{1,0:T(8,128)(2,1)}, bf16[512,128]{1,0:T(8,128)(2,1)}, bf16[512,128]{1,0:T(8,128)(2,1)}) fusion(bf16[512,128]{1,0:T(8,128)(2,1)S(1)} %collective-permute-done, bf16[512,128]{1,0:T(8,128)(2,1)S(1)} %collective-permute-done.1, bf16[512,128]{1,0:T(8,128)(2,1)S(1)} %collective-permute-done.2, f32[128]{0:T(128)S(1)} %get-tuple-element.58, ...), kind=kLoop, calls=%fused_computation.104 | loop fusion | flops 1835008 | bytes 923652 | tf_op jit(solution)/shard_map/convert_element_type | solution.py:74
  20.2 3.3 %collective-permute-start.3 = (bf16[512,128]{1,0:T(8,128)(2,1)}, bf16[512,128]{1,0:T(8,128)(2,1)}, u32[]{:S(2)}, u32[]{:S(2)}) collective-permute-start(bf16[512,128]{1,0:T(8,128)(2,1)} %get-tuple-element.32), channel_id=1, source_target_pairs={{0,1},{1,2},{2,3},{3,0},{4,5},{5,6},{6,7},{7,4},{8,9},{9,10},{10,1... | collective-permute-start | bytes 393224 | tf_op jit(solution)/shard_map/ppermute | solution.py:15
  23.5 1.6 %collective-permute-start.4 = (bf16[512,128]{1,0:T(8,128)(2,1)}, bf16[512,128]{1,0:T(8,128)(2,1)}, u32[]{:S(2)}, u32[]{:S(2)}) collective-permute-start(bf16[512,128]{1,0:T(8,128)(2,1)} %get-tuple-element.33), channel_id=1, source_target_pairs={{0,2},{1,3},{2,0},{3,1},{4,6},{5,7},{6,4},{7,5},{8,10},{9,11},{10,... | collective-permute-start | bytes 393224 | tf_op jit(solution)/shard_map/ppermute | solution.py:15
  25.1 0.7 collective-permute-start.5
  25.9 1.2 %convolution_convert_fusion.2 = bf16[512,512]{1,0:T(8,128)(2,1)} fusion(bf16[512,512]{1,0:T(8,128)(2,1)S(1)} %mul.490, bf16[512,512]{1,0:T(8,128)(2,1)S(1)} %bitcast.115), kind=kOutput, calls=%fused_computation.18 | convolution fusion | flops 268697600 | bytes 1572864 | tf_op jit(solution)/shard_map/dot_general | solution.py:81
  27.1 3.7 %all-to-all-start.1 = ((bf16[8,64,512]{2,1,0:T(8,128)(2,1)}), bf16[8,64,512]{2,1,0:T(8,128)(2,1)S(1)}, u32[]{:S(2)}, u32[]{:S(2)}) async-start(bf16[8,64,512]{2,1,0:T(8,128)(2,1)} %bitcast.5), calls=%async_computation.1 | async-start | bytes 1048576 | tf_op jit(solution)/shard_map/all_to_all | solution.py:20
  30.9 0.1 fusion.73
  31.0 1.0 %constant_dynamic-update-slice_fusion.2 = bf16[512,512]{1,0:T(8,128)(2,1)S(1)} fusion(bf16[512,512]{1,0:T(8,128)(2,1)S(1)} %fusion.73, bf16[512,128]{1,0:T(8,128)(2,1)} %collective-permute-done.3, s32[]{:T(128)S(6)} %select_n.80), kind=kLoop, calls=%fused_computation.165 | loop fusion | bytes 262148 | tf_op jit(solution)/shard_map/dynamic_update_slice | solution.py:34
  32.0 1.7 %collective-permute-done.4 = bf16[512,128]{1,0:T(8,128)(2,1)} collective-permute-done((bf16[512,128]{1,0:T(8,128)(2,1)}, bf16[512,128]{1,0:T(8,128)(2,1)}, u32[]{:S(2)}, u32[]{:S(2)}) %collective-permute-start.4) | collective-permute-done | bytes 131104 | tf_op jit(solution)/shard_map/ppermute | solution.py:15
  33.7 0.9 constant_dynamic-update-slice_fusion.1
  34.7 0.9 %constant_dynamic-update-slice_fusion = bf16[512,512]{1,0:T(8,128)(2,1)S(1)} fusion(bf16[512,512]{1,0:T(8,128)(2,1)S(1)} %constant_dynamic-update-slice_fusion.1, bf16[512,128]{1,0:T(8,128)(2,1)} %collective-permute-done.5, s32[]{:T(128)S(6)} %select_n.84), kind=kLoop, calls=%fused_computation.155 | loop fusion | bytes 262148 | tf_op jit(solution)/shard_map/dynamic_update_slice | solution.py:34
  35.7 0.8 copy-done.2
  36.4 4.1 %all-to-all-done.1 = bf16[8,64,512]{2,1,0:T(8,128)(2,1)S(1)} async-done(((bf16[8,64,512]{2,1,0:T(8,128)(2,1)}), bf16[8,64,512]{2,1,0:T(8,128)(2,1)S(1)}, u32[]{:S(2)}, u32[]{:S(2)}) %all-to-all-start.1) | async-done | bytes 524320 | tf_op jit(solution)/shard_map/all_to_all | solution.py:20
  40.6 0.4 fusion.31
  41.0 0.6 copy-done.3
  41.6 1.1 %multiply_convert_fusion = (bf16[512,512]{1,0:T(8,128)(2,1)S(1)}, bf16[512,512]{1,0:T(8,128)(2,1)S(1)}) fusion(bf16[512,512]{1,0:T(8,128)(2,1)S(1)} %copy-done.3, bf16[512,512]{1,0:T(8,128)(2,1)S(1)} %fusion.31, bf16[1,512,512]{2,1,0:T(8,128)(2,1)S(1)} %copy-done), kind=kOutput, calls=%fused_computation.50 | convolution fusion | flops 274464768 | bytes 2621440 | tf_op jit(solution)/shard_map/dot_general | solution.py:87
  42.8 1.6 %fusion.22 = (bf16[512,512]{1,0:T(8,128)(2,1)}, bf16[512,512]{1,0:T(8,128)(2,1)}) fusion(bf16[512,512]{1,0:T(8,128)(2,1)S(1)} %copy-done.6, f32[512]{0:T(512)S(1)} %copy-done.11, bf16[512,512]{1,0:T(8,128)(2,1)S(1)} %get-tuple-element.27, bf16[1,512,512]{2,1,0:T(8,128)(2,1)S(1)} %copy-done, bf16[512,512]{1,0:T(8,128)(2,1)S(1)} %copy-done.1), kind=kOutput, calls=%fused_computation.39 | convolution fusion | flops 271319040 | bytes 3147776 | tf_op jit(solution)/shard_map/dot_general | solution.py:101
  44.3 3.5 %all-to-all-start.2 = ((bf16[8,64,512]{2,1,0:T(8,128)(2,1)}), bf16[8,64,512]{2,1,0:T(8,128)(2,1)S(1)}, u32[]{:S(2)}, u32[]{:S(2)}) async-start(bf16[8,64,512]{2,1,0:T(8,128)(2,1)} %bitcast.121), calls=%async_computation.2 | async-start | bytes 1048576 | tf_op jit(solution)/shard_map/all_to_all | solution.py:20
  47.9 0.8 constant_dynamic-slice_fusion.13
  48.6 1.3 %collective-permute-start.7 = (bf16[512,128]{1,0:T(8,128)(2,1)}, bf16[512,128]{1,0:T(8,128)(2,1)S(1)}, u32[]{:S(2)}, u32[]{:S(2)}) collective-permute-start(bf16[512,128]{1,0:T(8,128)(2,1)} %get-tuple-element.39), channel_id=1, source_target_pairs={{0,1},{1,2},{2,3},{3,0},{4,5},{5,6},{6,7},{7,4},{8,9},{9,10},{10,1... | collective-permute-start | bytes 393224 | tf_op jit(solution)/shard_map/ppermute | solution.py:15
  49.9 1.3 %collective-permute-start.8 = (bf16[512,128]{1,0:T(8,128)(2,1)}, bf16[512,128]{1,0:T(8,128)(2,1)S(1)}, u32[]{:S(2)}, u32[]{:S(2)}) collective-permute-start(bf16[512,128]{1,0:T(8,128)(2,1)} %get-tuple-element.38), channel_id=1, source_target_pairs={{0,2},{1,3},{2,0},{3,1},{4,6},{5,7},{6,4},{7,5},{8,10},{9,11},{10,... | collective-permute-start | bytes 393224 | tf_op jit(solution)/shard_map/ppermute | solution.py:15
  51.2 1.2 %collective-permute-start.9 = (bf16[512,128]{1,0:T(8,128)(2,1)}, bf16[512,128]{1,0:T(8,128)(2,1)S(1)}, u32[]{:S(2)}, u32[]{:S(2)}) collective-permute-start(bf16[512,128]{1,0:T(8,128)(2,1)} %get-tuple-element.37), channel_id=1, source_target_pairs={{0,3},{1,0},{2,1},{3,2},{4,7},{5,4},{6,5},{7,6},{8,11},{9,8},{10,9... | collective-permute-start | bytes 393224 | tf_op jit(solution)/shard_map/ppermute | solution.py:15
  52.5 1.3 %fusion.110 = bf16[512,512]{1,0:T(8,128)(2,1)} fusion(bf16[512,512]{1,0:T(8,128)(2,1)S(1)} %fusion.31, bf16[512,512]{1,0:T(8,128)(2,1)S(1)} %copy-done.29), kind=kOutput, calls=%fused_computation.211 | convolution fusion | flops 268435456 | bytes 1572864 | tf_op jit(solution)/shard_map/dot_general | solution.py:103
  53.8 3.8 %all-to-all-done.2 = bf16[8,64,512]{2,1,0:T(8,128)(2,1)S(1)} async-done(((bf16[8,64,512]{2,1,0:T(8,128)(2,1)}), bf16[8,64,512]{2,1,0:T(8,128)(2,1)S(1)}, u32[]{:S(2)}, u32[]{:S(2)}) %all-to-all-start.2) | async-done | bytes 524320 | tf_op jit(solution)/shard_map/all_to_all | solution.py:20
  57.5 1.3 %convolution_convert_fusion.1 = bf16[512,512]{1,0:T(8,128)(2,1)} fusion(bf16[512,512]{1,0:T(8,128)(2,1)S(1)} %mul.490, bf16[512,512]{1,0:T(8,128)(2,1)S(1)} %bitcast.120), kind=kOutput, calls=%fused_computation.17 | convolution fusion | flops 268697600 | bytes 1572864 | tf_op jit(solution)/shard_map/dot_general | solution.py:108
  58.8 3.5 %all-to-all-start.3 = ((bf16[8,64,512]{2,1,0:T(8,128)(2,1)}), bf16[8,64,512]{2,1,0:T(8,128)(2,1)S(1)}, u32[]{:S(2)}, u32[]{:S(2)}) async-start(bf16[8,64,512]{2,1,0:T(8,128)(2,1)} %bitcast.119), calls=%async_computation.3 | async-start | bytes 1048576 | tf_op jit(solution)/shard_map/all_to_all | solution.py:20
  62.5 0.5 copy-done.12
  63.0 0.0 copy-done.13
  63.1 0.9 %fusion.68 = (bf16[512,128]{1,0:T(8,128)(2,1)}, bf16[512,128]{1,0:T(8,128)(2,1)}, bf16[512,128]{1,0:T(8,128)(2,1)}) fusion(bf16[512,128]{1,0:T(8,128)(2,1)S(1)} %collective-permute-done.7, bf16[512,128]{1,0:T(8,128)(2,1)S(1)} %collective-permute-done.8, bf16[512,128]{1,0:T(8,128)(2,1)S(1)} %collective-permute-done.9, f32[128]{0:T(128)S(1)} %copy-done.12, ...), kind=kLoop, calls=%fused_computation.120 | loop fusion | flops 1835008 | bytes 923652 | tf_op jit(solution)/shard_map/convert_element_type | solution.py:95
  64.0 3.1 %collective-permute-start.10 = (bf16[512,128]{1,0:T(8,128)(2,1)}, bf16[512,128]{1,0:T(8,128)(2,1)}, u32[]{:S(2)}, u32[]{:S(2)}) collective-permute-start(bf16[512,128]{1,0:T(8,128)(2,1)} %get-tuple-element.29), channel_id=1, source_target_pairs={{0,1},{1,2},{2,3},{3,0},{4,5},{5,6},{6,7},{7,4},{8,9},{9,10},{10,1... | collective-permute-start | bytes 393224 | tf_op jit(solution)/shard_map/ppermute | solution.py:15
  67.1 0.1 collective-permute-start.11
  67.2 2.3 %collective-permute-start.12 = (bf16[512,128]{1,0:T(8,128)(2,1)}, bf16[512,128]{1,0:T(8,128)(2,1)}, u32[]{:S(2)}, u32[]{:S(2)}) collective-permute-start(bf16[512,128]{1,0:T(8,128)(2,1)} %get-tuple-element.28), channel_id=1, source_target_pairs={{0,3},{1,0},{2,1},{3,2},{4,7},{5,4},{6,5},{7,6},{8,11},{9,8},{10,9... | collective-permute-start | bytes 393224 | tf_op jit(solution)/shard_map/ppermute | solution.py:15
  69.5 0.8 fusion.56
  70.2 1.8 %all-to-all-done.3 = bf16[8,64,512]{2,1,0:T(8,128)(2,1)S(1)} async-done(((bf16[8,64,512]{2,1,0:T(8,128)(2,1)}), bf16[8,64,512]{2,1,0:T(8,128)(2,1)S(1)}, u32[]{:S(2)}, u32[]{:S(2)}) %all-to-all-start.3) | async-done | bytes 524320 | tf_op jit(solution)/shard_map/all_to_all | solution.py:20
  72.0 0.6 fusion.107
  72.6 0.8 dynamic-slice_convert_fusion.1
  73.4 1.3 %collective-permute-start.6 = (bf16[128,512]{1,0:T(8,128)(2,1)}, bf16[128,512]{1,0:T(8,128)(2,1)S(1)}, u32[]{:S(2)}, u32[]{:S(2)}) collective-permute-start(bf16[128,512]{1,0:T(8,128)(2,1)} %get-tuple-element.36), channel_id=1, source_target_pairs={{0,1},{1,2},{2,3},{3,0},{4,5},{5,6},{6,7},{7,4},{8,9},{9,10},{10,1... | collective-permute-start | bytes 393224 | tf_op jit(solution)/shard_map/ppermute | solution.py:15
  74.7 1.3 %collective-permute-start.13 = (bf16[128,512]{1,0:T(8,128)(2,1)S(1)}, bf16[128,512]{1,0:T(8,128)(2,1)}, u32[]{:S(2)}, u32[]{:S(2)}) collective-permute-start(bf16[128,512]{1,0:T(8,128)(2,1)S(1)} %get-tuple-element.34), channel_id=1, source_target_pairs={{0,2},{1,3},{2,0},{3,1},{4,6},{5,7},{6,4},{7,5},{8,10},{9,11},{10,... | collective-permute-start | bytes 393224 | tf_op jit(solution)/shard_map/ppermute | solution.py:15
  75.9 3.5 %all-to-all-start.4 = ((bf16[8,64,512]{2,1,0:T(8,128)(2,1)}), bf16[8,64,512]{2,1,0:T(8,128)(2,1)S(1)}, u32[]{:S(2)}, u32[]{:S(2)}) async-start(bf16[8,64,512]{2,1,0:T(8,128)(2,1)} %bitcast.45), calls=%async_computation.4 | async-start | bytes 1048576 | tf_op jit(solution)/shard_map/all_to_all | solution.py:20
  79.4 3.2 %fusion.3 = bf16[512,512]{1,0:T(8,128)(2,1)} fusion(bf16[512,512]{1,0:T(8,128)(2,1)S(1)} %bitcast.118, bf16[512,512]{1,0:T(8,128)(2,1)} %get-tuple-element.75, bf16[512,512]{1,0:T(8,128)(2,1)S(1)} %copy-done.7, bf16[512,512]{1,0:T(8,128)(2,1)S(1)} %bitcast.116, bf16[1,512,512]{2,1,0:T(8,128)(2,1)} %param.11, f32[512]{0:T(512)S(1)} %copy-done.11, ...), kind=kOutput, calls=%fused_computation.20 | convolution fusion | flops 274726912 | bytes 3149824 | tf_op jit(solution)/shard_map/dot_general | solution.py:133
  82.6 1.2 %collective-permute-start.14 = (bf16[128,512]{1,0:T(8,128)(2,1)S(1)}, bf16[128,512]{1,0:T(8,128)(2,1)S(1)}, u32[]{:S(2)}, u32[]{:S(2)}) collective-permute-start(bf16[128,512]{1,0:T(8,128)(2,1)S(1)} %get-tuple-element.35), channel_id=1, source_target_pairs={{0,3},{1,0},{2,1},{3,2},{4,7},{5,4},{6,5},{7,6},{8,11},{9,8},{10,9... | collective-permute-start | bytes 393224 | tf_op jit(solution)/shard_map/ppermute | solution.py:15
  83.9 0.1 fusion.69
  84.0 1.0 %fusion.70 = bf16[512,512]{1,0:T(8,128)(2,1)S(1)} fusion(bf16[512,512]{1,0:T(8,128)(2,1)S(1)} %fusion.69, s32[]{:T(128)S(6)} %select_n.80, bf16[512,128]{1,0:T(8,128)(2,1)} %collective-permute-done.10, bf16[512,512]{1,0:T(8,128)(2,1)S(1)} %fusion.31), kind=kLoop, calls=%fused_computation.131 | loop fusion | flops 262144 | bytes 393220 | tf_op jit(solution)/shard_map/dynamic_update_slice | solution.py:34
  85.0 1.0 %fusion.71 = bf16[512,512]{1,0:T(8,128)(2,1)S(1)} fusion(bf16[512,512]{1,0:T(8,128)(2,1)S(1)} %fusion.70, s32[]{:T(128)S(6)} %select_n.82, bf16[512,128]{1,0:T(8,128)(2,1)} %collective-permute-done.11, bf16[512,512]{1,0:T(8,128)(2,1)S(1)} %fusion.31), kind=kLoop, calls=%fused_computation.132 | loop fusion | flops 262144 | bytes 393220 | tf_op jit(solution)/shard_map/dynamic_update_slice | solution.py:34
  85.9 1.0 %fusion.72 = bf16[512,512]{1,0:T(8,128)(2,1)S(1)} fusion(bf16[512,512]{1,0:T(8,128)(2,1)S(1)} %fusion.71, s32[]{:T(128)S(6)} %select_n.84, bf16[512,128]{1,0:T(8,128)(2,1)} %collective-permute-done.12, bf16[512,512]{1,0:T(8,128)(2,1)S(1)} %fusion.31), kind=kLoop, calls=%fused_computation.133 | loop fusion | flops 262144 | bytes 393220 | tf_op jit(solution)/shard_map/dynamic_update_slice | solution.py:34
  86.9 2.0 %collective-permute-done.13 = bf16[128,512]{1,0:T(8,128)(2,1)} collective-permute-done((bf16[128,512]{1,0:T(8,128)(2,1)S(1)}, bf16[128,512]{1,0:T(8,128)(2,1)}, u32[]{:S(2)}, u32[]{:S(2)}) %collective-permute-start.13) | collective-permute-done | bytes 131104 | tf_op jit(solution)/shard_map/ppermute | solution.py:15
  88.9 2.4 %collective-permute-done.14 = bf16[128,512]{1,0:T(8,128)(2,1)S(1)} collective-permute-done((bf16[128,512]{1,0:T(8,128)(2,1)S(1)}, bf16[128,512]{1,0:T(8,128)(2,1)S(1)}, u32[]{:S(2)}, u32[]{:S(2)}) %collective-permute-start.14) | collective-permute-done | bytes 131104 | tf_op jit(solution)/shard_map/ppermute | solution.py:15
  91.3 1.7 %add_bitcast_fusion = f32[1,128,512]{2,1,0:T(8,128)} fusion(bf16[128,512]{1,0:T(8,128)(2,1)S(1)} %collective-permute-done.14, bf16[128,512]{1,0:T(8,128)(2,1)} %collective-permute-done.13, bf16[128,512]{1,0:T(8,128)(2,1)S(1)} %collective-permute-done.6, bf16[512,512]{1,0:T(8,128)(2,1)} %copy-done.8, s32[]{:T(128)S(6)} %select_n.64), kind=kLoop, calls=%fused_computation.121 | loop fusion | flops 458752 | bytes 786436 | tf_op jit(solution)/shard_map/broadcast_in_dim | solution.py:121
  93.0 0.7 convert_reduce_fusion
  (69 shorter events, 0.2 us)
Async XLA Ops:
  0.6 40.3 %copy-start = (bf16[1,512,512]{2,1,0:T(8,128)(2,1)S(1)}, bf16[1,512,512]{2,1,0:T(8,128)(2,1)}, u32[]{:S(2)}) copy-start(bf16[1,512,512]{2,1,0:T(8,128)(2,1)} %param.13) | copy-start | bytes 1572868
  0.7 0.7 copy-start.26
  1.4 2.6 %copy-start.1 = (bf16[512,512]{1,0:T(8,128)(2,1)S(1)}, bf16[512,512]{1,0:T(8,128)(2,1)}, u32[]{:S(2)}) copy-start(bf16[512,512]{1,0:T(8,128)(2,1)} %param.15) | copy-start | bytes 1572868
  4.8 14.2 %collective-permute-start = (bf16[512,128]{1,0:T(8,128)(2,1)}, bf16[512,128]{1,0:T(8,128)(2,1)S(1)}, u32[]{:S(2)}, u32[]{:S(2)}) collective-permute-start(bf16[512,128]{1,0:T(8,128)(2,1)} %get-tuple-element.40), channel_id=1, source_target_pairs={{0,1},{1,2},{2,3},{3,0},{4,5},{5,6},{6,7},{7,4},{8,9},{9,10},{10,1... | collective-permute-start | bytes 393224 | tf_op jit(solution)/shard_map/ppermute | solution.py:15
  7.8 11.4 %collective-permute-start.1 = (bf16[512,128]{1,0:T(8,128)(2,1)}, bf16[512,128]{1,0:T(8,128)(2,1)S(1)}, u32[]{:S(2)}, u32[]{:S(2)}) collective-permute-start(bf16[512,128]{1,0:T(8,128)(2,1)} %get-tuple-element.42), channel_id=1, source_target_pairs={{0,2},{1,3},{2,0},{3,1},{4,6},{5,7},{6,4},{7,5},{8,10},{9,11},{10,... | collective-permute-start | bytes 393224 | tf_op jit(solution)/shard_map/ppermute | solution.py:15
  10.4 8.9 %collective-permute-start.2 = (bf16[512,128]{1,0:T(8,128)(2,1)}, bf16[512,128]{1,0:T(8,128)(2,1)S(1)}, u32[]{:S(2)}, u32[]{:S(2)}) collective-permute-start(bf16[512,128]{1,0:T(8,128)(2,1)} %get-tuple-element.41), channel_id=1, source_target_pairs={{0,3},{1,0},{2,1},{3,2},{4,7},{5,4},{6,5},{7,6},{8,11},{9,8},{10,9... | collective-permute-start | bytes 393224 | tf_op jit(solution)/shard_map/ppermute | solution.py:15
  11.8 14.1 %all-to-all-start = ((bf16[8,64,512]{2,1,0:T(8,128)(2,1)}), bf16[8,64,512]{2,1,0:T(8,128)(2,1)S(1)}, u32[]{:S(2)}, u32[]{:S(2)}) async-start(bf16[8,64,512]{2,1,0:T(8,128)(2,1)} %bitcast.3), calls=%async_computation | async-start | bytes 1048576 | tf_op jit(solution)/shard_map/all_to_all | solution.py:20
  15.5 0.7 copy-start.10
  20.2 10.8 %collective-permute-start.3 = (bf16[512,128]{1,0:T(8,128)(2,1)}, bf16[512,128]{1,0:T(8,128)(2,1)}, u32[]{:S(2)}, u32[]{:S(2)}) collective-permute-start(bf16[512,128]{1,0:T(8,128)(2,1)} %get-tuple-element.32), channel_id=1, source_target_pairs={{0,1},{1,2},{2,3},{3,0},{4,5},{5,6},{6,7},{7,4},{8,9},{9,10},{10,1... | collective-permute-start | bytes 393224 | tf_op jit(solution)/shard_map/ppermute | solution.py:15
  23.5 10.2 %collective-permute-start.4 = (bf16[512,128]{1,0:T(8,128)(2,1)}, bf16[512,128]{1,0:T(8,128)(2,1)}, u32[]{:S(2)}, u32[]{:S(2)}) collective-permute-start(bf16[512,128]{1,0:T(8,128)(2,1)} %get-tuple-element.33), channel_id=1, source_target_pairs={{0,2},{1,3},{2,0},{3,1},{4,6},{5,7},{6,4},{7,5},{8,10},{9,11},{10,... | collective-permute-start | bytes 393224 | tf_op jit(solution)/shard_map/ppermute | solution.py:15
  25.1 9.5 %collective-permute-start.5 = (bf16[512,128]{1,0:T(8,128)(2,1)}, bf16[512,128]{1,0:T(8,128)(2,1)}, u32[]{:S(2)}, u32[]{:S(2)}) collective-permute-start(bf16[512,128]{1,0:T(8,128)(2,1)} %get-tuple-element.31), channel_id=1, source_target_pairs={{0,3},{1,0},{2,1},{3,2},{4,7},{5,4},{6,5},{7,6},{8,11},{9,8},{10,9... | collective-permute-start | bytes 393224 | tf_op jit(solution)/shard_map/ppermute | solution.py:15
  27.1 13.5 %all-to-all-start.1 = ((bf16[8,64,512]{2,1,0:T(8,128)(2,1)}), bf16[8,64,512]{2,1,0:T(8,128)(2,1)S(1)}, u32[]{:S(2)}, u32[]{:S(2)}) async-start(bf16[8,64,512]{2,1,0:T(8,128)(2,1)} %bitcast.5), calls=%async_computation.1 | async-start | bytes 1048576 | tf_op jit(solution)/shard_map/all_to_all | solution.py:20
  31.0 9.6 %copy-start.5 = (bf16[512,512]{1,0:T(8,128)(2,1)S(1)}, bf16[512,512]{1,0:T(8,128)(2,1)}, u32[]{:S(2)}) copy-start(bf16[512,512]{1,0:T(8,128)(2,1)} %param.8) | copy-start | bytes 1572868
  34.7 5.9 %copy-start.11 = (f32[512]{0:T(512)S(1)}, f32[512]{0:T(512)}, u32[]{:S(2)}) copy-start(f32[512]{0:T(512)} %param.10) | copy-start | bytes 6148
  35.6 0.8 copy-start.2
  40.6 1.0 %copy-start.3 = (bf16[512,512]{1,0:T(8,128)(2,1)S(1)}, bf16[512,512]{1,0:T(8,128)(2,1)}, u32[]{:S(2)}) copy-start(bf16[512,512]{1,0:T(8,128)(2,1)} %copy-done.2) | copy-start | bytes 1572868
  41.6 1.1 %copy-start.6 = (bf16[512,512]{1,0:T(8,128)(2,1)S(1)}, bf16[512,512]{1,0:T(8,128)(2,1)}, u32[]{:S(2)}) copy-start(bf16[512,512]{1,0:T(8,128)(2,1)} %param.8) | copy-start | bytes 1572868
  42.7 1.6 %copy-start.28 = (bf16[512,512]{1,0:T(8,128)(2,1)}, bf16[512,512]{1,0:T(8,128)(2,1)S(1)}, u32[]{:S(2)}) copy-start(bf16[512,512]{1,0:T(8,128)(2,1)S(1)} %get-tuple-element.27) | copy-start | bytes 1572868
  44.3 13.2 %all-to-all-start.2 = ((bf16[8,64,512]{2,1,0:T(8,128)(2,1)}), bf16[8,64,512]{2,1,0:T(8,128)(2,1)S(1)}, u32[]{:S(2)}, u32[]{:S(2)}) async-start(bf16[8,64,512]{2,1,0:T(8,128)(2,1)} %bitcast.121), calls=%async_computation.2 | async-start | bytes 1048576 | tf_op jit(solution)/shard_map/all_to_all | solution.py:20
  47.8 4.6 %copy-start.29 = (bf16[512,512]{1,0:T(8,128)(2,1)S(1)}, bf16[512,512]{1,0:T(8,128)(2,1)}, u32[]{:S(2)}) copy-start(bf16[512,512]{1,0:T(8,128)(2,1)} %copy-done.28) | copy-start | bytes 1572868
  48.6 13.7 %collective-permute-start.7 = (bf16[512,128]{1,0:T(8,128)(2,1)}, bf16[512,128]{1,0:T(8,128)(2,1)S(1)}, u32[]{:S(2)}, u32[]{:S(2)}) collective-permute-start(bf16[512,128]{1,0:T(8,128)(2,1)} %get-tuple-element.39), channel_id=1, source_target_pairs={{0,1},{1,2},{2,3},{3,0},{4,5},{5,6},{6,7},{7,4},{8,9},{9,10},{10,1... | collective-permute-start | bytes 393224 | tf_op jit(solution)/shard_map/ppermute | solution.py:15
  49.9 12.4 %collective-permute-start.8 = (bf16[512,128]{1,0:T(8,128)(2,1)}, bf16[512,128]{1,0:T(8,128)(2,1)S(1)}, u32[]{:S(2)}, u32[]{:S(2)}) collective-permute-start(bf16[512,128]{1,0:T(8,128)(2,1)} %get-tuple-element.38), channel_id=1, source_target_pairs={{0,2},{1,3},{2,0},{3,1},{4,6},{5,7},{6,4},{7,5},{8,10},{9,11},{10,... | collective-permute-start | bytes 393224 | tf_op jit(solution)/shard_map/ppermute | solution.py:15
  51.2 11.1 %collective-permute-start.9 = (bf16[512,128]{1,0:T(8,128)(2,1)}, bf16[512,128]{1,0:T(8,128)(2,1)S(1)}, u32[]{:S(2)}, u32[]{:S(2)}) collective-permute-start(bf16[512,128]{1,0:T(8,128)(2,1)} %get-tuple-element.37), channel_id=1, source_target_pairs={{0,3},{1,0},{2,1},{3,2},{4,7},{5,4},{6,5},{7,6},{8,11},{9,8},{10,9... | collective-permute-start | bytes 393224 | tf_op jit(solution)/shard_map/ppermute | solution.py:15
  58.8 3.6 %copy-start.15 = (f32[128]{0:T(128)S(1)}, f32[128]{0:T(128)}, u32[]{:S(2)}) copy-start(f32[128]{0:T(128)} %get-tuple-element.47) | copy-start | bytes 1540
  58.8 3.6 %copy-start.16 = (f32[128]{0:T(128)S(1)}, f32[128]{0:T(128)}, u32[]{:S(2)}) copy-start(f32[128]{0:T(128)} %get-tuple-element.48) | copy-start | bytes 1540
  58.8 3.6 %copy-start.17 = (f32[128]{0:T(128)S(1)}, f32[128]{0:T(128)}, u32[]{:S(2)}) copy-start(f32[128]{0:T(128)} %get-tuple-element.49) | copy-start | bytes 1540
  58.8 3.7 %copy-start.18 = (f32[128]{0:T(128)S(1)}, f32[128]{0:T(128)}, u32[]{:S(2)}) copy-start(f32[128]{0:T(128)} %get-tuple-element.50) | copy-start | bytes 1540
  58.8 3.7 %copy-start.19 = (f32[128]{0:T(128)S(1)}, f32[128]{0:T(128)}, u32[]{:S(2)}) copy-start(f32[128]{0:T(128)} %get-tuple-element.51) | copy-start | bytes 1540
  58.8 3.7 %copy-start.20 = (f32[128]{0:T(128)S(1)}, f32[128]{0:T(128)}, u32[]{:S(2)}) copy-start(f32[128]{0:T(128)} %get-tuple-element.52) | copy-start | bytes 1540
  58.8 3.7 %copy-start.21 = (f32[128]{0:T(128)S(1)}, f32[128]{0:T(128)}, u32[]{:S(2)}) copy-start(f32[128]{0:T(128)} %get-tuple-element.53) | copy-start | bytes 1540
  58.8 3.7 %copy-start.22 = (f32[128]{0:T(128)S(1)}, f32[128]{0:T(128)}, u32[]{:S(2)}) copy-start(f32[128]{0:T(128)} %get-tuple-element.54) | copy-start | bytes 1540
  58.8 13.2 %all-to-all-start.3 = ((bf16[8,64,512]{2,1,0:T(8,128)(2,1)}), bf16[8,64,512]{2,1,0:T(8,128)(2,1)S(1)}, u32[]{:S(2)}, u32[]{:S(2)}) async-start(bf16[8,64,512]{2,1,0:T(8,128)(2,1)} %bitcast.119), calls=%async_computation.3 | async-start | bytes 1048576 | tf_op jit(solution)/shard_map/all_to_all | solution.py:20
  62.4 0.6 copy-start.12
  62.4 0.7 copy-start.13
  62.4 0.7 copy-start.14
  63.1 6.4 %copy-start.23 = (f32[128]{0:T(128)S(1)}, f32[128]{0:T(128)}, u32[]{:S(2)}) copy-start(f32[128]{0:T(128)} %get-tuple-element.55) | copy-start | bytes 1540
  63.1 6.4 %copy-start.24 = (f32[128]{0:T(128)S(1)}, f32[128]{0:T(128)}, u32[]{:S(2)}) copy-start(f32[128]{0:T(128)} %get-tuple-element.56) | copy-start | bytes 1540
  63.1 6.4 %copy-start.25 = (f32[128]{0:T(128)S(1)}, f32[128]{0:T(128)}, u32[]{:S(2)}) copy-start(f32[128]{0:T(128)} %get-tuple-element.57) | copy-start | bytes 1540
  64.0 8.0 %copy-start.7 = (bf16[512,512]{1,0:T(8,128)(2,1)S(1)}, bf16[512,512]{1,0:T(8,128)(2,1)}, u32[]{:S(2)}) copy-start(bf16[512,512]{1,0:T(8,128)(2,1)} %param.8) | copy-start | bytes 1572868
  64.0 18.6 %collective-permute-start.10 = (bf16[512,128]{1,0:T(8,128)(2,1)}, bf16[512,128]{1,0:T(8,128)(2,1)}, u32[]{:S(2)}, u32[]{:S(2)}) collective-permute-start(bf16[512,128]{1,0:T(8,128)(2,1)} %get-tuple-element.29), channel_id=1, source_target_pairs={{0,1},{1,2},{2,3},{3,0},{4,5},{5,6},{6,7},{7,4},{8,9},{9,10},{10,1... | collective-permute-start | bytes 393224 | tf_op jit(solution)/shard_map/ppermute | solution.py:15
  67.1 16.8 %collective-permute-start.11 = (bf16[512,128]{1,0:T(8,128)(2,1)}, bf16[512,128]{1,0:T(8,128)(2,1)}, u32[]{:S(2)}, u32[]{:S(2)}) collective-permute-start(bf16[512,128]{1,0:T(8,128)(2,1)} %get-tuple-element.30), channel_id=1, source_target_pairs={{0,2},{1,3},{2,0},{3,1},{4,6},{5,7},{6,4},{7,5},{8,10},{9,11},{10,... | collective-permute-start | bytes 393224 | tf_op jit(solution)/shard_map/ppermute | solution.py:15
  67.2 16.7 %collective-permute-start.12 = (bf16[512,128]{1,0:T(8,128)(2,1)}, bf16[512,128]{1,0:T(8,128)(2,1)}, u32[]{:S(2)}, u32[]{:S(2)}) collective-permute-start(bf16[512,128]{1,0:T(8,128)(2,1)} %get-tuple-element.28), channel_id=1, source_target_pairs={{0,3},{1,0},{2,1},{3,2},{4,7},{5,4},{6,5},{7,6},{8,11},{9,8},{10,9... | collective-permute-start | bytes 393224 | tf_op jit(solution)/shard_map/ppermute | solution.py:15
  69.5 2.6 %copy-start.27 = (f32[512]{0:T(512)S(1)}, f32[512]{0:T(512)}, u32[]{:S(2)}) copy-start(f32[512]{0:T(512)} %param.9) | copy-start | bytes 6148
  72.6 3.4 %copy-start.8 = (bf16[512,512]{1,0:T(8,128)(2,1)}, bf16[512,512]{1,0:T(8,128)(2,1)S(1)}, u32[]{:S(2)}) copy-start(bf16[512,512]{1,0:T(8,128)(2,1)S(1)} %fusion.107) | copy-start | bytes 1572868
  73.4 10.5 %collective-permute-start.6 = (bf16[128,512]{1,0:T(8,128)(2,1)}, bf16[128,512]{1,0:T(8,128)(2,1)S(1)}, u32[]{:S(2)}, u32[]{:S(2)}) collective-permute-start(bf16[128,512]{1,0:T(8,128)(2,1)} %get-tuple-element.36), channel_id=1, source_target_pairs={{0,1},{1,2},{2,3},{3,0},{4,5},{5,6},{6,7},{7,4},{8,9},{9,10},{10,1... | collective-permute-start | bytes 393224 | tf_op jit(solution)/shard_map/ppermute | solution.py:15
  74.7 14.3 %collective-permute-start.13 = (bf16[128,512]{1,0:T(8,128)(2,1)S(1)}, bf16[128,512]{1,0:T(8,128)(2,1)}, u32[]{:S(2)}, u32[]{:S(2)}) collective-permute-start(bf16[128,512]{1,0:T(8,128)(2,1)S(1)} %get-tuple-element.34), channel_id=1, source_target_pairs={{0,2},{1,3},{2,0},{3,1},{4,6},{5,7},{6,4},{7,5},{8,10},{9,11},{10,... | collective-permute-start | bytes 393224 | tf_op jit(solution)/shard_map/ppermute | solution.py:15
  75.9 17.1 %all-to-all-start.4 = ((bf16[8,64,512]{2,1,0:T(8,128)(2,1)}), bf16[8,64,512]{2,1,0:T(8,128)(2,1)S(1)}, u32[]{:S(2)}, u32[]{:S(2)}) async-start(bf16[8,64,512]{2,1,0:T(8,128)(2,1)} %bitcast.45), calls=%async_computation.4 | async-start | bytes 1048576 | tf_op jit(solution)/shard_map/all_to_all | solution.py:20
  82.6 1.3 %copy-start.9 = (bf16[512,128]{1,0:T(8,128)(2,1)S(1)}, bf16[512,128]{1,0:T(8,128)(2,1)}, u32[]{:S(2)}) copy-start(bf16[512,128]{1,0:T(8,128)(2,1)} %fusion.56) | copy-start | bytes 393220
  82.6 8.7 %collective-permute-start.14 = (bf16[128,512]{1,0:T(8,128)(2,1)S(1)}, bf16[128,512]{1,0:T(8,128)(2,1)S(1)}, u32[]{:S(2)}, u32[]{:S(2)}) collective-permute-start(bf16[128,512]{1,0:T(8,128)(2,1)S(1)} %get-tuple-element.35), channel_id=1, source_target_pairs={{0,3},{1,0},{2,1},{3,2},{4,7},{5,4},{6,5},{7,6},{8,11},{9,8},{10,9... | collective-permute-start | bytes 393224 | tf_op jit(solution)/shard_map/ppermute | solution.py:15
  86.9 6.8 %copy-start.4 = (bf16[512,512]{1,0:T(8,128)(2,1)}, bf16[512,512]{1,0:T(8,128)(2,1)S(1)}, u32[]{:S(2)}) copy-start(bf16[512,512]{1,0:T(8,128)(2,1)S(1)} %fusion.72) | copy-start | bytes 1572868

commit v15 on v6

--- a/solution.py
+++ b/solution.py
@@ -111,8 +111,10 @@
         "ch",
     )
     first_block, added_back = lax.optimization_barrier((block_arrived[1], added_back))
-    block_arrived[1] = first_block
-    block_grad = sum(part.astype(F32) for part in block_arrived)[None]
+    (early_sum,) = lax.optimization_barrier(
+        (block_arrived[0].astype(F32) + first_block.astype(F32),)
+    )
+    block_grad = (early_sum + block_arrived[2].astype(F32) + block_arrived[3].astype(F32))[None]
     outputs = place_chunks(
         [
             (lane_chunk(hidden, t, kq).astype(F32) + part.astype(F32)).astype(BF16)

time: 93.2 us -> 93.2 us (level)
  waiting for transfers between devices: 17.1 us -> 15.3 us
    ppermute x15, waiting for transfers between devices: 5.63 us -> 3.84 us  [exchange(): lax.ppermute(pieces[k], axis_name, [(i, (i + k) % n) for i in range(n)])]
    add x0 -> x1, other arithmetic: none -> 0.94 us  [on_device(): block_arrived[0].astype(F32) + first_block.astype(F32)]
  transfers between devices with their start and end apart: 20 -> 20, of which waited for: 8 -> 8; matrix products, arithmetic and copies ran while one was open for 25% -> 26% of each run, Pallas kernels for 0% -> 0%
where the time goes in v15:
time: 93.2 us; the launch traced here: 92.3 us
  starting transfers between devices  42.7 us (46%)
  waiting for transfers between devices  15.3 us (16%)
  other arithmetic  11.9 us (13%)
  local copies, waits for them, and re-layouts  10.8 us (12%)
  matrix products  10.3 us (11%)
  between operations  1.18 us (1%)
    ppermute x15, starting transfers between devices, exchange(): lax.ppermute(pieces[k], axis_name, [(i, (i + k) % n) for i in range(n)])  24.9 us
    all_to_all x5, starting transfers between devices, swap(): return lax.all_to_all(pieces, axis_name, 0, 0, tiled=True)  17.8 us
    all_to_all x5, waiting for transfers between devices, swap(): return lax.all_to_all(pieces, axis_name, 0, 0, tiled=True)  11.5 us
    ppermute x15, waiting for transfers between devices, exchange(): lax.ppermute(pieces[k], axis_name, [(i, (i + k) % n) for i in range(n)])  3.84 us
    convert_element_type x2, other arithmetic, on_device(): added_out = [sum((act_arrived[k].astype(F32) * coefficient(origin_of[k],...  3.51 us
    unnamed x59, local copies, waits for them, and re-layouts  3.34 us
    dot_general x1, matrix products, on_device(): spread = jnp.dot(first_blocks[0].T, first_grad, preferred_element_type=F32)  3.19 us
    dynamic_update_slice x5, other arithmetic, place_chunks(): out = lax.dynamic_update_slice_in_dim(out, chunk, start, axis=1)  3.1 us
  transfers between devices with their start and end apart: 20, of which 8 were waited for; matrix products, arithmetic and copies ran while one was open for 26% of the time, Pallas kernels for 0%

profile of v15, /device:TPU:0, one launch (start us, length us, event | category | flops | bytes accessed | tf_op | source)
XLA Modules:
  0.0 92.3 jit_solution(2537053423506679858)
XLA Ops:
  0.7 0.7 copy-done.25
  1.4 1.8 %fusion.8 = bf16[512,512]{0,1:T(8,128)(2,1)S(1)} fusion(bf16[1,512,512]{2,1,0:T(8,128)(2,1)} %param.11, bf16[512,512]{1,0:T(8,128)(2,1)} %param.8, f32[512]{0:T(512)S(1)} %copy-done.25), kind=kOutput, calls=%fused_computation.25 | convolution fusion | flops 270532608 | bytes 1574912 | tf_op jit(solution)/shard_map/dot_general | solution.py:59
  3.2 0.1 constant_dynamic-slice_fusion.35
  3.3 3.1 %collective-permute-start = (bf16[512,128]{1,0:T(8,128)(2,1)S(1)}, bf16[512,128]{1,0:T(8,128)(2,1)S(1)}, u32[]{:S(2)}, u32[]{:S(2)}) collective-permute-start(bf16[512,128]{1,0:T(8,128)(2,1)S(1)} %get-tuple-element.36), channel_id=1, source_target_pairs={{0,1},{1,2},{2,3},{3,0},{4,5},{5,6},{6,7},{7,4},{8,9},{9,10},{10,1... | collective-permute-start | bytes 393224 | tf_op jit(solution)/shard_map/ppermute | solution.py:14
  6.4 2.6 %collective-permute-start.1 = (bf16[512,128]{1,0:T(8,128)(2,1)S(1)}, bf16[512,128]{1,0:T(8,128)(2,1)S(1)}, u32[]{:S(2)}, u32[]{:S(2)}) collective-permute-start(bf16[512,128]{1,0:T(8,128)(2,1)S(1)} %get-tuple-element.38), channel_id=1, source_target_pairs={{0,2},{1,3},{2,0},{3,1},{4,6},{5,7},{6,4},{7,5},{8,10},{9,11},{10,... | collective-permute-start | bytes 393224 | tf_op jit(solution)/shard_map/ppermute | solution.py:14
  9.0 1.3 %collective-permute-start.2 = (bf16[512,128]{1,0:T(8,128)(2,1)S(1)}, bf16[512,128]{1,0:T(8,128)(2,1)S(1)}, u32[]{:S(2)}, u32[]{:S(2)}) collective-permute-start(bf16[512,128]{1,0:T(8,128)(2,1)S(1)} %get-tuple-element.37), channel_id=1, source_target_pairs={{0,3},{1,0},{2,1},{3,2},{4,7},{5,4},{6,5},{7,6},{8,11},{9,8},{10,9... | collective-permute-start | bytes 393224 | tf_op jit(solution)/shard_map/ppermute | solution.py:14
  10.3 1.0 %copy.25 = bf16[512,512]{1,0:T(8,128)(2,1)} copy(bf16[512,512]{0,1:T(8,128)(2,1)S(1)} %fusion.8) | data formatting | bytes 1048576 | tf_op jit(solution)/shard_map/optimization_barrier | solution.py:62
  11.3 3.7 %all-to-all-start = ((bf16[8,64,512]{2,1,0:T(8,128)(2,1)}), bf16[8,64,512]{2,1,0:T(8,128)(2,1)S(1)}, u32[]{:S(2)}, u32[]{:S(2)}) async-start(bf16[8,64,512]{2,1,0:T(8,128)(2,1)} %bitcast.2), calls=%async_computation | async-start | bytes 1048576 | tf_op jit(solution)/shard_map/all_to_all | solution.py:19
  15.0 0.7 fusion.78
  15.7 0.7 copy-done.10
  16.5 0.1 copy.30
  16.7 0.7 fusion.106
  17.4 0.2 collective-permute-done.1
  17.6 0.9 fusion.56
  18.5 3.3 %collective-permute-start.3 = (bf16[512,128]{1,0:T(8,128)(2,1)}, bf16[512,128]{1,0:T(8,128)(2,1)}, u32[]{:S(2)}, u32[]{:S(2)}) collective-permute-start(bf16[512,128]{1,0:T(8,128)(2,1)} %get-tuple-element.28), channel_id=1, source_target_pairs={{0,1},{1,2},{2,3},{3,0},{4,5},{5,6},{6,7},{7,4},{8,9},{9,10},{10,1... | collective-permute-start | bytes 393224 | tf_op jit(solution)/shard_map/ppermute | solution.py:14
  21.8 1.6 %collective-permute-start.4 = (bf16[512,128]{1,0:T(8,128)(2,1)S(1)}, bf16[512,128]{1,0:T(8,128)(2,1)}, u32[]{:S(2)}, u32[]{:S(2)}) collective-permute-start(bf16[512,128]{1,0:T(8,128)(2,1)S(1)} %get-tuple-element.29), channel_id=1, source_target_pairs={{0,2},{1,3},{2,0},{3,1},{4,6},{5,7},{6,4},{7,5},{8,10},{9,11},{10,... | collective-permute-start | bytes 393224 | tf_op jit(solution)/shard_map/ppermute | solution.py:14
  23.4 0.7 collective-permute-start.5
  24.2 0.6 all-to-all-done
  24.8 0.4 fusion.6
  25.2 0.9 %copy.28 = bf16[8,64,512]{2,1,0:T(8,128)(2,1)} copy(bf16[8,64,512]{2,0,1:T(8,128)(2,1)S(1)} %fusion.6) | data formatting | bytes 1048576 | tf_op jit(solution)/shard_map/convert_element_type | solution.py:77
  26.2 3.5 %all-to-all-start.1 = ((bf16[8,64,512]{2,1,0:T(8,128)(2,1)}), bf16[8,64,512]{2,1,0:T(8,128)(2,1)S(1)}, u32[]{:S(2)}, u32[]{:S(2)}) async-start(bf16[8,64,512]{2,1,0:T(8,128)(2,1)} %copy.28), calls=%async_computation.1 | async-start | bytes 1048576 | tf_op jit(solution)/shard_map/all_to_all | solution.py:19
  29.7 0.1 fusion.77
  29.9 1.0 %constant_dynamic-update-slice_fusion.2 = bf16[512,512]{1,0:T(8,128)(2,1)S(1)} fusion(bf16[512,512]{1,0:T(8,128)(2,1)S(1)} %fusion.77, bf16[512,128]{1,0:T(8,128)(2,1)} %collective-permute-done.3, s32[]{:T(128)S(6)} %select_n.80), kind=kLoop, calls=%fused_computation.167 | loop fusion | bytes 262148 | tf_op jit(solution)/shard_map/dynamic_update_slice | solution.py:33
  30.9 1.1 %collective-permute-done.4 = bf16[512,128]{1,0:T(8,128)(2,1)} collective-permute-done((bf16[512,128]{1,0:T(8,128)(2,1)S(1)}, bf16[512,128]{1,0:T(8,128)(2,1)}, u32[]{:S(2)}, u32[]{:S(2)}) %collective-permute-start.4) | collective-permute-done | bytes 131104 | tf_op jit(solution)/shard_map/ppermute | solution.py:14
  32.0 0.9 %constant_dynamic-update-slice_fusion.1 = bf16[512,512]{1,0:T(8,128)(2,1)S(1)} fusion(bf16[512,512]{1,0:T(8,128)(2,1)S(1)} %constant_dynamic-update-slice_fusion.2, bf16[512,128]{1,0:T(8,128)(2,1)} %collective-permute-done.4, s32[]{:T(128)S(6)} %select_n.82), kind=kLoop, calls=%fused_computation.162 | loop fusion | bytes 262148 | tf_op jit(solution)/shard_map/dynamic_update_slice | solution.py:33
  33.0 0.9 %constant_dynamic-update-slice_fusion = bf16[512,512]{1,0:T(8,128)(2,1)S(1)} fusion(bf16[512,512]{1,0:T(8,128)(2,1)S(1)} %constant_dynamic-update-slice_fusion.1, bf16[512,128]{1,0:T(8,128)(2,1)} %collective-permute-done.5, s32[]{:T(128)S(6)} %select_n.84), kind=kLoop, calls=%fused_computation.157 | loop fusion | bytes 262148 | tf_op jit(solution)/shard_map/dynamic_update_slice | solution.py:33
  33.9 5.4 %all-to-all-done.1 = bf16[8,64,512]{2,1,0:T(8,128)(2,1)S(1)} async-done(((bf16[8,64,512]{2,1,0:T(8,128)(2,1)}), bf16[8,64,512]{2,1,0:T(8,128)(2,1)S(1)}, u32[]{:S(2)}, u32[]{:S(2)}) %all-to-all-start.1) | async-done | bytes 524320 | tf_op jit(solution)/shard_map/all_to_all | solution.py:19
  39.4 0.4 fusion.33
  39.8 1.1 %multiply_convert_fusion = (bf16[512,512]{1,0:T(8,128)(2,1)S(1)}, bf16[512,512]{1,0:T(8,128)(2,1)S(1)}) fusion(bf16[512,512]{1,0:T(8,128)(2,1)S(1)} %constant_dynamic-update-slice_fusion, bf16[512,512]{1,0:T(8,128)(2,1)S(1)} %fusion.33, bf16[1,512,512]{2,1,0:T(8,128)(2,1)S(1)} %copy-done), kind=kOutput, calls=%fused_computation.52 | convolution fusion | flops 274464768 | bytes 2621440 | tf_op jit(solution)/shard_map/dot_general | solution.py:81
  40.9 1.6 %fusion.24 = (bf16[512,512]{1,0:T(8,128)(2,1)}, bf16[512,512]{1,0:T(8,128)(2,1)}) fusion(bf16[512,512]{1,0:T(8,128)(2,1)S(1)} %copy-done.4, f32[512]{0:T(512)S(1)} %copy-done.11, bf16[512,512]{1,0:T(8,128)(2,1)S(1)} %get-tuple-element.23, bf16[1,512,512]{2,1,0:T(8,128)(2,1)S(1)} %copy-done, bf16[512,512]{1,0:T(8,128)(2,1)S(1)} %copy-done.1), kind=kOutput, calls=%fused_computation.41 | convolution fusion | flops 271319040 | bytes 3147776 | tf_op jit(solution)/shard_map/dot_general | solution.py:95
  42.5 3.5 %all-to-all-start.2 = ((bf16[8,64,512]{2,1,0:T(8,128)(2,1)}), bf16[8,64,512]{2,1,0:T(8,128)(2,1)S(1)}, u32[]{:S(2)}, u32[]{:S(2)}) async-start(bf16[8,64,512]{2,1,0:T(8,128)(2,1)} %bitcast.22), calls=%async_computation.2 | async-start | bytes 1048576 | tf_op jit(solution)/shard_map/all_to_all | solution.py:19
  46.0 0.1 constant_dynamic-slice_fusion.13
  46.1 1.0 %collective-permute-start.7 = (bf16[512,128]{1,0:T(8,128)(2,1)S(1)}, bf16[512,128]{1,0:T(8,128)(2,1)S(1)}, u32[]{:S(2)}, u32[]{:S(2)}) collective-permute-start(bf16[512,128]{1,0:T(8,128)(2,1)S(1)} %get-tuple-element.35), channel_id=1, source_target_pairs={{0,1},{1,2},{2,3},{3,0},{4,5},{5,6},{6,7},{7,4},{8,9},{9,10},{10,1... | collective-permute-start | bytes 393224 | tf_op jit(solution)/shard_map/ppermute | solution.py:14
  47.1 1.3 %collective-permute-start.8 = (bf16[512,128]{1,0:T(8,128)(2,1)S(1)}, bf16[512,128]{1,0:T(8,128)(2,1)S(1)}, u32[]{:S(2)}, u32[]{:S(2)}) collective-permute-start(bf16[512,128]{1,0:T(8,128)(2,1)S(1)} %get-tuple-element.34), channel_id=1, source_target_pairs={{0,2},{1,3},{2,0},{3,1},{4,6},{5,7},{6,4},{7,5},{8,10},{9,11},{10,... | collective-permute-start | bytes 393224 | tf_op jit(solution)/shard_map/ppermute | solution.py:14
  48.4 1.6 %collective-permute-start.9 = (bf16[512,128]{1,0:T(8,128)(2,1)S(1)}, bf16[512,128]{1,0:T(8,128)(2,1)}, u32[]{:S(2)}, u32[]{:S(2)}) collective-permute-start(bf16[512,128]{1,0:T(8,128)(2,1)S(1)} %get-tuple-element.33), channel_id=1, source_target_pairs={{0,3},{1,0},{2,1},{3,2},{4,7},{5,4},{6,5},{7,6},{8,11},{9,8},{10,9... | collective-permute-start | bytes 393224 | tf_op jit(solution)/shard_map/ppermute | solution.py:14
  50.0 1.3 %fusion.113 = bf16[512,512]{1,0:T(8,128)(2,1)} fusion(bf16[512,512]{1,0:T(8,128)(2,1)S(1)} %fusion.33, bf16[512,512]{1,0:T(8,128)(2,1)S(1)} %copy-done.28), kind=kOutput, calls=%fused_computation.213 | convolution fusion | flops 268435456 | bytes 1572864 | tf_op jit(solution)/shard_map/dot_general | solution.py:97
  51.3 4.4 %all-to-all-done.2 = bf16[8,64,512]{2,1,0:T(8,128)(2,1)S(1)} async-done(((bf16[8,64,512]{2,1,0:T(8,128)(2,1)}), bf16[8,64,512]{2,1,0:T(8,128)(2,1)S(1)}, u32[]{:S(2)}, u32[]{:S(2)}) %all-to-all-start.2) | async-done | bytes 524320 | tf_op jit(solution)/shard_map/all_to_all | solution.py:19
  55.7 0.4 fusion.7
  56.1 0.9 %copy.31 = bf16[8,64,512]{2,1,0:T(8,128)(2,1)} copy(bf16[8,64,512]{2,0,1:T(8,128)(2,1)S(1)} %fusion.7) | data formatting | bytes 1048576 | tf_op jit(solution)/shard_map/convert_element_type | solution.py:104
  57.1 3.5 %all-to-all-start.3 = ((bf16[8,64,512]{2,1,0:T(8,128)(2,1)}), bf16[8,64,512]{2,1,0:T(8,128)(2,1)S(1)}, u32[]{:S(2)}, u32[]{:S(2)}) async-start(bf16[8,64,512]{2,1,0:T(8,128)(2,1)} %copy.31), calls=%async_computation.3 | async-start | bytes 1048576 | tf_op jit(solution)/shard_map/all_to_all | solution.py:19
  60.7 0.6 copy-done.12
  61.3 1.8 %fusion.72 = (bf16[512,128]{1,0:T(8,128)(2,1)}, bf16[512,128]{1,0:T(8,128)(2,1)}, bf16[512,128]{1,0:T(8,128)(2,1)}) fusion(bf16[512,128]{1,0:T(8,128)(2,1)S(1)} %collective-permute-done.7, bf16[512,128]{1,0:T(8,128)(2,1)S(1)} %collective-permute-done.8, bf16[512,128]{1,0:T(8,128)(2,1)} %collective-permute-done.9, f32[128]{0:T(128)S(1)} %get-tuple-element.40, ...), kind=kLoop, calls=%fused_computation.123 | loop fusion | flops 1835008 | bytes 923652 | tf_op jit(solution)/shard_map/convert_element_type | solution.py:89
  63.2 2.0 %collective-permute-start.10 = (bf16[512,128]{1,0:T(8,128)(2,1)}, bf16[512,128]{1,0:T(8,128)(2,1)}, u32[]{:S(2)}, u32[]{:S(2)}) collective-permute-start(bf16[512,128]{1,0:T(8,128)(2,1)} %get-tuple-element.25), channel_id=1, source_target_pairs={{0,1},{1,2},{2,3},{3,0},{4,5},{5,6},{6,7},{7,4},{8,9},{9,10},{10,1... | collective-permute-start | bytes 393224 | tf_op jit(solution)/shard_map/ppermute | solution.py:14
  65.2 0.3 collective-permute-start.11
  65.4 2.1 %collective-permute-start.12 = (bf16[512,128]{1,0:T(8,128)(2,1)}, bf16[512,128]{1,0:T(8,128)(2,1)}, u32[]{:S(2)}, u32[]{:S(2)}) collective-permute-start(bf16[512,128]{1,0:T(8,128)(2,1)} %get-tuple-element.24), channel_id=1, source_target_pairs={{0,3},{1,0},{2,1},{3,2},{4,7},{5,4},{6,5},{7,6},{8,11},{9,8},{10,9... | collective-permute-start | bytes 393224 | tf_op jit(solution)/shard_map/ppermute | solution.py:14
  67.6 1.7 %fusion.60 = bf16[512,128]{1,0:T(8,128)(2,1)} fusion(bf16[512,128]{1,0:T(8,128)(2,1)S(1)} %collective-permute-done.7, bf16[512,128]{1,0:T(8,128)(2,1)S(1)} %collective-permute-done.8, bf16[512,128]{1,0:T(8,128)(2,1)} %collective-permute-done.9, f32[128]{0:T(128)S(1)} %copy-done.22, f32[128]{0:T(128)S(1)} %copy-done.23, f32[128]{0:T(128)S(1)} %copy-done.24, ...), kind=kLoop, calls=%fused_computation.111 | loop fusion | flops 786432 | bytes 657412 | tf_op jit(solution)/shard_map/convert_element_type | solution.py:89
  69.2 1.0 %all-to-all-done.3 = bf16[8,64,512]{2,1,0:T(8,128)(2,1)S(1)} async-done(((bf16[8,64,512]{2,1,0:T(8,128)(2,1)}), bf16[8,64,512]{2,1,0:T(8,128)(2,1)S(1)}, u32[]{:S(2)}, u32[]{:S(2)}) %all-to-all-start.3) | async-done | bytes 524320 | tf_op jit(solution)/shard_map/all_to_all | solution.py:19
  70.3 0.6 fusion.110
  70.9 0.2 copy-done.6
  71.1 0.7 dynamic-slice_convert_fusion.1
  71.8 1.0 %collective-permute-start.6 = (bf16[128,512]{1,0:T(8,128)(2,1)}, bf16[128,512]{1,0:T(8,128)(2,1)S(1)}, u32[]{:S(2)}, u32[]{:S(2)}) collective-permute-start(bf16[128,512]{1,0:T(8,128)(2,1)} %get-tuple-element.32), channel_id=1, source_target_pairs={{0,1},{1,2},{2,3},{3,0},{4,5},{5,6},{6,7},{7,4},{8,9},{9,10},{10,1... | collective-permute-start | bytes 393224 | tf_op jit(solution)/shard_map/ppermute | solution.py:14
  72.7 1.3 %collective-permute-start.13 = (bf16[128,512]{1,0:T(8,128)(2,1)S(1)}, bf16[128,512]{1,0:T(8,128)(2,1)}, u32[]{:S(2)}, u32[]{:S(2)}) collective-permute-start(bf16[128,512]{1,0:T(8,128)(2,1)S(1)} %get-tuple-element.30), channel_id=1, source_target_pairs={{0,2},{1,3},{2,0},{3,1},{4,6},{5,7},{6,4},{7,5},{8,10},{9,11},{10,... | collective-permute-start | bytes 393224 | tf_op jit(solution)/shard_map/ppermute | solution.py:14
  74.0 3.6 %all-to-all-start.4 = ((bf16[8,64,512]{2,1,0:T(8,128)(2,1)}), bf16[8,64,512]{2,1,0:T(8,128)(2,1)S(1)}, u32[]{:S(2)}, u32[]{:S(2)}) async-start(bf16[8,64,512]{2,1,0:T(8,128)(2,1)} %bitcast.42), calls=%async_computation.4 | async-start | bytes 1048576 | tf_op jit(solution)/shard_map/all_to_all | solution.py:19
  77.7 3.2 %fusion.3 = bf16[512,512]{1,0:T(8,128)(2,1)} fusion(bf16[512,512]{1,0:T(8,128)(2,1)S(1)} %bitcast.112, bf16[512,512]{1,0:T(8,128)(2,1)} %get-tuple-element.71, bf16[512,512]{1,0:T(8,128)(2,1)S(1)} %copy-done.5, bf16[512,512]{1,0:T(8,128)(2,1)S(1)} %bitcast.110, bf16[1,512,512]{2,1,0:T(8,128)(2,1)} %param.11, f32[512]{0:T(512)S(1)} %copy-done.11, ...), kind=kOutput, calls=%fused_computation.20 | convolution fusion | flops 274726912 | bytes 3149824 | tf_op jit(solution)/shard_map/dot_general | solution.py:129
  80.9 1.7 %collective-permute-start.14 = (bf16[128,512]{1,0:T(8,128)(2,1)S(1)}, bf16[128,512]{1,0:T(8,128)(2,1)S(1)}, u32[]{:S(2)}, u32[]{:S(2)}) collective-permute-start(bf16[128,512]{1,0:T(8,128)(2,1)S(1)} %get-tuple-element.31), channel_id=1, source_target_pairs={{0,3},{1,0},{2,1},{3,2},{4,7},{5,4},{6,5},{7,6},{8,11},{9,8},{10,9... | collective-permute-start | bytes 393224 | tf_op jit(solution)/shard_map/ppermute | solution.py:14
  82.6 0.9 %convert_add_fusion.2 = f32[128,512]{1,0:T(8,128)S(1)} fusion(bf16[128,512]{1,0:T(8,128)(2,1)S(1)} %collective-permute-done.6, bf16[512,512]{1,0:T(8,128)(2,1)} %copy-done.8, s32[]{:T(128)S(6)} %select_n.64), kind=kLoop, calls=%fused_computation.127 | loop fusion | flops 196608 | bytes 524292 | tf_op jit(solution)/shard_map/add | solution.py:115
  83.6 0.9 copy-done.9
  84.5 1.0 %fusion.74 = bf16[512,512]{1,0:T(8,128)(2,1)S(1)} fusion(bf16[512,512]{1,0:T(8,128)(2,1)S(1)} %fusion.73, s32[]{:T(128)S(6)} %select_n.80, bf16[512,128]{1,0:T(8,128)(2,1)} %collective-permute-done.10, bf16[512,512]{1,0:T(8,128)(2,1)S(1)} %fusion.33), kind=kLoop, calls=%fused_computation.135 | loop fusion | flops 262144 | bytes 393220 | tf_op jit(solution)/shard_map/dynamic_update_slice | solution.py:33
  85.5 1.0 %fusion.75 = bf16[512,512]{1,0:T(8,128)(2,1)S(1)} fusion(bf16[512,512]{1,0:T(8,128)(2,1)S(1)} %fusion.74, s32[]{:T(128)S(6)} %select_n.82, bf16[512,128]{1,0:T(8,128)(2,1)} %collective-permute-done.11, bf16[512,512]{1,0:T(8,128)(2,1)S(1)} %fusion.33), kind=kLoop, calls=%fused_computation.136 | loop fusion | flops 262144 | bytes 393220 | tf_op jit(solution)/shard_map/dynamic_update_slice | solution.py:33
  86.5 1.0 %fusion.76 = bf16[512,512]{1,0:T(8,128)(2,1)S(1)} fusion(bf16[512,512]{1,0:T(8,128)(2,1)S(1)} %fusion.75, s32[]{:T(128)S(6)} %select_n.84, bf16[512,128]{1,0:T(8,128)(2,1)} %collective-permute-done.12, bf16[512,512]{1,0:T(8,128)(2,1)S(1)} %fusion.33), kind=kLoop, calls=%fused_computation.137 | loop fusion | flops 262144 | bytes 393220 | tf_op jit(solution)/shard_map/dynamic_update_slice | solution.py:33
  87.5 0.7 collective-permute-done.13
  88.1 1.8 %collective-permute-done.14 = bf16[128,512]{1,0:T(8,128)(2,1)S(1)} collective-permute-done((bf16[128,512]{1,0:T(8,128)(2,1)S(1)}, bf16[128,512]{1,0:T(8,128)(2,1)S(1)}, u32[]{:S(2)}, u32[]{:S(2)}) %collective-permute-start.14) | collective-permute-done | bytes 131104 | tf_op jit(solution)/shard_map/ppermute | solution.py:14
  89.9 1.7 %add_bitcast_fusion = f32[1,128,512]{2,1,0:T(8,128)} fusion(bf16[128,512]{1,0:T(8,128)(2,1)S(1)} %collective-permute-done.14, f32[128,512]{1,0:T(8,128)S(1)} %convert_add_fusion.2, bf16[128,512]{1,0:T(8,128)(2,1)} %collective-permute-done.13), kind=kLoop, calls=%fused_computation.124 | loop fusion | flops 262144 | bytes 786432 | tf_op jit(solution)/shard_map/broadcast_in_dim | solution.py:117
  91.5 0.7 convert_reduce_fusion
  (68 shorter events, 0.3 us)
Async XLA Ops:
  0.6 39.1 %copy-start = (bf16[1,512,512]{2,1,0:T(8,128)(2,1)S(1)}, bf16[1,512,512]{2,1,0:T(8,128)(2,1)}, u32[]{:S(2)}) copy-start(bf16[1,512,512]{2,1,0:T(8,128)(2,1)} %param.13) | copy-start | bytes 1572868
  0.7 0.7 copy-start.25
  1.4 1.8 %copy-start.1 = (bf16[512,512]{1,0:T(8,128)(2,1)S(1)}, bf16[512,512]{1,0:T(8,128)(2,1)}, u32[]{:S(2)}) copy-start(bf16[512,512]{1,0:T(8,128)(2,1)} %param.15) | copy-start | bytes 1572868
  3.3 14.1 %collective-permute-start = (bf16[512,128]{1,0:T(8,128)(2,1)S(1)}, bf16[512,128]{1,0:T(8,128)(2,1)S(1)}, u32[]{:S(2)}, u32[]{:S(2)}) collective-permute-start(bf16[512,128]{1,0:T(8,128)(2,1)S(1)} %get-tuple-element.36), channel_id=1, source_target_pairs={{0,1},{1,2},{2,3},{3,0},{4,5},{5,6},{6,7},{7,4},{8,9},{9,10},{10,1... | collective-permute-start | bytes 393224 | tf_op jit(solution)/shard_map/ppermute | solution.py:14
  6.4 11.2 %collective-permute-start.1 = (bf16[512,128]{1,0:T(8,128)(2,1)S(1)}, bf16[512,128]{1,0:T(8,128)(2,1)S(1)}, u32[]{:S(2)}, u32[]{:S(2)}) collective-permute-start(bf16[512,128]{1,0:T(8,128)(2,1)S(1)} %get-tuple-element.38), channel_id=1, source_target_pairs={{0,2},{1,3},{2,0},{3,1},{4,6},{5,7},{6,4},{7,5},{8,10},{9,11},{10,... | collective-permute-start | bytes 393224 | tf_op jit(solution)/shard_map/ppermute | solution.py:14
  9.0 8.6 %collective-permute-start.2 = (bf16[512,128]{1,0:T(8,128)(2,1)S(1)}, bf16[512,128]{1,0:T(8,128)(2,1)S(1)}, u32[]{:S(2)}, u32[]{:S(2)}) collective-permute-start(bf16[512,128]{1,0:T(8,128)(2,1)S(1)} %get-tuple-element.37), channel_id=1, source_target_pairs={{0,3},{1,0},{2,1},{3,2},{4,7},{5,4},{6,5},{7,6},{8,11},{9,8},{10,9... | collective-permute-start | bytes 393224 | tf_op jit(solution)/shard_map/ppermute | solution.py:14
  11.3 13.5 %all-to-all-start = ((bf16[8,64,512]{2,1,0:T(8,128)(2,1)}), bf16[8,64,512]{2,1,0:T(8,128)(2,1)S(1)}, u32[]{:S(2)}, u32[]{:S(2)}) async-start(bf16[8,64,512]{2,1,0:T(8,128)(2,1)} %bitcast.2), calls=%async_computation | async-start | bytes 1048576 | tf_op jit(solution)/shard_map/all_to_all | solution.py:19
  15.7 0.7 copy-start.10
  18.5 11.4 %collective-permute-start.3 = (bf16[512,128]{1,0:T(8,128)(2,1)}, bf16[512,128]{1,0:T(8,128)(2,1)}, u32[]{:S(2)}, u32[]{:S(2)}) collective-permute-start(bf16[512,128]{1,0:T(8,128)(2,1)} %get-tuple-element.28), channel_id=1, source_target_pairs={{0,1},{1,2},{2,3},{3,0},{4,5},{5,6},{6,7},{7,4},{8,9},{9,10},{10,1... | collective-permute-start | bytes 393224 | tf_op jit(solution)/shard_map/ppermute | solution.py:14
  21.8 10.2 %collective-permute-start.4 = (bf16[512,128]{1,0:T(8,128)(2,1)S(1)}, bf16[512,128]{1,0:T(8,128)(2,1)}, u32[]{:S(2)}, u32[]{:S(2)}) collective-permute-start(bf16[512,128]{1,0:T(8,128)(2,1)S(1)} %get-tuple-element.29), channel_id=1, source_target_pairs={{0,2},{1,3},{2,0},{3,1},{4,6},{5,7},{6,4},{7,5},{8,10},{9,11},{10,... | collective-permute-start | bytes 393224 | tf_op jit(solution)/shard_map/ppermute | solution.py:14
  23.4 9.6 %collective-permute-start.5 = (bf16[512,128]{1,0:T(8,128)(2,1)S(1)}, bf16[512,128]{1,0:T(8,128)(2,1)}, u32[]{:S(2)}, u32[]{:S(2)}) collective-permute-start(bf16[512,128]{1,0:T(8,128)(2,1)S(1)} %get-tuple-element.27), channel_id=1, source_target_pairs={{0,3},{1,0},{2,1},{3,2},{4,7},{5,4},{6,5},{7,6},{8,11},{9,8},{10,9... | collective-permute-start | bytes 393224 | tf_op jit(solution)/shard_map/ppermute | solution.py:14
  26.2 13.2 %all-to-all-start.1 = ((bf16[8,64,512]{2,1,0:T(8,128)(2,1)}), bf16[8,64,512]{2,1,0:T(8,128)(2,1)S(1)}, u32[]{:S(2)}, u32[]{:S(2)}) async-start(bf16[8,64,512]{2,1,0:T(8,128)(2,1)} %copy.28), calls=%async_computation.1 | async-start | bytes 1048576 | tf_op jit(solution)/shard_map/all_to_all | solution.py:19
  29.9 9.5 %copy-start.3 = (bf16[512,512]{1,0:T(8,128)(2,1)S(1)}, bf16[512,512]{1,0:T(8,128)(2,1)}, u32[]{:S(2)}) copy-start(bf16[512,512]{1,0:T(8,128)(2,1)} %param.8) | copy-start | bytes 1572868
  33.0 6.4 %copy-start.11 = (f32[512]{0:T(512)S(1)}, f32[512]{0:T(512)}, u32[]{:S(2)}) copy-start(f32[512]{0:T(512)} %param.10) | copy-start | bytes 6148
  39.8 1.2 %copy-start.4 = (bf16[512,512]{1,0:T(8,128)(2,1)S(1)}, bf16[512,512]{1,0:T(8,128)(2,1)}, u32[]{:S(2)}) copy-start(bf16[512,512]{1,0:T(8,128)(2,1)} %param.8) | copy-start | bytes 1572868
  40.9 1.6 %copy-start.27 = (bf16[512,512]{1,0:T(8,128)(2,1)}, bf16[512,512]{1,0:T(8,128)(2,1)S(1)}, u32[]{:S(2)}) copy-start(bf16[512,512]{1,0:T(8,128)(2,1)S(1)} %get-tuple-element.23) | copy-start | bytes 1572868
  42.5 13.2 %all-to-all-start.2 = ((bf16[8,64,512]{2,1,0:T(8,128)(2,1)}), bf16[8,64,512]{2,1,0:T(8,128)(2,1)S(1)}, u32[]{:S(2)}, u32[]{:S(2)}) async-start(bf16[8,64,512]{2,1,0:T(8,128)(2,1)} %bitcast.22), calls=%async_computation.2 | async-start | bytes 1048576 | tf_op jit(solution)/shard_map/all_to_all | solution.py:19
  46.0 4.0 %copy-start.28 = (bf16[512,512]{1,0:T(8,128)(2,1)S(1)}, bf16[512,512]{1,0:T(8,128)(2,1)}, u32[]{:S(2)}) copy-start(bf16[512,512]{1,0:T(8,128)(2,1)} %copy-done.27) | copy-start | bytes 1572868
  46.1 14.5 %collective-permute-start.7 = (bf16[512,128]{1,0:T(8,128)(2,1)S(1)}, bf16[512,128]{1,0:T(8,128)(2,1)S(1)}, u32[]{:S(2)}, u32[]{:S(2)}) collective-permute-start(bf16[512,128]{1,0:T(8,128)(2,1)S(1)} %get-tuple-element.35), channel_id=1, source_target_pairs={{0,1},{1,2},{2,3},{3,0},{4,5},{5,6},{6,7},{7,4},{8,9},{9,10},{10,1... | collective-permute-start | bytes 393224 | tf_op jit(solution)/shard_map/ppermute | solution.py:14
  47.1 13.5 %collective-permute-start.8 = (bf16[512,128]{1,0:T(8,128)(2,1)S(1)}, bf16[512,128]{1,0:T(8,128)(2,1)S(1)}, u32[]{:S(2)}, u32[]{:S(2)}) collective-permute-start(bf16[512,128]{1,0:T(8,128)(2,1)S(1)} %get-tuple-element.34), channel_id=1, source_target_pairs={{0,2},{1,3},{2,0},{3,1},{4,6},{5,7},{6,4},{7,5},{8,10},{9,11},{10,... | collective-permute-start | bytes 393224 | tf_op jit(solution)/shard_map/ppermute | solution.py:14
  48.4 12.2 %collective-permute-start.9 = (bf16[512,128]{1,0:T(8,128)(2,1)S(1)}, bf16[512,128]{1,0:T(8,128)(2,1)}, u32[]{:S(2)}, u32[]{:S(2)}) collective-permute-start(bf16[512,128]{1,0:T(8,128)(2,1)S(1)} %get-tuple-element.33), channel_id=1, source_target_pairs={{0,3},{1,0},{2,1},{3,2},{4,7},{5,4},{6,5},{7,6},{8,11},{9,8},{10,9... | collective-permute-start | bytes 393224 | tf_op jit(solution)/shard_map/ppermute | solution.py:14
  57.0 3.6 %copy-start.15 = (f32[128]{0:T(128)S(1)}, f32[128]{0:T(128)}, u32[]{:S(2)}) copy-start(f32[128]{0:T(128)} %get-tuple-element.44) | copy-start | bytes 1540
  57.0 3.6 %copy-start.16 = (f32[128]{0:T(128)S(1)}, f32[128]{0:T(128)}, u32[]{:S(2)}) copy-start(f32[128]{0:T(128)} %get-tuple-element.45) | copy-start | bytes 1540
  57.0 3.6 %copy-start.17 = (f32[128]{0:T(128)S(1)}, f32[128]{0:T(128)}, u32[]{:S(2)}) copy-start(f32[128]{0:T(128)} %get-tuple-element.46) | copy-start | bytes 1540
  57.0 3.6 %copy-start.18 = (f32[128]{0:T(128)S(1)}, f32[128]{0:T(128)}, u32[]{:S(2)}) copy-start(f32[128]{0:T(128)} %get-tuple-element.47) | copy-start | bytes 1540
  57.1 3.6 %copy-start.19 = (f32[128]{0:T(128)S(1)}, f32[128]{0:T(128)}, u32[]{:S(2)}) copy-start(f32[128]{0:T(128)} %get-tuple-element.48) | copy-start | bytes 1540
  57.1 3.6 %copy-start.20 = (f32[128]{0:T(128)S(1)}, f32[128]{0:T(128)}, u32[]{:S(2)}) copy-start(f32[128]{0:T(128)} %get-tuple-element.49) | copy-start | bytes 1540
  57.1 3.6 %copy-start.21 = (f32[128]{0:T(128)S(1)}, f32[128]{0:T(128)}, u32[]{:S(2)}) copy-start(f32[128]{0:T(128)} %get-tuple-element.50) | copy-start | bytes 1540
  57.1 13.2 %all-to-all-start.3 = ((bf16[8,64,512]{2,1,0:T(8,128)(2,1)}), bf16[8,64,512]{2,1,0:T(8,128)(2,1)S(1)}, u32[]{:S(2)}, u32[]{:S(2)}) async-start(bf16[8,64,512]{2,1,0:T(8,128)(2,1)} %copy.31), calls=%async_computation.3 | async-start | bytes 1048576 | tf_op jit(solution)/shard_map/all_to_all | solution.py:19
  60.6 0.7 copy-start.12
  60.6 0.7 copy-start.13
  60.7 0.7 copy-start.14
  61.3 6.2 %copy-start.22 = (f32[128]{0:T(128)S(1)}, f32[128]{0:T(128)}, u32[]{:S(2)}) copy-start(f32[128]{0:T(128)} %get-tuple-element.51) | copy-start | bytes 1540
  61.3 6.2 %copy-start.23 = (f32[128]{0:T(128)S(1)}, f32[128]{0:T(128)}, u32[]{:S(2)}) copy-start(f32[128]{0:T(128)} %get-tuple-element.52) | copy-start | bytes 1540
  61.3 6.2 %copy-start.24 = (f32[128]{0:T(128)S(1)}, f32[128]{0:T(128)}, u32[]{:S(2)}) copy-start(f32[128]{0:T(128)} %get-tuple-element.53) | copy-start | bytes 1540
  63.2 7.1 %copy-start.5 = (bf16[512,512]{1,0:T(8,128)(2,1)S(1)}, bf16[512,512]{1,0:T(8,128)(2,1)}, u32[]{:S(2)}) copy-start(bf16[512,512]{1,0:T(8,128)(2,1)} %param.8) | copy-start | bytes 1572868
  63.2 17.7 %collective-permute-start.10 = (bf16[512,128]{1,0:T(8,128)(2,1)}, bf16[512,128]{1,0:T(8,128)(2,1)}, u32[]{:S(2)}, u32[]{:S(2)}) collective-permute-start(bf16[512,128]{1,0:T(8,128)(2,1)} %get-tuple-element.25), channel_id=1, source_target_pairs={{0,1},{1,2},{2,3},{3,0},{4,5},{5,6},{6,7},{7,4},{8,9},{9,10},{10,1... | collective-permute-start | bytes 393224 | tf_op jit(solution)/shard_map/ppermute | solution.py:14
  65.2 17.4 %collective-permute-start.11 = (bf16[512,128]{1,0:T(8,128)(2,1)}, bf16[512,128]{1,0:T(8,128)(2,1)}, u32[]{:S(2)}, u32[]{:S(2)}) collective-permute-start(bf16[512,128]{1,0:T(8,128)(2,1)} %get-tuple-element.26), channel_id=1, source_target_pairs={{0,2},{1,3},{2,0},{3,1},{4,6},{5,7},{6,4},{7,5},{8,10},{9,11},{10,... | collective-permute-start | bytes 393224 | tf_op jit(solution)/shard_map/ppermute | solution.py:14
  65.4 17.2 %collective-permute-start.12 = (bf16[512,128]{1,0:T(8,128)(2,1)}, bf16[512,128]{1,0:T(8,128)(2,1)}, u32[]{:S(2)}, u32[]{:S(2)}) collective-permute-start(bf16[512,128]{1,0:T(8,128)(2,1)} %get-tuple-element.24), channel_id=1, source_target_pairs={{0,3},{1,0},{2,1},{3,2},{4,7},{5,4},{6,5},{7,6},{8,11},{9,8},{10,9... | collective-permute-start | bytes 393224 | tf_op jit(solution)/shard_map/ppermute | solution.py:14
  67.6 2.7 %copy-start.26 = (f32[512]{0:T(512)S(1)}, f32[512]{0:T(512)}, u32[]{:S(2)}) copy-start(f32[512]{0:T(512)} %param.9) | copy-start | bytes 6148
  70.3 0.8 copy-start.6
  71.1 3.0 %copy-start.8 = (bf16[512,512]{1,0:T(8,128)(2,1)}, bf16[512,512]{1,0:T(8,128)(2,1)S(1)}, u32[]{:S(2)}) copy-start(bf16[512,512]{1,0:T(8,128)(2,1)S(1)} %fusion.110) | copy-start | bytes 1572868
  71.8 10.8 %collective-permute-start.6 = (bf16[128,512]{1,0:T(8,128)(2,1)}, bf16[128,512]{1,0:T(8,128)(2,1)S(1)}, u32[]{:S(2)}, u32[]{:S(2)}) collective-permute-start(bf16[128,512]{1,0:T(8,128)(2,1)} %get-tuple-element.32), channel_id=1, source_target_pairs={{0,1},{1,2},{2,3},{3,0},{4,5},{5,6},{6,7},{7,4},{8,9},{9,10},{10,1... | collective-permute-start | bytes 393224 | tf_op jit(solution)/shard_map/ppermute | solution.py:14
  72.7 15.4 %collective-permute-start.13 = (bf16[128,512]{1,0:T(8,128)(2,1)S(1)}, bf16[128,512]{1,0:T(8,128)(2,1)}, u32[]{:S(2)}, u32[]{:S(2)}) collective-permute-start(bf16[128,512]{1,0:T(8,128)(2,1)S(1)} %get-tuple-element.30), channel_id=1, source_target_pairs={{0,2},{1,3},{2,0},{3,1},{4,6},{5,7},{6,4},{7,5},{8,10},{9,11},{10,... | collective-permute-start | bytes 393224 | tf_op jit(solution)/shard_map/ppermute | solution.py:14
  74.0 3.6 %copy-start.7 = (bf16[8,64,512]{2,1,0:T(8,128)(2,1)S(1)}, bf16[8,64,512]{2,1,0:T(8,128)(2,1)}, u32[]{:S(2)}) copy-start(bf16[8,64,512]{2,1,0:T(8,128)(2,1)} %copy-done.6) | copy-start | bytes 1572868
  74.0 17.5 %all-to-all-start.4 = ((bf16[8,64,512]{2,1,0:T(8,128)(2,1)}), bf16[8,64,512]{2,1,0:T(8,128)(2,1)S(1)}, u32[]{:S(2)}, u32[]{:S(2)}) async-start(bf16[8,64,512]{2,1,0:T(8,128)(2,1)} %bitcast.42), calls=%async_computation.4 | async-start | bytes 1048576 | tf_op jit(solution)/shard_map/all_to_all | solution.py:19
  80.9 9.0 %collective-permute-start.14 = (bf16[128,512]{1,0:T(8,128)(2,1)S(1)}, bf16[128,512]{1,0:T(8,128)(2,1)S(1)}, u32[]{:S(2)}, u32[]{:S(2)}) collective-permute-start(bf16[128,512]{1,0:T(8,128)(2,1)S(1)} %get-tuple-element.31), channel_id=1, source_target_pairs={{0,3},{1,0},{2,1},{3,2},{4,7},{5,4},{6,5},{7,6},{8,11},{9,8},{10,9... | collective-permute-start | bytes 393224 | tf_op jit(solution)/shard_map/ppermute | solution.py:14
  83.6 0.9 copy-start.9
  87.4 4.8 %copy-start.2 = (bf16[512,512]{1,0:T(8,128)(2,1)}, bf16[512,512]{1,0:T(8,128)(2,1)S(1)}, u32[]{:S(2)}) copy-start(bf16[512,512]{1,0:T(8,128)(2,1)S(1)} %fusion.76) | copy-start | bytes 1572868

commit v16 on v6

--- a/solution.py
+++ b/solution.py
@@ -59,8 +59,7 @@
     mixed_first = jnp.dot(first_blocks[0], gated, preferred_element_type=F32).astype(BF16)
 
     upstream = cotangent
-    upstream_late, mixed_first = lax.optimization_barrier((upstream, mixed_first))
-    cot_arrived = exchange([lane_chunk(upstream_late, t, kq) for t in chunk_of], "ch")
+    cot_arrived = exchange([lane_chunk(upstream, t, kq) for t in chunk_of], "ch")
     act_grad_out = [
         sum(
             cot_arrived[k].astype(F32) * coefficient(chunk_of[p], origin_of[k])

time: 93.2 us -> 92.8 us (level)
  waiting for transfers between devices: 17.1 us -> 19.2 us
  other arithmetic: 11.1 us -> 9.31 us
  starting transfers between devices: 42.7 us -> 41.1 us
    all_to_all x5, waiting for transfers between devices: 11.5 us -> 15 us  [swap(): return lax.all_to_all(pieces, axis_name, 0, 0, tiled=True)]
    ppermute x15, starting transfers between devices: 24.9 us -> 23.1 us  [exchange(): lax.ppermute(pieces[k], axis_name, [(i, (i + k) % n) for i in range(n)])]
    convert_element_type x2, other arithmetic: 3.51 us -> 1.72 us  [on_device(): added_out = [sum((act_arrived[k].astype(F32) * coefficient(origin_of[k],...]
    ppermute x15, waiting for transfers between devices: 5.63 us -> 4.22 us  [exchange(): lax.ppermute(pieces[k], axis_name, [(i, (i + k) % n) for i in range(n)])]
    dynamic_slice x2, local copies, waits for them, and re-layouts: 0.16 us -> 1.25 us  [lane_chunk(): return lax.dynamic_slice_in_dim(x, index * size, size, axis=1)]
    optimization_barrier x1 -> x0, local copies, waits for them, and re-layouts: 1 us -> none  [on_device(): lax.optimization_barrier((upstream, mixed_first))]
    unnamed x59 -> x69, local copies, waits for them, and re-layouts: 2.49 us -> 2.63 us
  transfers between devices with their start and end apart: 20 -> 20, of which waited for: 8 -> 7; matrix products, arithmetic and copies ran while one was open for 25% -> 25% of each run, Pallas kernels for 0% -> 0%
where the time goes in v16:
time: 92.8 us; the launch traced here: 92 us
  starting transfers between devices  41.1 us (44%)
  waiting for transfers between devices  19.2 us (21%)
  matrix products  11 us (12%)
  local copies, waits for them, and re-layouts  10.2 us (11%)
  other arithmetic  9.31 us (10%)
  between operations  1.21 us (1%)
    ppermute x15, starting transfers between devices, exchange(): lax.ppermute(pieces[k], axis_name, [(i, (i + k) % n) for i in range(n)])  23.1 us
    all_to_all x5, starting transfers between devices, swap(): return lax.all_to_all(pieces, axis_name, 0, 0, tiled=True)  18 us
    all_to_all x5, waiting for transfers between devices, swap(): return lax.all_to_all(pieces, axis_name, 0, 0, tiled=True)  15 us
    ppermute x15, waiting for transfers between devices, exchange(): lax.ppermute(pieces[k], axis_name, [(i, (i + k) % n) for i in range(n)])  4.22 us
    dot_general x1, matrix products, on_device(): spread = jnp.dot(first_blocks[0].T, first_grad, preferred_element_type=F32)  3.19 us
    dynamic_update_slice x5, other arithmetic, place_chunks(): out = lax.dynamic_update_slice_in_dim(out, chunk, start, axis=1)  3.11 us
    dynamic_update_slice x3, local copies, waits for them, and re-layouts, place_chunks(): out = lax.dynamic_update_slice_in_dim(out, chunk, start, axis=1)  2.82 us
    unnamed x69, local copies, waits for them, and re-layouts  2.63 us
  transfers between devices with their start and end apart: 20, of which 7 were waited for; matrix products, arithmetic and copies ran while one was open for 25% of the time, Pallas kernels for 0%

profile of v16, /device:TPU:0, one launch (start us, length us, event | category | flops | bytes accessed | tf_op | source)
XLA Modules:
  0.0 92.0 jit_solution(8623398323372133003)
XLA Ops:
  0.6 0.0 copy-start
  0.7 1.2 %constant_dynamic-slice_fusion.35 = (bf16[512,128]{1,0:T(8,128)(2,1)S(1)}, bf16[512,128]{1,0:T(8,128)(2,1)S(1)}, bf16[512,128]{1,0:T(8,128)(2,1)S(1)}) fusion(bf16[512,512]{1,0:T(8,128)(2,1)} %param.15, s32[]{:T(128)S(6)} %select_n.68, s32[]{:T(128)S(6)} %select_n.76, s32[]{:T(128)S(6)} %select_n.72), kind=kLoop, calls=%fused_computation.175 | loop fusion | bytes 786444 | tf_op jit(solution)/shard_map/dynamic_slice | solution.py:27
  1.9 3.1 %collective-permute-start = (bf16[512,128]{1,0:T(8,128)(2,1)S(1)}, bf16[512,128]{1,0:T(8,128)(2,1)S(1)}, u32[]{:S(2)}, u32[]{:S(2)}) collective-permute-start(bf16[512,128]{1,0:T(8,128)(2,1)S(1)} %get-tuple-element.32), channel_id=1, source_target_pairs={{0,1},{1,2},{2,3},{3,0},{4,5},{5,6},{6,7},{7,4},{8,9},{9,10},{10,1... | collective-permute-start | bytes 393224 | tf_op jit(solution)/shard_map/ppermute | solution.py:14
  5.0 2.6 %collective-permute-start.1 = (bf16[512,128]{1,0:T(8,128)(2,1)S(1)}, bf16[512,128]{1,0:T(8,128)(2,1)S(1)}, u32[]{:S(2)}, u32[]{:S(2)}) collective-permute-start(bf16[512,128]{1,0:T(8,128)(2,1)S(1)} %get-tuple-element.34), channel_id=1, source_target_pairs={{0,2},{1,3},{2,0},{3,1},{4,6},{5,7},{6,4},{7,5},{8,10},{9,11},{10,... | collective-permute-start | bytes 393224 | tf_op jit(solution)/shard_map/ppermute | solution.py:14
  7.6 1.3 %collective-permute-start.2 = (bf16[512,128]{1,0:T(8,128)(2,1)S(1)}, bf16[512,128]{1,0:T(8,128)(2,1)S(1)}, u32[]{:S(2)}, u32[]{:S(2)}) collective-permute-start(bf16[512,128]{1,0:T(8,128)(2,1)S(1)} %get-tuple-element.33), channel_id=1, source_target_pairs={{0,3},{1,0},{2,1},{3,2},{4,7},{5,4},{6,5},{7,6},{8,11},{9,8},{10,9... | collective-permute-start | bytes 393224 | tf_op jit(solution)/shard_map/ppermute | solution.py:14
  8.9 2.4 %convolution_convert_fusion = bf16[512,512]{0,1:T(8,128)(2,1)} fusion(bf16[1,512,512]{2,1,0:T(8,128)(2,1)} %param.11, bf16[512,512]{1,0:T(8,128)(2,1)S(1)} %copy-done.3, f32[512]{0:T(512)S(1)} %copy-done.30), kind=kOutput, calls=%fused_computation.16 | convolution fusion | flops 270532608 | bytes 1574912 | tf_op jit(solution)/shard_map/dot_general | solution.py:59
  11.3 3.9 %all-to-all-start = ((bf16[8,64,512]{2,1,0:T(8,128)(2,1)}), bf16[8,64,512]{2,1,0:T(8,128)(2,1)S(1)}, u32[]{:S(2)}, u32[]{:S(2)}) async-start(bf16[8,64,512]{2,1,0:T(8,128)(2,1)} %bitcast.2), calls=%async_computation | async-start | bytes 1048576 | tf_op jit(solution)/shard_map/all_to_all | solution.py:19
  15.2 0.7 fusion.77
  15.9 0.7 copy-done.12
  16.6 0.1 copy.28
  16.8 0.7 fusion.105
  17.5 0.0 copy-start.8
  17.5 1.0 %fusion.55 = (bf16[512,128]{1,0:T(8,128)(2,1)}, bf16[512,128]{1,0:T(8,128)(2,1)}, bf16[512,128]{1,0:T(8,128)(2,1)}) fusion(bf16[512,128]{1,0:T(8,128)(2,1)S(1)} %collective-permute-done, bf16[512,128]{1,0:T(8,128)(2,1)S(1)} %collective-permute-done.1, bf16[512,128]{1,0:T(8,128)(2,1)S(1)} %collective-permute-done.2, f32[128]{0:T(128)S(1)} %get-tuple-element.50, ...), kind=kLoop, calls=%fused_computation.106 | loop fusion | flops 1835008 | bytes 923652 | tf_op jit(solution)/shard_map/convert_element_type | solution.py:67
  18.5 1.9 %collective-permute-start.3 = (bf16[512,128]{1,0:T(8,128)(2,1)}, bf16[512,128]{1,0:T(8,128)(2,1)}, u32[]{:S(2)}, u32[]{:S(2)}) collective-permute-start(bf16[512,128]{1,0:T(8,128)(2,1)} %get-tuple-element.24), channel_id=1, source_target_pairs={{0,1},{1,2},{2,3},{3,0},{4,5},{5,6},{6,7},{7,4},{8,9},{9,10},{10,1... | collective-permute-start | bytes 393224 | tf_op jit(solution)/shard_map/ppermute | solution.py:14
  20.4 1.6 %collective-permute-start.4 = (bf16[512,128]{1,0:T(8,128)(2,1)}, bf16[512,128]{1,0:T(8,128)(2,1)}, u32[]{:S(2)}, u32[]{:S(2)}) collective-permute-start(bf16[512,128]{1,0:T(8,128)(2,1)} %get-tuple-element.25), channel_id=1, source_target_pairs={{0,2},{1,3},{2,0},{3,1},{4,6},{5,7},{6,4},{7,5},{8,10},{9,11},{10,... | collective-permute-start | bytes 393224 | tf_op jit(solution)/shard_map/ppermute | solution.py:14
  22.1 0.7 collective-permute-start.5
  22.8 2.1 %all-to-all-done = bf16[8,64,512]{2,1,0:T(8,128)(2,1)S(1)} async-done(((bf16[8,64,512]{2,1,0:T(8,128)(2,1)}), bf16[8,64,512]{2,1,0:T(8,128)(2,1)S(1)}, u32[]{:S(2)}, u32[]{:S(2)}) %all-to-all-start) | async-done | bytes 524320 | tf_op jit(solution)/shard_map/all_to_all | solution.py:19
  24.9 0.4 fusion.6
  25.4 0.9 %copy.26 = bf16[8,64,512]{2,1,0:T(8,128)(2,1)} copy(bf16[8,64,512]{2,0,1:T(8,128)(2,1)S(1)} %fusion.6) | data formatting | bytes 1048576 | tf_op jit(solution)/shard_map/convert_element_type | solution.py:76
  26.3 3.5 %all-to-all-start.1 = ((bf16[8,64,512]{2,1,0:T(8,128)(2,1)}), bf16[8,64,512]{2,1,0:T(8,128)(2,1)S(1)}, u32[]{:S(2)}, u32[]{:S(2)}) async-start(bf16[8,64,512]{2,1,0:T(8,128)(2,1)} %copy.26), calls=%async_computation.1 | async-start | bytes 1048576 | tf_op jit(solution)/shard_map/all_to_all | solution.py:19
  29.9 0.8 copy-done.9
  30.7 0.1 fusion.76
  30.9 0.9 %constant_dynamic-update-slice_fusion.2 = bf16[512,512]{1,0:T(8,128)(2,1)S(1)} fusion(bf16[512,512]{1,0:T(8,128)(2,1)S(1)} %fusion.76, bf16[512,128]{1,0:T(8,128)(2,1)} %collective-permute-done.3, s32[]{:T(128)S(6)} %select_n.80), kind=kLoop, calls=%fused_computation.165 | loop fusion | bytes 262148 | tf_op jit(solution)/shard_map/dynamic_update_slice | solution.py:33
  31.8 0.5 collective-permute-done.4
  32.3 0.9 %constant_dynamic-update-slice_fusion.1 = bf16[512,512]{1,0:T(8,128)(2,1)S(1)} fusion(bf16[512,512]{1,0:T(8,128)(2,1)S(1)} %constant_dynamic-update-slice_fusion.2, bf16[512,128]{1,0:T(8,128)(2,1)} %collective-permute-done.4, s32[]{:T(128)S(6)} %select_n.82), kind=kLoop, calls=%fused_computation.160 | loop fusion | bytes 262148 | tf_op jit(solution)/shard_map/dynamic_update_slice | solution.py:33
  33.2 0.9 %constant_dynamic-update-slice_fusion = bf16[512,512]{1,0:T(8,128)(2,1)S(1)} fusion(bf16[512,512]{1,0:T(8,128)(2,1)S(1)} %constant_dynamic-update-slice_fusion.1, bf16[512,128]{1,0:T(8,128)(2,1)} %collective-permute-done.5, s32[]{:T(128)S(6)} %select_n.84), kind=kLoop, calls=%fused_computation.155 | loop fusion | bytes 262148 | tf_op jit(solution)/shard_map/dynamic_update_slice | solution.py:33
  34.2 5.3 %all-to-all-done.1 = bf16[8,64,512]{2,1,0:T(8,128)(2,1)S(1)} async-done(((bf16[8,64,512]{2,1,0:T(8,128)(2,1)}), bf16[8,64,512]{2,1,0:T(8,128)(2,1)S(1)}, u32[]{:S(2)}, u32[]{:S(2)}) %all-to-all-start.1) | async-done | bytes 524320 | tf_op jit(solution)/shard_map/all_to_all | solution.py:19
  39.5 0.4 fusion.32
  39.9 1.1 %multiply_convert_fusion = (bf16[512,512]{1,0:T(8,128)(2,1)S(1)}, bf16[512,512]{1,0:T(8,128)(2,1)S(1)}) fusion(bf16[512,512]{1,0:T(8,128)(2,1)S(1)} %constant_dynamic-update-slice_fusion, bf16[512,512]{1,0:T(8,128)(2,1)S(1)} %fusion.32, bf16[1,512,512]{2,1,0:T(8,128)(2,1)S(1)} %copy-done), kind=kOutput, calls=%fused_computation.51 | convolution fusion | flops 274464768 | bytes 2621440 | tf_op jit(solution)/shard_map/dot_general | solution.py:80
  41.0 1.6 %fusion.23 = (bf16[512,512]{1,0:T(8,128)(2,1)}, bf16[512,512]{1,0:T(8,128)(2,1)}) fusion(bf16[512,512]{1,0:T(8,128)(2,1)S(1)} %copy-done.4, f32[512]{0:T(512)S(1)} %copy-done.13, bf16[512,512]{1,0:T(8,128)(2,1)S(1)} %get-tuple-element.19, bf16[1,512,512]{2,1,0:T(8,128)(2,1)S(1)} %copy-done, bf16[512,512]{1,0:T(8,128)(2,1)S(1)} %copy-done.1), kind=kOutput, calls=%fused_computation.40 | convolution fusion | flops 271319040 | bytes 3147776 | tf_op jit(solution)/shard_map/dot_general | solution.py:94
  42.6 3.5 %all-to-all-start.2 = ((bf16[8,64,512]{2,1,0:T(8,128)(2,1)}), bf16[8,64,512]{2,1,0:T(8,128)(2,1)S(1)}, u32[]{:S(2)}, u32[]{:S(2)}) async-start(bf16[8,64,512]{2,1,0:T(8,128)(2,1)} %bitcast.22), calls=%async_computation.2 | async-start | bytes 1048576 | tf_op jit(solution)/shard_map/all_to_all | solution.py:19
  46.1 0.1 constant_dynamic-slice_fusion.13
  46.2 0.7 collective-permute-start.7
  47.0 0.3 collective-permute-start.8
  47.3 2.8 %collective-permute-start.9 = (bf16[512,128]{1,0:T(8,128)(2,1)S(1)}, bf16[512,128]{1,0:T(8,128)(2,1)S(1)}, u32[]{:S(2)}, u32[]{:S(2)}) collective-permute-start(bf16[512,128]{1,0:T(8,128)(2,1)S(1)} %get-tuple-element.29), channel_id=1, source_target_pairs={{0,3},{1,0},{2,1},{3,2},{4,7},{5,4},{6,5},{7,6},{8,11},{9,8},{10,9... | collective-permute-start | bytes 393224 | tf_op jit(solution)/shard_map/ppermute | solution.py:14
  50.1 1.3 %fusion.112 = bf16[512,512]{1,0:T(8,128)(2,1)} fusion(bf16[512,512]{1,0:T(8,128)(2,1)S(1)} %fusion.32, bf16[512,512]{1,0:T(8,128)(2,1)S(1)} %copy-done.33), kind=kOutput, calls=%fused_computation.211 | convolution fusion | flops 268435456 | bytes 1572864 | tf_op jit(solution)/shard_map/dot_general | solution.py:96
  51.4 4.4 %all-to-all-done.2 = bf16[8,64,512]{2,1,0:T(8,128)(2,1)S(1)} async-done(((bf16[8,64,512]{2,1,0:T(8,128)(2,1)}), bf16[8,64,512]{2,1,0:T(8,128)(2,1)S(1)}, u32[]{:S(2)}, u32[]{:S(2)}) %all-to-all-start.2) | async-done | bytes 524320 | tf_op jit(solution)/shard_map/all_to_all | solution.py:19
  55.8 0.4 fusion.7
  56.2 0.9 %copy.29 = bf16[8,64,512]{2,1,0:T(8,128)(2,1)} copy(bf16[8,64,512]{2,0,1:T(8,128)(2,1)S(1)} %fusion.7) | data formatting | bytes 1048576 | tf_op jit(solution)/shard_map/convert_element_type | solution.py:103
  57.2 3.5 %all-to-all-start.3 = ((bf16[8,64,512]{2,1,0:T(8,128)(2,1)}), bf16[8,64,512]{2,1,0:T(8,128)(2,1)S(1)}, u32[]{:S(2)}, u32[]{:S(2)}) async-start(bf16[8,64,512]{2,1,0:T(8,128)(2,1)} %copy.29), calls=%async_computation.3 | async-start | bytes 1048576 | tf_op jit(solution)/shard_map/all_to_all | solution.py:19
  60.9 0.5 copy-done.14
  61.3 0.1 copy-done.15
  61.5 0.9 %fusion.71 = (bf16[512,128]{1,0:T(8,128)(2,1)}, bf16[512,128]{1,0:T(8,128)(2,1)}, bf16[512,128]{1,0:T(8,128)(2,1)}) fusion(bf16[512,128]{1,0:T(8,128)(2,1)S(1)} %collective-permute-done.7, bf16[512,128]{1,0:T(8,128)(2,1)S(1)} %collective-permute-done.8, bf16[512,128]{1,0:T(8,128)(2,1)S(1)} %collective-permute-done.9, f32[128]{0:T(128)S(1)} %get-tuple-element.36, ...), kind=kLoop, calls=%fused_computation.122 | loop fusion | flops 1835008 | bytes 923652 | tf_op jit(solution)/shard_map/convert_element_type | solution.py:88
  62.4 1.6 %collective-permute-start.10 = (bf16[512,128]{1,0:T(8,128)(2,1)}, bf16[512,128]{1,0:T(8,128)(2,1)}, u32[]{:S(2)}, u32[]{:S(2)}) collective-permute-start(bf16[512,128]{1,0:T(8,128)(2,1)} %get-tuple-element.21), channel_id=1, source_target_pairs={{0,1},{1,2},{2,3},{3,0},{4,5},{5,6},{6,7},{7,4},{8,9},{9,10},{10,1... | collective-permute-start | bytes 393224 | tf_op jit(solution)/shard_map/ppermute | solution.py:14
  64.0 0.3 collective-permute-start.11
  64.3 2.1 %collective-permute-start.12 = (bf16[512,128]{1,0:T(8,128)(2,1)}, bf16[512,128]{1,0:T(8,128)(2,1)}, u32[]{:S(2)}, u32[]{:S(2)}) collective-permute-start(bf16[512,128]{1,0:T(8,128)(2,1)} %get-tuple-element.20), channel_id=1, source_target_pairs={{0,3},{1,0},{2,1},{3,2},{4,7},{5,4},{6,5},{7,6},{8,11},{9,8},{10,9... | collective-permute-start | bytes 393224 | tf_op jit(solution)/shard_map/ppermute | solution.py:14
  66.4 0.8 fusion.59
  67.2 3.2 %all-to-all-done.3 = bf16[8,64,512]{2,1,0:T(8,128)(2,1)S(1)} async-done(((bf16[8,64,512]{2,1,0:T(8,128)(2,1)}), bf16[8,64,512]{2,1,0:T(8,128)(2,1)S(1)}, u32[]{:S(2)}, u32[]{:S(2)}) %all-to-all-start.3) | async-done | bytes 524320 | tf_op jit(solution)/shard_map/all_to_all | solution.py:19
  70.4 0.6 fusion.109
  71.0 0.2 copy-done.6
  71.2 0.8 dynamic-slice_convert_fusion.1
  72.0 0.7 collective-permute-start.6
  72.7 0.3 collective-permute-start.13
  73.0 3.6 %all-to-all-start.4 = ((bf16[8,64,512]{2,1,0:T(8,128)(2,1)}), bf16[8,64,512]{2,1,0:T(8,128)(2,1)S(1)}, u32[]{:S(2)}, u32[]{:S(2)}) async-start(bf16[8,64,512]{2,1,0:T(8,128)(2,1)} %bitcast.42), calls=%async_computation.4 | async-start | bytes 1048576 | tf_op jit(solution)/shard_map/all_to_all | solution.py:19
  76.7 3.2 %fusion.3 = bf16[512,512]{1,0:T(8,128)(2,1)} fusion(bf16[512,512]{1,0:T(8,128)(2,1)S(1)} %bitcast.112, bf16[512,512]{1,0:T(8,128)(2,1)} %get-tuple-element.67, bf16[512,512]{1,0:T(8,128)(2,1)S(1)} %copy-done.5, bf16[512,512]{1,0:T(8,128)(2,1)S(1)} %bitcast.110, bf16[1,512,512]{2,1,0:T(8,128)(2,1)} %param.11, f32[512]{0:T(512)S(1)} %copy-done.13, ...), kind=kOutput, calls=%fused_computation.20 | convolution fusion | flops 274726912 | bytes 3149824 | tf_op jit(solution)/shard_map/dot_general | solution.py:126
  79.9 2.9 %collective-permute-start.14 = (bf16[128,512]{1,0:T(8,128)(2,1)S(1)}, bf16[128,512]{1,0:T(8,128)(2,1)S(1)}, u32[]{:S(2)}, u32[]{:S(2)}) collective-permute-start(bf16[128,512]{1,0:T(8,128)(2,1)S(1)} %get-tuple-element.27), channel_id=1, source_target_pairs={{0,3},{1,0},{2,1},{3,2},{4,7},{5,4},{6,5},{7,6},{8,11},{9,8},{10,9... | collective-permute-start | bytes 393224 | tf_op jit(solution)/shard_map/ppermute | solution.py:14
  82.8 0.1 fusion.72
  82.9 1.0 %fusion.73 = bf16[512,512]{1,0:T(8,128)(2,1)S(1)} fusion(bf16[512,512]{1,0:T(8,128)(2,1)S(1)} %fusion.72, s32[]{:T(128)S(6)} %select_n.80, bf16[512,128]{1,0:T(8,128)(2,1)} %collective-permute-done.10, bf16[512,512]{1,0:T(8,128)(2,1)S(1)} %fusion.32), kind=kLoop, calls=%fused_computation.133 | loop fusion | flops 262144 | bytes 393220 | tf_op jit(solution)/shard_map/dynamic_update_slice | solution.py:33
  83.8 1.0 %fusion.74 = bf16[512,512]{1,0:T(8,128)(2,1)S(1)} fusion(bf16[512,512]{1,0:T(8,128)(2,1)S(1)} %fusion.73, s32[]{:T(128)S(6)} %select_n.82, bf16[512,128]{1,0:T(8,128)(2,1)} %collective-permute-done.11, bf16[512,512]{1,0:T(8,128)(2,1)S(1)} %fusion.32), kind=kLoop, calls=%fused_computation.134 | loop fusion | flops 262144 | bytes 393220 | tf_op jit(solution)/shard_map/dynamic_update_slice | solution.py:33
  84.8 1.0 %fusion.75 = bf16[512,512]{1,0:T(8,128)(2,1)S(1)} fusion(bf16[512,512]{1,0:T(8,128)(2,1)S(1)} %fusion.74, s32[]{:T(128)S(6)} %select_n.84, bf16[512,128]{1,0:T(8,128)(2,1)} %collective-permute-done.12, bf16[512,512]{1,0:T(8,128)(2,1)S(1)} %fusion.32), kind=kLoop, calls=%fused_computation.135 | loop fusion | flops 262144 | bytes 393220 | tf_op jit(solution)/shard_map/dynamic_update_slice | solution.py:33
  85.8 1.6 %collective-permute-done.13 = bf16[128,512]{1,0:T(8,128)(2,1)} collective-permute-done((bf16[128,512]{1,0:T(8,128)(2,1)}, bf16[128,512]{1,0:T(8,128)(2,1)}, u32[]{:S(2)}, u32[]{:S(2)}) %collective-permute-start.13) | collective-permute-done | bytes 131104 | tf_op jit(solution)/shard_map/ppermute | solution.py:14
  87.4 2.1 %collective-permute-done.14 = bf16[128,512]{1,0:T(8,128)(2,1)S(1)} collective-permute-done((bf16[128,512]{1,0:T(8,128)(2,1)S(1)}, bf16[128,512]{1,0:T(8,128)(2,1)S(1)}, u32[]{:S(2)}, u32[]{:S(2)}) %collective-permute-start.14) | collective-permute-done | bytes 131104 | tf_op jit(solution)/shard_map/ppermute | solution.py:14
  89.5 1.7 %add_bitcast_fusion = f32[1,128,512]{2,1,0:T(8,128)} fusion(bf16[128,512]{1,0:T(8,128)(2,1)S(1)} %collective-permute-done.14, bf16[128,512]{1,0:T(8,128)(2,1)} %collective-permute-done.13, bf16[128,512]{1,0:T(8,128)(2,1)S(1)} %collective-permute-done.6, bf16[512,512]{1,0:T(8,128)(2,1)} %copy-done.10, s32[]{:T(128)S(6)} %select_n.64), kind=kLoop, calls=%fused_computation.123 | loop fusion | flops 458752 | bytes 786436 | tf_op jit(solution)/shard_map/broadcast_in_dim | solution.py:114
  91.2 0.7 convert_reduce_fusion
  (76 shorter events, 0.2 us)
Async XLA Ops:
  0.6 39.2 %copy-start = (bf16[1,512,512]{2,1,0:T(8,128)(2,1)S(1)}, bf16[1,512,512]{2,1,0:T(8,128)(2,1)}, u32[]{:S(2)}) copy-start(bf16[1,512,512]{2,1,0:T(8,128)(2,1)} %param.13) | copy-start | bytes 1572868
  0.6 8.3 %copy-start.3 = (bf16[512,512]{1,0:T(8,128)(2,1)S(1)}, bf16[512,512]{1,0:T(8,128)(2,1)}, u32[]{:S(2)}) copy-start(bf16[512,512]{1,0:T(8,128)(2,1)} %param.8) | copy-start | bytes 1572868
  1.9 7.0 %copy-start.30 = (f32[512]{0:T(512)S(1)}, f32[512]{0:T(512)}, u32[]{:S(2)}) copy-start(f32[512]{0:T(512)} %param.9) | copy-start | bytes 6148
  1.9 15.6 %collective-permute-start = (bf16[512,128]{1,0:T(8,128)(2,1)S(1)}, bf16[512,128]{1,0:T(8,128)(2,1)S(1)}, u32[]{:S(2)}, u32[]{:S(2)}) collective-permute-start(bf16[512,128]{1,0:T(8,128)(2,1)S(1)} %get-tuple-element.32), channel_id=1, source_target_pairs={{0,1},{1,2},{2,3},{3,0},{4,5},{5,6},{6,7},{7,4},{8,9},{9,10},{10,1... | collective-permute-start | bytes 393224 | tf_op jit(solution)/shard_map/ppermute | solution.py:14
  5.0 12.5 %collective-permute-start.1 = (bf16[512,128]{1,0:T(8,128)(2,1)S(1)}, bf16[512,128]{1,0:T(8,128)(2,1)S(1)}, u32[]{:S(2)}, u32[]{:S(2)}) collective-permute-start(bf16[512,128]{1,0:T(8,128)(2,1)S(1)} %get-tuple-element.34), channel_id=1, source_target_pairs={{0,2},{1,3},{2,0},{3,1},{4,6},{5,7},{6,4},{7,5},{8,10},{9,11},{10,... | collective-permute-start | bytes 393224 | tf_op jit(solution)/shard_map/ppermute | solution.py:14
  7.6 9.9 %collective-permute-start.2 = (bf16[512,128]{1,0:T(8,128)(2,1)S(1)}, bf16[512,128]{1,0:T(8,128)(2,1)S(1)}, u32[]{:S(2)}, u32[]{:S(2)}) collective-permute-start(bf16[512,128]{1,0:T(8,128)(2,1)S(1)} %get-tuple-element.33), channel_id=1, source_target_pairs={{0,3},{1,0},{2,1},{3,2},{4,7},{5,4},{6,5},{7,6},{8,11},{9,8},{10,9... | collective-permute-start | bytes 393224 | tf_op jit(solution)/shard_map/ppermute | solution.py:14
  11.3 6.2 %copy-start.1 = (bf16[512,512]{1,0:T(8,128)(2,1)S(1)}, bf16[512,512]{1,0:T(8,128)(2,1)}, u32[]{:S(2)}) copy-start(bf16[512,512]{1,0:T(8,128)(2,1)} %param.15) | copy-start | bytes 1572868
  11.3 13.6 %all-to-all-start = ((bf16[8,64,512]{2,1,0:T(8,128)(2,1)}), bf16[8,64,512]{2,1,0:T(8,128)(2,1)S(1)}, u32[]{:S(2)}, u32[]{:S(2)}) async-start(bf16[8,64,512]{2,1,0:T(8,128)(2,1)} %bitcast.2), calls=%async_computation | async-start | bytes 1048576 | tf_op jit(solution)/shard_map/all_to_all | solution.py:19
  15.9 0.7 copy-start.12
  17.5 1.0 %copy-start.8 = (bf16[512,128]{1,0:T(8,128)(2,1)}, bf16[512,128]{1,0:T(8,128)(2,1)S(1)}, u32[]{:S(2)}) copy-start(bf16[512,128]{1,0:T(8,128)(2,1)S(1)} %collective-permute-done.2) | copy-start | bytes 393220
  18.5 12.4 %collective-permute-start.3 = (bf16[512,128]{1,0:T(8,128)(2,1)}, bf16[512,128]{1,0:T(8,128)(2,1)}, u32[]{:S(2)}, u32[]{:S(2)}) collective-permute-start(bf16[512,128]{1,0:T(8,128)(2,1)} %get-tuple-element.24), channel_id=1, source_target_pairs={{0,1},{1,2},{2,3},{3,0},{4,5},{5,6},{6,7},{7,4},{8,9},{9,10},{10,1... | collective-permute-start | bytes 393224 | tf_op jit(solution)/shard_map/ppermute | solution.py:14
  20.4 11.8 %collective-permute-start.4 = (bf16[512,128]{1,0:T(8,128)(2,1)}, bf16[512,128]{1,0:T(8,128)(2,1)}, u32[]{:S(2)}, u32[]{:S(2)}) collective-permute-start(bf16[512,128]{1,0:T(8,128)(2,1)} %get-tuple-element.25), channel_id=1, source_target_pairs={{0,2},{1,3},{2,0},{3,1},{4,6},{5,7},{6,4},{7,5},{8,10},{9,11},{10,... | collective-permute-start | bytes 393224 | tf_op jit(solution)/shard_map/ppermute | solution.py:14
  22.1 11.1 %collective-permute-start.5 = (bf16[512,128]{1,0:T(8,128)(2,1)}, bf16[512,128]{1,0:T(8,128)(2,1)}, u32[]{:S(2)}, u32[]{:S(2)}) collective-permute-start(bf16[512,128]{1,0:T(8,128)(2,1)} %get-tuple-element.23), channel_id=1, source_target_pairs={{0,3},{1,0},{2,1},{3,2},{4,7},{5,4},{6,5},{7,6},{8,11},{9,8},{10,9... | collective-permute-start | bytes 393224 | tf_op jit(solution)/shard_map/ppermute | solution.py:14
  26.3 13.2 %all-to-all-start.1 = ((bf16[8,64,512]{2,1,0:T(8,128)(2,1)}), bf16[8,64,512]{2,1,0:T(8,128)(2,1)S(1)}, u32[]{:S(2)}, u32[]{:S(2)}) async-start(bf16[8,64,512]{2,1,0:T(8,128)(2,1)} %copy.26), calls=%async_computation.1 | async-start | bytes 1048576 | tf_op jit(solution)/shard_map/all_to_all | solution.py:19
  29.8 0.9 copy-start.9
  29.8 0.9 copy-start.27
  29.8 0.9 copy-start.28
  29.8 0.9 copy-start.29
  33.2 6.3 %copy-start.13 = (f32[512]{0:T(512)S(1)}, f32[512]{0:T(512)}, u32[]{:S(2)}) copy-start(f32[512]{0:T(512)} %param.10) | copy-start | bytes 6148
  39.9 1.2 %copy-start.4 = (bf16[512,512]{1,0:T(8,128)(2,1)S(1)}, bf16[512,512]{1,0:T(8,128)(2,1)}, u32[]{:S(2)}) copy-start(bf16[512,512]{1,0:T(8,128)(2,1)} %param.8) | copy-start | bytes 1572868
  41.0 1.6 %copy-start.32 = (bf16[512,512]{1,0:T(8,128)(2,1)}, bf16[512,512]{1,0:T(8,128)(2,1)S(1)}, u32[]{:S(2)}) copy-start(bf16[512,512]{1,0:T(8,128)(2,1)S(1)} %get-tuple-element.19) | copy-start | bytes 1572868
  42.6 13.2 %all-to-all-start.2 = ((bf16[8,64,512]{2,1,0:T(8,128)(2,1)}), bf16[8,64,512]{2,1,0:T(8,128)(2,1)S(1)}, u32[]{:S(2)}, u32[]{:S(2)}) async-start(bf16[8,64,512]{2,1,0:T(8,128)(2,1)} %bitcast.22), calls=%async_computation.2 | async-start | bytes 1048576 | tf_op jit(solution)/shard_map/all_to_all | solution.py:19
  46.1 4.0 %copy-start.33 = (bf16[512,512]{1,0:T(8,128)(2,1)S(1)}, bf16[512,512]{1,0:T(8,128)(2,1)}, u32[]{:S(2)}) copy-start(bf16[512,512]{1,0:T(8,128)(2,1)} %copy-done.32) | copy-start | bytes 1572868
  46.2 14.5 %collective-permute-start.7 = (bf16[512,128]{1,0:T(8,128)(2,1)S(1)}, bf16[512,128]{1,0:T(8,128)(2,1)S(1)}, u32[]{:S(2)}, u32[]{:S(2)}) collective-permute-start(bf16[512,128]{1,0:T(8,128)(2,1)S(1)} %get-tuple-element.31), channel_id=1, source_target_pairs={{0,1},{1,2},{2,3},{3,0},{4,5},{5,6},{6,7},{7,4},{8,9},{9,10},{10,1... | collective-permute-start | bytes 393224 | tf_op jit(solution)/shard_map/ppermute | solution.py:14
  47.0 13.8 %collective-permute-start.8 = (bf16[512,128]{1,0:T(8,128)(2,1)S(1)}, bf16[512,128]{1,0:T(8,128)(2,1)S(1)}, u32[]{:S(2)}, u32[]{:S(2)}) collective-permute-start(bf16[512,128]{1,0:T(8,128)(2,1)S(1)} %get-tuple-element.30), channel_id=1, source_target_pairs={{0,2},{1,3},{2,0},{3,1},{4,6},{5,7},{6,4},{7,5},{8,10},{9,11},{10,... | collective-permute-start | bytes 393224 | tf_op jit(solution)/shard_map/ppermute | solution.py:14
  47.3 13.4 %collective-permute-start.9 = (bf16[512,128]{1,0:T(8,128)(2,1)S(1)}, bf16[512,128]{1,0:T(8,128)(2,1)S(1)}, u32[]{:S(2)}, u32[]{:S(2)}) collective-permute-start(bf16[512,128]{1,0:T(8,128)(2,1)S(1)} %get-tuple-element.29), channel_id=1, source_target_pairs={{0,3},{1,0},{2,1},{3,2},{4,7},{5,4},{6,5},{7,6},{8,11},{9,8},{10,9... | collective-permute-start | bytes 393224 | tf_op jit(solution)/shard_map/ppermute | solution.py:14
  57.2 3.6 %copy-start.17 = (f32[128]{0:T(128)S(1)}, f32[128]{0:T(128)}, u32[]{:S(2)}) copy-start(f32[128]{0:T(128)} %get-tuple-element.40) | copy-start | bytes 1540
  57.2 3.6 %copy-start.18 = (f32[128]{0:T(128)S(1)}, f32[128]{0:T(128)}, u32[]{:S(2)}) copy-start(f32[128]{0:T(128)} %get-tuple-element.41) | copy-start | bytes 1540
  57.2 3.6 %copy-start.19 = (f32[128]{0:T(128)S(1)}, f32[128]{0:T(128)}, u32[]{:S(2)}) copy-start(f32[128]{0:T(128)} %get-tuple-element.42) | copy-start | bytes 1540
  57.2 3.6 %copy-start.20 = (f32[128]{0:T(128)S(1)}, f32[128]{0:T(128)}, u32[]{:S(2)}) copy-start(f32[128]{0:T(128)} %get-tuple-element.43) | copy-start | bytes 1540
  57.2 3.6 %copy-start.21 = (f32[128]{0:T(128)S(1)}, f32[128]{0:T(128)}, u32[]{:S(2)}) copy-start(f32[128]{0:T(128)} %get-tuple-element.44) | copy-start | bytes 1540
  57.2 3.6 %copy-start.22 = (f32[128]{0:T(128)S(1)}, f32[128]{0:T(128)}, u32[]{:S(2)}) copy-start(f32[128]{0:T(128)} %get-tuple-element.45) | copy-start | bytes 1540
  57.2 3.6 %copy-start.23 = (f32[128]{0:T(128)S(1)}, f32[128]{0:T(128)}, u32[]{:S(2)}) copy-start(f32[128]{0:T(128)} %get-tuple-element.46) | copy-start | bytes 1540
  57.2 13.2 %all-to-all-start.3 = ((bf16[8,64,512]{2,1,0:T(8,128)(2,1)}), bf16[8,64,512]{2,1,0:T(8,128)(2,1)S(1)}, u32[]{:S(2)}, u32[]{:S(2)}) async-start(bf16[8,64,512]{2,1,0:T(8,128)(2,1)} %copy.29), calls=%async_computation.3 | async-start | bytes 1048576 | tf_op jit(solution)/shard_map/all_to_all | solution.py:19
  60.8 0.6 copy-start.14
  60.8 0.7 copy-start.15
  60.8 0.7 copy-start.16
  61.5 5.0 %copy-start.24 = (f32[128]{0:T(128)S(1)}, f32[128]{0:T(128)}, u32[]{:S(2)}) copy-start(f32[128]{0:T(128)} %get-tuple-element.47) | copy-start | bytes 1540
  61.5 5.0 %copy-start.25 = (f32[128]{0:T(128)S(1)}, f32[128]{0:T(128)}, u32[]{:S(2)}) copy-start(f32[128]{0:T(128)} %get-tuple-element.48) | copy-start | bytes 1540
  61.5 5.0 %copy-start.26 = (f32[128]{0:T(128)S(1)}, f32[128]{0:T(128)}, u32[]{:S(2)}) copy-start(f32[128]{0:T(128)} %get-tuple-element.49) | copy-start | bytes 1540
  62.4 8.0 %copy-start.5 = (bf16[512,512]{1,0:T(8,128)(2,1)S(1)}, bf16[512,512]{1,0:T(8,128)(2,1)}, u32[]{:S(2)}) copy-start(bf16[512,512]{1,0:T(8,128)(2,1)} %param.8) | copy-start | bytes 1572868
  62.4 17.5 %collective-permute-start.10 = (bf16[512,128]{1,0:T(8,128)(2,1)}, bf16[512,128]{1,0:T(8,128)(2,1)}, u32[]{:S(2)}, u32[]{:S(2)}) collective-permute-start(bf16[512,128]{1,0:T(8,128)(2,1)} %get-tuple-element.21), channel_id=1, source_target_pairs={{0,1},{1,2},{2,3},{3,0},{4,5},{5,6},{6,7},{7,4},{8,9},{9,10},{10,1... | collective-permute-start | bytes 393224 | tf_op jit(solution)/shard_map/ppermute | solution.py:14
  64.0 18.7 %collective-permute-start.11 = (bf16[512,128]{1,0:T(8,128)(2,1)}, bf16[512,128]{1,0:T(8,128)(2,1)}, u32[]{:S(2)}, u32[]{:S(2)}) collective-permute-start(bf16[512,128]{1,0:T(8,128)(2,1)} %get-tuple-element.22), channel_id=1, source_target_pairs={{0,2},{1,3},{2,0},{3,1},{4,6},{5,7},{6,4},{7,5},{8,10},{9,11},{10,... | collective-permute-start | bytes 393224 | tf_op jit(solution)/shard_map/ppermute | solution.py:14
  64.3 18.4 %collective-permute-start.12 = (bf16[512,128]{1,0:T(8,128)(2,1)}, bf16[512,128]{1,0:T(8,128)(2,1)}, u32[]{:S(2)}, u32[]{:S(2)}) collective-permute-start(bf16[512,128]{1,0:T(8,128)(2,1)} %get-tuple-element.20), channel_id=1, source_target_pairs={{0,3},{1,0},{2,1},{3,2},{4,7},{5,4},{6,5},{7,6},{8,11},{9,8},{10,9... | collective-permute-start | bytes 393224 | tf_op jit(solution)/shard_map/ppermute | solution.py:14
  66.4 4.0 %copy-start.31 = (f32[512]{0:T(512)S(1)}, f32[512]{0:T(512)}, u32[]{:S(2)}) copy-start(f32[512]{0:T(512)} %param.9) | copy-start | bytes 6148
  70.4 0.8 copy-start.6
  71.2 1.8 %copy-start.10 = (bf16[512,512]{1,0:T(8,128)(2,1)}, bf16[512,512]{1,0:T(8,128)(2,1)S(1)}, u32[]{:S(2)}) copy-start(bf16[512,512]{1,0:T(8,128)(2,1)S(1)} %fusion.109) | copy-start | bytes 1572868
  72.0 10.7 %collective-permute-start.6 = (bf16[128,512]{1,0:T(8,128)(2,1)}, bf16[128,512]{1,0:T(8,128)(2,1)S(1)}, u32[]{:S(2)}, u32[]{:S(2)}) collective-permute-start(bf16[128,512]{1,0:T(8,128)(2,1)} %get-tuple-element.28), channel_id=1, source_target_pairs={{0,1},{1,2},{2,3},{3,0},{4,5},{5,6},{6,7},{7,4},{8,9},{9,10},{10,1... | collective-permute-start | bytes 393224 | tf_op jit(solution)/shard_map/ppermute | solution.py:14
  72.7 14.7 %collective-permute-start.13 = (bf16[128,512]{1,0:T(8,128)(2,1)}, bf16[128,512]{1,0:T(8,128)(2,1)}, u32[]{:S(2)}, u32[]{:S(2)}) collective-permute-start(bf16[128,512]{1,0:T(8,128)(2,1)} %get-tuple-element.26), channel_id=1, source_target_pairs={{0,2},{1,3},{2,0},{3,1},{4,6},{5,7},{6,4},{7,5},{8,10},{9,11},{10,... | collective-permute-start | bytes 393224 | tf_op jit(solution)/shard_map/ppermute | solution.py:14
  73.0 3.6 %copy-start.7 = (bf16[8,64,512]{2,1,0:T(8,128)(2,1)S(1)}, bf16[8,64,512]{2,1,0:T(8,128)(2,1)}, u32[]{:S(2)}) copy-start(bf16[8,64,512]{2,1,0:T(8,128)(2,1)} %copy-done.6) | copy-start | bytes 1572868
  73.0 18.2 %all-to-all-start.4 = ((bf16[8,64,512]{2,1,0:T(8,128)(2,1)}), bf16[8,64,512]{2,1,0:T(8,128)(2,1)S(1)}, u32[]{:S(2)}, u32[]{:S(2)}) async-start(bf16[8,64,512]{2,1,0:T(8,128)(2,1)} %bitcast.42), calls=%async_computation.4 | async-start | bytes 1048576 | tf_op jit(solution)/shard_map/all_to_all | solution.py:19
  79.9 2.9 %copy-start.11 = (bf16[512,128]{1,0:T(8,128)(2,1)S(1)}, bf16[512,128]{1,0:T(8,128)(2,1)}, u32[]{:S(2)}) copy-start(bf16[512,128]{1,0:T(8,128)(2,1)} %fusion.59) | copy-start | bytes 393220
  79.9 9.6 %collective-permute-start.14 = (bf16[128,512]{1,0:T(8,128)(2,1)S(1)}, bf16[128,512]{1,0:T(8,128)(2,1)S(1)}, u32[]{:S(2)}, u32[]{:S(2)}) collective-permute-start(bf16[128,512]{1,0:T(8,128)(2,1)S(1)} %get-tuple-element.27), channel_id=1, source_target_pairs={{0,3},{1,0},{2,1},{3,2},{4,7},{5,4},{6,5},{7,6},{8,11},{9,8},{10,9... | collective-permute-start | bytes 393224 | tf_op jit(solution)/shard_map/ppermute | solution.py:14
  85.8 6.2 %copy-start.2 = (bf16[512,512]{1,0:T(8,128)(2,1)}, bf16[512,512]{1,0:T(8,128)(2,1)S(1)}, u32[]{:S(2)}) copy-start(bf16[512,512]{1,0:T(8,128)(2,1)S(1)} %fusion.75) | copy-start | bytes 1572868
